TPU v7x, 32 devices: a whole 2x2x4 slice. The times are simulated.
32 devices in a mesh: dp: 16 (over z, y, x), tensor: 2 (over core).
Axes of the slice: x: 2, y: 2, z: 4, core: 2. Of those that a mesh axis runs over, the one named last changes fastest.
Arguments:
- tokens: bfloat16 [2048, 5120], P('dp', 'tensor'), may hold values from -6 to 6
- cotangent: bfloat16 [2048, 5120], P('dp', 'tensor'), may hold values from -6 to 6
- w_gate: bfloat16 [2, 27, 5, 128, 128], P('tensor'), may hold values from -0.25 to 0.25
- w_up: bfloat16 [2, 27, 5, 128, 128], P('tensor'), may hold values from -0.25 to 0.25
- w_down: bfloat16 [2, 27, 5, 128, 128], P('tensor'), may hold values from -0.25 to 0.25
- col_index: int32 [54, 5], P('tensor'), may hold values from 0 to 39, as said below
- row_count: int32 [54], P('tensor'), may hold values from 2 to 5, as said below
- adam_m: float32 [3, 2, 17280, 128], P(None, 'tensor', 'dp'), may hold values from -4 to 4
- adam_v: float32 [3, 2, 17280, 128], P(None, 'tensor', 'dp'), may hold values from 0.02 to 0.5
Outputs:
- token_grads: bfloat16 [2048, 5120], P('dp', 'tensor')
- first_moment: float32 [3, 2, 17280, 128], P(None, 'tensor', 'dp')
- second_moment: float32 [3, 2, 17280, 128], P(None, 'tensor', 'dp')
- update_dir: float32 [3, 2, 17280, 128], P(None, 'tensor', 'dp')
Inputs may be any that keep to these rules, and one draw needn't show every extreme that they name: `col_index`: in each row the first row_count entries are distinct width blocks. `row_count`: some hidden block has exactly 5 live slots.
All inputs are finite; a program needn't handle non-finite values.
Results may differ from a plain program's by a relative error of at most 0.0085.
Values may be sent and summed in bfloat16 or wider, within the bound.
No kernel may reach another device: no remote copies, remote signals or barrier semaphores. Data moves between devices by JAX's collectives and lax.ppermute only.
A program may use at most 192 MiB of HBM per device.

v0:
```python
import math

import jax
import jax.numpy as jnp
from jax import lax
from jax.sharding import PartitionSpec as P

D = 5120
BLK = 128


def shards(tokens, cotangent, w_gate, w_up, w_down, col_index, row_count, adam_m, adam_v):
    full_tok, full_cot = (
        lax.all_gather(tokens, "tensor", axis=1, tiled=True),
        lax.all_gather(cotangent, "tensor", axis=1, tiled=True),
    )
    tok_rows = full_tok.shape[0]
    gate_w = w_gate[0]
    up_w = w_up[0]
    down_w = w_down[0]
    slot_count = gate_w.shape[1]
    own_rows = gate_w.shape[0] * slot_count * BLK
    live_mask = jnp.arange(slot_count)[None, :] < row_count[:, None]
    keep_bf = live_mask.astype(jnp.bfloat16)[:, :, None, None]
    gate_eff = gate_w * keep_bf
    up_eff = up_w * keep_bf
    down_eff = down_w * keep_bf
    x_blocks = full_tok.reshape(tok_rows, D // BLK, BLK)[:, col_index]
    dy_blocks = full_cot.reshape(tok_rows, D // BLK, BLK)[:, col_index]
    gate_act = jnp.einsum("thpk,hpkj->thj", x_blocks, gate_eff, preferred_element_type=jnp.float32)
    up_act = jnp.einsum("thpk,hpkj->thj", x_blocks, up_eff, preferred_element_type=jnp.float32)
    sig_gate = jax.nn.sigmoid(gate_act)
    silu_gate = gate_act * sig_gate
    hidden = (silu_gate * up_act).astype(jnp.bfloat16)
    d_hidden = jnp.einsum("thpk,hpjk->thj", dy_blocks, down_eff, preferred_element_type=jnp.float32)
    live_f = live_mask.astype(jnp.float32)[:, :, None, None]
    grad_down = (
        jnp.einsum("thj,thpk->hpjk", hidden, dy_blocks, preferred_element_type=jnp.float32) * live_f
    )
    d_gate = (d_hidden * up_act * sig_gate * (1.0 + gate_act * (1.0 - sig_gate))).astype(
        jnp.bfloat16
    )
    d_up = (d_hidden * silu_gate).astype(jnp.bfloat16)
    grad_gate = (
        jnp.einsum("thpk,thj->hpkj", x_blocks, d_gate, preferred_element_type=jnp.float32) * live_f
    )
    grad_up = (
        jnp.einsum("thpk,thj->hpkj", x_blocks, d_up, preferred_element_type=jnp.float32) * live_f
    )
    back_term = jnp.einsum("thj,hpkj->thpk", d_gate, gate_eff, preferred_element_type=jnp.float32)
    back_term = back_term + jnp.einsum(
        "thj,hpkj->thpk", d_up, up_eff, preferred_element_type=jnp.float32
    )
    onehot = (col_index[:, :, None] == jnp.arange(D // BLK)[None, None, :]).astype(jnp.float32)
    dx_blocks = jnp.einsum("thpk,hpd->tdk", back_term, onehot, precision=lax.Precision.HIGHEST)
    dx_part = dx_blocks.reshape(tok_rows, D)
    reduced = lax.psum_scatter(
        jnp.stack([grad_gate, grad_up, grad_down]).reshape(3, 1, own_rows, BLK),
        "dp",
        scatter_dimension=2,
        tiled=True,
    )
    token_grads = lax.psum_scatter(
        dx_part.astype(jnp.bfloat16), "tensor", scatter_dimension=1, tiled=True
    )
    grad_scale = 1.0 / math.sqrt(lax.axis_size("dp") * tok_rows)
    grad_all = reduced * grad_scale
    m_new = 0.9 * adam_m + 0.1 * grad_all
    v_new = 0.95 * adam_v + 0.05 * grad_all * grad_all
    step_dir = m_new / (jnp.sqrt(v_new) + 1e-08)
    return (token_grads, m_new, v_new, step_dir)


def solution(mesh):
    in_specs = (
        P("dp", "tensor"),
        P("dp", "tensor"),
        P("tensor", None, None, None, None),
        P("tensor", None, None, None, None),
        P("tensor", None, None, None, None),
        P("tensor", None),
        P("tensor"),
        P(None, "tensor", "dp", None),
        P(None, "tensor", "dp", None),
    )
    out_specs = (
        P("dp", "tensor"),
        P(None, "tensor", "dp", None),
        P(None, "tensor", "dp", None),
        P(None, "tensor", "dp", None),
    )
    return jax.shard_map(shards, mesh=mesh, in_specs=in_specs, out_specs=out_specs, check_vma=False)
```

profile of v0, /device:TPU:0, one launch (start us, length us, event | category | flops | bytes accessed | tf_op | source)
XLA Modules:
  0.0 495.7 jit_solution(11804990757761188444)
XLA Ops:
  7.2 0.0 all-gather.5.cloned.1.call-start
  7.2 2.2 copy.35
  9.4 0.0 all-gather.5.cloned.1.call-update
  9.4 0.0 all-gather.3.cloned.1.call-start
  9.4 2.2 copy.32
  11.6 0.0 all-gather.3.cloned.1.call-update
  11.6 0.0 reduce-scatter.5.cloned.1.call-start
  11.7 0.7 fusion.35
  12.4 0.7 compare_select_fusion
  13.1 0.1 copy.33
  13.2 0.1 reshape.68
  13.3 8.9 %all-gather.5.cloned.1.call-done = bf16[128,5120]{0,1:T(8,128)(2,1)} async-done(((bf16[128,2560]{0,1:T(8,128)(2,1)}), bf16[128,5120]{0,1:T(8,128)(2,1)}) %all-gather.5.cloned.1.call-update) | async-done | bytes 1310736 | tf_op jit(solution)/shard_map/all_gather | solution.py:14
  22.3 1.8 copy.36
  24.0 7.5 %gather_fusion.1 = bf16[135,128,128]{2,1,0:T(8,128)(2,1)} fusion(bf16[128,40,128]{2,0,1:T(8,128)(2,1)S(1)} %copy.36, s32[1024]{0:T(1024)S(1)} %pad_clamp_fusion), kind=kCustom, calls=%fused_computation.1 | custom fusion | bytes 8847900 | tf_op jit(solution)/shard_map/gather | solution.py:28
  31.6 0.0 copy-start
  31.6 5.9 %fusion.6 = f32[27,128,128,1]{2,1,3,0:T(8,128)S(1)} fusion(bf16[128,27,5,128]{3,0,2,1:T(8,128)(2,1)} %bitcast.129, bf16[1,27,5,128,128]{4,3,2,1,0:T(8,128)(2,1)} %param.11, bf16[27,5]{1,0:T(8,128)(2,1)S(1)} %get-tuple-element.10), kind=kOutput, calls=%fused_computation.16 | convolution fusion | flops 568442880 | bytes 10617102 | tf_op jit(solution)/shard_map/thpk,hpkj->thj/dot_general | solution.py:30
  37.5 0.0 copy-done
  37.5 5.4 %fusion.8 = f32[27,128,128,1]{2,1,3,0:T(8,128)} fusion(bf16[128,27,5,128]{3,0,2,1:T(8,128)(2,1)S(1)} %bitcast.131, bf16[1,27,5,128,128]{4,3,2,1,0:T(8,128)(2,1)} %param.12, bf16[27,5]{1,0:T(8,128)(2,1)S(1)} %get-tuple-element.10), kind=kOutput, calls=%fused_computation.18 | convolution fusion | flops 568442880 | bytes 10617102 | tf_op jit(solution)/shard_map/thpk,hpkj->thj/dot_general | solution.py:31
  43.0 1.8 copy.34
  44.8 7.7 %gather_fusion = bf16[135,128,128]{2,1,0:T(8,128)(2,1)} fusion(bf16[128,40,128]{2,0,1:T(8,128)(2,1)S(1)} %copy.34, s32[1024]{0:T(1024)S(1)} %pad_clamp_fusion), kind=kCustom, calls=%fused_computation | custom fusion | bytes 8847900 | tf_op jit(solution)/shard_map/gather | solution.py:29
  52.5 0.0 copy-start.2
  52.5 0.0 copy-start.3
  52.5 7.1 %fusion.27 = (bf16[128,27,128,1]{0,2,3,1:T(8,128)(2,1)}, bf16[128,27,128]{0,2,1:T(8,128)(2,1)S(1)}) fusion(f32[27,128,128,1]{2,1,3,0:T(8,128)S(1)} %fusion.6, f32[27,128,128,1]{2,1,3,0:T(8,128)} %fusion.8, bf16[128,27,5,128]{3,0,2,1:T(8,128)(2,1)} %bitcast.137, bf16[1,27,5,128,128]{4,3,2,1,0:T(8,128)(2,1)} %param.13, bf16[27,5]{1,0:T(8,128)(2,1)S(1)} %get-tuple-element.10), kind=kOutput, calls=%fused_computation.44 | convolution fusion | flops 574193664 | bytes 14156046 | tf_op jit(solution)/shard_map/thpk,hpjk->thj/dot_general | solution.py:35
  59.6 0.0 copy-done.3
  59.6 5.5 %multiply_bitcast_fusion = f32[27,5,128,128]{2,3,1,0:T(8,128)} fusion(f32[27,5]{1,0:T(8,128)S(1)} %get-tuple-element.9, bf16[128,27,5,128]{3,0,2,1:T(8,128)(2,1)S(1)} %bitcast.138, f32[27,128,128,1]{2,1,3,0:T(8,128)S(1)} %copy-done.3, f32[27,128,128,1]{2,1,3,0:T(8,128)S(1)} %fusion.6), kind=kOutput, calls=%fused_computation.3 | convolution fusion | flops 571097088 | bytes 16810524 | tf_op jit(solution)/shard_map/thj,thpk->hpjk/dot_general | solution.py:38
  65.1 10.4 %copy.48 = f32[27,5,128,128]{3,2,1,0:T(8,128)} copy(f32[27,5,128,128]{2,3,1,0:T(8,128)} %multiply_bitcast_fusion) | data formatting | bytes 17694720 | tf_op jit(solution)/shard_map/mul | solution.py:38
  75.5 7.2 %copy.37 = bf16[27,5,128,128]{2,3,1,0:T(8,128)(2,1)} copy(bf16[27,5,128,128]{3,2,1,0:T(8,128)(2,1)} %bitcast.130) | data formatting | bytes 8847360 | tf_op jit(solution)/shard_map/gather | solution.py:28
  82.7 0.0 slice-start.1
  82.7 3.7 broadcast_multiply_fusion
  86.5 0.0 slice-start.2
  86.5 1.3 broadcast_multiply_fusion.1
  87.8 1.0 slice-done.1
  88.8 0.2 slice-done.2
  89.0 9.0 %pad_maximum_fusion = f32[3,1,17280,128]{3,2,1,0:T(8,128)} fusion(f32[1,1,17280,128]{3,2,1,0:T(8,128)S(1)} %bitcast.134, f32[1,1,17280,128]{3,2,1,0:T(8,128)S(1)} %bitcast.135, f32[1,1,17280,128]{3,2,1,0:T(8,128)S(1)} %bitcast.136), kind=kLoop, calls=%fused_computation.2 | loop fusion | flops 13271040 | bytes 53084160 | tf_op jit(solution)/shard_map/stack | solution.py:58
  98.0 0.0 reduce-scatter.5.cloned.1.call-update
  98.0 0.0 reduce-scatter.3.cloned.1.call-start
  98.1 3.6 fusion.5
  101.7 7.8 %add_bitcast_fusion = f32[128,27,5,128]{0,3,2,1:T(8,128)} fusion(f32[27,5,128,128]{3,2,1,0:T(8,128)S(1)} %fusion.5, bf16[128,27,128,1]{0,2,3,1:T(8,128)(2,1)S(1)} %copy-done.4, bf16[1,27,5,128,128]{4,3,2,1,0:T(8,128)(2,1)} %param.12, bf16[27,5]{1,0:T(8,128)(2,1)S(1)} %get-tuple-element.10), kind=kOutput, calls=%fused_computation.4 | convolution fusion | flops 570654720 | bytes 23003406 | tf_op jit(solution)/shard_map/thj,hpkj->thpk/dot_general | solution.py:51
  109.5 11.2 %copy.44 = f32[128,27,5,128]{3,1,2,0:T(8,128)} copy(f32[128,27,5,128]{0,3,2,1:T(8,128)} %add_bitcast_fusion) | data formatting | bytes 17694720 | tf_op jit(solution)/shard_map/add | solution.py:51
  120.7 8.2 %bitcast_convert_fusion = bf16[40,128,128]{2,0,1:T(8,128)(2,1)S(1)} fusion(f32[128,27,5,128]{3,1,2,0:T(8,128)} %copy.44, s32[27,5]{0,1:T(8,128)S(1)} %copy-done.7), kind=kOutput, calls=%fused_computation.19 | convolution fusion | flops 1062343936 | bytes 10158620 | tf_op jit(solution)/shard_map/thpk,hpd->tdk/dot_general | solution.py:55
  129.0 0.0 copy-start.5
  129.0 0.0 copy-start.6
  129.0 1.3 copy.77
  130.3 0.0 reduce-scatter.3.cloned.1.call-update
  130.3 348.2 %reduce-scatter.5.cloned.1.call-done = f32[3,1,1080,128]{3,2,1,0:T(8,128)} async-done(((f32[3,1,17280,128]{3,2,1,0:T(8,128)}), f32[3,1,1080,128]{3,2,1,0:T(8,128)}) %reduce-scatter.5.cloned.1.call-update) | async-done | bytes 1658896 | tf_op jit(solution)/shard_map/reduce_scatter | solution.py:57
  478.6 0.0 copy-done.5
  478.6 4.3 add_divide_fusion
  482.8 6.3 %reduce-scatter.3.cloned.1.call-done = bf16[128,2560]{1,0:T(8,128)(2,1)} async-done(((bf16[128,5120]{1,0:T(8,128)(2,1)}), bf16[128,2560]{1,0:T(8,128)(2,1)}) %reduce-scatter.3.cloned.1.call-update) | async-done | bytes 655376 | tf_op jit(solution)/shard_map/reduce_scatter | solution.py:63
  (13 shorter events, 0.0 us)
Async XLA Ops:
  7.2 15.1 %all-gather.5.cloned.1.call-start = ((), (), s32[]{:S(2)}) async-start(), calls=%async_computation.3 | async-start | bytes 1966080 | tf_op jit(solution)/shard_map/all_gather | solution.py:14
  9.4 33.6 %all-gather.3.cloned.1.call-start = ((), (), s32[]{:S(2)}) async-start(), calls=%async_computation.2 | async-start | bytes 1966080 | tf_op jit(solution)/shard_map/all_gather | solution.py:15
  11.6 466.9 %reduce-scatter.5.cloned.1.call-start = ((), (), s32[]{:S(2)}) async-start(), calls=%async_computation.5 | async-start | bytes 28200960 | tf_op jit(solution)/shard_map/reduce_scatter | solution.py:57
  31.6 6.0 %copy-start = (bf16[135,128,128]{2,1,0:T(8,128)(2,1)S(1)}, bf16[135,128,128]{2,1,0:T(8,128)(2,1)}, u32[]{:S(2)}) copy-start(bf16[135,128,128]{2,1,0:T(8,128)(2,1)} %gather_fusion.1) | copy-start | bytes 13271044
  52.5 7.1 %copy-start.2 = (bf16[135,128,128]{2,1,0:T(8,128)(2,1)S(1)}, bf16[135,128,128]{2,1,0:T(8,128)(2,1)}, u32[]{:S(2)}) copy-start(bf16[135,128,128]{2,1,0:T(8,128)(2,1)} %gather_fusion) | copy-start | bytes 13271044
  52.5 7.1 %copy-start.3 = (f32[27,128,128,1]{2,1,3,0:T(8,128)S(1)}, f32[27,128,128,1]{2,1,3,0:T(8,128)}, u32[]{:S(2)}) copy-start(f32[27,128,128,1]{2,1,3,0:T(8,128)} %fusion.8) | copy-start | bytes 5308420
  75.5 7.2 %copy-start.4 = (bf16[128,27,128,1]{0,2,3,1:T(8,128)(2,1)S(1)}, bf16[128,27,128,1]{0,2,3,1:T(8,128)(2,1)}, u32[]{:S(2)}) copy-start(bf16[128,27,128,1]{0,2,3,1:T(8,128)(2,1)} %get-tuple-element.7) | copy-start | bytes 2654212
  82.7 3.7 copy-start.1
  82.7 5.1 %slice-start = ((s8[8847360]{0:T(1024)(128)(4,1)}), s8[4194304]{0:T(1024)(128)(4,1)S(1)}, s32[]{:S(2)}) async-start(s8[8847360]{0:T(1024)(128)(4,1)} %bitcast.132), calls=%async_computation.6 | async-start | bytes 8388608
  82.7 6.1 %slice-start.1 = ((s8[8847360]{0:T(1024)(128)(4,1)}), s8[4194304]{0:T(1024)(128)(4,1)S(1)}, s32[]{:S(2)}) async-start(s8[8847360]{0:T(1024)(128)(4,1)} %bitcast.132), calls=%async_computation.7 | async-start | bytes 8388608
  86.5 2.5 slice-start.2
  98.0 391.2 %reduce-scatter.3.cloned.1.call-start = ((), (), s32[]{:S(2)}) async-start(), calls=%async_computation.4 | async-start | bytes 1966080 | tf_op jit(solution)/shard_map/reduce_scatter | solution.py:63
  109.5 11.2 %copy-start.7 = (s32[27,5]{0,1:T(8,128)S(1)}, s32[27,5]{0,1:T(8,128)}, u32[]{:S(2)}) copy-start(s32[27,5]{0,1:T(8,128)} %param.14) | copy-start | bytes 1624
  129.0 349.6 %copy-start.5 = (f32[3,1,1080,128]{3,2,1,0:T(8,128)S(1)}, f32[3,1,1080,128]{3,2,1,0:T(8,128)}, u32[]{:S(2)}) copy-start(f32[3,1,1080,128]{3,2,1,0:T(8,128)} %param.17) | copy-start | bytes 4976644
  129.0 349.6 %copy-start.6 = (f32[3,1,1080,128]{3,2,1,0:T(8,128)S(1)}, f32[3,1,1080,128]{3,2,1,0:T(8,128)}, u32[]{:S(2)}) copy-start(f32[3,1,1080,128]{3,2,1,0:T(8,128)} %param.16) | copy-start | bytes 4976644
Sparse Core Ops, SparseCore 0:
  10.1 12.1 all-gather.4
  24.4 10.5 all-gather.2
  98.2 380.3 reduce-scatter.4
  481.3 7.8 reduce-scatter.2
where the time goes:
time: 497 us; the launch traced here: 496 us
  waiting for transfers between devices  364 us (73%)
  local copies, waits for them, and re-layouts  54.7 us (11%)
  matrix products  48.7 us (10%)
  other arithmetic  14.7 us (3%)
  between operations  13.9 us (3%)
    reduce_scatter x1, waiting for transfers between devices, shards(): lax.psum_scatter(jnp.stack([grad_gate, grad_up, grad_down]).reshape(3, 1,...  348 us
    gather x2, local copies, waits for them, and re-layouts, shards(): x_blocks = full_tok.reshape(tok_rows, D // BLK, BLK)[:, col_index]  14.8 us
    add x1, local copies, waits for them, and re-layouts, shards(): back_term + jnp.einsum('thj,hpkj->thpk', d_up, up_eff, preferred_element_...  11.2 us
    mul x1, local copies, waits for them, and re-layouts, shards(): jnp.einsum('thj,thpk->hpjk', hidden, dy_blocks, preferred_element_type=jn...  10.4 us
  transfers between devices with their start and end apart: 4, of which 3 were waited for; matrix products, arithmetic and copies ran while one was open for 12% of the time, Pallas kernels for 0%

commit v1 on v0

--- a/solution.py
+++ b/solution.py
@@ -1,3 +1,4 @@
+import functools
 import math
 
 import jax
@@ -9,7 +10,43 @@
 BLK = 128
 
 
-def shards(tokens, cotangent, w_gate, w_up, w_down, col_index, row_count, adam_m, adam_v):
+def ring_order(n):
+    if n != 16:
+        return list(range(n))
+    plane = [(0, 0), (1, 0), (1, 1), (0, 1)]
+    order = []
+    for q, (x, y) in enumerate(plane):
+        zs = range(4) if q % 2 == 0 else range(3, -1, -1)
+        order += [z * 4 + y * 2 + x for z in zs]
+    return order
+
+
+def ring_reduce_scatter(full, n, nt, order, wire_dtype):
+    chunk = full.shape[1] // n
+    pos_of = [0] * n
+    for p, d in enumerate(order):
+        pos_of[d] = p
+    me = jnp.asarray(pos_of, jnp.int32)[lax.axis_index("dp")]
+    step = 1 - 2 * (lax.axis_index("tensor") % 2)
+    order_arr = jnp.asarray(order, jnp.int32)
+
+    def own(s):
+        p = (me - step * (1 + s)) % n
+        return lax.dynamic_slice_in_dim(full, order_arr[p] * chunk, chunk, axis=1)
+
+    perm = []
+    for p in range(n):
+        for t in range(nt):
+            hop = 1 if t % 2 == 0 else -1
+            perm.append((order[p] * nt + t, order[(p + hop) % n] * nt + t))
+    acc = own(0)
+    for s in range(1, n):
+        moved = lax.ppermute(acc.astype(wire_dtype), ("dp", "tensor"), perm)
+        acc = moved.astype(jnp.float32) + own(s)
+    return acc
+
+
+def shards(n_dp, n_t, tokens, cotangent, w_gate, w_up, w_down, col_index, row_count, adam_m, adam_v):
     full_tok, full_cot = (
         lax.all_gather(tokens, "tensor", axis=1, tiled=True),
         lax.all_gather(cotangent, "tensor", axis=1, tiled=True),
@@ -54,16 +91,17 @@
     onehot = (col_index[:, :, None] == jnp.arange(D // BLK)[None, None, :]).astype(jnp.float32)
     dx_blocks = jnp.einsum("thpk,hpd->tdk", back_term, onehot, precision=lax.Precision.HIGHEST)
     dx_part = dx_blocks.reshape(tok_rows, D)
-    reduced = lax.psum_scatter(
-        jnp.stack([grad_gate, grad_up, grad_down]).reshape(3, 1, own_rows, BLK),
-        "dp",
-        scatter_dimension=2,
-        tiled=True,
-    )
+    reduced = ring_reduce_scatter(
+        jnp.stack([grad_gate, grad_up, grad_down]).reshape(3, own_rows, BLK),
+        n_dp,
+        n_t,
+        ring_order(n_dp),
+        jnp.float32,
+    )[:, None]
     token_grads = lax.psum_scatter(
         dx_part.astype(jnp.bfloat16), "tensor", scatter_dimension=1, tiled=True
     )
-    grad_scale = 1.0 / math.sqrt(lax.axis_size("dp") * tok_rows)
+    grad_scale = 1.0 / math.sqrt(n_dp * tok_rows)
     grad_all = reduced * grad_scale
     m_new = 0.9 * adam_m + 0.1 * grad_all
     v_new = 0.95 * adam_v + 0.05 * grad_all * grad_all
@@ -89,4 +127,5 @@
         P(None, "tensor", "dp", None),
         P(None, "tensor", "dp", None),
     )
-    return jax.shard_map(shards, mesh=mesh, in_specs=in_specs, out_specs=out_specs, check_vma=False)
+    body = functools.partial(shards, mesh.shape["dp"], mesh.shape["tensor"])
+    return jax.shard_map(body, mesh=mesh, in_specs=in_specs, out_specs=out_specs, check_vma=False)

time: 497 us -> 509 us (1.024)
  waiting for transfers between devices: 364 us -> 265 us
  other arithmetic: 14.7 us -> 58.6 us
  starting transfers between devices: 0.16 us -> 31.7 us
  between operations: 13.9 us -> 34.8 us
  local copies, waits for them, and re-layouts: 54.7 us -> 63.8 us
    reduce_scatter x1 -> x0, waiting for transfers between devices: 348 us -> none  [shards(): lax.psum_scatter(jnp.stack([grad_gate, grad_up, grad_down]).reshape(3, 1,...]
    ppermute x0 -> x15, waiting for transfers between devices: none -> 265 us  [ring_reduce_scatter(): moved = lax.ppermute(acc.astype(wire_dtype), ('dp', 'tensor'), perm)]
    add x0 -> x14, other arithmetic: none -> 46.1 us  [ring_reduce_scatter(): acc = moved.astype(jnp.float32) + own(s)]
    ppermute x0 -> x15, starting transfers between devices: none -> 31.6 us  [ring_reduce_scatter(): moved = lax.ppermute(acc.astype(wire_dtype), ('dp', 'tensor'), perm)]
    all_gather x1, waiting for transfers between devices: 8.94 us -> 0.02 us  [shards(): lax.all_gather(tokens, 'tensor', axis=1, tiled=True)]
    unnamed x25 -> x41, local copies, waits for them, and re-layouts: 6.88 us -> 13.5 us
    reduce_scatter x1, waiting for transfers between devices: 6.35 us -> 0.01 us  [shards(): lax.psum_scatter(dx_part.astype(jnp.bfloat16), 'tensor', scatter_dimensio...]
  transfers between devices with their start and end apart: 4 -> 18, of which waited for: 3 -> 14; matrix products, arithmetic and copies ran while one was open for 12% -> 12% of each run, Pallas kernels for 0% -> 0%
where the time goes in v1:
time: 509 us; the launch traced here: 508 us
  waiting for transfers between devices  265 us (52%)
  local copies, waits for them, and re-layouts  63.8 us (13%)
  other arithmetic  58.6 us (12%)
  matrix products  53.5 us (11%)
  between operations  34.8 us (7%)
  starting transfers between devices  31.7 us (6%)
    ppermute x15, waiting for transfers between devices, ring_reduce_scatter(): moved = lax.ppermute(acc.astype(wire_dtype), ('dp', 'tensor'), perm)  265 us
    add x14, other arithmetic, ring_reduce_scatter(): acc = moved.astype(jnp.float32) + own(s)  46.1 us
    ppermute x15, starting transfers between devices, ring_reduce_scatter(): moved = lax.ppermute(acc.astype(wire_dtype), ('dp', 'tensor'), perm)  31.6 us
    gather x2, local copies, waits for them, and re-layouts, shards(): x_blocks = full_tok.reshape(tok_rows, D // BLK, BLK)[:, col_index]  14.7 us
    unnamed x41, local copies, waits for them, and re-layouts  13.5 us
    add x1, local copies, waits for them, and re-layouts, shards(): back_term + jnp.einsum('thj,hpkj->thpk', d_up, up_eff, preferred_element_...  11.1 us
    mul x1, local copies, waits for them, and re-layouts, shards(): jnp.einsum('thj,thpk->hpjk', hidden, dy_blocks, preferred_element_type=jn...  10.5 us
  transfers between devices with their start and end apart: 18, of which 14 were waited for; matrix products, arithmetic and copies ran while one was open for 12% of the time, Pallas kernels for 0%

profile of v1, /device:TPU:0, one launch (start us, length us, event | category | flops | bytes accessed | tf_op | source)
XLA Modules:
  0.0 507.7 jit_solution(18239257096520631560)
XLA Ops:
  7.2 2.2 copy.45
  25.6 7.5 %gather_fusion.1 = bf16[135,128,128]{2,1,0:T(8,128)(2,1)} fusion(bf16[128,40,128]{2,0,1:T(8,128)(2,1)S(1)} %copy.46, s32[1024]{0:T(1024)S(1)} %pad_clamp_fusion), kind=kCustom, calls=%fused_computation.1 | custom fusion | bytes 8847900 | tf_op jit(solution)/shard_map/gather | solution.py:65
  33.1 5.6 %fusion.6 = f32[27,128,128,1]{2,1,3,0:T(8,128)S(1)} fusion(bf16[128,27,5,128]{3,0,2,1:T(8,128)(2,1)} %bitcast.166, bf16[1,27,5,128,128]{4,3,2,1,0:T(8,128)(2,1)} %param.13, bf16[27,5]{1,0:T(8,128)(2,1)S(1)} %get-tuple-element.38), kind=kOutput, calls=%fused_computation.16 | convolution fusion | flops 568442880 | bytes 10617102 | tf_op jit(solution)/shard_map/thpk,hpkj->thj/dot_general | solution.py:67
  38.8 5.5 %fusion.8 = f32[27,128,128,1]{2,1,3,0:T(8,128)} fusion(bf16[128,27,5,128]{3,0,2,1:T(8,128)(2,1)S(1)} %bitcast.168, bf16[1,27,5,128,128]{4,3,2,1,0:T(8,128)(2,1)} %param.14, bf16[27,5]{1,0:T(8,128)(2,1)S(1)} %get-tuple-element.38), kind=kOutput, calls=%fused_computation.18 | convolution fusion | flops 568442880 | bytes 10617102 | tf_op jit(solution)/shard_map/thpk,hpkj->thj/dot_general | solution.py:68
  46.0 7.7 %gather_fusion = bf16[135,128,128]{2,1,0:T(8,128)(2,1)} fusion(bf16[128,40,128]{2,0,1:T(8,128)(2,1)S(1)} %copy.44, s32[1024]{0:T(1024)S(1)} %pad_clamp_fusion), kind=kCustom, calls=%fused_computation | custom fusion | bytes 8847900 | tf_op jit(solution)/shard_map/gather | solution.py:66
  53.8 7.3 %fusion.27 = (bf16[128,27,128,1]{0,2,3,1:T(8,128)(2,1)}, bf16[128,27,128]{0,2,1:T(8,128)(2,1)}) fusion(f32[27,128,128,1]{2,1,3,0:T(8,128)S(1)} %fusion.6, f32[27,128,128,1]{2,1,3,0:T(8,128)} %fusion.8, bf16[128,27,5,128]{3,0,2,1:T(8,128)(2,1)} %bitcast.174, bf16[1,27,5,128,128]{4,3,2,1,0:T(8,128)(2,1)} %param.15, bf16[27,5]{1,0:T(8,128)(2,1)S(1)} %get-tuple-element.38), kind=kOutput, calls=%fused_computation.61 | convolution fusion | flops 574193664 | bytes 14156046 | tf_op jit(solution)/shard_map/thpk,hpjk->thj/dot_general | solution.py:72
  61.1 5.5 %multiply_bitcast_fusion = f32[27,5,128,128]{2,3,1,0:T(8,128)} fusion(f32[27,5]{1,0:T(8,128)S(1)} %get-tuple-element.37, bf16[128,27,5,128]{3,0,2,1:T(8,128)(2,1)S(1)} %bitcast.175, f32[27,128,128,1]{2,1,3,0:T(8,128)S(1)} %copy-done.4, f32[27,128,128,1]{2,1,3,0:T(8,128)S(1)} %fusion.6), kind=kOutput, calls=%fused_computation.3 | convolution fusion | flops 571097088 | bytes 16810524 | tf_op jit(solution)/shard_map/thj,thpk->hpjk/dot_general | solution.py:75
  66.6 10.5 %copy.59 = f32[27,5,128,128]{3,2,1,0:T(8,128)} copy(f32[27,5,128,128]{2,3,1,0:T(8,128)} %multiply_bitcast_fusion) | data formatting | bytes 17694720 | tf_op jit(solution)/shard_map/mul | solution.py:75
  77.1 7.2 %copy.47 = bf16[27,5,128,128]{2,3,1,0:T(8,128)(2,1)} copy(bf16[27,5,128,128]{3,2,1,0:T(8,128)(2,1)} %bitcast.167) | data formatting | bytes 8847360 | tf_op jit(solution)/shard_map/gather | solution.py:65
  84.3 8.2 %broadcast_multiply_fusion = f32[27,5,128,128]{3,2,1,0:T(8,128)} fusion(f32[27,5]{1,0:T(8,128)S(1)} %get-tuple-element.37, bf16[128,27,128,1]{0,2,3,1:T(8,128)(2,1)S(1)} %copy-done.6, bf16[27,5,128,128]{2,3,1,0:T(8,128)(2,1)} %copy.47), kind=kOutput, calls=%fused_computation.13 | convolution fusion | flops 568442880 | bytes 14156316 | tf_op jit(solution)/shard_map/thpk,thj->hpkj/dot_general | solution.py:85
  92.5 4.8 broadcast_multiply_fusion.1
  97.3 7.6 %pad_maximum_fusion = f32[3,17280,128]{2,1,0:T(8,128)S(1)} fusion(f32[1,17280,128]{2,1,0:T(8,128)S(1)} %bitcast.171, f32[1,17280,128]{2,1,0:T(8,128)} %bitcast.172, f32[1,17280,128]{2,1,0:T(8,128)} %bitcast.173), kind=kLoop, calls=%fused_computation.2 | loop fusion | flops 13271040 | bytes 53084160 | tf_op jit(solution)/shard_map/stack | solution.py:95
  104.9 8.8 %copy-done = f32[3,17280,128]{2,1,0:T(8,128)} copy-done((f32[3,17280,128]{2,1,0:T(8,128)}, f32[3,17280,128]{2,1,0:T(8,128)S(1)}, u32[]{:S(2)}) %copy-start) | copy-done | bytes 26542104
  115.0 3.0 collective-permute-start
  118.6 18.9 %collective-permute-done = f32[3,1080,128]{2,1,0:T(8,128)} collective-permute-done((f32[3,1080,128]{2,1,0:T(8,128)}, f32[3,1080,128]{2,1,0:T(8,128)}, u32[]{:S(2)}, u32[]{:S(2)}) %collective-permute-start) | collective-permute-done | bytes 1658912 | tf_op jit(solution)/shard_map/ppermute | solution.py:44
  137.5 3.3 dynamic-slice_add_fusion.14
  143.4 19.0 %collective-permute-done.1 = f32[3,1080,128]{2,1,0:T(8,128)} collective-permute-done((f32[3,1080,128]{2,1,0:T(8,128)}, f32[3,1080,128]{2,1,0:T(8,128)}, u32[]{:S(2)}, u32[]{:S(2)}) %collective-permute-start.1) | collective-permute-done | bytes 1658912 | tf_op jit(solution)/shard_map/ppermute | solution.py:44
  162.4 3.3 dynamic-slice_add_fusion.13
  168.4 18.9 %collective-permute-done.2 = f32[3,1080,128]{2,1,0:T(8,128)} collective-permute-done((f32[3,1080,128]{2,1,0:T(8,128)}, f32[3,1080,128]{2,1,0:T(8,128)}, u32[]{:S(2)}, u32[]{:S(2)}) %collective-permute-start.2) | collective-permute-done | bytes 1658912 | tf_op jit(solution)/shard_map/ppermute | solution.py:44
  187.4 3.3 dynamic-slice_add_fusion.12
  193.3 19.0 %collective-permute-done.3 = f32[3,1080,128]{2,1,0:T(8,128)} collective-permute-done((f32[3,1080,128]{2,1,0:T(8,128)}, f32[3,1080,128]{2,1,0:T(8,128)}, u32[]{:S(2)}, u32[]{:S(2)}) %collective-permute-start.3) | collective-permute-done | bytes 1658912 | tf_op jit(solution)/shard_map/ppermute | solution.py:44
  212.3 3.3 dynamic-slice_add_fusion.11
  218.3 18.9 %collective-permute-done.4 = f32[3,1080,128]{2,1,0:T(8,128)} collective-permute-done((f32[3,1080,128]{2,1,0:T(8,128)}, f32[3,1080,128]{2,1,0:T(8,128)}, u32[]{:S(2)}, u32[]{:S(2)}) %collective-permute-start.4) | collective-permute-done | bytes 1658912 | tf_op jit(solution)/shard_map/ppermute | solution.py:44
  237.2 3.3 dynamic-slice_add_fusion.10
  243.1 19.0 %collective-permute-done.5 = f32[3,1080,128]{2,1,0:T(8,128)} collective-permute-done((f32[3,1080,128]{2,1,0:T(8,128)}, f32[3,1080,128]{2,1,0:T(8,128)}, u32[]{:S(2)}, u32[]{:S(2)}) %collective-permute-start.5) | collective-permute-done | bytes 1658912 | tf_op jit(solution)/shard_map/ppermute | solution.py:44
  262.1 3.3 dynamic-slice_add_fusion.9
  268.1 19.0 %collective-permute-done.6 = f32[3,1080,128]{2,1,0:T(8,128)} collective-permute-done((f32[3,1080,128]{2,1,0:T(8,128)}, f32[3,1080,128]{2,1,0:T(8,128)}, u32[]{:S(2)}, u32[]{:S(2)}) %collective-permute-start.6) | collective-permute-done | bytes 1658912 | tf_op jit(solution)/shard_map/ppermute | solution.py:44
  287.0 3.3 dynamic-slice_add_fusion.8
  293.0 18.9 %collective-permute-done.7 = f32[3,1080,128]{2,1,0:T(8,128)} collective-permute-done((f32[3,1080,128]{2,1,0:T(8,128)}, f32[3,1080,128]{2,1,0:T(8,128)}, u32[]{:S(2)}, u32[]{:S(2)}) %collective-permute-start.7) | collective-permute-done | bytes 1658912 | tf_op jit(solution)/shard_map/ppermute | solution.py:44
  312.0 3.3 dynamic-slice_add_fusion.7
  318.0 18.9 %collective-permute-done.8 = f32[3,1080,128]{2,1,0:T(8,128)} collective-permute-done((f32[3,1080,128]{2,1,0:T(8,128)}, f32[3,1080,128]{2,1,0:T(8,128)}, u32[]{:S(2)}, u32[]{:S(2)}) %collective-permute-start.8) | collective-permute-done | bytes 1658912 | tf_op jit(solution)/shard_map/ppermute | solution.py:44
  336.9 3.3 dynamic-slice_add_fusion.6
  342.9 18.9 %collective-permute-done.9 = f32[3,1080,128]{2,1,0:T(8,128)} collective-permute-done((f32[3,1080,128]{2,1,0:T(8,128)}, f32[3,1080,128]{2,1,0:T(8,128)}, u32[]{:S(2)}, u32[]{:S(2)}) %collective-permute-start.9) | collective-permute-done | bytes 1658912 | tf_op jit(solution)/shard_map/ppermute | solution.py:44
  361.8 3.3 dynamic-slice_add_fusion.5
  367.7 19.0 %collective-permute-done.10 = f32[3,1080,128]{2,1,0:T(8,128)} collective-permute-done((f32[3,1080,128]{2,1,0:T(8,128)}, f32[3,1080,128]{2,1,0:T(8,128)}, u32[]{:S(2)}, u32[]{:S(2)}) %collective-permute-start.10) | collective-permute-done | bytes 1658912 | tf_op jit(solution)/shard_map/ppermute | solution.py:44
  386.7 3.3 dynamic-slice_add_fusion.4
  392.7 18.9 %collective-permute-done.11 = f32[3,1080,128]{2,1,0:T(8,128)} collective-permute-done((f32[3,1080,128]{2,1,0:T(8,128)}, f32[3,1080,128]{2,1,0:T(8,128)}, u32[]{:S(2)}, u32[]{:S(2)}) %collective-permute-start.11) | collective-permute-done | bytes 1658912 | tf_op jit(solution)/shard_map/ppermute | solution.py:44
  411.7 3.3 dynamic-slice_add_fusion.3
  418.3 18.3 %collective-permute-done.12 = f32[3,1080,128]{2,1,0:T(8,128)} collective-permute-done((f32[3,1080,128]{2,1,0:T(8,128)}, f32[3,1080,128]{2,1,0:T(8,128)}, u32[]{:S(2)}, u32[]{:S(2)}) %collective-permute-start.12) | collective-permute-done | bytes 1658912 | tf_op jit(solution)/shard_map/ppermute | solution.py:44
  436.6 3.4 dynamic-slice_add_fusion.2
  440.0 2.1 collective-permute-start.13
  442.1 3.6 fusion.5
  445.7 4.7 add_bitcast_fusion
  450.5 11.1 %copy.54 = f32[128,27,5,128]{3,1,2,0:T(8,128)} copy(f32[128,27,5,128]{0,3,2,1:T(8,128)} %add_bitcast_fusion) | data formatting | bytes 17694720 | tf_op jit(solution)/shard_map/add | solution.py:88
  461.6 8.2 %bitcast_convert_fusion = bf16[40,128,128]{2,0,1:T(8,128)(2,1)S(1)} fusion(f32[128,27,5,128]{3,1,2,0:T(8,128)} %copy.54, s32[27,5]{0,1:T(8,128)S(1)} %copy-done.11), kind=kOutput, calls=%fused_computation.19 | convolution fusion | flops 1062343936 | bytes 10158620 | tf_op jit(solution)/shard_map/thpk,hpd->tdk/dot_general | solution.py:92
  471.2 3.4 dynamic-slice_add_fusion.1
  476.9 19.4 %collective-permute-done.14 = f32[3,1080,128]{2,1,0:T(8,128)} collective-permute-done((f32[3,1080,128]{2,1,0:T(8,128)}, f32[3,1080,128]{2,1,0:T(8,128)}, u32[]{:S(2)}, u32[]{:S(2)}) %collective-permute-start.14) | collective-permute-done | bytes 1658912 | tf_op jit(solution)/shard_map/ppermute | solution.py:44
  496.3 4.8 divide_bitcast_fusion
  (74 shorter events, 35.7 us)
Async XLA Ops:
  7.2 3.5 copy-start.13
  7.2 2.4 copy-start.9
  7.2 16.6 %all-gather.5.cloned.1.call-start = ((), (), s32[]{:S(2)}) async-start(), calls=%async_computation.2 | async-start | bytes 1966080 | tf_op jit(solution)/shard_map/all_gather | solution.py:51
  9.5 12.5 %copy-start.12 = (s32[27]{0:T(128)S(1)}, s32[27]{0:T(128)}, u32[]{:S(2)}) copy-start(s32[27]{0:T(128)} %param.17) | copy-start | bytes 328
  9.5 12.6 %copy-start.11 = (s32[27,5]{0,1:T(8,128)S(1)}, s32[27,5]{0,1:T(8,128)}, u32[]{:S(2)}) copy-start(s32[27,5]{0,1:T(8,128)} %param.16) | copy-start | bytes 1624
  9.5 12.9 %copy-start.10 = (s32[16]{0:T(128)S(1)}, s32[16]{0:T(128)}, u32[]{:S(2)}) copy-start(s32[16]{0:T(128)} %constant.162.clone) | copy-start | bytes 196
  9.5 34.8 %all-gather.3.cloned.1.call-start = ((), (), s32[]{:S(2)}) async-start(), calls=%async_computation.1 | async-start | bytes 1966080 | tf_op jit(solution)/shard_map/all_gather | solution.py:52
  10.6 490.5 %reduce-scatter.2.cloned.1.call-start = ((), (), s32[]{:S(2)}) async-start(), calls=%async_computation.3 | async-start | bytes 1966080 | tf_op jit(solution)/shard_map/reduce_scatter | solution.py:101
  33.1 5.6 %copy-start.1 = (bf16[135,128,128]{2,1,0:T(8,128)(2,1)S(1)}, bf16[135,128,128]{2,1,0:T(8,128)(2,1)}, u32[]{:S(2)}) copy-start(bf16[135,128,128]{2,1,0:T(8,128)(2,1)} %gather_fusion.1) | copy-start | bytes 13271044
  53.7 7.4 %copy-start.3 = (bf16[135,128,128]{2,1,0:T(8,128)(2,1)S(1)}, bf16[135,128,128]{2,1,0:T(8,128)(2,1)}, u32[]{:S(2)}) copy-start(bf16[135,128,128]{2,1,0:T(8,128)(2,1)} %gather_fusion) | copy-start | bytes 13271044
  53.7 7.4 %copy-start.4 = (f32[27,128,128,1]{2,1,3,0:T(8,128)S(1)}, f32[27,128,128,1]{2,1,3,0:T(8,128)}, u32[]{:S(2)}) copy-start(f32[27,128,128,1]{2,1,3,0:T(8,128)} %fusion.8) | copy-start | bytes 5308420
  77.1 7.2 %copy-start.6 = (bf16[128,27,128,1]{0,2,3,1:T(8,128)(2,1)S(1)}, bf16[128,27,128,1]{0,2,3,1:T(8,128)(2,1)}, u32[]{:S(2)}) copy-start(bf16[128,27,128,1]{0,2,3,1:T(8,128)(2,1)} %get-tuple-element.19) | copy-start | bytes 2654212
  84.2 8.2 %copy-start.2 = (bf16[27,5,128,128]{2,3,1,0:T(8,128)(2,1)S(1)}, bf16[27,5,128,128]{2,3,1,0:T(8,128)(2,1)}, u32[]{:S(2)}) copy-start(bf16[27,5,128,128]{2,3,1,0:T(8,128)(2,1)} %copy.47) | copy-start | bytes 13271044
  84.2 8.2 %copy-start.5 = (bf16[128,27,128]{0,2,1:T(8,128)(2,1)S(1)}, bf16[128,27,128]{0,2,1:T(8,128)(2,1)}, u32[]{:S(2)}) copy-start(bf16[128,27,128]{0,2,1:T(8,128)(2,1)} %get-tuple-element.20) | copy-start | bytes 2654212
  84.3 13.1 %slice-start = ((s8[8847360]{0:T(1024)(128)(4,1)}), s8[4194304]{0:T(1024)(128)(4,1)S(1)}, s32[]{:S(2)}) async-start(s8[8847360]{0:T(1024)(128)(4,1)} %bitcast.169), calls=%async_computation.4 | async-start | bytes 8388608
  84.3 13.0 %slice-start.1 = ((s8[8847360]{0:T(1024)(128)(4,1)}), s8[4194304]{0:T(1024)(128)(4,1)S(1)}, s32[]{:S(2)}) async-start(s8[8847360]{0:T(1024)(128)(4,1)} %bitcast.169), calls=%async_computation.5 | async-start | bytes 8388608
  92.5 4.8 slice-start.2
  104.9 8.8 %copy-start = (f32[3,17280,128]{2,1,0:T(8,128)}, f32[3,17280,128]{2,1,0:T(8,128)S(1)}, u32[]{:S(2)}) copy-start(f32[3,17280,128]{2,1,0:T(8,128)S(1)} %pad_maximum_fusion) | copy-start | bytes 79626240
  115.0 22.5 %collective-permute-start = (f32[3,1080,128]{2,1,0:T(8,128)}, f32[3,1080,128]{2,1,0:T(8,128)}, u32[]{:S(2)}, u32[]{:S(2)}) collective-permute-start(f32[3,1080,128]{2,1,0:T(8,128)} %constant_dynamic-slice_fusion), channel_id=1, source_target_pairs={{0,8},{1,5},{8,16},{9,1},{16,24},{17,9},{24,26},{25,17},{26,18},{2... | collective-permute-start | bytes 4976648 | tf_op jit(solution)/shard_map/ppermute | solution.py:44
  140.8 21.7 %collective-permute-start.1 = (f32[3,1080,128]{2,1,0:T(8,128)}, f32[3,1080,128]{2,1,0:T(8,128)}, u32[]{:S(2)}, u32[]{:S(2)}) collective-permute-start(f32[3,1080,128]{2,1,0:T(8,128)} %dynamic-slice_add_fusion.14), channel_id=1, source_target_pairs={{0,8},{1,5},{8,16},{9,1},{16,24},{17,9},{24,26},{25,17},{26,18},{2... | collective-permute-start | bytes 4976648 | tf_op jit(solution)/shard_map/ppermute | solution.py:44
  165.7 21.7 %collective-permute-start.2 = (f32[3,1080,128]{2,1,0:T(8,128)}, f32[3,1080,128]{2,1,0:T(8,128)}, u32[]{:S(2)}, u32[]{:S(2)}) collective-permute-start(f32[3,1080,128]{2,1,0:T(8,128)} %dynamic-slice_add_fusion.13), channel_id=1, source_target_pairs={{0,8},{1,5},{8,16},{9,1},{16,24},{17,9},{24,26},{25,17},{26,18},{2... | collective-permute-start | bytes 4976648 | tf_op jit(solution)/shard_map/ppermute | solution.py:44
  190.6 21.7 %collective-permute-start.3 = (f32[3,1080,128]{2,1,0:T(8,128)}, f32[3,1080,128]{2,1,0:T(8,128)}, u32[]{:S(2)}, u32[]{:S(2)}) collective-permute-start(f32[3,1080,128]{2,1,0:T(8,128)} %dynamic-slice_add_fusion.12), channel_id=1, source_target_pairs={{0,8},{1,5},{8,16},{9,1},{16,24},{17,9},{24,26},{25,17},{26,18},{2... | collective-permute-start | bytes 4976648 | tf_op jit(solution)/shard_map/ppermute | solution.py:44
  215.5 21.7 %collective-permute-start.4 = (f32[3,1080,128]{2,1,0:T(8,128)}, f32[3,1080,128]{2,1,0:T(8,128)}, u32[]{:S(2)}, u32[]{:S(2)}) collective-permute-start(f32[3,1080,128]{2,1,0:T(8,128)} %dynamic-slice_add_fusion.11), channel_id=1, source_target_pairs={{0,8},{1,5},{8,16},{9,1},{16,24},{17,9},{24,26},{25,17},{26,18},{2... | collective-permute-start | bytes 4976648 | tf_op jit(solution)/shard_map/ppermute | solution.py:44
  240.5 21.7 %collective-permute-start.5 = (f32[3,1080,128]{2,1,0:T(8,128)}, f32[3,1080,128]{2,1,0:T(8,128)}, u32[]{:S(2)}, u32[]{:S(2)}) collective-permute-start(f32[3,1080,128]{2,1,0:T(8,128)} %dynamic-slice_add_fusion.10), channel_id=1, source_target_pairs={{0,8},{1,5},{8,16},{9,1},{16,24},{17,9},{24,26},{25,17},{26,18},{2... | collective-permute-start | bytes 4976648 | tf_op jit(solution)/shard_map/ppermute | solution.py:44
  265.4 21.7 %collective-permute-start.6 = (f32[3,1080,128]{2,1,0:T(8,128)}, f32[3,1080,128]{2,1,0:T(8,128)}, u32[]{:S(2)}, u32[]{:S(2)}) collective-permute-start(f32[3,1080,128]{2,1,0:T(8,128)} %dynamic-slice_add_fusion.9), channel_id=1, source_target_pairs={{0,8},{1,5},{8,16},{9,1},{16,24},{17,9},{24,26},{25,17},{26,18},{2... | collective-permute-start | bytes 4976648 | tf_op jit(solution)/shard_map/ppermute | solution.py:44
  290.3 21.7 %collective-permute-start.7 = (f32[3,1080,128]{2,1,0:T(8,128)}, f32[3,1080,128]{2,1,0:T(8,128)}, u32[]{:S(2)}, u32[]{:S(2)}) collective-permute-start(f32[3,1080,128]{2,1,0:T(8,128)} %dynamic-slice_add_fusion.8), channel_id=1, source_target_pairs={{0,8},{1,5},{8,16},{9,1},{16,24},{17,9},{24,26},{25,17},{26,18},{2... | collective-permute-start | bytes 4976648 | tf_op jit(solution)/shard_map/ppermute | solution.py:44
  315.2 21.7 %collective-permute-start.8 = (f32[3,1080,128]{2,1,0:T(8,128)}, f32[3,1080,128]{2,1,0:T(8,128)}, u32[]{:S(2)}, u32[]{:S(2)}) collective-permute-start(f32[3,1080,128]{2,1,0:T(8,128)} %dynamic-slice_add_fusion.7), channel_id=1, source_target_pairs={{0,8},{1,5},{8,16},{9,1},{16,24},{17,9},{24,26},{25,17},{26,18},{2... | collective-permute-start | bytes 4976648 | tf_op jit(solution)/shard_map/ppermute | solution.py:44
  340.2 21.7 %collective-permute-start.9 = (f32[3,1080,128]{2,1,0:T(8,128)}, f32[3,1080,128]{2,1,0:T(8,128)}, u32[]{:S(2)}, u32[]{:S(2)}) collective-permute-start(f32[3,1080,128]{2,1,0:T(8,128)} %dynamic-slice_add_fusion.6), channel_id=1, source_target_pairs={{0,8},{1,5},{8,16},{9,1},{16,24},{17,9},{24,26},{25,17},{26,18},{2... | collective-permute-start | bytes 4976648 | tf_op jit(solution)/shard_map/ppermute | solution.py:44
  365.1 21.7 %collective-permute-start.10 = (f32[3,1080,128]{2,1,0:T(8,128)}, f32[3,1080,128]{2,1,0:T(8,128)}, u32[]{:S(2)}, u32[]{:S(2)}) collective-permute-start(f32[3,1080,128]{2,1,0:T(8,128)} %dynamic-slice_add_fusion.5), channel_id=1, source_target_pairs={{0,8},{1,5},{8,16},{9,1},{16,24},{17,9},{24,26},{25,17},{26,18},{2... | collective-permute-start | bytes 4976648 | tf_op jit(solution)/shard_map/ppermute | solution.py:44
  390.0 21.7 %collective-permute-start.11 = (f32[3,1080,128]{2,1,0:T(8,128)}, f32[3,1080,128]{2,1,0:T(8,128)}, u32[]{:S(2)}, u32[]{:S(2)}) collective-permute-start(f32[3,1080,128]{2,1,0:T(8,128)} %dynamic-slice_add_fusion.4), channel_id=1, source_target_pairs={{0,8},{1,5},{8,16},{9,1},{16,24},{17,9},{24,26},{25,17},{26,18},{2... | collective-permute-start | bytes 4976648 | tf_op jit(solution)/shard_map/ppermute | solution.py:44
  414.9 21.7 %collective-permute-start.12 = (f32[3,1080,128]{2,1,0:T(8,128)}, f32[3,1080,128]{2,1,0:T(8,128)}, u32[]{:S(2)}, u32[]{:S(2)}) collective-permute-start(f32[3,1080,128]{2,1,0:T(8,128)} %dynamic-slice_add_fusion.3), channel_id=1, source_target_pairs={{0,8},{1,5},{8,16},{9,1},{16,24},{17,9},{24,26},{25,17},{26,18},{2... | collective-permute-start | bytes 4976648 | tf_op jit(solution)/shard_map/ppermute | solution.py:44
  436.6 9.1 %slice-start.3 = ((s8[4423680]{0:T(1024)(128)(4,1)}), s8[4194304]{0:T(1024)(128)(4,1)S(1)}, s32[]{:S(2)}) async-start(s8[4423680]{0:T(1024)(128)(4,1)} %bitcast.176), calls=%async_computation.7 | async-start | bytes 8388608
  440.0 5.7 %slice-start.4 = ((s8[4423680]{0:T(1024)(128)(4,1)}), s8[229376]{0:T(1024)(128)(4,1)S(1)}, s32[]{:S(2)}) async-start(s8[4423680]{0:T(1024)(128)(4,1)} %bitcast.176), calls=%async_computation.8 | async-start | bytes 458752
  440.0 31.2 %collective-permute-start.13 = (f32[3,1080,128]{2,1,0:T(8,128)}, f32[3,1080,128]{2,1,0:T(8,128)}, u32[]{:S(2)}, u32[]{:S(2)}) collective-permute-start(f32[3,1080,128]{2,1,0:T(8,128)} %dynamic-slice_add_fusion.2), channel_id=1, source_target_pairs={{0,8},{1,5},{8,16},{9,1},{16,24},{17,9},{24,26},{25,17},{26,18},{2... | collective-permute-start | bytes 4976648 | tf_op jit(solution)/shard_map/ppermute | solution.py:44
  471.2 25.1 %copy-start.7 = (f32[3,1,1080,128]{3,2,1,0:T(8,128)S(1)}, f32[3,1,1080,128]{3,2,1,0:T(8,128)}, u32[]{:S(2)}) copy-start(f32[3,1,1080,128]{3,2,1,0:T(8,128)} %param.19) | copy-start | bytes 4976644
  471.2 25.1 %copy-start.8 = (f32[3,1,1080,128]{3,2,1,0:T(8,128)S(1)}, f32[3,1,1080,128]{3,2,1,0:T(8,128)}, u32[]{:S(2)}) copy-start(f32[3,1,1080,128]{3,2,1,0:T(8,128)} %param.18) | copy-start | bytes 4976644
  474.6 21.7 %collective-permute-start.14 = (f32[3,1080,128]{2,1,0:T(8,128)}, f32[3,1080,128]{2,1,0:T(8,128)}, u32[]{:S(2)}, u32[]{:S(2)}) collective-permute-start(f32[3,1080,128]{2,1,0:T(8,128)} %dynamic-slice_add_fusion.1), channel_id=1, source_target_pairs={{0,8},{1,5},{8,16},{9,1},{16,24},{17,9},{24,26},{25,17},{26,18},{2... | collective-permute-start | bytes 4976648 | tf_op jit(solution)/shard_map/ppermute | solution.py:44
Sparse Core Ops, SparseCore 0:
  10.1 12.1 all-gather.4
  24.4 10.5 all-gather.2
  471.3 8.9 reduce-scatter.1

commit v2 on v1

--- a/solution.py
+++ b/solution.py
@@ -21,8 +21,8 @@
     return order
 
 
-def ring_reduce_scatter(full, n, nt, order, wire_dtype):
-    chunk = full.shape[1] // n
+def ring_reduce_scatter(streams, n, nt, order, wire_dtype):
+    chunk = streams[0].shape[0] // n
     pos_of = [0] * n
     for p, d in enumerate(order):
         pos_of[d] = p
@@ -30,20 +30,21 @@
     step = 1 - 2 * (lax.axis_index("tensor") % 2)
     order_arr = jnp.asarray(order, jnp.int32)
 
-    def own(s):
+    def own(full, s):
         p = (me - step * (1 + s)) % n
-        return lax.dynamic_slice_in_dim(full, order_arr[p] * chunk, chunk, axis=1)
+        return lax.dynamic_slice_in_dim(full, order_arr[p] * chunk, chunk, axis=0)
 
     perm = []
     for p in range(n):
         for t in range(nt):
             hop = 1 if t % 2 == 0 else -1
             perm.append((order[p] * nt + t, order[(p + hop) % n] * nt + t))
-    acc = own(0)
+    accs = [own(full, 0) for full in streams]
     for s in range(1, n):
-        moved = lax.ppermute(acc.astype(wire_dtype), ("dp", "tensor"), perm)
-        acc = moved.astype(jnp.float32) + own(s)
-    return acc
+        for i, full in enumerate(streams):
+            moved = lax.ppermute(accs[i].astype(wire_dtype), ("dp", "tensor"), perm)
+            accs[i] = moved.astype(jnp.float32) + own(full, s)
+    return accs
 
 
 def shards(n_dp, n_t, tokens, cotangent, w_gate, w_up, w_down, col_index, row_count, adam_m, adam_v):
@@ -91,12 +92,14 @@
     onehot = (col_index[:, :, None] == jnp.arange(D // BLK)[None, None, :]).astype(jnp.float32)
     dx_blocks = jnp.einsum("thpk,hpd->tdk", back_term, onehot, precision=lax.Precision.HIGHEST)
     dx_part = dx_blocks.reshape(tok_rows, D)
-    reduced = ring_reduce_scatter(
-        jnp.stack([grad_gate, grad_up, grad_down]).reshape(3, own_rows, BLK),
-        n_dp,
-        n_t,
-        ring_order(n_dp),
-        jnp.float32,
+    reduced = jnp.stack(
+        ring_reduce_scatter(
+            [g.reshape(own_rows, BLK) for g in (grad_gate, grad_up, grad_down)],
+            n_dp,
+            n_t,
+            ring_order(n_dp),
+            jnp.bfloat16,
+        )
     )[:, None]
     token_grads = lax.psum_scatter(
         dx_part.astype(jnp.bfloat16), "tensor", scatter_dimension=1, tiled=True

time: 509 us -> 283 us (0.56)
  waiting for transfers between devices: 265 us -> 26.6 us
  starting transfers between devices: 31.7 us -> 69.2 us
  other arithmetic: 58.6 us -> 43.8 us
  local copies, waits for them, and re-layouts: 63.8 us -> 57.6 us
  matrix products: 53.5 us -> 47.7 us
    ppermute x15 -> x45, waiting for transfers between devices: 265 us -> 26.5 us  [ring_reduce_scatter(): moved = lax.ppermute(accs[i].astype(wire_dtype), ('dp', 'tensor'), perm)]
    add x14 -> x0, other arithmetic: 46.1 us -> none  [ring_reduce_scatter(): acc = moved.astype(jnp.float32) + own(s)]
    convert_element_type x0 -> x42, other arithmetic: none -> 38.6 us  [ring_reduce_scatter(): moved = lax.ppermute(accs[i].astype(wire_dtype), ('dp', 'tensor'), perm)]
    ppermute x15 -> x45, starting transfers between devices: 31.6 us -> 69 us  [ring_reduce_scatter(): moved = lax.ppermute(accs[i].astype(wire_dtype), ('dp', 'tensor'), perm)]
    unnamed x41 -> x37, local copies, waits for them, and re-layouts: 13.5 us -> 5.75 us
    another operation x1 -> x3, other arithmetic: 7.62 us -> 2.27 us  [shards(): jnp.stack(ring_reduce_scatter([g.reshape(own_rows, BLK) for g in (grad_ga...]
  transfers between devices with their start and end apart: 18 -> 48, of which waited for: 14 -> 42; matrix products, arithmetic and copies ran while one was open for 12% -> 34% of each run, Pallas kernels for 0% -> 0%
where the time goes in v2:
time: 283 us; the launch traced here: 280 us
  starting transfers between devices  69.2 us (24%)
  local copies, waits for them, and re-layouts  57.6 us (20%)
  matrix products  47.7 us (17%)
  other arithmetic  43.8 us (15%)
  between operations  35.1 us (12%)
  waiting for transfers between devices  26.6 us (9%)
    ppermute x45, starting transfers between devices, ring_reduce_scatter(): moved = lax.ppermute(accs[i].astype(wire_dtype), ('dp', 'tensor'), perm)  69 us
    convert_element_type x42, other arithmetic, ring_reduce_scatter(): moved = lax.ppermute(accs[i].astype(wire_dtype), ('dp', 'tensor'), perm)  38.6 us
    ppermute x45, waiting for transfers between devices, ring_reduce_scatter(): moved = lax.ppermute(accs[i].astype(wire_dtype), ('dp', 'tensor'), perm)  26.5 us
    gather x2, local copies, waits for them, and re-layouts, shards(): x_blocks = full_tok.reshape(tok_rows, D // BLK, BLK)[:, col_index]  14.6 us
    add x1, local copies, waits for them, and re-layouts, shards(): back_term + jnp.einsum('thj,hpkj->thpk', d_up, up_eff, preferred_element_...  11.2 us
    mul x1, local copies, waits for them, and re-layouts, shards(): jnp.einsum('thj,thpk->hpjk', hidden, dy_blocks, preferred_element_type=jn...  10.4 us
    dot_general x1, matrix products, shards(): jnp.einsum('thpk,hpd->tdk', back_term, onehot, precision=lax.Precision.HI...  8.17 us
    gather x1, local copies, waits for them, and re-layouts, shards(): dy_blocks = full_cot.reshape(tok_rows, D // BLK, BLK)[:, col_index]  7.7 us
  transfers between devices with their start and end apart: 48, of which 42 were waited for; matrix products, arithmetic and copies ran while one was open for 34% of the time, Pallas kernels for 0%

profile of v2, /device:TPU:0, one launch (start us, length us, event | category | flops | bytes accessed | tf_op | source)
XLA Modules:
  0.0 279.9 jit_solution(4120393331318728541)
XLA Ops:
  7.2 2.2 copy.37
  9.5 2.2 copy.34
  34.9 1.8 copy.38
  36.7 1.8 copy.36
  38.5 7.5 %gather_fusion.1 = bf16[135,128,128]{2,1,0:T(8,128)(2,1)} fusion(bf16[128,40,128]{2,0,1:T(8,128)(2,1)S(1)} %copy.38, s32[1024]{0:T(1024)S(1)} %pad_clamp_fusion), kind=kCustom, calls=%fused_computation.1 | custom fusion | bytes 8847900 | tf_op jit(solution)/shard_map/gather | solution.py:66
  46.0 5.5 %fusion.8 = f32[27,128,128,1]{2,1,3,0:T(8,128)S(1)} fusion(bf16[128,27,5,128]{3,0,2,1:T(8,128)(2,1)} %bitcast.152, bf16[1,27,5,128,128]{4,3,2,1,0:T(8,128)(2,1)} %param.14, bf16[27,5]{1,0:T(8,128)(2,1)S(1)} %get-tuple-element.26), kind=kOutput, calls=%fused_computation.17 | convolution fusion | flops 568442880 | bytes 10617102 | tf_op jit(solution)/shard_map/thpk,hpkj->thj/dot_general | solution.py:69
  51.6 5.4 %fusion.6 = f32[27,128,128,1]{2,1,3,0:T(8,128)} fusion(bf16[128,27,5,128]{3,0,2,1:T(8,128)(2,1)S(1)} %bitcast.154, bf16[1,27,5,128,128]{4,3,2,1,0:T(8,128)(2,1)} %param.13, bf16[27,5]{1,0:T(8,128)(2,1)S(1)} %get-tuple-element.26), kind=kOutput, calls=%fused_computation.15 | convolution fusion | flops 568442880 | bytes 10617102 | tf_op jit(solution)/shard_map/thpk,hpkj->thj/dot_general | solution.py:68
  57.0 7.7 %gather_fusion = bf16[135,128,128]{2,1,0:T(8,128)(2,1)} fusion(bf16[128,40,128]{2,0,1:T(8,128)(2,1)S(1)} %copy.36, s32[1024]{0:T(1024)S(1)} %pad_clamp_fusion), kind=kCustom, calls=%fused_computation | custom fusion | bytes 8847900 | tf_op jit(solution)/shard_map/gather | solution.py:67
  64.7 7.1 %fusion.27 = (bf16[128,27,128,1]{0,2,3,1:T(8,128)(2,1)}, bf16[128,27,128]{0,2,1:T(8,128)(2,1)S(1)}) fusion(f32[27,128,128,1]{2,1,3,0:T(8,128)} %fusion.6, f32[27,128,128,1]{2,1,3,0:T(8,128)S(1)} %fusion.8, bf16[128,27,5,128]{3,0,2,1:T(8,128)(2,1)} %bitcast.205, bf16[1,27,5,128,128]{4,3,2,1,0:T(8,128)(2,1)} %param.15, bf16[27,5]{1,0:T(8,128)(2,1)S(1)} %get-tuple-element.26), kind=kOutput, calls=%fused_computation.44 | convolution fusion | flops 574193664 | bytes 14156046 | tf_op jit(solution)/shard_map/thpk,hpjk->thj/dot_general | solution.py:73
  71.8 5.5 %multiply_bitcast_fusion = f32[27,5,128,128]{2,3,1,0:T(8,128)} fusion(f32[27,5]{1,0:T(8,128)S(1)} %get-tuple-element.25, bf16[128,27,5,128]{3,0,2,1:T(8,128)(2,1)S(1)} %bitcast.206, f32[27,128,128,1]{2,1,3,0:T(8,128)S(1)} %fusion.8, f32[27,128,128,1]{2,1,3,0:T(8,128)S(1)} %copy-done.4), kind=kOutput, calls=%fused_computation.2 | convolution fusion | flops 571097088 | bytes 16810524 | tf_op jit(solution)/shard_map/thj,thpk->hpjk/dot_general | solution.py:76
  77.4 10.4 %copy.50 = f32[27,5,128,128]{3,2,1,0:T(8,128)} copy(f32[27,5,128,128]{2,3,1,0:T(8,128)} %multiply_bitcast_fusion) | data formatting | bytes 17694720 | tf_op jit(solution)/shard_map/mul | solution.py:76
  88.8 3.1 %collective-permute-start.30 = (bf16[1080,128]{1,0:T(8,128)(2,1)S(1)}, bf16[1080,128]{1,0:T(8,128)(2,1)}, u32[]{:S(2)}, u32[]{:S(2)}) collective-permute-start(bf16[1080,128]{1,0:T(8,128)(2,1)S(1)} %dynamic-slice_convert_fusion), channel_id=1, source_target_pairs={{0,8},{1,5},{8,16},{9,1},{16,24},{17,9},{24,26},{25,17},{26,18},{2... | collective-permute-start | bytes 829448 | tf_op jit(solution)/shard_map/ppermute | solution.py:45
  91.8 7.1 %copy.39 = bf16[27,5,128,128]{2,3,1,0:T(8,128)(2,1)} copy(bf16[27,5,128,128]{3,2,1,0:T(8,128)(2,1)} %bitcast.153) | data formatting | bytes 8847360 | tf_op jit(solution)/shard_map/gather | solution.py:66
  99.0 3.8 %fusion.5 = f32[27,5,128,128]{3,2,1,0:T(8,128)S(1)} fusion(bf16[1,27,5,128,128]{4,3,2,1,0:T(8,128)(2,1)} %param.13, bf16[27,5]{1,0:T(8,128)(2,1)S(1)} %get-tuple-element.26, bf16[128,27,128]{0,2,1:T(8,128)(2,1)S(1)} %get-tuple-element.8), kind=kOutput, calls=%fused_computation.14 | convolution fusion | flops 568442880 | bytes 14156046 | tf_op jit(solution)/shard_map/thj,hpkj->thpk/dot_general | solution.py:88
  102.8 2.6 broadcast_multiply_fusion.1
  105.5 1.6 collective-permute-start
  107.1 4.8 %broadcast_multiply_fusion = f32[27,5,128,128]{3,2,1,0:T(8,128)} fusion(f32[27,5]{1,0:T(8,128)S(1)} %get-tuple-element.25, bf16[128,27,128,1]{0,2,3,1:T(8,128)(2,1)S(1)} %copy-done.6, bf16[27,5,128,128]{2,3,1,0:T(8,128)(2,1)S(1)} %copy-done.1), kind=kOutput, calls=%fused_computation.12 | convolution fusion | flops 568442880 | bytes 14156316 | tf_op jit(solution)/shard_map/thpk,thj->hpkj/dot_general | solution.py:86
  113.0 1.6 collective-permute-start.15
  114.7 4.8 %add_bitcast_fusion = f32[128,27,5,128]{0,3,2,1:T(8,128)} fusion(f32[27,5,128,128]{3,2,1,0:T(8,128)S(1)} %fusion.5, bf16[128,27,128,1]{0,2,3,1:T(8,128)(2,1)S(1)} %copy-done.6, bf16[1,27,5,128,128]{4,3,2,1,0:T(8,128)(2,1)S(1)} %bitcast.208, bf16[27,5]{1,0:T(8,128)(2,1)S(1)} %get-tuple-element.26), kind=kOutput, calls=%fused_computation.3 | convolution fusion | flops 570654720 | bytes 23003406 | tf_op jit(solution)/shard_map/thj,hpkj->thpk/dot_general | solution.py:89
  119.4 11.2 %copy.46 = f32[128,27,5,128]{3,1,2,0:T(8,128)} copy(f32[128,27,5,128]{0,3,2,1:T(8,128)} %add_bitcast_fusion) | data formatting | bytes 17694720 | tf_op jit(solution)/shard_map/add | solution.py:89
  130.6 8.2 %bitcast_convert_fusion = bf16[40,128,128]{2,0,1:T(8,128)(2,1)S(1)} fusion(f32[128,27,5,128]{3,1,2,0:T(8,128)} %copy.46, s32[27,5]{0,1:T(8,128)S(1)} %copy-done.10), kind=kOutput, calls=%fused_computation.18 | convolution fusion | flops 1062343936 | bytes 10158620 | tf_op jit(solution)/shard_map/thpk,hpd->tdk/dot_general | solution.py:93
  141.4 1.5 collective-permute-start.31
  149.1 1.5 collective-permute-start.32
  152.0 1.5 collective-permute-start.2
  155.0 1.5 collective-permute-start.17
  158.0 1.5 collective-permute-start.33
  160.9 1.5 collective-permute-start.3
  163.9 1.5 collective-permute-start.18
  166.9 1.5 collective-permute-start.34
  169.8 1.5 collective-permute-start.4
  172.8 1.5 collective-permute-start.19
  175.7 1.5 collective-permute-start.35
  178.7 1.5 collective-permute-start.5
  181.7 1.5 collective-permute-start.20
  184.6 1.5 collective-permute-start.36
  187.6 1.5 collective-permute-start.6
  190.6 1.5 collective-permute-start.21
  192.5 1.5 collective-permute-start.37
  196.5 1.5 collective-permute-start.7
  199.4 1.5 collective-permute-start.22
  205.4 1.5 collective-permute-start.8
  217.2 1.5 collective-permute-start.24
  228.0 1.5 collective-permute-start.41
  236.9 1.5 collective-permute-start.42
  240.9 1.5 collective-permute-start.12
  263.5 2.9 %collective-permute-done.14 = bf16[1080,128]{1,0:T(8,128)(2,1)S(1)} collective-permute-done((bf16[1080,128]{1,0:T(8,128)(2,1)S(1)}, bf16[1080,128]{1,0:T(8,128)(2,1)S(1)}, u32[]{:S(2)}, u32[]{:S(2)}) %collective-permute-start.14) | collective-permute-done | bytes 276512 | tf_op jit(solution)/shard_map/ppermute | solution.py:45
  267.6 1.9 collective-permute-done.29
  270.5 2.8 %add_divide_fusion = (f32[3,1,1080,128]{3,2,1,0:T(8,128)}, f32[3,1,1080,128]{3,2,1,0:T(8,128)}, f32[3,1,1080,128]{3,2,1,0:T(8,128)}) fusion(f32[1,1,1080,128]{3,2,1,0:T(8,128)S(1)} %add_bitcast_fusion.1, f32[1,1,1080,128]{3,2,1,0:T(8,128)S(1)} %add_bitcast_fusion.2, f32[1,1,1080,128]{3,2,1,0:T(8,128)S(1)} %add_bitcast_fusion.3, ...), kind=kLoop, calls=%fused_computation.40 | loop fusion | flops 4976640 | bytes 9953280 | tf_op jit(solution)/shard_map/div | solution.py:111
  (162 shorter events, 94.8 us)
Async XLA Ops:
  7.2 27.7 %all-gather.5.cloned.1.call-start = ((), (), s32[]{:S(2)}) async-start(), calls=%async_computation.2 | async-start | bytes 1966080 | tf_op jit(solution)/shard_map/all_gather | solution.py:52
  9.4 27.3 %all-gather.3.cloned.1.call-start = ((), (), s32[]{:S(2)}) async-start(), calls=%async_computation.1 | async-start | bytes 1966080 | tf_op jit(solution)/shard_map/all_gather | solution.py:53
  11.7 261.7 %reduce-scatter.2.cloned.1.call-start = ((), (), s32[]{:S(2)}) async-start(), calls=%async_computation.3 | async-start | bytes 1966080 | tf_op jit(solution)/shard_map/reduce_scatter | solution.py:104
  88.8 51.4 %collective-permute-start.30 = (bf16[1080,128]{1,0:T(8,128)(2,1)S(1)}, bf16[1080,128]{1,0:T(8,128)(2,1)}, u32[]{:S(2)}, u32[]{:S(2)}) collective-permute-start(bf16[1080,128]{1,0:T(8,128)(2,1)S(1)} %dynamic-slice_convert_fusion), channel_id=1, source_target_pairs={{0,8},{1,5},{8,16},{9,1},{16,24},{17,9},{24,26},{25,17},{26,18},{2... | collective-permute-start | bytes 829448 | tf_op jit(solution)/shard_map/ppermute | solution.py:45
  105.5 37.4 %collective-permute-start = (bf16[1080,128]{1,0:T(8,128)(2,1)S(1)}, bf16[1080,128]{1,0:T(8,128)(2,1)}, u32[]{:S(2)}, u32[]{:S(2)}) collective-permute-start(bf16[1080,128]{1,0:T(8,128)(2,1)S(1)} %dynamic-slice_convert_fusion.2), channel_id=1, source_target_pairs={{0,8},{1,5},{8,16},{9,1},{16,24},{17,9},{24,26},{25,17},{26,18},{2... | collective-permute-start | bytes 829448 | tf_op jit(solution)/shard_map/ppermute | solution.py:45
  113.0 32.2 %collective-permute-start.15 = (bf16[1080,128]{1,0:T(8,128)(2,1)S(1)}, bf16[1080,128]{1,0:T(8,128)(2,1)S(1)}, u32[]{:S(2)}, u32[]{:S(2)}) collective-permute-start(bf16[1080,128]{1,0:T(8,128)(2,1)S(1)} %dynamic-slice_convert_fusion.1), channel_id=1, source_target_pairs={{0,8},{1,5},{8,16},{9,1},{16,24},{17,9},{24,26},{25,17},{26,18},{2... | collective-permute-start | bytes 829448 | tf_op jit(solution)/shard_map/ppermute | solution.py:45
  141.4 6.6 %collective-permute-start.31 = (bf16[1080,128]{1,0:T(8,128)(2,1)S(1)}, bf16[1080,128]{1,0:T(8,128)(2,1)S(1)}, u32[]{:S(2)}, u32[]{:S(2)}) collective-permute-start(bf16[1080,128]{1,0:T(8,128)(2,1)S(1)} %add_convert_fusion.13), channel_id=1, source_target_pairs={{0,8},{1,5},{8,16},{9,1},{16,24},{17,9},{24,26},{25,17},{26,18},{2... | collective-permute-start | bytes 829448 | tf_op jit(solution)/shard_map/ppermute | solution.py:45
  144.1 6.8 %collective-permute-start.1 = (bf16[1080,128]{1,0:T(8,128)(2,1)S(1)}, bf16[1080,128]{1,0:T(8,128)(2,1)S(1)}, u32[]{:S(2)}, u32[]{:S(2)}) collective-permute-start(bf16[1080,128]{1,0:T(8,128)(2,1)S(1)} %add_convert_fusion.41), channel_id=1, source_target_pairs={{0,8},{1,5},{8,16},{9,1},{16,24},{17,9},{24,26},{25,17},{26,18},{2... | collective-permute-start | bytes 829448 | tf_op jit(solution)/shard_map/ppermute | solution.py:45
  146.4 7.5 %collective-permute-start.16 = (bf16[1080,128]{1,0:T(8,128)(2,1)S(1)}, bf16[1080,128]{1,0:T(8,128)(2,1)S(1)}, u32[]{:S(2)}, u32[]{:S(2)}) collective-permute-start(bf16[1080,128]{1,0:T(8,128)(2,1)S(1)} %add_convert_fusion.27), channel_id=1, source_target_pairs={{0,8},{1,5},{8,16},{9,1},{16,24},{17,9},{24,26},{25,17},{26,18},{2... | collective-permute-start | bytes 829448 | tf_op jit(solution)/shard_map/ppermute | solution.py:45
  149.1 7.8 %collective-permute-start.32 = (bf16[1080,128]{1,0:T(8,128)(2,1)S(1)}, bf16[1080,128]{1,0:T(8,128)(2,1)S(1)}, u32[]{:S(2)}, u32[]{:S(2)}) collective-permute-start(bf16[1080,128]{1,0:T(8,128)(2,1)S(1)} %add_convert_fusion.12), channel_id=1, source_target_pairs={{0,8},{1,5},{8,16},{9,1},{16,24},{17,9},{24,26},{25,17},{26,18},{2... | collective-permute-start | bytes 829448 | tf_op jit(solution)/shard_map/ppermute | solution.py:45
  152.0 7.8 %collective-permute-start.2 = (bf16[1080,128]{1,0:T(8,128)(2,1)S(1)}, bf16[1080,128]{1,0:T(8,128)(2,1)S(1)}, u32[]{:S(2)}, u32[]{:S(2)}) collective-permute-start(bf16[1080,128]{1,0:T(8,128)(2,1)S(1)} %add_convert_fusion.40), channel_id=1, source_target_pairs={{0,8},{1,5},{8,16},{9,1},{16,24},{17,9},{24,26},{25,17},{26,18},{2... | collective-permute-start | bytes 829448 | tf_op jit(solution)/shard_map/ppermute | solution.py:45
  155.0 7.8 %collective-permute-start.17 = (bf16[1080,128]{1,0:T(8,128)(2,1)S(1)}, bf16[1080,128]{1,0:T(8,128)(2,1)S(1)}, u32[]{:S(2)}, u32[]{:S(2)}) collective-permute-start(bf16[1080,128]{1,0:T(8,128)(2,1)S(1)} %add_convert_fusion.26), channel_id=1, source_target_pairs={{0,8},{1,5},{8,16},{9,1},{16,24},{17,9},{24,26},{25,17},{26,18},{2... | collective-permute-start | bytes 829448 | tf_op jit(solution)/shard_map/ppermute | solution.py:45
  158.0 7.8 %collective-permute-start.33 = (bf16[1080,128]{1,0:T(8,128)(2,1)S(1)}, bf16[1080,128]{1,0:T(8,128)(2,1)S(1)}, u32[]{:S(2)}, u32[]{:S(2)}) collective-permute-start(bf16[1080,128]{1,0:T(8,128)(2,1)S(1)} %add_convert_fusion.11), channel_id=1, source_target_pairs={{0,8},{1,5},{8,16},{9,1},{16,24},{17,9},{24,26},{25,17},{26,18},{2... | collective-permute-start | bytes 829448 | tf_op jit(solution)/shard_map/ppermute | solution.py:45
  160.9 7.8 %collective-permute-start.3 = (bf16[1080,128]{1,0:T(8,128)(2,1)S(1)}, bf16[1080,128]{1,0:T(8,128)(2,1)S(1)}, u32[]{:S(2)}, u32[]{:S(2)}) collective-permute-start(bf16[1080,128]{1,0:T(8,128)(2,1)S(1)} %add_convert_fusion.39), channel_id=1, source_target_pairs={{0,8},{1,5},{8,16},{9,1},{16,24},{17,9},{24,26},{25,17},{26,18},{2... | collective-permute-start | bytes 829448 | tf_op jit(solution)/shard_map/ppermute | solution.py:45
  163.9 7.8 %collective-permute-start.18 = (bf16[1080,128]{1,0:T(8,128)(2,1)S(1)}, bf16[1080,128]{1,0:T(8,128)(2,1)S(1)}, u32[]{:S(2)}, u32[]{:S(2)}) collective-permute-start(bf16[1080,128]{1,0:T(8,128)(2,1)S(1)} %add_convert_fusion.25), channel_id=1, source_target_pairs={{0,8},{1,5},{8,16},{9,1},{16,24},{17,9},{24,26},{25,17},{26,18},{2... | collective-permute-start | bytes 829448 | tf_op jit(solution)/shard_map/ppermute | solution.py:45
  166.9 7.8 %collective-permute-start.34 = (bf16[1080,128]{1,0:T(8,128)(2,1)S(1)}, bf16[1080,128]{1,0:T(8,128)(2,1)S(1)}, u32[]{:S(2)}, u32[]{:S(2)}) collective-permute-start(bf16[1080,128]{1,0:T(8,128)(2,1)S(1)} %add_convert_fusion.10), channel_id=1, source_target_pairs={{0,8},{1,5},{8,16},{9,1},{16,24},{17,9},{24,26},{25,17},{26,18},{2... | collective-permute-start | bytes 829448 | tf_op jit(solution)/shard_map/ppermute | solution.py:45
  169.8 7.8 %collective-permute-start.4 = (bf16[1080,128]{1,0:T(8,128)(2,1)S(1)}, bf16[1080,128]{1,0:T(8,128)(2,1)S(1)}, u32[]{:S(2)}, u32[]{:S(2)}) collective-permute-start(bf16[1080,128]{1,0:T(8,128)(2,1)S(1)} %add_convert_fusion.38), channel_id=1, source_target_pairs={{0,8},{1,5},{8,16},{9,1},{16,24},{17,9},{24,26},{25,17},{26,18},{2... | collective-permute-start | bytes 829448 | tf_op jit(solution)/shard_map/ppermute | solution.py:45
  172.8 7.8 %collective-permute-start.19 = (bf16[1080,128]{1,0:T(8,128)(2,1)S(1)}, bf16[1080,128]{1,0:T(8,128)(2,1)S(1)}, u32[]{:S(2)}, u32[]{:S(2)}) collective-permute-start(bf16[1080,128]{1,0:T(8,128)(2,1)S(1)} %add_convert_fusion.24), channel_id=1, source_target_pairs={{0,8},{1,5},{8,16},{9,1},{16,24},{17,9},{24,26},{25,17},{26,18},{2... | collective-permute-start | bytes 829448 | tf_op jit(solution)/shard_map/ppermute | solution.py:45
  175.7 7.8 %collective-permute-start.35 = (bf16[1080,128]{1,0:T(8,128)(2,1)S(1)}, bf16[1080,128]{1,0:T(8,128)(2,1)S(1)}, u32[]{:S(2)}, u32[]{:S(2)}) collective-permute-start(bf16[1080,128]{1,0:T(8,128)(2,1)S(1)} %add_convert_fusion.9), channel_id=1, source_target_pairs={{0,8},{1,5},{8,16},{9,1},{16,24},{17,9},{24,26},{25,17},{26,18},{2... | collective-permute-start | bytes 829448 | tf_op jit(solution)/shard_map/ppermute | solution.py:45
  178.7 7.8 %collective-permute-start.5 = (bf16[1080,128]{1,0:T(8,128)(2,1)S(1)}, bf16[1080,128]{1,0:T(8,128)(2,1)S(1)}, u32[]{:S(2)}, u32[]{:S(2)}) collective-permute-start(bf16[1080,128]{1,0:T(8,128)(2,1)S(1)} %add_convert_fusion.37), channel_id=1, source_target_pairs={{0,8},{1,5},{8,16},{9,1},{16,24},{17,9},{24,26},{25,17},{26,18},{2... | collective-permute-start | bytes 829448 | tf_op jit(solution)/shard_map/ppermute | solution.py:45
  181.7 7.8 %collective-permute-start.20 = (bf16[1080,128]{1,0:T(8,128)(2,1)S(1)}, bf16[1080,128]{1,0:T(8,128)(2,1)S(1)}, u32[]{:S(2)}, u32[]{:S(2)}) collective-permute-start(bf16[1080,128]{1,0:T(8,128)(2,1)S(1)} %add_convert_fusion.23), channel_id=1, source_target_pairs={{0,8},{1,5},{8,16},{9,1},{16,24},{17,9},{24,26},{25,17},{26,18},{2... | collective-permute-start | bytes 829448 | tf_op jit(solution)/shard_map/ppermute | solution.py:45
  184.6 7.8 %collective-permute-start.36 = (bf16[1080,128]{1,0:T(8,128)(2,1)S(1)}, bf16[1080,128]{1,0:T(8,128)(2,1)S(1)}, u32[]{:S(2)}, u32[]{:S(2)}) collective-permute-start(bf16[1080,128]{1,0:T(8,128)(2,1)S(1)} %add_convert_fusion.8), channel_id=1, source_target_pairs={{0,8},{1,5},{8,16},{9,1},{16,24},{17,9},{24,26},{25,17},{26,18},{2... | collective-permute-start | bytes 829448 | tf_op jit(solution)/shard_map/ppermute | solution.py:45
  187.6 7.8 %collective-permute-start.6 = (bf16[1080,128]{1,0:T(8,128)(2,1)S(1)}, bf16[1080,128]{1,0:T(8,128)(2,1)S(1)}, u32[]{:S(2)}, u32[]{:S(2)}) collective-permute-start(bf16[1080,128]{1,0:T(8,128)(2,1)S(1)} %add_convert_fusion.36), channel_id=1, source_target_pairs={{0,8},{1,5},{8,16},{9,1},{16,24},{17,9},{24,26},{25,17},{26,18},{2... | collective-permute-start | bytes 829448 | tf_op jit(solution)/shard_map/ppermute | solution.py:45
  190.6 7.8 %collective-permute-start.21 = (bf16[1080,128]{1,0:T(8,128)(2,1)S(1)}, bf16[1080,128]{1,0:T(8,128)(2,1)S(1)}, u32[]{:S(2)}, u32[]{:S(2)}) collective-permute-start(bf16[1080,128]{1,0:T(8,128)(2,1)S(1)} %add_convert_fusion.22), channel_id=1, source_target_pairs={{0,8},{1,5},{8,16},{9,1},{16,24},{17,9},{24,26},{25,17},{26,18},{2... | collective-permute-start | bytes 829448 | tf_op jit(solution)/shard_map/ppermute | solution.py:45
  192.5 8.8 %collective-permute-start.37 = (bf16[1080,128]{1,0:T(8,128)(2,1)S(1)}, bf16[1080,128]{1,0:T(8,128)(2,1)S(1)}, u32[]{:S(2)}, u32[]{:S(2)}) collective-permute-start(bf16[1080,128]{1,0:T(8,128)(2,1)S(1)} %add_convert_fusion.7), channel_id=1, source_target_pairs={{0,8},{1,5},{8,16},{9,1},{16,24},{17,9},{24,26},{25,17},{26,18},{2... | collective-permute-start | bytes 829448 | tf_op jit(solution)/shard_map/ppermute | solution.py:45
  196.5 7.8 %collective-permute-start.7 = (bf16[1080,128]{1,0:T(8,128)(2,1)S(1)}, bf16[1080,128]{1,0:T(8,128)(2,1)S(1)}, u32[]{:S(2)}, u32[]{:S(2)}) collective-permute-start(bf16[1080,128]{1,0:T(8,128)(2,1)S(1)} %add_convert_fusion.35), channel_id=1, source_target_pairs={{0,8},{1,5},{8,16},{9,1},{16,24},{17,9},{24,26},{25,17},{26,18},{2... | collective-permute-start | bytes 829448 | tf_op jit(solution)/shard_map/ppermute | solution.py:45
  199.4 7.8 %collective-permute-start.22 = (bf16[1080,128]{1,0:T(8,128)(2,1)S(1)}, bf16[1080,128]{1,0:T(8,128)(2,1)S(1)}, u32[]{:S(2)}, u32[]{:S(2)}) collective-permute-start(bf16[1080,128]{1,0:T(8,128)(2,1)S(1)} %add_convert_fusion.21), channel_id=1, source_target_pairs={{0,8},{1,5},{8,16},{9,1},{16,24},{17,9},{24,26},{25,17},{26,18},{2... | collective-permute-start | bytes 829448 | tf_op jit(solution)/shard_map/ppermute | solution.py:45
  201.4 8.8 %collective-permute-start.38 = (bf16[1080,128]{1,0:T(8,128)(2,1)S(1)}, bf16[1080,128]{1,0:T(8,128)(2,1)S(1)}, u32[]{:S(2)}, u32[]{:S(2)}) collective-permute-start(bf16[1080,128]{1,0:T(8,128)(2,1)S(1)} %add_convert_fusion.6), channel_id=1, source_target_pairs={{0,8},{1,5},{8,16},{9,1},{16,24},{17,9},{24,26},{25,17},{26,18},{2... | collective-permute-start | bytes 829448 | tf_op jit(solution)/shard_map/ppermute | solution.py:45
  205.4 7.8 %collective-permute-start.8 = (bf16[1080,128]{1,0:T(8,128)(2,1)S(1)}, bf16[1080,128]{1,0:T(8,128)(2,1)S(1)}, u32[]{:S(2)}, u32[]{:S(2)}) collective-permute-start(bf16[1080,128]{1,0:T(8,128)(2,1)S(1)} %add_convert_fusion.34), channel_id=1, source_target_pairs={{0,8},{1,5},{8,16},{9,1},{16,24},{17,9},{24,26},{25,17},{26,18},{2... | collective-permute-start | bytes 829448 | tf_op jit(solution)/shard_map/ppermute | solution.py:45
  208.3 7.8 %collective-permute-start.23 = (bf16[1080,128]{1,0:T(8,128)(2,1)S(1)}, bf16[1080,128]{1,0:T(8,128)(2,1)S(1)}, u32[]{:S(2)}, u32[]{:S(2)}) collective-permute-start(bf16[1080,128]{1,0:T(8,128)(2,1)S(1)} %add_convert_fusion.20), channel_id=1, source_target_pairs={{0,8},{1,5},{8,16},{9,1},{16,24},{17,9},{24,26},{25,17},{26,18},{2... | collective-permute-start | bytes 829448 | tf_op jit(solution)/shard_map/ppermute | solution.py:45
  210.2 8.8 %collective-permute-start.39 = (bf16[1080,128]{1,0:T(8,128)(2,1)S(1)}, bf16[1080,128]{1,0:T(8,128)(2,1)S(1)}, u32[]{:S(2)}, u32[]{:S(2)}) collective-permute-start(bf16[1080,128]{1,0:T(8,128)(2,1)S(1)} %add_convert_fusion.5), channel_id=1, source_target_pairs={{0,8},{1,5},{8,16},{9,1},{16,24},{17,9},{24,26},{25,17},{26,18},{2... | collective-permute-start | bytes 829448 | tf_op jit(solution)/shard_map/ppermute | solution.py:45
  214.3 7.8 %collective-permute-start.9 = (bf16[1080,128]{1,0:T(8,128)(2,1)S(1)}, bf16[1080,128]{1,0:T(8,128)(2,1)S(1)}, u32[]{:S(2)}, u32[]{:S(2)}) collective-permute-start(bf16[1080,128]{1,0:T(8,128)(2,1)S(1)} %add_convert_fusion.33), channel_id=1, source_target_pairs={{0,8},{1,5},{8,16},{9,1},{16,24},{17,9},{24,26},{25,17},{26,18},{2... | collective-permute-start | bytes 829448 | tf_op jit(solution)/shard_map/ppermute | solution.py:45
  217.2 7.8 %collective-permute-start.24 = (bf16[1080,128]{1,0:T(8,128)(2,1)S(1)}, bf16[1080,128]{1,0:T(8,128)(2,1)S(1)}, u32[]{:S(2)}, u32[]{:S(2)}) collective-permute-start(bf16[1080,128]{1,0:T(8,128)(2,1)S(1)} %add_convert_fusion.19), channel_id=1, source_target_pairs={{0,8},{1,5},{8,16},{9,1},{16,24},{17,9},{24,26},{25,17},{26,18},{2... | collective-permute-start | bytes 829448 | tf_op jit(solution)/shard_map/ppermute | solution.py:45
  219.1 8.8 %collective-permute-start.40 = (bf16[1080,128]{1,0:T(8,128)(2,1)S(1)}, bf16[1080,128]{1,0:T(8,128)(2,1)S(1)}, u32[]{:S(2)}, u32[]{:S(2)}) collective-permute-start(bf16[1080,128]{1,0:T(8,128)(2,1)S(1)} %add_convert_fusion.4), channel_id=1, source_target_pairs={{0,8},{1,5},{8,16},{9,1},{16,24},{17,9},{24,26},{25,17},{26,18},{2... | collective-permute-start | bytes 829448 | tf_op jit(solution)/shard_map/ppermute | solution.py:45
  223.1 7.8 %collective-permute-start.10 = (bf16[1080,128]{1,0:T(8,128)(2,1)S(1)}, bf16[1080,128]{1,0:T(8,128)(2,1)S(1)}, u32[]{:S(2)}, u32[]{:S(2)}) collective-permute-start(bf16[1080,128]{1,0:T(8,128)(2,1)S(1)} %add_convert_fusion.32), channel_id=1, source_target_pairs={{0,8},{1,5},{8,16},{9,1},{16,24},{17,9},{24,26},{25,17},{26,18},{2... | collective-permute-start | bytes 829448 | tf_op jit(solution)/shard_map/ppermute | solution.py:45
  226.1 7.8 %collective-permute-start.25 = (bf16[1080,128]{1,0:T(8,128)(2,1)S(1)}, bf16[1080,128]{1,0:T(8,128)(2,1)S(1)}, u32[]{:S(2)}, u32[]{:S(2)}) collective-permute-start(bf16[1080,128]{1,0:T(8,128)(2,1)S(1)} %add_convert_fusion.18), channel_id=1, source_target_pairs={{0,8},{1,5},{8,16},{9,1},{16,24},{17,9},{24,26},{25,17},{26,18},{2... | collective-permute-start | bytes 829448 | tf_op jit(solution)/shard_map/ppermute | solution.py:45
  228.0 8.8 %collective-permute-start.41 = (bf16[1080,128]{1,0:T(8,128)(2,1)S(1)}, bf16[1080,128]{1,0:T(8,128)(2,1)S(1)}, u32[]{:S(2)}, u32[]{:S(2)}) collective-permute-start(bf16[1080,128]{1,0:T(8,128)(2,1)S(1)} %add_convert_fusion.3), channel_id=1, source_target_pairs={{0,8},{1,5},{8,16},{9,1},{16,24},{17,9},{24,26},{25,17},{26,18},{2... | collective-permute-start | bytes 829448 | tf_op jit(solution)/shard_map/ppermute | solution.py:45
  232.0 7.8 %collective-permute-start.11 = (bf16[1080,128]{1,0:T(8,128)(2,1)S(1)}, bf16[1080,128]{1,0:T(8,128)(2,1)S(1)}, u32[]{:S(2)}, u32[]{:S(2)}) collective-permute-start(bf16[1080,128]{1,0:T(8,128)(2,1)S(1)} %add_convert_fusion.31), channel_id=1, source_target_pairs={{0,8},{1,5},{8,16},{9,1},{16,24},{17,9},{24,26},{25,17},{26,18},{2... | collective-permute-start | bytes 829448 | tf_op jit(solution)/shard_map/ppermute | solution.py:45
  235.0 7.8 %collective-permute-start.26 = (bf16[1080,128]{1,0:T(8,128)(2,1)S(1)}, bf16[1080,128]{1,0:T(8,128)(2,1)S(1)}, u32[]{:S(2)}, u32[]{:S(2)}) collective-permute-start(bf16[1080,128]{1,0:T(8,128)(2,1)S(1)} %add_convert_fusion.17), channel_id=1, source_target_pairs={{0,8},{1,5},{8,16},{9,1},{16,24},{17,9},{24,26},{25,17},{26,18},{2... | collective-permute-start | bytes 829448 | tf_op jit(solution)/shard_map/ppermute | solution.py:45
  236.9 8.8 %collective-permute-start.42 = (bf16[1080,128]{1,0:T(8,128)(2,1)S(1)}, bf16[1080,128]{1,0:T(8,128)(2,1)S(1)}, u32[]{:S(2)}, u32[]{:S(2)}) collective-permute-start(bf16[1080,128]{1,0:T(8,128)(2,1)S(1)} %add_convert_fusion.2), channel_id=1, source_target_pairs={{0,8},{1,5},{8,16},{9,1},{16,24},{17,9},{24,26},{25,17},{26,18},{2... | collective-permute-start | bytes 829448 | tf_op jit(solution)/shard_map/ppermute | solution.py:45
  240.9 7.8 %collective-permute-start.12 = (bf16[1080,128]{1,0:T(8,128)(2,1)S(1)}, bf16[1080,128]{1,0:T(8,128)(2,1)S(1)}, u32[]{:S(2)}, u32[]{:S(2)}) collective-permute-start(bf16[1080,128]{1,0:T(8,128)(2,1)S(1)} %add_convert_fusion.30), channel_id=1, source_target_pairs={{0,8},{1,5},{8,16},{9,1},{16,24},{17,9},{24,26},{25,17},{26,18},{2... | collective-permute-start | bytes 829448 | tf_op jit(solution)/shard_map/ppermute | solution.py:45
  243.9 7.8 %collective-permute-start.27 = (bf16[1080,128]{1,0:T(8,128)(2,1)S(1)}, bf16[1080,128]{1,0:T(8,128)(2,1)S(1)}, u32[]{:S(2)}, u32[]{:S(2)}) collective-permute-start(bf16[1080,128]{1,0:T(8,128)(2,1)S(1)} %add_convert_fusion.16), channel_id=1, source_target_pairs={{0,8},{1,5},{8,16},{9,1},{16,24},{17,9},{24,26},{25,17},{26,18},{2... | collective-permute-start | bytes 829448 | tf_op jit(solution)/shard_map/ppermute | solution.py:45
  245.8 8.8 %collective-permute-start.43 = (bf16[1080,128]{1,0:T(8,128)(2,1)S(1)}, bf16[1080,128]{1,0:T(8,128)(2,1)S(1)}, u32[]{:S(2)}, u32[]{:S(2)}) collective-permute-start(bf16[1080,128]{1,0:T(8,128)(2,1)S(1)} %add_convert_fusion.1), channel_id=1, source_target_pairs={{0,8},{1,5},{8,16},{9,1},{16,24},{17,9},{24,26},{25,17},{26,18},{2... | collective-permute-start | bytes 829448 | tf_op jit(solution)/shard_map/ppermute | solution.py:45
  249.8 7.7 %collective-permute-start.13 = (bf16[1080,128]{1,0:T(8,128)(2,1)S(1)}, bf16[1080,128]{1,0:T(8,128)(2,1)S(1)}, u32[]{:S(2)}, u32[]{:S(2)}) collective-permute-start(bf16[1080,128]{1,0:T(8,128)(2,1)S(1)} %add_convert_fusion.29), channel_id=1, source_target_pairs={{0,8},{1,5},{8,16},{9,1},{16,24},{17,9},{24,26},{25,17},{26,18},{2... | collective-permute-start | bytes 829448 | tf_op jit(solution)/shard_map/ppermute | solution.py:45
  252.8 7.8 %collective-permute-start.28 = (bf16[1080,128]{1,0:T(8,128)(2,1)S(1)}, bf16[1080,128]{1,0:T(8,128)(2,1)S(1)}, u32[]{:S(2)}, u32[]{:S(2)}) collective-permute-start(bf16[1080,128]{1,0:T(8,128)(2,1)S(1)} %add_convert_fusion.15), channel_id=1, source_target_pairs={{0,8},{1,5},{8,16},{9,1},{16,24},{17,9},{24,26},{25,17},{26,18},{2... | collective-permute-start | bytes 829448 | tf_op jit(solution)/shard_map/ppermute | solution.py:45
  254.7 8.8 %collective-permute-start.44 = (bf16[1080,128]{1,0:T(8,128)(2,1)S(1)}, bf16[1080,128]{1,0:T(8,128)(2,1)S(1)}, u32[]{:S(2)}, u32[]{:S(2)}) collective-permute-start(bf16[1080,128]{1,0:T(8,128)(2,1)S(1)} %add_convert_fusion), channel_id=1, source_target_pairs={{0,8},{1,5},{8,16},{9,1},{16,24},{17,9},{24,26},{25,17},{26,18},{2... | collective-permute-start | bytes 829448 | tf_op jit(solution)/shard_map/ppermute | solution.py:45
  258.7 7.8 %collective-permute-start.14 = (bf16[1080,128]{1,0:T(8,128)(2,1)S(1)}, bf16[1080,128]{1,0:T(8,128)(2,1)S(1)}, u32[]{:S(2)}, u32[]{:S(2)}) collective-permute-start(bf16[1080,128]{1,0:T(8,128)(2,1)S(1)} %add_convert_fusion.28), channel_id=1, source_target_pairs={{0,8},{1,5},{8,16},{9,1},{16,24},{17,9},{24,26},{25,17},{26,18},{2... | collective-permute-start | bytes 829448 | tf_op jit(solution)/shard_map/ppermute | solution.py:45
  261.7 7.8 %collective-permute-start.29 = (bf16[1080,128]{1,0:T(8,128)(2,1)S(1)}, bf16[1080,128]{1,0:T(8,128)(2,1)S(1)}, u32[]{:S(2)}, u32[]{:S(2)}) collective-permute-start(bf16[1080,128]{1,0:T(8,128)(2,1)S(1)} %add_convert_fusion.14), channel_id=1, source_target_pairs={{0,8},{1,5},{8,16},{9,1},{16,24},{17,9},{24,26},{25,17},{26,18},{2... | collective-permute-start | bytes 829448 | tf_op jit(solution)/shard_map/ppermute | solution.py:45
  (17 other events, 320.8 us)
Sparse Core Ops, SparseCore 0:
  10.1 12.1 all-gather.4
  24.4 10.6 all-gather.2
  140.3 7.5 reduce-scatter.1

commit v3 on v2

--- a/solution.py
+++ b/solution.py
@@ -4,6 +4,8 @@
 import jax
 import jax.numpy as jnp
 from jax import lax
+from jax.experimental import pallas as pl
+from jax.experimental.pallas import tpu as pltpu
 from jax.sharding import PartitionSpec as P
 
 D = 5120
@@ -47,51 +49,89 @@
     return accs
 
 
+def _ffn_kernel(col_ref, cnt_ref, tok_ref, cot_ref, wg_ref, wu_ref, wd_ref,
+                gg_ref, gu_ref, gd_ref, dx_ref):
+    h = pl.program_id(0)
+    slots = wg_ref.shape[1]
+    count = cnt_ref[h]
+
+    @pl.when(h == 0)
+    def _():
+        dx_ref[...] = jnp.zeros_like(dx_ref)
+
+    offs, xs, dys, wgs, wus, wds = [], [], [], [], [], []
+    for p in range(slots):
+        off = pl.multiple_of(col_ref[h, p] * BLK, BLK)
+        live = p < count
+        offs.append(off)
+        xs.append(tok_ref[:, pl.ds(off, BLK)])
+        dys.append(cot_ref[:, pl.ds(off, BLK)])
+        wgs.append(jnp.where(live, wg_ref[0, p], jnp.zeros_like(wg_ref[0, p])))
+        wus.append(jnp.where(live, wu_ref[0, p], jnp.zeros_like(wu_ref[0, p])))
+        wds.append(jnp.where(live, wd_ref[0, p], jnp.zeros_like(wd_ref[0, p])))
+    f32 = jnp.float32
+    nt = (((1,), (1,)), ((), ()))
+    tn = (((0,), (0,)), ((), ()))
+    gate = sum(jnp.dot(xs[p], wgs[p], preferred_element_type=f32) for p in range(slots))
+    up = sum(jnp.dot(xs[p], wus[p], preferred_element_type=f32) for p in range(slots))
+    d_hidden = sum(
+        lax.dot_general(dys[p], wds[p], nt, preferred_element_type=f32) for p in range(slots)
+    )
+    sig = 1.0 / (1.0 + jnp.exp(-gate))
+    silu = gate * sig
+    hidden = (silu * up).astype(jnp.bfloat16)
+    d_gate = (d_hidden * up * sig * (1.0 + gate * (1.0 - sig))).astype(jnp.bfloat16)
+    d_up = (d_hidden * silu).astype(jnp.bfloat16)
+    for p in range(slots):
+        live = p < count
+        zero = jnp.zeros((BLK, BLK), f32)
+        gg = lax.dot_general(xs[p], d_gate, tn, preferred_element_type=f32)
+        gu = lax.dot_general(xs[p], d_up, tn, preferred_element_type=f32)
+        gd = lax.dot_general(hidden, dys[p], tn, preferred_element_type=f32)
+        gg_ref[0, p] = jnp.where(live, gg, zero)
+        gu_ref[0, p] = jnp.where(live, gu, zero)
+        gd_ref[0, p] = jnp.where(live, gd, zero)
+        back = lax.dot_general(d_gate, wgs[p], nt, preferred_element_type=f32)
+        back = back + lax.dot_general(d_up, wus[p], nt, preferred_element_type=f32)
+        dx_ref[:, pl.ds(offs[p], BLK)] += back
+
+
+def ffn_block_terms(col_index, row_count, full_tok, full_cot, gate_w, up_w, down_w):
+    hblk, slots = col_index.shape
+    rows, width = full_tok.shape
+    wspec = pl.BlockSpec((1, slots, BLK, BLK), lambda h, c, n: (h, 0, 0, 0))
+    full = pl.BlockSpec((rows, width), lambda h, c, n: (0, 0))
+    grad = jax.ShapeDtypeStruct((hblk, slots, BLK, BLK), jnp.float32)
+    flops = 2 * rows * hblk * slots * BLK * BLK * 9
+    return pl.pallas_call(
+        _ffn_kernel,
+        grid_spec=pltpu.PrefetchScalarGridSpec(
+            num_scalar_prefetch=2,
+            grid=(hblk,),
+            in_specs=[full, full, wspec, wspec, wspec],
+            out_specs=[wspec, wspec, wspec, full],
+        ),
+        out_shape=[grad, grad, grad, jax.ShapeDtypeStruct((rows, width), jnp.float32)],
+        compiler_params=pltpu.CompilerParams(dimension_semantics=("arbitrary",)),
+        cost_estimate=pl.CostEstimate(
+            flops=flops,
+            transcendentals=rows * hblk * BLK,
+            bytes_accessed=3 * hblk * slots * BLK * BLK * 6 + rows * width * 8,
+        ),
+        name="ffn_block_terms",
+    )(col_index, row_count, full_tok, full_cot, gate_w, up_w, down_w)
+
+
 def shards(n_dp, n_t, tokens, cotangent, w_gate, w_up, w_down, col_index, row_count, adam_m, adam_v):
     full_tok, full_cot = (
         lax.all_gather(tokens, "tensor", axis=1, tiled=True),
         lax.all_gather(cotangent, "tensor", axis=1, tiled=True),
     )
     tok_rows = full_tok.shape[0]
-    gate_w = w_gate[0]
-    up_w = w_up[0]
-    down_w = w_down[0]
-    slot_count = gate_w.shape[1]
-    own_rows = gate_w.shape[0] * slot_count * BLK
-    live_mask = jnp.arange(slot_count)[None, :] < row_count[:, None]
-    keep_bf = live_mask.astype(jnp.bfloat16)[:, :, None, None]
-    gate_eff = gate_w * keep_bf
-    up_eff = up_w * keep_bf
-    down_eff = down_w * keep_bf
-    x_blocks = full_tok.reshape(tok_rows, D // BLK, BLK)[:, col_index]
-    dy_blocks = full_cot.reshape(tok_rows, D // BLK, BLK)[:, col_index]
-    gate_act = jnp.einsum("thpk,hpkj->thj", x_blocks, gate_eff, preferred_element_type=jnp.float32)
-    up_act = jnp.einsum("thpk,hpkj->thj", x_blocks, up_eff, preferred_element_type=jnp.float32)
-    sig_gate = jax.nn.sigmoid(gate_act)
-    silu_gate = gate_act * sig_gate
-    hidden = (silu_gate * up_act).astype(jnp.bfloat16)
-    d_hidden = jnp.einsum("thpk,hpjk->thj", dy_blocks, down_eff, preferred_element_type=jnp.float32)
-    live_f = live_mask.astype(jnp.float32)[:, :, None, None]
-    grad_down = (
-        jnp.einsum("thj,thpk->hpjk", hidden, dy_blocks, preferred_element_type=jnp.float32) * live_f
+    own_rows = w_gate.shape[1] * w_gate.shape[2] * BLK
+    grad_gate, grad_up, grad_down, dx_part = ffn_block_terms(
+        col_index, row_count, full_tok, full_cot, w_gate[0], w_up[0], w_down[0]
     )
-    d_gate = (d_hidden * up_act * sig_gate * (1.0 + gate_act * (1.0 - sig_gate))).astype(
-        jnp.bfloat16
-    )
-    d_up = (d_hidden * silu_gate).astype(jnp.bfloat16)
-    grad_gate = (
-        jnp.einsum("thpk,thj->hpkj", x_blocks, d_gate, preferred_element_type=jnp.float32) * live_f
-    )
-    grad_up = (
-        jnp.einsum("thpk,thj->hpkj", x_blocks, d_up, preferred_element_type=jnp.float32) * live_f
-    )
-    back_term = jnp.einsum("thj,hpkj->thpk", d_gate, gate_eff, preferred_element_type=jnp.float32)
-    back_term = back_term + jnp.einsum(
-        "thj,hpkj->thpk", d_up, up_eff, preferred_element_type=jnp.float32
-    )
-    onehot = (col_index[:, :, None] == jnp.arange(D // BLK)[None, None, :]).astype(jnp.float32)
-    dx_blocks = jnp.einsum("thpk,hpd->tdk", back_term, onehot, precision=lax.Precision.HIGHEST)
-    dx_part = dx_blocks.reshape(tok_rows, D)
     reduced = jnp.stack(
         ring_reduce_scatter(
             [g.reshape(own_rows, BLK) for g in (grad_gate, grad_up, grad_down)],

time: 283 us -> 226 us (0.80)
  local copies, waits for them, and re-layouts: 57.6 us -> 8.06 us
  matrix products: 47.7 us -> 0 us
  Pallas kernels: 0 us -> 37.1 us
  waiting for transfers between devices: 26.6 us -> 41.6 us
  other arithmetic: 43.8 us -> 32.7 us
    dot_general x9 -> x0, matrix products: 47.7 us -> none  [the longest x1 8.17 us: shards(): jnp.einsum('thpk,hpd->tdk', back_term, onehot, precision=lax.Precision.HI...]
    pallas_call x0 -> x1, Pallas kernels: none -> 37.1 us  [ffn_block_terms(): pl.pallas_call(_ffn_kernel, grid_spec=pltpu.PrefetchScalarGridSpec(num_sc...]
    gather x3 -> x0, local copies, waits for them, and re-layouts: 22.3 us -> none  [the longest x2 14.6 us: shards(): x_blocks = full_tok.reshape(tok_rows, D // BLK, BLK)[:, col_index]]
    ppermute x45, waiting for transfers between devices: 26.5 us -> 40.2 us  [ring_reduce_scatter(): moved = lax.ppermute(accs[i].astype(wire_dtype), ('dp', 'tensor'), perm)]
    convert_element_type x42, other arithmetic: 38.6 us -> 25.7 us  [ring_reduce_scatter(): moved = lax.ppermute(accs[i].astype(wire_dtype), ('dp', 'tensor'), perm)]
    add x1 -> x0, local copies, waits for them, and re-layouts: 11.2 us -> none  [shards(): back_term + jnp.einsum('thj,hpkj->thpk', d_up, up_eff, preferred_element_...]
    mul x1 -> x0, local copies, waits for them, and re-layouts: 10.4 us -> none  [shards(): jnp.einsum('thj,thpk->hpjk', hidden, dy_blocks, preferred_element_type=jn...]
    unnamed x37 -> x9, local copies, waits for them, and re-layouts: 5.75 us -> 1.4 us
  transfers between devices with their start and end apart: 48 -> 48, of which waited for: 42 -> 41; matrix products, arithmetic and copies ran while one was open for 34% -> 17% of each run, Pallas kernels for 0% -> 0%
where the time goes in v3:
time: 226 us; the launch traced here: 224 us
  starting transfers between devices  69.2 us (31%)
  waiting for transfers between devices  41.6 us (18%)
  Pallas kernels  37.1 us (16%)
  between operations  34.9 us (15%)
  other arithmetic  32.7 us (14%)
  local copies, waits for them, and re-layouts  8.06 us (4%)
    ppermute x45, starting transfers between devices, ring_reduce_scatter(): moved = lax.ppermute(accs[i].astype(wire_dtype), ('dp', 'tensor'), perm)  69.1 us
    ppermute x45, waiting for transfers between devices, ring_reduce_scatter(): moved = lax.ppermute(accs[i].astype(wire_dtype), ('dp', 'tensor'), perm)  40.2 us
    pallas_call x1, Pallas kernels, ffn_block_terms(): pl.pallas_call(_ffn_kernel, grid_spec=pltpu.PrefetchScalarGridSpec(num_sc...  37.1 us
    convert_element_type x42, other arithmetic, ring_reduce_scatter(): moved = lax.ppermute(accs[i].astype(wire_dtype), ('dp', 'tensor'), perm)  25.7 us
  transfers between devices with their start and end apart: 48, of which 41 were waited for; matrix products, arithmetic and copies ran while one was open for 17% of the time, Pallas kernels for 0%

profile of v3, /device:TPU:0, one launch (start us, length us, event | category | flops | bytes accessed | tf_op | source)
XLA Modules:
  0.0 223.5 jit_solution(12200929509462770956)
XLA Ops:
  20.7 2.0 fusion
  34.2 37.1 %ffn_block_terms.1 = (f32[27,5,128,128]{3,2,1,0:T(8,128)}, f32[27,5,128,128]{3,2,1,0:T(8,128)}, f32[27,5,128,128]{3,2,1,0:T(8,128)}, f32[128,5120]{1,0:T(8,128)}) custom-call(s32[27,5]{1,0:T(8,128)} %copy.15.col_ref, s32[27]{0:T(128)} %cnt_ref.1, bf16[128,5120]{1,0:T(8,128)(2,1)} %all-gather.3.cloned.1.call-done.tok_ref, ...), custom_call_target="tpu_custom_call" | custom-call | flops 5096079360 | bytes 45056000 | tf_op jit(solution)/shard_map/ffn_block_terms/pallas_call | solution.py:106
  71.3 3.0 %convert_element_type.273 = bf16[128,5120]{1,0:T(8,128)(2,1)} convert(f32[128,5120]{1,0:T(8,128)} %get-tuple-element.8) | non-fusion elementwise | flops 655360 | bytes 3932160 | tf_op jit(solution)/shard_map/convert_element_type | solution.py:145
  75.5 3.1 %collective-permute-start.30 = (bf16[1080,128]{1,0:T(8,128)(2,1)S(1)}, bf16[1080,128]{1,0:T(8,128)(2,1)S(1)}, u32[]{:S(2)}, u32[]{:S(2)}) collective-permute-start(bf16[1080,128]{1,0:T(8,128)(2,1)S(1)} %dynamic-slice_convert_fusion), channel_id=1, source_target_pairs={{0,8},{1,5},{8,16},{9,1},{16,24},{17,9},{24,26},{25,17},{26,18},{2... | collective-permute-start | bytes 829448 | tf_op jit(solution)/shard_map/ppermute | solution.py:47
  79.7 1.6 collective-permute-start.15
  82.4 1.6 collective-permute-start
  84.0 2.0 add_convert_fusion.13
  86.0 1.5 collective-permute-start.31
  91.0 1.6 collective-permute-start.1
  96.7 1.5 collective-permute-start.17
  99.7 1.5 collective-permute-start.2
  102.6 1.5 collective-permute-start.33
  105.6 1.5 collective-permute-start.18
  107.5 1.5 collective-permute-start.3
  111.5 1.5 collective-permute-start.34
  114.5 1.5 collective-permute-start.19
  116.4 1.5 collective-permute-start.4
  120.4 1.5 collective-permute-start.35
  123.4 1.5 collective-permute-start.20
  125.3 1.5 collective-permute-start.5
  129.3 1.5 collective-permute-start.36
  131.2 1.5 collective-permute-start.21
  134.2 1.5 collective-permute-start.6
  138.2 1.5 collective-permute-start.37
  140.1 1.5 collective-permute-start.22
  143.0 1.5 collective-permute-start.7
  147.1 1.5 collective-permute-start.38
  149.0 1.5 collective-permute-start.23
  151.9 1.5 collective-permute-start.8
  155.9 1.5 collective-permute-start.39
  157.9 1.5 collective-permute-start.24
  160.8 1.5 collective-permute-start.9
  164.8 1.5 collective-permute-start.40
  166.7 1.5 collective-permute-start.25
  169.7 1.5 collective-permute-start.10
  173.7 1.5 collective-permute-start.41
  175.6 1.5 collective-permute-start.26
  178.6 1.5 collective-permute-start.11
  182.6 1.5 collective-permute-start.42
  187.5 1.5 collective-permute-start.12
  191.5 1.5 collective-permute-start.43
  193.4 1.5 collective-permute-start.28
  196.4 1.5 collective-permute-start.13
  200.4 1.5 collective-permute-start.44
  205.3 1.5 collective-permute-start.14
  209.3 1.9 collective-permute-done.29
  211.2 2.9 %collective-permute-done.14 = bf16[1080,128]{1,0:T(8,128)(2,1)S(1)} collective-permute-done((bf16[1080,128]{1,0:T(8,128)(2,1)S(1)}, bf16[1080,128]{1,0:T(8,128)(2,1)S(1)}, u32[]{:S(2)}, u32[]{:S(2)}) %collective-permute-start.14) | collective-permute-done | bytes 276512 | tf_op jit(solution)/shard_map/ppermute | solution.py:47
  214.2 2.8 %add_divide_fusion = (f32[3,1,1080,128]{3,2,1,0:T(8,128)}, f32[3,1,1080,128]{3,2,1,0:T(8,128)}, f32[3,1,1080,128]{3,2,1,0:T(8,128)}) fusion(f32[1,1,1080,128]{3,2,1,0:T(8,128)S(1)} %add_bitcast_fusion, f32[1,1,1080,128]{3,2,1,0:T(8,128)S(1)} %add_bitcast_fusion.1, f32[1,1,1080,128]{3,2,1,0:T(8,128)S(1)} %add_bitcast_fusion.2, ...), kind=kLoop, calls=%fused_computation.1 | loop fusion | flops 4976640 | bytes 9953280 | tf_op jit(solution)/shard_map/div | solution.py:151
  (113 shorter events, 73.6 us)
Async XLA Ops:
  7.2 27.0 %all-gather.3.cloned.1.call-start = ((), (), s32[]{:S(2)}) async-start(), calls=%async_computation.1 | async-start | bytes 1966080 | tf_op jit(solution)/shard_map/all_gather | solution.py:127
  7.9 26.3 %all-gather.5.cloned.1.call-start = ((), (), s32[]{:S(2)}) async-start(), calls=%async_computation.2 | async-start | bytes 1966080 | tf_op jit(solution)/shard_map/all_gather | solution.py:128
  8.6 208.3 %reduce-scatter.2.cloned.1.call-start = ((), (), s32[]{:S(2)}) async-start(), calls=%async_computation.3 | async-start | bytes 1966080 | tf_op jit(solution)/shard_map/reduce_scatter | solution.py:144
  75.5 8.5 %collective-permute-start.30 = (bf16[1080,128]{1,0:T(8,128)(2,1)S(1)}, bf16[1080,128]{1,0:T(8,128)(2,1)S(1)}, u32[]{:S(2)}, u32[]{:S(2)}) collective-permute-start(bf16[1080,128]{1,0:T(8,128)(2,1)S(1)} %dynamic-slice_convert_fusion), channel_id=1, source_target_pairs={{0,8},{1,5},{8,16},{9,1},{16,24},{17,9},{24,26},{25,17},{26,18},{2... | collective-permute-start | bytes 829448 | tf_op jit(solution)/shard_map/ppermute | solution.py:47
  79.7 7.9 %collective-permute-start.15 = (bf16[1080,128]{1,0:T(8,128)(2,1)S(1)}, bf16[1080,128]{1,0:T(8,128)(2,1)S(1)}, u32[]{:S(2)}, u32[]{:S(2)}) collective-permute-start(bf16[1080,128]{1,0:T(8,128)(2,1)S(1)} %dynamic-slice_convert_fusion.1), channel_id=1, source_target_pairs={{0,8},{1,5},{8,16},{9,1},{16,24},{17,9},{24,26},{25,17},{26,18},{2... | collective-permute-start | bytes 829448 | tf_op jit(solution)/shard_map/ppermute | solution.py:47
  82.4 7.5 %collective-permute-start = (bf16[1080,128]{1,0:T(8,128)(2,1)S(1)}, bf16[1080,128]{1,0:T(8,128)(2,1)S(1)}, u32[]{:S(2)}, u32[]{:S(2)}) collective-permute-start(bf16[1080,128]{1,0:T(8,128)(2,1)S(1)} %dynamic-slice_convert_fusion.2), channel_id=1, source_target_pairs={{0,8},{1,5},{8,16},{9,1},{16,24},{17,9},{24,26},{25,17},{26,18},{2... | collective-permute-start | bytes 829448 | tf_op jit(solution)/shard_map/ppermute | solution.py:47
  86.0 6.6 %collective-permute-start.31 = (bf16[1080,128]{1,0:T(8,128)(2,1)S(1)}, bf16[1080,128]{1,0:T(8,128)(2,1)S(1)}, u32[]{:S(2)}, u32[]{:S(2)}) collective-permute-start(bf16[1080,128]{1,0:T(8,128)(2,1)S(1)} %add_convert_fusion.13), channel_id=1, source_target_pairs={{0,8},{1,5},{8,16},{9,1},{16,24},{17,9},{24,26},{25,17},{26,18},{2... | collective-permute-start | bytes 829448 | tf_op jit(solution)/shard_map/ppermute | solution.py:47
  88.7 6.9 %collective-permute-start.16 = (bf16[1080,128]{1,0:T(8,128)(2,1)S(1)}, bf16[1080,128]{1,0:T(8,128)(2,1)S(1)}, u32[]{:S(2)}, u32[]{:S(2)}) collective-permute-start(bf16[1080,128]{1,0:T(8,128)(2,1)S(1)} %add_convert_fusion.27), channel_id=1, source_target_pairs={{0,8},{1,5},{8,16},{9,1},{16,24},{17,9},{24,26},{25,17},{26,18},{2... | collective-permute-start | bytes 829448 | tf_op jit(solution)/shard_map/ppermute | solution.py:47
  91.0 7.6 %collective-permute-start.1 = (bf16[1080,128]{1,0:T(8,128)(2,1)S(1)}, bf16[1080,128]{1,0:T(8,128)(2,1)S(1)}, u32[]{:S(2)}, u32[]{:S(2)}) collective-permute-start(bf16[1080,128]{1,0:T(8,128)(2,1)S(1)} %add_convert_fusion.41), channel_id=1, source_target_pairs={{0,8},{1,5},{8,16},{9,1},{16,24},{17,9},{24,26},{25,17},{26,18},{2... | collective-permute-start | bytes 829448 | tf_op jit(solution)/shard_map/ppermute | solution.py:47
  93.7 7.8 %collective-permute-start.32 = (bf16[1080,128]{1,0:T(8,128)(2,1)S(1)}, bf16[1080,128]{1,0:T(8,128)(2,1)S(1)}, u32[]{:S(2)}, u32[]{:S(2)}) collective-permute-start(bf16[1080,128]{1,0:T(8,128)(2,1)S(1)} %add_convert_fusion.12), channel_id=1, source_target_pairs={{0,8},{1,5},{8,16},{9,1},{16,24},{17,9},{24,26},{25,17},{26,18},{2... | collective-permute-start | bytes 829448 | tf_op jit(solution)/shard_map/ppermute | solution.py:47
  96.7 7.8 %collective-permute-start.17 = (bf16[1080,128]{1,0:T(8,128)(2,1)S(1)}, bf16[1080,128]{1,0:T(8,128)(2,1)S(1)}, u32[]{:S(2)}, u32[]{:S(2)}) collective-permute-start(bf16[1080,128]{1,0:T(8,128)(2,1)S(1)} %add_convert_fusion.26), channel_id=1, source_target_pairs={{0,8},{1,5},{8,16},{9,1},{16,24},{17,9},{24,26},{25,17},{26,18},{2... | collective-permute-start | bytes 829448 | tf_op jit(solution)/shard_map/ppermute | solution.py:47
  99.7 7.8 %collective-permute-start.2 = (bf16[1080,128]{1,0:T(8,128)(2,1)S(1)}, bf16[1080,128]{1,0:T(8,128)(2,1)S(1)}, u32[]{:S(2)}, u32[]{:S(2)}) collective-permute-start(bf16[1080,128]{1,0:T(8,128)(2,1)S(1)} %add_convert_fusion.40), channel_id=1, source_target_pairs={{0,8},{1,5},{8,16},{9,1},{16,24},{17,9},{24,26},{25,17},{26,18},{2... | collective-permute-start | bytes 829448 | tf_op jit(solution)/shard_map/ppermute | solution.py:47
  102.6 7.8 %collective-permute-start.33 = (bf16[1080,128]{1,0:T(8,128)(2,1)S(1)}, bf16[1080,128]{1,0:T(8,128)(2,1)S(1)}, u32[]{:S(2)}, u32[]{:S(2)}) collective-permute-start(bf16[1080,128]{1,0:T(8,128)(2,1)S(1)} %add_convert_fusion.11), channel_id=1, source_target_pairs={{0,8},{1,5},{8,16},{9,1},{16,24},{17,9},{24,26},{25,17},{26,18},{2... | collective-permute-start | bytes 829448 | tf_op jit(solution)/shard_map/ppermute | solution.py:47
  105.6 7.8 %collective-permute-start.18 = (bf16[1080,128]{1,0:T(8,128)(2,1)S(1)}, bf16[1080,128]{1,0:T(8,128)(2,1)S(1)}, u32[]{:S(2)}, u32[]{:S(2)}) collective-permute-start(bf16[1080,128]{1,0:T(8,128)(2,1)S(1)} %add_convert_fusion.25), channel_id=1, source_target_pairs={{0,8},{1,5},{8,16},{9,1},{16,24},{17,9},{24,26},{25,17},{26,18},{2... | collective-permute-start | bytes 829448 | tf_op jit(solution)/shard_map/ppermute | solution.py:47
  107.5 8.8 %collective-permute-start.3 = (bf16[1080,128]{1,0:T(8,128)(2,1)S(1)}, bf16[1080,128]{1,0:T(8,128)(2,1)S(1)}, u32[]{:S(2)}, u32[]{:S(2)}) collective-permute-start(bf16[1080,128]{1,0:T(8,128)(2,1)S(1)} %add_convert_fusion.39), channel_id=1, source_target_pairs={{0,8},{1,5},{8,16},{9,1},{16,24},{17,9},{24,26},{25,17},{26,18},{2... | collective-permute-start | bytes 829448 | tf_op jit(solution)/shard_map/ppermute | solution.py:47
  111.5 7.8 %collective-permute-start.34 = (bf16[1080,128]{1,0:T(8,128)(2,1)S(1)}, bf16[1080,128]{1,0:T(8,128)(2,1)S(1)}, u32[]{:S(2)}, u32[]{:S(2)}) collective-permute-start(bf16[1080,128]{1,0:T(8,128)(2,1)S(1)} %add_convert_fusion.10), channel_id=1, source_target_pairs={{0,8},{1,5},{8,16},{9,1},{16,24},{17,9},{24,26},{25,17},{26,18},{2... | collective-permute-start | bytes 829448 | tf_op jit(solution)/shard_map/ppermute | solution.py:47
  114.5 7.8 %collective-permute-start.19 = (bf16[1080,128]{1,0:T(8,128)(2,1)S(1)}, bf16[1080,128]{1,0:T(8,128)(2,1)S(1)}, u32[]{:S(2)}, u32[]{:S(2)}) collective-permute-start(bf16[1080,128]{1,0:T(8,128)(2,1)S(1)} %add_convert_fusion.24), channel_id=1, source_target_pairs={{0,8},{1,5},{8,16},{9,1},{16,24},{17,9},{24,26},{25,17},{26,18},{2... | collective-permute-start | bytes 829448 | tf_op jit(solution)/shard_map/ppermute | solution.py:47
  116.4 8.8 %collective-permute-start.4 = (bf16[1080,128]{1,0:T(8,128)(2,1)S(1)}, bf16[1080,128]{1,0:T(8,128)(2,1)S(1)}, u32[]{:S(2)}, u32[]{:S(2)}) collective-permute-start(bf16[1080,128]{1,0:T(8,128)(2,1)S(1)} %add_convert_fusion.38), channel_id=1, source_target_pairs={{0,8},{1,5},{8,16},{9,1},{16,24},{17,9},{24,26},{25,17},{26,18},{2... | collective-permute-start | bytes 829448 | tf_op jit(solution)/shard_map/ppermute | solution.py:47
  120.4 7.8 %collective-permute-start.35 = (bf16[1080,128]{1,0:T(8,128)(2,1)S(1)}, bf16[1080,128]{1,0:T(8,128)(2,1)S(1)}, u32[]{:S(2)}, u32[]{:S(2)}) collective-permute-start(bf16[1080,128]{1,0:T(8,128)(2,1)S(1)} %add_convert_fusion.9), channel_id=1, source_target_pairs={{0,8},{1,5},{8,16},{9,1},{16,24},{17,9},{24,26},{25,17},{26,18},{2... | collective-permute-start | bytes 829448 | tf_op jit(solution)/shard_map/ppermute | solution.py:47
  123.4 7.8 %collective-permute-start.20 = (bf16[1080,128]{1,0:T(8,128)(2,1)S(1)}, bf16[1080,128]{1,0:T(8,128)(2,1)S(1)}, u32[]{:S(2)}, u32[]{:S(2)}) collective-permute-start(bf16[1080,128]{1,0:T(8,128)(2,1)S(1)} %add_convert_fusion.23), channel_id=1, source_target_pairs={{0,8},{1,5},{8,16},{9,1},{16,24},{17,9},{24,26},{25,17},{26,18},{2... | collective-permute-start | bytes 829448 | tf_op jit(solution)/shard_map/ppermute | solution.py:47
  125.3 8.8 %collective-permute-start.5 = (bf16[1080,128]{1,0:T(8,128)(2,1)S(1)}, bf16[1080,128]{1,0:T(8,128)(2,1)S(1)}, u32[]{:S(2)}, u32[]{:S(2)}) collective-permute-start(bf16[1080,128]{1,0:T(8,128)(2,1)S(1)} %add_convert_fusion.37), channel_id=1, source_target_pairs={{0,8},{1,5},{8,16},{9,1},{16,24},{17,9},{24,26},{25,17},{26,18},{2... | collective-permute-start | bytes 829448 | tf_op jit(solution)/shard_map/ppermute | solution.py:47
  129.3 7.8 %collective-permute-start.36 = (bf16[1080,128]{1,0:T(8,128)(2,1)S(1)}, bf16[1080,128]{1,0:T(8,128)(2,1)S(1)}, u32[]{:S(2)}, u32[]{:S(2)}) collective-permute-start(bf16[1080,128]{1,0:T(8,128)(2,1)S(1)} %add_convert_fusion.8), channel_id=1, source_target_pairs={{0,8},{1,5},{8,16},{9,1},{16,24},{17,9},{24,26},{25,17},{26,18},{2... | collective-permute-start | bytes 829448 | tf_op jit(solution)/shard_map/ppermute | solution.py:47
  131.2 8.8 %collective-permute-start.21 = (bf16[1080,128]{1,0:T(8,128)(2,1)S(1)}, bf16[1080,128]{1,0:T(8,128)(2,1)S(1)}, u32[]{:S(2)}, u32[]{:S(2)}) collective-permute-start(bf16[1080,128]{1,0:T(8,128)(2,1)S(1)} %add_convert_fusion.22), channel_id=1, source_target_pairs={{0,8},{1,5},{8,16},{9,1},{16,24},{17,9},{24,26},{25,17},{26,18},{2... | collective-permute-start | bytes 829448 | tf_op jit(solution)/shard_map/ppermute | solution.py:47
  134.2 8.8 %collective-permute-start.6 = (bf16[1080,128]{1,0:T(8,128)(2,1)S(1)}, bf16[1080,128]{1,0:T(8,128)(2,1)S(1)}, u32[]{:S(2)}, u32[]{:S(2)}) collective-permute-start(bf16[1080,128]{1,0:T(8,128)(2,1)S(1)} %add_convert_fusion.36), channel_id=1, source_target_pairs={{0,8},{1,5},{8,16},{9,1},{16,24},{17,9},{24,26},{25,17},{26,18},{2... | collective-permute-start | bytes 829448 | tf_op jit(solution)/shard_map/ppermute | solution.py:47
  138.2 7.8 %collective-permute-start.37 = (bf16[1080,128]{1,0:T(8,128)(2,1)S(1)}, bf16[1080,128]{1,0:T(8,128)(2,1)S(1)}, u32[]{:S(2)}, u32[]{:S(2)}) collective-permute-start(bf16[1080,128]{1,0:T(8,128)(2,1)S(1)} %add_convert_fusion.7), channel_id=1, source_target_pairs={{0,8},{1,5},{8,16},{9,1},{16,24},{17,9},{24,26},{25,17},{26,18},{2... | collective-permute-start | bytes 829448 | tf_op jit(solution)/shard_map/ppermute | solution.py:47
  140.1 8.8 %collective-permute-start.22 = (bf16[1080,128]{1,0:T(8,128)(2,1)S(1)}, bf16[1080,128]{1,0:T(8,128)(2,1)S(1)}, u32[]{:S(2)}, u32[]{:S(2)}) collective-permute-start(bf16[1080,128]{1,0:T(8,128)(2,1)S(1)} %add_convert_fusion.21), channel_id=1, source_target_pairs={{0,8},{1,5},{8,16},{9,1},{16,24},{17,9},{24,26},{25,17},{26,18},{2... | collective-permute-start | bytes 829448 | tf_op jit(solution)/shard_map/ppermute | solution.py:47
  143.0 8.8 %collective-permute-start.7 = (bf16[1080,128]{1,0:T(8,128)(2,1)S(1)}, bf16[1080,128]{1,0:T(8,128)(2,1)S(1)}, u32[]{:S(2)}, u32[]{:S(2)}) collective-permute-start(bf16[1080,128]{1,0:T(8,128)(2,1)S(1)} %add_convert_fusion.35), channel_id=1, source_target_pairs={{0,8},{1,5},{8,16},{9,1},{16,24},{17,9},{24,26},{25,17},{26,18},{2... | collective-permute-start | bytes 829448 | tf_op jit(solution)/shard_map/ppermute | solution.py:47
  147.1 7.8 %collective-permute-start.38 = (bf16[1080,128]{1,0:T(8,128)(2,1)S(1)}, bf16[1080,128]{1,0:T(8,128)(2,1)S(1)}, u32[]{:S(2)}, u32[]{:S(2)}) collective-permute-start(bf16[1080,128]{1,0:T(8,128)(2,1)S(1)} %add_convert_fusion.6), channel_id=1, source_target_pairs={{0,8},{1,5},{8,16},{9,1},{16,24},{17,9},{24,26},{25,17},{26,18},{2... | collective-permute-start | bytes 829448 | tf_op jit(solution)/shard_map/ppermute | solution.py:47
  149.0 8.8 %collective-permute-start.23 = (bf16[1080,128]{1,0:T(8,128)(2,1)S(1)}, bf16[1080,128]{1,0:T(8,128)(2,1)S(1)}, u32[]{:S(2)}, u32[]{:S(2)}) collective-permute-start(bf16[1080,128]{1,0:T(8,128)(2,1)S(1)} %add_convert_fusion.20), channel_id=1, source_target_pairs={{0,8},{1,5},{8,16},{9,1},{16,24},{17,9},{24,26},{25,17},{26,18},{2... | collective-permute-start | bytes 829448 | tf_op jit(solution)/shard_map/ppermute | solution.py:47
  151.9 8.8 %collective-permute-start.8 = (bf16[1080,128]{1,0:T(8,128)(2,1)S(1)}, bf16[1080,128]{1,0:T(8,128)(2,1)S(1)}, u32[]{:S(2)}, u32[]{:S(2)}) collective-permute-start(bf16[1080,128]{1,0:T(8,128)(2,1)S(1)} %add_convert_fusion.34), channel_id=1, source_target_pairs={{0,8},{1,5},{8,16},{9,1},{16,24},{17,9},{24,26},{25,17},{26,18},{2... | collective-permute-start | bytes 829448 | tf_op jit(solution)/shard_map/ppermute | solution.py:47
  155.9 7.8 %collective-permute-start.39 = (bf16[1080,128]{1,0:T(8,128)(2,1)S(1)}, bf16[1080,128]{1,0:T(8,128)(2,1)S(1)}, u32[]{:S(2)}, u32[]{:S(2)}) collective-permute-start(bf16[1080,128]{1,0:T(8,128)(2,1)S(1)} %add_convert_fusion.5), channel_id=1, source_target_pairs={{0,8},{1,5},{8,16},{9,1},{16,24},{17,9},{24,26},{25,17},{26,18},{2... | collective-permute-start | bytes 829448 | tf_op jit(solution)/shard_map/ppermute | solution.py:47
  157.9 8.8 %collective-permute-start.24 = (bf16[1080,128]{1,0:T(8,128)(2,1)S(1)}, bf16[1080,128]{1,0:T(8,128)(2,1)S(1)}, u32[]{:S(2)}, u32[]{:S(2)}) collective-permute-start(bf16[1080,128]{1,0:T(8,128)(2,1)S(1)} %add_convert_fusion.19), channel_id=1, source_target_pairs={{0,8},{1,5},{8,16},{9,1},{16,24},{17,9},{24,26},{25,17},{26,18},{2... | collective-permute-start | bytes 829448 | tf_op jit(solution)/shard_map/ppermute | solution.py:47
  160.8 8.8 %collective-permute-start.9 = (bf16[1080,128]{1,0:T(8,128)(2,1)S(1)}, bf16[1080,128]{1,0:T(8,128)(2,1)S(1)}, u32[]{:S(2)}, u32[]{:S(2)}) collective-permute-start(bf16[1080,128]{1,0:T(8,128)(2,1)S(1)} %add_convert_fusion.33), channel_id=1, source_target_pairs={{0,8},{1,5},{8,16},{9,1},{16,24},{17,9},{24,26},{25,17},{26,18},{2... | collective-permute-start | bytes 829448 | tf_op jit(solution)/shard_map/ppermute | solution.py:47
  164.8 7.8 %collective-permute-start.40 = (bf16[1080,128]{1,0:T(8,128)(2,1)S(1)}, bf16[1080,128]{1,0:T(8,128)(2,1)S(1)}, u32[]{:S(2)}, u32[]{:S(2)}) collective-permute-start(bf16[1080,128]{1,0:T(8,128)(2,1)S(1)} %add_convert_fusion.4), channel_id=1, source_target_pairs={{0,8},{1,5},{8,16},{9,1},{16,24},{17,9},{24,26},{25,17},{26,18},{2... | collective-permute-start | bytes 829448 | tf_op jit(solution)/shard_map/ppermute | solution.py:47
  166.7 8.8 %collective-permute-start.25 = (bf16[1080,128]{1,0:T(8,128)(2,1)S(1)}, bf16[1080,128]{1,0:T(8,128)(2,1)S(1)}, u32[]{:S(2)}, u32[]{:S(2)}) collective-permute-start(bf16[1080,128]{1,0:T(8,128)(2,1)S(1)} %add_convert_fusion.18), channel_id=1, source_target_pairs={{0,8},{1,5},{8,16},{9,1},{16,24},{17,9},{24,26},{25,17},{26,18},{2... | collective-permute-start | bytes 829448 | tf_op jit(solution)/shard_map/ppermute | solution.py:47
  169.7 8.8 %collective-permute-start.10 = (bf16[1080,128]{1,0:T(8,128)(2,1)S(1)}, bf16[1080,128]{1,0:T(8,128)(2,1)S(1)}, u32[]{:S(2)}, u32[]{:S(2)}) collective-permute-start(bf16[1080,128]{1,0:T(8,128)(2,1)S(1)} %add_convert_fusion.32), channel_id=1, source_target_pairs={{0,8},{1,5},{8,16},{9,1},{16,24},{17,9},{24,26},{25,17},{26,18},{2... | collective-permute-start | bytes 829448 | tf_op jit(solution)/shard_map/ppermute | solution.py:47
  173.7 7.8 %collective-permute-start.41 = (bf16[1080,128]{1,0:T(8,128)(2,1)S(1)}, bf16[1080,128]{1,0:T(8,128)(2,1)S(1)}, u32[]{:S(2)}, u32[]{:S(2)}) collective-permute-start(bf16[1080,128]{1,0:T(8,128)(2,1)S(1)} %add_convert_fusion.3), channel_id=1, source_target_pairs={{0,8},{1,5},{8,16},{9,1},{16,24},{17,9},{24,26},{25,17},{26,18},{2... | collective-permute-start | bytes 829448 | tf_op jit(solution)/shard_map/ppermute | solution.py:47
  175.6 8.8 %collective-permute-start.26 = (bf16[1080,128]{1,0:T(8,128)(2,1)S(1)}, bf16[1080,128]{1,0:T(8,128)(2,1)S(1)}, u32[]{:S(2)}, u32[]{:S(2)}) collective-permute-start(bf16[1080,128]{1,0:T(8,128)(2,1)S(1)} %add_convert_fusion.17), channel_id=1, source_target_pairs={{0,8},{1,5},{8,16},{9,1},{16,24},{17,9},{24,26},{25,17},{26,18},{2... | collective-permute-start | bytes 829448 | tf_op jit(solution)/shard_map/ppermute | solution.py:47
  178.6 8.8 %collective-permute-start.11 = (bf16[1080,128]{1,0:T(8,128)(2,1)S(1)}, bf16[1080,128]{1,0:T(8,128)(2,1)S(1)}, u32[]{:S(2)}, u32[]{:S(2)}) collective-permute-start(bf16[1080,128]{1,0:T(8,128)(2,1)S(1)} %add_convert_fusion.31), channel_id=1, source_target_pairs={{0,8},{1,5},{8,16},{9,1},{16,24},{17,9},{24,26},{25,17},{26,18},{2... | collective-permute-start | bytes 829448 | tf_op jit(solution)/shard_map/ppermute | solution.py:47
  182.6 7.8 %collective-permute-start.42 = (bf16[1080,128]{1,0:T(8,128)(2,1)S(1)}, bf16[1080,128]{1,0:T(8,128)(2,1)S(1)}, u32[]{:S(2)}, u32[]{:S(2)}) collective-permute-start(bf16[1080,128]{1,0:T(8,128)(2,1)S(1)} %add_convert_fusion.2), channel_id=1, source_target_pairs={{0,8},{1,5},{8,16},{9,1},{16,24},{17,9},{24,26},{25,17},{26,18},{2... | collective-permute-start | bytes 829448 | tf_op jit(solution)/shard_map/ppermute | solution.py:47
  184.5 8.8 %collective-permute-start.27 = (bf16[1080,128]{1,0:T(8,128)(2,1)S(1)}, bf16[1080,128]{1,0:T(8,128)(2,1)S(1)}, u32[]{:S(2)}, u32[]{:S(2)}) collective-permute-start(bf16[1080,128]{1,0:T(8,128)(2,1)S(1)} %add_convert_fusion.16), channel_id=1, source_target_pairs={{0,8},{1,5},{8,16},{9,1},{16,24},{17,9},{24,26},{25,17},{26,18},{2... | collective-permute-start | bytes 829448 | tf_op jit(solution)/shard_map/ppermute | solution.py:47
  187.5 8.8 %collective-permute-start.12 = (bf16[1080,128]{1,0:T(8,128)(2,1)S(1)}, bf16[1080,128]{1,0:T(8,128)(2,1)S(1)}, u32[]{:S(2)}, u32[]{:S(2)}) collective-permute-start(bf16[1080,128]{1,0:T(8,128)(2,1)S(1)} %add_convert_fusion.30), channel_id=1, source_target_pairs={{0,8},{1,5},{8,16},{9,1},{16,24},{17,9},{24,26},{25,17},{26,18},{2... | collective-permute-start | bytes 829448 | tf_op jit(solution)/shard_map/ppermute | solution.py:47
  191.5 7.8 %collective-permute-start.43 = (bf16[1080,128]{1,0:T(8,128)(2,1)S(1)}, bf16[1080,128]{1,0:T(8,128)(2,1)S(1)}, u32[]{:S(2)}, u32[]{:S(2)}) collective-permute-start(bf16[1080,128]{1,0:T(8,128)(2,1)S(1)} %add_convert_fusion.1), channel_id=1, source_target_pairs={{0,8},{1,5},{8,16},{9,1},{16,24},{17,9},{24,26},{25,17},{26,18},{2... | collective-permute-start | bytes 829448 | tf_op jit(solution)/shard_map/ppermute | solution.py:47
  193.4 8.8 %collective-permute-start.28 = (bf16[1080,128]{1,0:T(8,128)(2,1)S(1)}, bf16[1080,128]{1,0:T(8,128)(2,1)S(1)}, u32[]{:S(2)}, u32[]{:S(2)}) collective-permute-start(bf16[1080,128]{1,0:T(8,128)(2,1)S(1)} %add_convert_fusion.15), channel_id=1, source_target_pairs={{0,8},{1,5},{8,16},{9,1},{16,24},{17,9},{24,26},{25,17},{26,18},{2... | collective-permute-start | bytes 829448 | tf_op jit(solution)/shard_map/ppermute | solution.py:47
  196.4 8.8 %collective-permute-start.13 = (bf16[1080,128]{1,0:T(8,128)(2,1)S(1)}, bf16[1080,128]{1,0:T(8,128)(2,1)S(1)}, u32[]{:S(2)}, u32[]{:S(2)}) collective-permute-start(bf16[1080,128]{1,0:T(8,128)(2,1)S(1)} %add_convert_fusion.29), channel_id=1, source_target_pairs={{0,8},{1,5},{8,16},{9,1},{16,24},{17,9},{24,26},{25,17},{26,18},{2... | collective-permute-start | bytes 829448 | tf_op jit(solution)/shard_map/ppermute | solution.py:47
  200.4 7.8 %collective-permute-start.44 = (bf16[1080,128]{1,0:T(8,128)(2,1)S(1)}, bf16[1080,128]{1,0:T(8,128)(2,1)S(1)}, u32[]{:S(2)}, u32[]{:S(2)}) collective-permute-start(bf16[1080,128]{1,0:T(8,128)(2,1)S(1)} %add_convert_fusion), channel_id=1, source_target_pairs={{0,8},{1,5},{8,16},{9,1},{16,24},{17,9},{24,26},{25,17},{26,18},{2... | collective-permute-start | bytes 829448 | tf_op jit(solution)/shard_map/ppermute | solution.py:47
  202.3 8.8 %collective-permute-start.29 = (bf16[1080,128]{1,0:T(8,128)(2,1)S(1)}, bf16[1080,128]{1,0:T(8,128)(2,1)S(1)}, u32[]{:S(2)}, u32[]{:S(2)}) collective-permute-start(bf16[1080,128]{1,0:T(8,128)(2,1)S(1)} %add_convert_fusion.14), channel_id=1, source_target_pairs={{0,8},{1,5},{8,16},{9,1},{16,24},{17,9},{24,26},{25,17},{26,18},{2... | collective-permute-start | bytes 829448 | tf_op jit(solution)/shard_map/ppermute | solution.py:47
  205.3 8.8 %collective-permute-start.14 = (bf16[1080,128]{1,0:T(8,128)(2,1)S(1)}, bf16[1080,128]{1,0:T(8,128)(2,1)S(1)}, u32[]{:S(2)}, u32[]{:S(2)}) collective-permute-start(bf16[1080,128]{1,0:T(8,128)(2,1)S(1)} %add_convert_fusion.28), channel_id=1, source_target_pairs={{0,8},{1,5},{8,16},{9,1},{16,24},{17,9},{24,26},{25,17},{26,18},{2... | collective-permute-start | bytes 829448 | tf_op jit(solution)/shard_map/ppermute | solution.py:47
  (4 other events, 170.8 us)
Sparse Core Ops, SparseCore 0:
  9.5 12.1 all-gather.2
  23.2 10.5 all-gather.4
  74.4 11.4 reduce-scatter.1

commit v4 on v3

--- a/solution.py
+++ b/solution.py
@@ -123,10 +123,19 @@
 
 
 def shards(n_dp, n_t, tokens, cotangent, w_gate, w_up, w_down, col_index, row_count, adam_m, adam_v):
-    full_tok, full_cot = (
-        lax.all_gather(tokens, "tensor", axis=1, tiled=True),
-        lax.all_gather(cotangent, "tensor", axis=1, tiled=True),
-    )
+    swap = [(0, 1), (1, 0)]
+    first = lax.axis_index("tensor") == 0
+    if n_t == 2:
+        other_tok, other_cot = lax.ppermute((tokens, cotangent), "tensor", swap)
+        full_tok = jnp.concatenate(
+            [jnp.where(first, tokens, other_tok), jnp.where(first, other_tok, tokens)], axis=1
+        )
+        full_cot = jnp.concatenate(
+            [jnp.where(first, cotangent, other_cot), jnp.where(first, other_cot, cotangent)], axis=1
+        )
+    else:
+        full_tok = lax.all_gather(tokens, "tensor", axis=1, tiled=True)
+        full_cot = lax.all_gather(cotangent, "tensor", axis=1, tiled=True)
     tok_rows = full_tok.shape[0]
     own_rows = w_gate.shape[1] * w_gate.shape[2] * BLK
     grad_gate, grad_up, grad_down, dx_part = ffn_block_terms(
@@ -141,9 +150,16 @@
             jnp.bfloat16,
         )
     )[:, None]
-    token_grads = lax.psum_scatter(
-        dx_part.astype(jnp.bfloat16), "tensor", scatter_dimension=1, tiled=True
-    )
+    if n_t == 2:
+        half = tokens.shape[1]
+        lo, hi = dx_part[:, :half], dx_part[:, half:]
+        mine = jnp.where(first, lo, hi)
+        theirs = lax.ppermute(jnp.where(first, hi, lo).astype(jnp.bfloat16), "tensor", swap)
+        token_grads = (mine + theirs.astype(jnp.float32)).astype(jnp.bfloat16)
+    else:
+        token_grads = lax.psum_scatter(
+            dx_part.astype(jnp.bfloat16), "tensor", scatter_dimension=1, tiled=True
+        )
     grad_scale = 1.0 / math.sqrt(n_dp * tok_rows)
     grad_all = reduced * grad_scale
     m_new = 0.9 * adam_m + 0.1 * grad_all

time: 226 us -> 215 us (0.951)
  between operations: 34.9 us -> 21.7 us
  starting transfers between devices: 69.2 us -> 78.1 us
  other arithmetic: 32.7 us -> 25.4 us
    convert_element_type x42, other arithmetic: 25.7 us -> 13.2 us  [ring_reduce_scatter(): moved = lax.ppermute(accs[i].astype(wire_dtype), ('dp', 'tensor'), perm)]
    ppermute x45, starting transfers between devices: 69.1 us -> 76.9 us  [ring_reduce_scatter(): moved = lax.ppermute(accs[i].astype(wire_dtype), ('dp', 'tensor'), perm)]
    ppermute x45, waiting for transfers between devices: 40.2 us -> 42.7 us  [ring_reduce_scatter(): moved = lax.ppermute(accs[i].astype(wire_dtype), ('dp', 'tensor'), perm)]
    convert_element_type x1 -> x2, other arithmetic: 2.95 us -> 5.36 us  [the longest x1 3.38 us: shards(): token_grads = (mine + theirs.astype(jnp.float32)).astype(jnp.bfloat16)]
    concatenate x0 -> x2, other arithmetic: none -> 2.38 us  [the longest x1 1.19 us: shards(): jnp.concatenate([jnp.where(first, tokens, other_tok), jnp.where(first, ot...]
  transfers between devices with their start and end apart: 48 -> 48, of which waited for: 41 -> 36; matrix products, arithmetic and copies ran while one was open for 17% -> 12% of each run, Pallas kernels for 0% -> 0%
where the time goes in v4:
time: 215 us; the launch traced here: 213 us
  starting transfers between devices  78.1 us (36%)
  waiting for transfers between devices  42.7 us (20%)
  Pallas kernels  37 us (17%)
  other arithmetic  25.4 us (12%)
  between operations  21.7 us (10%)
  local copies, waits for them, and re-layouts  8.38 us (4%)
    ppermute x45, starting transfers between devices, ring_reduce_scatter(): moved = lax.ppermute(accs[i].astype(wire_dtype), ('dp', 'tensor'), perm)  76.9 us
    ppermute x45, waiting for transfers between devices, ring_reduce_scatter(): moved = lax.ppermute(accs[i].astype(wire_dtype), ('dp', 'tensor'), perm)  42.7 us
    pallas_call x1, Pallas kernels, ffn_block_terms(): pl.pallas_call(_ffn_kernel, grid_spec=pltpu.PrefetchScalarGridSpec(num_sc...  37 us
    convert_element_type x42, other arithmetic, ring_reduce_scatter(): moved = lax.ppermute(accs[i].astype(wire_dtype), ('dp', 'tensor'), perm)  13.2 us
  transfers between devices with their start and end apart: 48, of which 36 were waited for; matrix products, arithmetic and copies ran while one was open for 12% of the time, Pallas kernels for 0%

profile of v4, /device:TPU:0, one launch (start us, length us, event | category | flops | bytes accessed | tf_op | source)
XLA Modules:
  0.0 213.3 jit_solution(12319028803427516804)
XLA Ops:
  13.2 2.0 fusion
  30.5 37.0 %ffn_block_terms.1 = (f32[27,5,128,128]{3,2,1,0:T(8,128)}, f32[27,5,128,128]{3,2,1,0:T(8,128)}, f32[27,5,128,128]{3,2,1,0:T(8,128)}, f32[128,5120]{1,0:T(8,128)}) custom-call(s32[27,5]{1,0:T(8,128)} %copy.15.col_ref, s32[27]{0:T(128)} %cnt_ref.1, bf16[128,5120]{1,0:T(8,128)(2,1)} %pad_maximum_fusion.1.tok_ref, bf16[128,5120]{1,0:T(8,128)(2,1)} %pad_maximum_fusion.2.cot_ref, ...), custom_call_target="tpu_custom_call" | custom-call | flops 5096079360 | bytes 45056000 | tf_op jit(solution)/shard_map/ffn_block_terms/pallas_call | solution.py:106
  67.5 2.0 select_convert_fusion
  71.6 2.6 %collective-permute-start.33 = (bf16[1080,128]{1,0:T(8,128)(2,1)S(1)}, bf16[1080,128]{1,0:T(8,128)(2,1)S(1)}, u32[]{:S(2)}, u32[]{:S(2)}) collective-permute-start(bf16[1080,128]{1,0:T(8,128)(2,1)S(1)} %dynamic-slice_convert_fusion), channel_id=1, source_target_pairs={{0,8},{1,5},{8,16},{9,1},{16,24},{17,9},{24,26},{25,17},{26,18},{2... | collective-permute-start | bytes 829448 | tf_op jit(solution)/shard_map/ppermute | solution.py:47
  78.0 1.6 collective-permute-start.3
  86.0 1.8 collective-permute-start.4
  88.9 1.8 collective-permute-start.35
  91.9 1.8 collective-permute-start.20
  93.8 1.8 collective-permute-start.5
  95.6 3.4 %add_convert_fusion = bf16[128,2560]{1,0:T(8,128)(2,1)} fusion(bf16[128,2560]{1,0:T(8,128)(2,1)S(1)} %collective-permute-done.2, f32[128,5120]{1,0:T(8,128)} %get-tuple-element.8, pred[]{:T(512)S(6)} %eq.53), kind=kLoop, calls=%fused_computation.6 | loop fusion | flops 1310720 | bytes 3932161 | tf_op jit(solution)/shard_map/convert_element_type | solution.py:158
  100.1 1.7 collective-permute-start.36
  103.0 1.6 collective-permute-start.21
  107.9 1.7 collective-permute-start.37
  109.7 1.7 collective-permute-start.22
  112.7 1.7 collective-permute-start.7
  116.7 1.7 collective-permute-start.38
  118.6 1.7 collective-permute-start.23
  121.6 1.7 collective-permute-start.8
  125.6 1.7 collective-permute-start.39
  127.5 1.7 collective-permute-start.24
  130.5 1.7 collective-permute-start.9
  133.4 1.7 collective-permute-start.40
  136.4 1.7 collective-permute-start.25
  139.4 1.7 collective-permute-start.10
  142.3 1.7 collective-permute-start.41
  145.3 1.7 collective-permute-start.26
  148.3 1.7 collective-permute-start.11
  151.2 1.7 collective-permute-start.42
  154.2 1.7 collective-permute-start.27
  157.1 1.7 collective-permute-start.12
  160.1 1.7 collective-permute-start.43
  163.1 1.7 collective-permute-start.28
  166.0 1.7 collective-permute-start.13
  169.0 1.7 collective-permute-start.44
  172.0 1.7 collective-permute-start.29
  174.9 1.7 collective-permute-start.14
  177.9 1.7 collective-permute-start.45
  180.9 1.7 collective-permute-start.30
  183.8 1.7 collective-permute-start.15
  186.8 1.7 collective-permute-start.46
  189.8 1.7 collective-permute-start.31
  192.7 1.7 collective-permute-start.16
  195.7 1.7 collective-permute-start.47
  198.6 1.7 collective-permute-start.32
  201.6 1.7 collective-permute-start.17
  204.5 2.9 %collective-permute-done.32 = bf16[1080,128]{1,0:T(8,128)(2,1)S(1)} collective-permute-done((bf16[1080,128]{1,0:T(8,128)(2,1)S(1)}, bf16[1080,128]{1,0:T(8,128)(2,1)S(1)}, u32[]{:S(2)}, u32[]{:S(2)}) %collective-permute-start.32) | collective-permute-done | bytes 276512 | tf_op jit(solution)/shard_map/ppermute | solution.py:47
  207.5 2.9 %collective-permute-done.17 = bf16[1080,128]{1,0:T(8,128)(2,1)S(1)} collective-permute-done((bf16[1080,128]{1,0:T(8,128)(2,1)S(1)}, bf16[1080,128]{1,0:T(8,128)(2,1)S(1)}, u32[]{:S(2)}, u32[]{:S(2)}) %collective-permute-start.17) | collective-permute-done | bytes 276512 | tf_op jit(solution)/shard_map/ppermute | solution.py:47
  210.5 2.8 %add_divide_fusion = (f32[3,1,1080,128]{3,2,1,0:T(8,128)}, f32[3,1,1080,128]{3,2,1,0:T(8,128)}, f32[3,1,1080,128]{3,2,1,0:T(8,128)}) fusion(f32[1,1,1080,128]{3,2,1,0:T(8,128)S(1)} %add_bitcast_fusion, f32[1,1,1080,128]{3,2,1,0:T(8,128)S(1)} %add_bitcast_fusion.1, f32[1,1,1080,128]{3,2,1,0:T(8,128)S(1)} %add_bitcast_fusion.2, ...), kind=kLoop, calls=%fused_computation.1 | loop fusion | flops 4976640 | bytes 9953280 | tf_op jit(solution)/shard_map/div | solution.py:167
  (116 shorter events, 67.8 us)
Async XLA Ops:
  0.6 26.1 %collective-permute-start.1 = (bf16[128,2560]{1,0:T(8,128)(2,1)}, bf16[128,2560]{1,0:T(8,128)(2,1)S(1)}, u32[]{:S(2)}, u32[]{:S(2)}) collective-permute-start(bf16[128,2560]{1,0:T(8,128)(2,1)} %param.12), channel_id=1, source_target_pairs={{0,1},{1,0},{2,3},{3,2},{4,5},{5,4},{6,7},{7,6},{8,9},{9,8},{10,11... | collective-permute-start | bytes 1966088 | tf_op jit(solution)/shard_map/ppermute | solution.py:129
  1.1 25.5 %collective-permute-start = (bf16[128,2560]{1,0:T(8,128)(2,1)}, bf16[128,2560]{1,0:T(8,128)(2,1)S(1)}, u32[]{:S(2)}, u32[]{:S(2)}) collective-permute-start(bf16[128,2560]{1,0:T(8,128)(2,1)} %param.11), channel_id=1, source_target_pairs={{0,1},{1,0},{2,3},{3,2},{4,5},{5,4},{6,7},{7,6},{8,9},{9,8},{10,11... | collective-permute-start | bytes 1966088 | tf_op jit(solution)/shard_map/ppermute | solution.py:129
  69.5 26.1 %collective-permute-start.2 = (bf16[128,2560]{1,0:T(8,128)(2,1)S(1)}, bf16[128,2560]{1,0:T(8,128)(2,1)S(1)}, u32[]{:S(2)}, u32[]{:S(2)}) collective-permute-start(bf16[128,2560]{1,0:T(8,128)(2,1)S(1)} %select_convert_fusion), channel_id=1, source_target_pairs={{0,1},{1,0},{2,3},{3,2},{4,5},{5,4},{6,7},{7,6},{8,9},{9,8},{10,11... | collective-permute-start | bytes 1966088 | tf_op jit(solution)/shard_map/ppermute | solution.py:157
  71.6 8.0 %collective-permute-start.33 = (bf16[1080,128]{1,0:T(8,128)(2,1)S(1)}, bf16[1080,128]{1,0:T(8,128)(2,1)S(1)}, u32[]{:S(2)}, u32[]{:S(2)}) collective-permute-start(bf16[1080,128]{1,0:T(8,128)(2,1)S(1)} %dynamic-slice_convert_fusion), channel_id=1, source_target_pairs={{0,8},{1,5},{8,16},{9,1},{16,24},{17,9},{24,26},{25,17},{26,18},{2... | collective-permute-start | bytes 829448 | tf_op jit(solution)/shard_map/ppermute | solution.py:47
  75.3 7.0 %collective-permute-start.18 = (bf16[1080,128]{1,0:T(8,128)(2,1)S(1)}, bf16[1080,128]{1,0:T(8,128)(2,1)S(1)}, u32[]{:S(2)}, u32[]{:S(2)}) collective-permute-start(bf16[1080,128]{1,0:T(8,128)(2,1)S(1)} %dynamic-slice_convert_fusion.1), channel_id=1, source_target_pairs={{0,8},{1,5},{8,16},{9,1},{16,24},{17,9},{24,26},{25,17},{26,18},{2... | collective-permute-start | bytes 829448 | tf_op jit(solution)/shard_map/ppermute | solution.py:47
  78.0 6.9 %collective-permute-start.3 = (bf16[1080,128]{1,0:T(8,128)(2,1)S(1)}, bf16[1080,128]{1,0:T(8,128)(2,1)S(1)}, u32[]{:S(2)}, u32[]{:S(2)}) collective-permute-start(bf16[1080,128]{1,0:T(8,128)(2,1)S(1)} %dynamic-slice_convert_fusion.2), channel_id=1, source_target_pairs={{0,8},{1,5},{8,16},{9,1},{16,24},{17,9},{24,26},{25,17},{26,18},{2... | collective-permute-start | bytes 829448 | tf_op jit(solution)/shard_map/ppermute | solution.py:47
  80.7 7.1 %collective-permute-start.34 = (bf16[1080,128]{1,0:T(8,128)(2,1)S(1)}, bf16[1080,128]{1,0:T(8,128)(2,1)S(1)}, u32[]{:S(2)}, u32[]{:S(2)}) collective-permute-start(bf16[1080,128]{1,0:T(8,128)(2,1)S(1)} %add_convert_fusion.14), channel_id=1, source_target_pairs={{0,8},{1,5},{8,16},{9,1},{16,24},{17,9},{24,26},{25,17},{26,18},{2... | collective-permute-start | bytes 829448 | tf_op jit(solution)/shard_map/ppermute | solution.py:47
  83.4 7.4 %collective-permute-start.19 = (bf16[1080,128]{1,0:T(8,128)(2,1)S(1)}, bf16[1080,128]{1,0:T(8,128)(2,1)S(1)}, u32[]{:S(2)}, u32[]{:S(2)}) collective-permute-start(bf16[1080,128]{1,0:T(8,128)(2,1)S(1)} %add_convert_fusion.28), channel_id=1, source_target_pairs={{0,8},{1,5},{8,16},{9,1},{16,24},{17,9},{24,26},{25,17},{26,18},{2... | collective-permute-start | bytes 829448 | tf_op jit(solution)/shard_map/ppermute | solution.py:47
  86.0 7.8 %collective-permute-start.4 = (bf16[1080,128]{1,0:T(8,128)(2,1)S(1)}, bf16[1080,128]{1,0:T(8,128)(2,1)S(1)}, u32[]{:S(2)}, u32[]{:S(2)}) collective-permute-start(bf16[1080,128]{1,0:T(8,128)(2,1)S(1)} %add_convert_fusion.42), channel_id=1, source_target_pairs={{0,8},{1,5},{8,16},{9,1},{16,24},{17,9},{24,26},{25,17},{26,18},{2... | collective-permute-start | bytes 829448 | tf_op jit(solution)/shard_map/ppermute | solution.py:47
  88.9 10.1 %collective-permute-start.35 = (bf16[1080,128]{1,0:T(8,128)(2,1)S(1)}, bf16[1080,128]{1,0:T(8,128)(2,1)S(1)}, u32[]{:S(2)}, u32[]{:S(2)}) collective-permute-start(bf16[1080,128]{1,0:T(8,128)(2,1)S(1)} %add_convert_fusion.13), channel_id=1, source_target_pairs={{0,8},{1,5},{8,16},{9,1},{16,24},{17,9},{24,26},{25,17},{26,18},{2... | collective-permute-start | bytes 829448 | tf_op jit(solution)/shard_map/ppermute | solution.py:47
  91.9 10.0 %collective-permute-start.20 = (bf16[1080,128]{1,0:T(8,128)(2,1)S(1)}, bf16[1080,128]{1,0:T(8,128)(2,1)S(1)}, u32[]{:S(2)}, u32[]{:S(2)}) collective-permute-start(bf16[1080,128]{1,0:T(8,128)(2,1)S(1)} %add_convert_fusion.27), channel_id=1, source_target_pairs={{0,8},{1,5},{8,16},{9,1},{16,24},{17,9},{24,26},{25,17},{26,18},{2... | collective-permute-start | bytes 829448 | tf_op jit(solution)/shard_map/ppermute | solution.py:47
  93.8 10.8 %collective-permute-start.5 = (bf16[1080,128]{1,0:T(8,128)(2,1)S(1)}, bf16[1080,128]{1,0:T(8,128)(2,1)S(1)}, u32[]{:S(2)}, u32[]{:S(2)}) collective-permute-start(bf16[1080,128]{1,0:T(8,128)(2,1)S(1)} %add_convert_fusion.41), channel_id=1, source_target_pairs={{0,8},{1,5},{8,16},{9,1},{16,24},{17,9},{24,26},{25,17},{26,18},{2... | collective-permute-start | bytes 829448 | tf_op jit(solution)/shard_map/ppermute | solution.py:47
  100.1 6.6 %collective-permute-start.36 = (bf16[1080,128]{1,0:T(8,128)(2,1)S(1)}, bf16[1080,128]{1,0:T(8,128)(2,1)S(1)}, u32[]{:S(2)}, u32[]{:S(2)}) collective-permute-start(bf16[1080,128]{1,0:T(8,128)(2,1)S(1)} %add_convert_fusion.12), channel_id=1, source_target_pairs={{0,8},{1,5},{8,16},{9,1},{16,24},{17,9},{24,26},{25,17},{26,18},{2... | collective-permute-start | bytes 829448 | tf_op jit(solution)/shard_map/ppermute | solution.py:47
  103.0 6.7 %collective-permute-start.21 = (bf16[1080,128]{1,0:T(8,128)(2,1)S(1)}, bf16[1080,128]{1,0:T(8,128)(2,1)S(1)}, u32[]{:S(2)}, u32[]{:S(2)}) collective-permute-start(bf16[1080,128]{1,0:T(8,128)(2,1)S(1)} %add_convert_fusion.26), channel_id=1, source_target_pairs={{0,8},{1,5},{8,16},{9,1},{16,24},{17,9},{24,26},{25,17},{26,18},{2... | collective-permute-start | bytes 829448 | tf_op jit(solution)/shard_map/ppermute | solution.py:47
  104.7 8.0 %collective-permute-start.6 = (bf16[1080,128]{1,0:T(8,128)(2,1)S(1)}, bf16[1080,128]{1,0:T(8,128)(2,1)S(1)}, u32[]{:S(2)}, u32[]{:S(2)}) collective-permute-start(bf16[1080,128]{1,0:T(8,128)(2,1)S(1)} %add_convert_fusion.40), channel_id=1, source_target_pairs={{0,8},{1,5},{8,16},{9,1},{16,24},{17,9},{24,26},{25,17},{26,18},{2... | collective-permute-start | bytes 829448 | tf_op jit(solution)/shard_map/ppermute | solution.py:47
  107.9 7.8 %collective-permute-start.37 = (bf16[1080,128]{1,0:T(8,128)(2,1)S(1)}, bf16[1080,128]{1,0:T(8,128)(2,1)S(1)}, u32[]{:S(2)}, u32[]{:S(2)}) collective-permute-start(bf16[1080,128]{1,0:T(8,128)(2,1)S(1)} %add_convert_fusion.11), channel_id=1, source_target_pairs={{0,8},{1,5},{8,16},{9,1},{16,24},{17,9},{24,26},{25,17},{26,18},{2... | collective-permute-start | bytes 829448 | tf_op jit(solution)/shard_map/ppermute | solution.py:47
  109.7 8.8 %collective-permute-start.22 = (bf16[1080,128]{1,0:T(8,128)(2,1)S(1)}, bf16[1080,128]{1,0:T(8,128)(2,1)S(1)}, u32[]{:S(2)}, u32[]{:S(2)}) collective-permute-start(bf16[1080,128]{1,0:T(8,128)(2,1)S(1)} %add_convert_fusion.25), channel_id=1, source_target_pairs={{0,8},{1,5},{8,16},{9,1},{16,24},{17,9},{24,26},{25,17},{26,18},{2... | collective-permute-start | bytes 829448 | tf_op jit(solution)/shard_map/ppermute | solution.py:47
  112.7 8.8 %collective-permute-start.7 = (bf16[1080,128]{1,0:T(8,128)(2,1)S(1)}, bf16[1080,128]{1,0:T(8,128)(2,1)S(1)}, u32[]{:S(2)}, u32[]{:S(2)}) collective-permute-start(bf16[1080,128]{1,0:T(8,128)(2,1)S(1)} %add_convert_fusion.39), channel_id=1, source_target_pairs={{0,8},{1,5},{8,16},{9,1},{16,24},{17,9},{24,26},{25,17},{26,18},{2... | collective-permute-start | bytes 829448 | tf_op jit(solution)/shard_map/ppermute | solution.py:47
  116.7 7.8 %collective-permute-start.38 = (bf16[1080,128]{1,0:T(8,128)(2,1)S(1)}, bf16[1080,128]{1,0:T(8,128)(2,1)S(1)}, u32[]{:S(2)}, u32[]{:S(2)}) collective-permute-start(bf16[1080,128]{1,0:T(8,128)(2,1)S(1)} %add_convert_fusion.10), channel_id=1, source_target_pairs={{0,8},{1,5},{8,16},{9,1},{16,24},{17,9},{24,26},{25,17},{26,18},{2... | collective-permute-start | bytes 829448 | tf_op jit(solution)/shard_map/ppermute | solution.py:47
  118.6 8.8 %collective-permute-start.23 = (bf16[1080,128]{1,0:T(8,128)(2,1)S(1)}, bf16[1080,128]{1,0:T(8,128)(2,1)S(1)}, u32[]{:S(2)}, u32[]{:S(2)}) collective-permute-start(bf16[1080,128]{1,0:T(8,128)(2,1)S(1)} %add_convert_fusion.24), channel_id=1, source_target_pairs={{0,8},{1,5},{8,16},{9,1},{16,24},{17,9},{24,26},{25,17},{26,18},{2... | collective-permute-start | bytes 829448 | tf_op jit(solution)/shard_map/ppermute | solution.py:47
  121.6 8.8 %collective-permute-start.8 = (bf16[1080,128]{1,0:T(8,128)(2,1)S(1)}, bf16[1080,128]{1,0:T(8,128)(2,1)S(1)}, u32[]{:S(2)}, u32[]{:S(2)}) collective-permute-start(bf16[1080,128]{1,0:T(8,128)(2,1)S(1)} %add_convert_fusion.38), channel_id=1, source_target_pairs={{0,8},{1,5},{8,16},{9,1},{16,24},{17,9},{24,26},{25,17},{26,18},{2... | collective-permute-start | bytes 829448 | tf_op jit(solution)/shard_map/ppermute | solution.py:47
  125.6 7.8 %collective-permute-start.39 = (bf16[1080,128]{1,0:T(8,128)(2,1)S(1)}, bf16[1080,128]{1,0:T(8,128)(2,1)S(1)}, u32[]{:S(2)}, u32[]{:S(2)}) collective-permute-start(bf16[1080,128]{1,0:T(8,128)(2,1)S(1)} %add_convert_fusion.9), channel_id=1, source_target_pairs={{0,8},{1,5},{8,16},{9,1},{16,24},{17,9},{24,26},{25,17},{26,18},{2... | collective-permute-start | bytes 829448 | tf_op jit(solution)/shard_map/ppermute | solution.py:47
  127.5 8.8 %collective-permute-start.24 = (bf16[1080,128]{1,0:T(8,128)(2,1)S(1)}, bf16[1080,128]{1,0:T(8,128)(2,1)S(1)}, u32[]{:S(2)}, u32[]{:S(2)}) collective-permute-start(bf16[1080,128]{1,0:T(8,128)(2,1)S(1)} %add_convert_fusion.23), channel_id=1, source_target_pairs={{0,8},{1,5},{8,16},{9,1},{16,24},{17,9},{24,26},{25,17},{26,18},{2... | collective-permute-start | bytes 829448 | tf_op jit(solution)/shard_map/ppermute | solution.py:47
  130.5 8.8 %collective-permute-start.9 = (bf16[1080,128]{1,0:T(8,128)(2,1)S(1)}, bf16[1080,128]{1,0:T(8,128)(2,1)S(1)}, u32[]{:S(2)}, u32[]{:S(2)}) collective-permute-start(bf16[1080,128]{1,0:T(8,128)(2,1)S(1)} %add_convert_fusion.37), channel_id=1, source_target_pairs={{0,8},{1,5},{8,16},{9,1},{16,24},{17,9},{24,26},{25,17},{26,18},{2... | collective-permute-start | bytes 829448 | tf_op jit(solution)/shard_map/ppermute | solution.py:47
  133.4 8.8 %collective-permute-start.40 = (bf16[1080,128]{1,0:T(8,128)(2,1)S(1)}, bf16[1080,128]{1,0:T(8,128)(2,1)S(1)}, u32[]{:S(2)}, u32[]{:S(2)}) collective-permute-start(bf16[1080,128]{1,0:T(8,128)(2,1)S(1)} %add_convert_fusion.8), channel_id=1, source_target_pairs={{0,8},{1,5},{8,16},{9,1},{16,24},{17,9},{24,26},{25,17},{26,18},{2... | collective-permute-start | bytes 829448 | tf_op jit(solution)/shard_map/ppermute | solution.py:47
  136.4 8.8 %collective-permute-start.25 = (bf16[1080,128]{1,0:T(8,128)(2,1)S(1)}, bf16[1080,128]{1,0:T(8,128)(2,1)S(1)}, u32[]{:S(2)}, u32[]{:S(2)}) collective-permute-start(bf16[1080,128]{1,0:T(8,128)(2,1)S(1)} %add_convert_fusion.22), channel_id=1, source_target_pairs={{0,8},{1,5},{8,16},{9,1},{16,24},{17,9},{24,26},{25,17},{26,18},{2... | collective-permute-start | bytes 829448 | tf_op jit(solution)/shard_map/ppermute | solution.py:47
  139.4 8.8 %collective-permute-start.10 = (bf16[1080,128]{1,0:T(8,128)(2,1)S(1)}, bf16[1080,128]{1,0:T(8,128)(2,1)S(1)}, u32[]{:S(2)}, u32[]{:S(2)}) collective-permute-start(bf16[1080,128]{1,0:T(8,128)(2,1)S(1)} %add_convert_fusion.36), channel_id=1, source_target_pairs={{0,8},{1,5},{8,16},{9,1},{16,24},{17,9},{24,26},{25,17},{26,18},{2... | collective-permute-start | bytes 829448 | tf_op jit(solution)/shard_map/ppermute | solution.py:47
  142.3 8.8 %collective-permute-start.41 = (bf16[1080,128]{1,0:T(8,128)(2,1)S(1)}, bf16[1080,128]{1,0:T(8,128)(2,1)S(1)}, u32[]{:S(2)}, u32[]{:S(2)}) collective-permute-start(bf16[1080,128]{1,0:T(8,128)(2,1)S(1)} %add_convert_fusion.7), channel_id=1, source_target_pairs={{0,8},{1,5},{8,16},{9,1},{16,24},{17,9},{24,26},{25,17},{26,18},{2... | collective-permute-start | bytes 829448 | tf_op jit(solution)/shard_map/ppermute | solution.py:47
  145.3 8.8 %collective-permute-start.26 = (bf16[1080,128]{1,0:T(8,128)(2,1)S(1)}, bf16[1080,128]{1,0:T(8,128)(2,1)S(1)}, u32[]{:S(2)}, u32[]{:S(2)}) collective-permute-start(bf16[1080,128]{1,0:T(8,128)(2,1)S(1)} %add_convert_fusion.21), channel_id=1, source_target_pairs={{0,8},{1,5},{8,16},{9,1},{16,24},{17,9},{24,26},{25,17},{26,18},{2... | collective-permute-start | bytes 829448 | tf_op jit(solution)/shard_map/ppermute | solution.py:47
  148.3 8.8 %collective-permute-start.11 = (bf16[1080,128]{1,0:T(8,128)(2,1)S(1)}, bf16[1080,128]{1,0:T(8,128)(2,1)S(1)}, u32[]{:S(2)}, u32[]{:S(2)}) collective-permute-start(bf16[1080,128]{1,0:T(8,128)(2,1)S(1)} %add_convert_fusion.35), channel_id=1, source_target_pairs={{0,8},{1,5},{8,16},{9,1},{16,24},{17,9},{24,26},{25,17},{26,18},{2... | collective-permute-start | bytes 829448 | tf_op jit(solution)/shard_map/ppermute | solution.py:47
  151.2 8.8 %collective-permute-start.42 = (bf16[1080,128]{1,0:T(8,128)(2,1)S(1)}, bf16[1080,128]{1,0:T(8,128)(2,1)S(1)}, u32[]{:S(2)}, u32[]{:S(2)}) collective-permute-start(bf16[1080,128]{1,0:T(8,128)(2,1)S(1)} %add_convert_fusion.6), channel_id=1, source_target_pairs={{0,8},{1,5},{8,16},{9,1},{16,24},{17,9},{24,26},{25,17},{26,18},{2... | collective-permute-start | bytes 829448 | tf_op jit(solution)/shard_map/ppermute | solution.py:47
  154.2 8.8 %collective-permute-start.27 = (bf16[1080,128]{1,0:T(8,128)(2,1)S(1)}, bf16[1080,128]{1,0:T(8,128)(2,1)S(1)}, u32[]{:S(2)}, u32[]{:S(2)}) collective-permute-start(bf16[1080,128]{1,0:T(8,128)(2,1)S(1)} %add_convert_fusion.20), channel_id=1, source_target_pairs={{0,8},{1,5},{8,16},{9,1},{16,24},{17,9},{24,26},{25,17},{26,18},{2... | collective-permute-start | bytes 829448 | tf_op jit(solution)/shard_map/ppermute | solution.py:47
  157.1 8.8 %collective-permute-start.12 = (bf16[1080,128]{1,0:T(8,128)(2,1)S(1)}, bf16[1080,128]{1,0:T(8,128)(2,1)S(1)}, u32[]{:S(2)}, u32[]{:S(2)}) collective-permute-start(bf16[1080,128]{1,0:T(8,128)(2,1)S(1)} %add_convert_fusion.34), channel_id=1, source_target_pairs={{0,8},{1,5},{8,16},{9,1},{16,24},{17,9},{24,26},{25,17},{26,18},{2... | collective-permute-start | bytes 829448 | tf_op jit(solution)/shard_map/ppermute | solution.py:47
  160.1 8.8 %collective-permute-start.43 = (bf16[1080,128]{1,0:T(8,128)(2,1)S(1)}, bf16[1080,128]{1,0:T(8,128)(2,1)S(1)}, u32[]{:S(2)}, u32[]{:S(2)}) collective-permute-start(bf16[1080,128]{1,0:T(8,128)(2,1)S(1)} %add_convert_fusion.5), channel_id=1, source_target_pairs={{0,8},{1,5},{8,16},{9,1},{16,24},{17,9},{24,26},{25,17},{26,18},{2... | collective-permute-start | bytes 829448 | tf_op jit(solution)/shard_map/ppermute | solution.py:47
  163.1 8.8 %collective-permute-start.28 = (bf16[1080,128]{1,0:T(8,128)(2,1)S(1)}, bf16[1080,128]{1,0:T(8,128)(2,1)S(1)}, u32[]{:S(2)}, u32[]{:S(2)}) collective-permute-start(bf16[1080,128]{1,0:T(8,128)(2,1)S(1)} %add_convert_fusion.19), channel_id=1, source_target_pairs={{0,8},{1,5},{8,16},{9,1},{16,24},{17,9},{24,26},{25,17},{26,18},{2... | collective-permute-start | bytes 829448 | tf_op jit(solution)/shard_map/ppermute | solution.py:47
  166.0 8.8 %collective-permute-start.13 = (bf16[1080,128]{1,0:T(8,128)(2,1)S(1)}, bf16[1080,128]{1,0:T(8,128)(2,1)S(1)}, u32[]{:S(2)}, u32[]{:S(2)}) collective-permute-start(bf16[1080,128]{1,0:T(8,128)(2,1)S(1)} %add_convert_fusion.33), channel_id=1, source_target_pairs={{0,8},{1,5},{8,16},{9,1},{16,24},{17,9},{24,26},{25,17},{26,18},{2... | collective-permute-start | bytes 829448 | tf_op jit(solution)/shard_map/ppermute | solution.py:47
  169.0 8.8 %collective-permute-start.44 = (bf16[1080,128]{1,0:T(8,128)(2,1)S(1)}, bf16[1080,128]{1,0:T(8,128)(2,1)S(1)}, u32[]{:S(2)}, u32[]{:S(2)}) collective-permute-start(bf16[1080,128]{1,0:T(8,128)(2,1)S(1)} %add_convert_fusion.4), channel_id=1, source_target_pairs={{0,8},{1,5},{8,16},{9,1},{16,24},{17,9},{24,26},{25,17},{26,18},{2... | collective-permute-start | bytes 829448 | tf_op jit(solution)/shard_map/ppermute | solution.py:47
  172.0 8.8 %collective-permute-start.29 = (bf16[1080,128]{1,0:T(8,128)(2,1)S(1)}, bf16[1080,128]{1,0:T(8,128)(2,1)S(1)}, u32[]{:S(2)}, u32[]{:S(2)}) collective-permute-start(bf16[1080,128]{1,0:T(8,128)(2,1)S(1)} %add_convert_fusion.18), channel_id=1, source_target_pairs={{0,8},{1,5},{8,16},{9,1},{16,24},{17,9},{24,26},{25,17},{26,18},{2... | collective-permute-start | bytes 829448 | tf_op jit(solution)/shard_map/ppermute | solution.py:47
  174.9 8.8 %collective-permute-start.14 = (bf16[1080,128]{1,0:T(8,128)(2,1)S(1)}, bf16[1080,128]{1,0:T(8,128)(2,1)S(1)}, u32[]{:S(2)}, u32[]{:S(2)}) collective-permute-start(bf16[1080,128]{1,0:T(8,128)(2,1)S(1)} %add_convert_fusion.32), channel_id=1, source_target_pairs={{0,8},{1,5},{8,16},{9,1},{16,24},{17,9},{24,26},{25,17},{26,18},{2... | collective-permute-start | bytes 829448 | tf_op jit(solution)/shard_map/ppermute | solution.py:47
  177.9 8.8 %collective-permute-start.45 = (bf16[1080,128]{1,0:T(8,128)(2,1)S(1)}, bf16[1080,128]{1,0:T(8,128)(2,1)S(1)}, u32[]{:S(2)}, u32[]{:S(2)}) collective-permute-start(bf16[1080,128]{1,0:T(8,128)(2,1)S(1)} %add_convert_fusion.3), channel_id=1, source_target_pairs={{0,8},{1,5},{8,16},{9,1},{16,24},{17,9},{24,26},{25,17},{26,18},{2... | collective-permute-start | bytes 829448 | tf_op jit(solution)/shard_map/ppermute | solution.py:47
  180.9 8.8 %collective-permute-start.30 = (bf16[1080,128]{1,0:T(8,128)(2,1)S(1)}, bf16[1080,128]{1,0:T(8,128)(2,1)S(1)}, u32[]{:S(2)}, u32[]{:S(2)}) collective-permute-start(bf16[1080,128]{1,0:T(8,128)(2,1)S(1)} %add_convert_fusion.17), channel_id=1, source_target_pairs={{0,8},{1,5},{8,16},{9,1},{16,24},{17,9},{24,26},{25,17},{26,18},{2... | collective-permute-start | bytes 829448 | tf_op jit(solution)/shard_map/ppermute | solution.py:47
  183.8 8.8 %collective-permute-start.15 = (bf16[1080,128]{1,0:T(8,128)(2,1)S(1)}, bf16[1080,128]{1,0:T(8,128)(2,1)S(1)}, u32[]{:S(2)}, u32[]{:S(2)}) collective-permute-start(bf16[1080,128]{1,0:T(8,128)(2,1)S(1)} %add_convert_fusion.31), channel_id=1, source_target_pairs={{0,8},{1,5},{8,16},{9,1},{16,24},{17,9},{24,26},{25,17},{26,18},{2... | collective-permute-start | bytes 829448 | tf_op jit(solution)/shard_map/ppermute | solution.py:47
  186.8 8.8 %collective-permute-start.46 = (bf16[1080,128]{1,0:T(8,128)(2,1)S(1)}, bf16[1080,128]{1,0:T(8,128)(2,1)S(1)}, u32[]{:S(2)}, u32[]{:S(2)}) collective-permute-start(bf16[1080,128]{1,0:T(8,128)(2,1)S(1)} %add_convert_fusion.2), channel_id=1, source_target_pairs={{0,8},{1,5},{8,16},{9,1},{16,24},{17,9},{24,26},{25,17},{26,18},{2... | collective-permute-start | bytes 829448 | tf_op jit(solution)/shard_map/ppermute | solution.py:47
  189.8 8.8 %collective-permute-start.31 = (bf16[1080,128]{1,0:T(8,128)(2,1)S(1)}, bf16[1080,128]{1,0:T(8,128)(2,1)S(1)}, u32[]{:S(2)}, u32[]{:S(2)}) collective-permute-start(bf16[1080,128]{1,0:T(8,128)(2,1)S(1)} %add_convert_fusion.16), channel_id=1, source_target_pairs={{0,8},{1,5},{8,16},{9,1},{16,24},{17,9},{24,26},{25,17},{26,18},{2... | collective-permute-start | bytes 829448 | tf_op jit(solution)/shard_map/ppermute | solution.py:47
  192.7 8.8 %collective-permute-start.16 = (bf16[1080,128]{1,0:T(8,128)(2,1)S(1)}, bf16[1080,128]{1,0:T(8,128)(2,1)S(1)}, u32[]{:S(2)}, u32[]{:S(2)}) collective-permute-start(bf16[1080,128]{1,0:T(8,128)(2,1)S(1)} %add_convert_fusion.30), channel_id=1, source_target_pairs={{0,8},{1,5},{8,16},{9,1},{16,24},{17,9},{24,26},{25,17},{26,18},{2... | collective-permute-start | bytes 829448 | tf_op jit(solution)/shard_map/ppermute | solution.py:47
  195.7 8.8 %collective-permute-start.47 = (bf16[1080,128]{1,0:T(8,128)(2,1)S(1)}, bf16[1080,128]{1,0:T(8,128)(2,1)S(1)}, u32[]{:S(2)}, u32[]{:S(2)}) collective-permute-start(bf16[1080,128]{1,0:T(8,128)(2,1)S(1)} %add_convert_fusion.1), channel_id=1, source_target_pairs={{0,8},{1,5},{8,16},{9,1},{16,24},{17,9},{24,26},{25,17},{26,18},{2... | collective-permute-start | bytes 829448 | tf_op jit(solution)/shard_map/ppermute | solution.py:47
  198.6 8.8 %collective-permute-start.32 = (bf16[1080,128]{1,0:T(8,128)(2,1)S(1)}, bf16[1080,128]{1,0:T(8,128)(2,1)S(1)}, u32[]{:S(2)}, u32[]{:S(2)}) collective-permute-start(bf16[1080,128]{1,0:T(8,128)(2,1)S(1)} %add_convert_fusion.15), channel_id=1, source_target_pairs={{0,8},{1,5},{8,16},{9,1},{16,24},{17,9},{24,26},{25,17},{26,18},{2... | collective-permute-start | bytes 829448 | tf_op jit(solution)/shard_map/ppermute | solution.py:47
  201.6 8.8 %collective-permute-start.17 = (bf16[1080,128]{1,0:T(8,128)(2,1)S(1)}, bf16[1080,128]{1,0:T(8,128)(2,1)S(1)}, u32[]{:S(2)}, u32[]{:S(2)}) collective-permute-start(bf16[1080,128]{1,0:T(8,128)(2,1)S(1)} %add_convert_fusion.29), channel_id=1, source_target_pairs={{0,8},{1,5},{8,16},{9,1},{16,24},{17,9},{24,26},{25,17},{26,18},{2... | collective-permute-start | bytes 829448 | tf_op jit(solution)/shard_map/ppermute | solution.py:47
  (5 other events, 109.1 us)

commit v5 on v4

--- a/solution.py
+++ b/solution.py
@@ -2,6 +2,7 @@
 import math
 
 import jax
+import numpy as np
 import jax.numpy as jnp
 from jax import lax
 from jax.experimental import pallas as pl
@@ -28,13 +29,17 @@
     pos_of = [0] * n
     for p, d in enumerate(order):
         pos_of[d] = p
-    me = jnp.asarray(pos_of, jnp.int32)[lax.axis_index("dp")]
-    step = 1 - 2 * (lax.axis_index("tensor") % 2)
-    order_arr = jnp.asarray(order, jnp.int32)
+    table = np.zeros((n * nt, n), np.int32)
+    for d in range(n):
+        for t in range(nt):
+            hop = 1 if t % 2 == 0 else -1
+            for s in range(n):
+                table[d * nt + t, s] = order[(pos_of[d] - hop * (1 + s)) % n] * chunk
+    device = lax.axis_index("dp") * nt + lax.axis_index("tensor")
+    offsets = jnp.asarray(table)[device]
 
     def own(full, s):
-        p = (me - step * (1 + s)) % n
-        return lax.dynamic_slice_in_dim(full, order_arr[p] * chunk, chunk, axis=0)
+        return lax.dynamic_slice_in_dim(full, offsets[s], chunk, axis=0)
 
     perm = []
     for p in range(n):

time: 215 us -> 223 us (1.037)
  between operations: 21.7 us -> 31.2 us
    dynamic_slice x2 -> x1, local copies, waits for them, and re-layouts: 3.24 us -> 0.69 us  [ring_reduce_scatter(): offsets = jnp.asarray(table)[device]]
  transfers between devices with their start and end apart: 48 -> 48, of which waited for: 36 -> 36; matrix products, arithmetic and copies ran while one was open for 12% -> 11% of each run, Pallas kernels for 0% -> 0%
where the time goes in v5:
time: 223 us; the launch traced here: 221 us
  starting transfers between devices  78.7 us (35%)
  waiting for transfers between devices  40.5 us (18%)
  Pallas kernels  37.1 us (17%)
  between operations  31.2 us (14%)
  other arithmetic  26.9 us (12%)
  local copies, waits for them, and re-layouts  6.62 us (3%)
    ppermute x45, starting transfers between devices, ring_reduce_scatter(): moved = lax.ppermute(accs[i].astype(wire_dtype), ('dp', 'tensor'), perm)  77.7 us
    ppermute x45, waiting for transfers between devices, ring_reduce_scatter(): moved = lax.ppermute(accs[i].astype(wire_dtype), ('dp', 'tensor'), perm)  40.5 us
    pallas_call x1, Pallas kernels, ffn_block_terms(): pl.pallas_call(_ffn_kernel, grid_spec=pltpu.PrefetchScalarGridSpec(num_sc...  37.1 us
    convert_element_type x42, other arithmetic, ring_reduce_scatter(): moved = lax.ppermute(accs[i].astype(wire_dtype), ('dp', 'tensor'), perm)  14.6 us
  transfers between devices with their start and end apart: 48, of which 36 were waited for; matrix products, arithmetic and copies ran while one was open for 11% of the time, Pallas kernels for 0%

profile of v5, /device:TPU:0, one launch (start us, length us, event | category | flops | bytes accessed | tf_op | source)
XLA Modules:
  0.0 221.1 jit_solution(16680731956645000245)
XLA Ops:
  38.2 37.1 %ffn_block_terms.1 = (f32[27,5,128,128]{3,2,1,0:T(8,128)}, f32[27,5,128,128]{3,2,1,0:T(8,128)}, f32[27,5,128,128]{3,2,1,0:T(8,128)}, f32[128,5120]{1,0:T(8,128)}) custom-call(s32[27,5]{1,0:T(8,128)} %copy.14.col_ref, s32[27]{0:T(128)} %cnt_ref.1, bf16[128,5120]{1,0:T(8,128)(2,1)} %pad_maximum_fusion.1.tok_ref, bf16[128,5120]{1,0:T(8,128)(2,1)} %pad_maximum_fusion.2.cot_ref, ...), custom_call_target="tpu_custom_call" | custom-call | flops 5096079360 | bytes 45056000 | tf_op jit(solution)/shard_map/ffn_block_terms/pallas_call | solution.py:111
  75.3 2.0 select_convert_fusion
  79.3 2.6 %collective-permute-start.33 = (bf16[1080,128]{1,0:T(8,128)(2,1)S(1)}, bf16[1080,128]{1,0:T(8,128)(2,1)S(1)}, u32[]{:S(2)}, u32[]{:S(2)}) collective-permute-start(bf16[1080,128]{1,0:T(8,128)(2,1)S(1)} %dynamic-slice_convert_fusion), channel_id=1, source_target_pairs={{0,8},{1,5},{8,16},{9,1},{16,24},{17,9},{24,26},{25,17},{26,18},{2... | collective-permute-start | bytes 829448 | tf_op jit(solution)/shard_map/ppermute | solution.py:52
  83.0 1.6 collective-permute-start.18
  85.7 1.6 collective-permute-start.3
  93.7 1.8 collective-permute-start.4
  96.7 1.8 collective-permute-start.35
  99.6 1.8 collective-permute-start.20
  101.6 1.8 collective-permute-start.5
  103.4 3.4 %add_convert_fusion = bf16[128,2560]{1,0:T(8,128)(2,1)} fusion(bf16[128,2560]{1,0:T(8,128)(2,1)S(1)} %collective-permute-done.2, f32[128,5120]{1,0:T(8,128)} %get-tuple-element.8, pred[]{:T(512)S(6)} %eq.3), kind=kLoop, calls=%fused_computation.6 | loop fusion | flops 1310720 | bytes 3932161 | tf_op jit(solution)/shard_map/convert_element_type | solution.py:163
  107.9 1.7 collective-permute-start.36
  110.8 1.6 collective-permute-start.21
  115.6 1.7 collective-permute-start.37
  117.5 1.7 collective-permute-start.22
  120.5 1.7 collective-permute-start.7
  124.5 1.7 collective-permute-start.38
  126.4 1.7 collective-permute-start.23
  129.4 1.7 collective-permute-start.8
  133.4 1.7 collective-permute-start.39
  135.3 1.7 collective-permute-start.24
  138.3 1.7 collective-permute-start.9
  141.2 1.7 collective-permute-start.40
  144.2 1.7 collective-permute-start.25
  147.2 1.7 collective-permute-start.10
  150.1 1.7 collective-permute-start.41
  153.1 1.7 collective-permute-start.26
  156.1 1.7 collective-permute-start.11
  159.0 1.7 collective-permute-start.42
  162.0 1.7 collective-permute-start.27
  164.9 1.7 collective-permute-start.12
  167.9 1.7 collective-permute-start.43
  170.9 1.7 collective-permute-start.28
  173.8 1.7 collective-permute-start.13
  176.8 1.7 collective-permute-start.44
  179.8 1.7 collective-permute-start.29
  182.7 1.7 collective-permute-start.14
  185.7 1.7 collective-permute-start.45
  188.6 1.7 collective-permute-start.30
  191.6 1.7 collective-permute-start.15
  194.6 1.7 collective-permute-start.46
  197.6 1.7 collective-permute-start.31
  200.5 1.7 collective-permute-start.16
  203.5 1.7 collective-permute-start.47
  206.4 1.7 collective-permute-start.32
  209.4 1.7 collective-permute-start.17
  212.3 2.9 %collective-permute-done.32 = bf16[1080,128]{1,0:T(8,128)(2,1)S(1)} collective-permute-done((bf16[1080,128]{1,0:T(8,128)(2,1)S(1)}, bf16[1080,128]{1,0:T(8,128)(2,1)S(1)}, u32[]{:S(2)}, u32[]{:S(2)}) %collective-permute-start.32) | collective-permute-done | bytes 276512 | tf_op jit(solution)/shard_map/ppermute | solution.py:52
  215.3 2.9 %collective-permute-done.17 = bf16[1080,128]{1,0:T(8,128)(2,1)S(1)} collective-permute-done((bf16[1080,128]{1,0:T(8,128)(2,1)S(1)}, bf16[1080,128]{1,0:T(8,128)(2,1)S(1)}, u32[]{:S(2)}, u32[]{:S(2)}) %collective-permute-start.17) | collective-permute-done | bytes 276512 | tf_op jit(solution)/shard_map/ppermute | solution.py:52
  218.3 2.8 %add_divide_fusion = (f32[3,1,1080,128]{3,2,1,0:T(8,128)}, f32[3,1,1080,128]{3,2,1,0:T(8,128)}, f32[3,1,1080,128]{3,2,1,0:T(8,128)}) fusion(f32[1,1,1080,128]{3,2,1,0:T(8,128)S(1)} %add_bitcast_fusion, f32[1,1,1080,128]{3,2,1,0:T(8,128)S(1)} %add_bitcast_fusion.1, f32[1,1,1080,128]{3,2,1,0:T(8,128)S(1)} %add_bitcast_fusion.2, ...), kind=kLoop, calls=%fused_computation.1 | loop fusion | flops 4976640 | bytes 9953280 | tf_op jit(solution)/shard_map/div | solution.py:172
  (116 shorter events, 65.6 us)
Async XLA Ops:
  0.6 33.7 %collective-permute-start.1 = (bf16[128,2560]{1,0:T(8,128)(2,1)}, bf16[128,2560]{1,0:T(8,128)(2,1)S(1)}, u32[]{:S(2)}, u32[]{:S(2)}) collective-permute-start(bf16[128,2560]{1,0:T(8,128)(2,1)} %param.11), channel_id=1, source_target_pairs={{0,1},{1,0},{2,3},{3,2},{4,5},{5,4},{6,7},{7,6},{8,9},{9,8},{10,11... | collective-permute-start | bytes 1966088 | tf_op jit(solution)/shard_map/ppermute | solution.py:134
  1.1 33.2 %collective-permute-start = (bf16[128,2560]{1,0:T(8,128)(2,1)}, bf16[128,2560]{1,0:T(8,128)(2,1)S(1)}, u32[]{:S(2)}, u32[]{:S(2)}) collective-permute-start(bf16[128,2560]{1,0:T(8,128)(2,1)} %param.10), channel_id=1, source_target_pairs={{0,1},{1,0},{2,3},{3,2},{4,5},{5,4},{6,7},{7,6},{8,9},{9,8},{10,11... | collective-permute-start | bytes 1966088 | tf_op jit(solution)/shard_map/ppermute | solution.py:134
  77.3 26.1 %collective-permute-start.2 = (bf16[128,2560]{1,0:T(8,128)(2,1)S(1)}, bf16[128,2560]{1,0:T(8,128)(2,1)S(1)}, u32[]{:S(2)}, u32[]{:S(2)}) collective-permute-start(bf16[128,2560]{1,0:T(8,128)(2,1)S(1)} %select_convert_fusion), channel_id=1, source_target_pairs={{0,1},{1,0},{2,3},{3,2},{4,5},{5,4},{6,7},{7,6},{8,9},{9,8},{10,11... | collective-permute-start | bytes 1966088 | tf_op jit(solution)/shard_map/ppermute | solution.py:162
  79.3 8.1 %collective-permute-start.33 = (bf16[1080,128]{1,0:T(8,128)(2,1)S(1)}, bf16[1080,128]{1,0:T(8,128)(2,1)S(1)}, u32[]{:S(2)}, u32[]{:S(2)}) collective-permute-start(bf16[1080,128]{1,0:T(8,128)(2,1)S(1)} %dynamic-slice_convert_fusion), channel_id=1, source_target_pairs={{0,8},{1,5},{8,16},{9,1},{16,24},{17,9},{24,26},{25,17},{26,18},{2... | collective-permute-start | bytes 829448 | tf_op jit(solution)/shard_map/ppermute | solution.py:52
  83.0 7.1 %collective-permute-start.18 = (bf16[1080,128]{1,0:T(8,128)(2,1)S(1)}, bf16[1080,128]{1,0:T(8,128)(2,1)S(1)}, u32[]{:S(2)}, u32[]{:S(2)}) collective-permute-start(bf16[1080,128]{1,0:T(8,128)(2,1)S(1)} %dynamic-slice_convert_fusion.1), channel_id=1, source_target_pairs={{0,8},{1,5},{8,16},{9,1},{16,24},{17,9},{24,26},{25,17},{26,18},{2... | collective-permute-start | bytes 829448 | tf_op jit(solution)/shard_map/ppermute | solution.py:52
  85.7 6.8 %collective-permute-start.3 = (bf16[1080,128]{1,0:T(8,128)(2,1)S(1)}, bf16[1080,128]{1,0:T(8,128)(2,1)S(1)}, u32[]{:S(2)}, u32[]{:S(2)}) collective-permute-start(bf16[1080,128]{1,0:T(8,128)(2,1)S(1)} %dynamic-slice_convert_fusion.2), channel_id=1, source_target_pairs={{0,8},{1,5},{8,16},{9,1},{16,24},{17,9},{24,26},{25,17},{26,18},{2... | collective-permute-start | bytes 829448 | tf_op jit(solution)/shard_map/ppermute | solution.py:52
  88.5 7.0 %collective-permute-start.34 = (bf16[1080,128]{1,0:T(8,128)(2,1)S(1)}, bf16[1080,128]{1,0:T(8,128)(2,1)S(1)}, u32[]{:S(2)}, u32[]{:S(2)}) collective-permute-start(bf16[1080,128]{1,0:T(8,128)(2,1)S(1)} %add_convert_fusion.14), channel_id=1, source_target_pairs={{0,8},{1,5},{8,16},{9,1},{16,24},{17,9},{24,26},{25,17},{26,18},{2... | collective-permute-start | bytes 829448 | tf_op jit(solution)/shard_map/ppermute | solution.py:52
  91.2 7.3 %collective-permute-start.19 = (bf16[1080,128]{1,0:T(8,128)(2,1)S(1)}, bf16[1080,128]{1,0:T(8,128)(2,1)S(1)}, u32[]{:S(2)}, u32[]{:S(2)}) collective-permute-start(bf16[1080,128]{1,0:T(8,128)(2,1)S(1)} %add_convert_fusion.28), channel_id=1, source_target_pairs={{0,8},{1,5},{8,16},{9,1},{16,24},{17,9},{24,26},{25,17},{26,18},{2... | collective-permute-start | bytes 829448 | tf_op jit(solution)/shard_map/ppermute | solution.py:52
  93.7 7.7 %collective-permute-start.4 = (bf16[1080,128]{1,0:T(8,128)(2,1)S(1)}, bf16[1080,128]{1,0:T(8,128)(2,1)S(1)}, u32[]{:S(2)}, u32[]{:S(2)}) collective-permute-start(bf16[1080,128]{1,0:T(8,128)(2,1)S(1)} %add_convert_fusion.42), channel_id=1, source_target_pairs={{0,8},{1,5},{8,16},{9,1},{16,24},{17,9},{24,26},{25,17},{26,18},{2... | collective-permute-start | bytes 829448 | tf_op jit(solution)/shard_map/ppermute | solution.py:52
  96.7 10.1 %collective-permute-start.35 = (bf16[1080,128]{1,0:T(8,128)(2,1)S(1)}, bf16[1080,128]{1,0:T(8,128)(2,1)S(1)}, u32[]{:S(2)}, u32[]{:S(2)}) collective-permute-start(bf16[1080,128]{1,0:T(8,128)(2,1)S(1)} %add_convert_fusion.13), channel_id=1, source_target_pairs={{0,8},{1,5},{8,16},{9,1},{16,24},{17,9},{24,26},{25,17},{26,18},{2... | collective-permute-start | bytes 829448 | tf_op jit(solution)/shard_map/ppermute | solution.py:52
  99.6 10.0 %collective-permute-start.20 = (bf16[1080,128]{1,0:T(8,128)(2,1)S(1)}, bf16[1080,128]{1,0:T(8,128)(2,1)S(1)}, u32[]{:S(2)}, u32[]{:S(2)}) collective-permute-start(bf16[1080,128]{1,0:T(8,128)(2,1)S(1)} %add_convert_fusion.27), channel_id=1, source_target_pairs={{0,8},{1,5},{8,16},{9,1},{16,24},{17,9},{24,26},{25,17},{26,18},{2... | collective-permute-start | bytes 829448 | tf_op jit(solution)/shard_map/ppermute | solution.py:52
  101.6 10.9 %collective-permute-start.5 = (bf16[1080,128]{1,0:T(8,128)(2,1)S(1)}, bf16[1080,128]{1,0:T(8,128)(2,1)S(1)}, u32[]{:S(2)}, u32[]{:S(2)}) collective-permute-start(bf16[1080,128]{1,0:T(8,128)(2,1)S(1)} %add_convert_fusion.41), channel_id=1, source_target_pairs={{0,8},{1,5},{8,16},{9,1},{16,24},{17,9},{24,26},{25,17},{26,18},{2... | collective-permute-start | bytes 829448 | tf_op jit(solution)/shard_map/ppermute | solution.py:52
  107.9 6.6 %collective-permute-start.36 = (bf16[1080,128]{1,0:T(8,128)(2,1)S(1)}, bf16[1080,128]{1,0:T(8,128)(2,1)S(1)}, u32[]{:S(2)}, u32[]{:S(2)}) collective-permute-start(bf16[1080,128]{1,0:T(8,128)(2,1)S(1)} %add_convert_fusion.12), channel_id=1, source_target_pairs={{0,8},{1,5},{8,16},{9,1},{16,24},{17,9},{24,26},{25,17},{26,18},{2... | collective-permute-start | bytes 829448 | tf_op jit(solution)/shard_map/ppermute | solution.py:52
  110.8 6.7 %collective-permute-start.21 = (bf16[1080,128]{1,0:T(8,128)(2,1)S(1)}, bf16[1080,128]{1,0:T(8,128)(2,1)S(1)}, u32[]{:S(2)}, u32[]{:S(2)}) collective-permute-start(bf16[1080,128]{1,0:T(8,128)(2,1)S(1)} %add_convert_fusion.26), channel_id=1, source_target_pairs={{0,8},{1,5},{8,16},{9,1},{16,24},{17,9},{24,26},{25,17},{26,18},{2... | collective-permute-start | bytes 829448 | tf_op jit(solution)/shard_map/ppermute | solution.py:52
  112.5 7.9 %collective-permute-start.6 = (bf16[1080,128]{1,0:T(8,128)(2,1)S(1)}, bf16[1080,128]{1,0:T(8,128)(2,1)S(1)}, u32[]{:S(2)}, u32[]{:S(2)}) collective-permute-start(bf16[1080,128]{1,0:T(8,128)(2,1)S(1)} %add_convert_fusion.40), channel_id=1, source_target_pairs={{0,8},{1,5},{8,16},{9,1},{16,24},{17,9},{24,26},{25,17},{26,18},{2... | collective-permute-start | bytes 829448 | tf_op jit(solution)/shard_map/ppermute | solution.py:52
  115.6 7.7 %collective-permute-start.37 = (bf16[1080,128]{1,0:T(8,128)(2,1)S(1)}, bf16[1080,128]{1,0:T(8,128)(2,1)S(1)}, u32[]{:S(2)}, u32[]{:S(2)}) collective-permute-start(bf16[1080,128]{1,0:T(8,128)(2,1)S(1)} %add_convert_fusion.11), channel_id=1, source_target_pairs={{0,8},{1,5},{8,16},{9,1},{16,24},{17,9},{24,26},{25,17},{26,18},{2... | collective-permute-start | bytes 829448 | tf_op jit(solution)/shard_map/ppermute | solution.py:52
  117.5 8.8 %collective-permute-start.22 = (bf16[1080,128]{1,0:T(8,128)(2,1)S(1)}, bf16[1080,128]{1,0:T(8,128)(2,1)S(1)}, u32[]{:S(2)}, u32[]{:S(2)}) collective-permute-start(bf16[1080,128]{1,0:T(8,128)(2,1)S(1)} %add_convert_fusion.25), channel_id=1, source_target_pairs={{0,8},{1,5},{8,16},{9,1},{16,24},{17,9},{24,26},{25,17},{26,18},{2... | collective-permute-start | bytes 829448 | tf_op jit(solution)/shard_map/ppermute | solution.py:52
  120.5 8.8 %collective-permute-start.7 = (bf16[1080,128]{1,0:T(8,128)(2,1)S(1)}, bf16[1080,128]{1,0:T(8,128)(2,1)S(1)}, u32[]{:S(2)}, u32[]{:S(2)}) collective-permute-start(bf16[1080,128]{1,0:T(8,128)(2,1)S(1)} %add_convert_fusion.39), channel_id=1, source_target_pairs={{0,8},{1,5},{8,16},{9,1},{16,24},{17,9},{24,26},{25,17},{26,18},{2... | collective-permute-start | bytes 829448 | tf_op jit(solution)/shard_map/ppermute | solution.py:52
  124.5 7.7 %collective-permute-start.38 = (bf16[1080,128]{1,0:T(8,128)(2,1)S(1)}, bf16[1080,128]{1,0:T(8,128)(2,1)S(1)}, u32[]{:S(2)}, u32[]{:S(2)}) collective-permute-start(bf16[1080,128]{1,0:T(8,128)(2,1)S(1)} %add_convert_fusion.10), channel_id=1, source_target_pairs={{0,8},{1,5},{8,16},{9,1},{16,24},{17,9},{24,26},{25,17},{26,18},{2... | collective-permute-start | bytes 829448 | tf_op jit(solution)/shard_map/ppermute | solution.py:52
  126.4 8.8 %collective-permute-start.23 = (bf16[1080,128]{1,0:T(8,128)(2,1)S(1)}, bf16[1080,128]{1,0:T(8,128)(2,1)S(1)}, u32[]{:S(2)}, u32[]{:S(2)}) collective-permute-start(bf16[1080,128]{1,0:T(8,128)(2,1)S(1)} %add_convert_fusion.24), channel_id=1, source_target_pairs={{0,8},{1,5},{8,16},{9,1},{16,24},{17,9},{24,26},{25,17},{26,18},{2... | collective-permute-start | bytes 829448 | tf_op jit(solution)/shard_map/ppermute | solution.py:52
  129.4 8.8 %collective-permute-start.8 = (bf16[1080,128]{1,0:T(8,128)(2,1)S(1)}, bf16[1080,128]{1,0:T(8,128)(2,1)S(1)}, u32[]{:S(2)}, u32[]{:S(2)}) collective-permute-start(bf16[1080,128]{1,0:T(8,128)(2,1)S(1)} %add_convert_fusion.38), channel_id=1, source_target_pairs={{0,8},{1,5},{8,16},{9,1},{16,24},{17,9},{24,26},{25,17},{26,18},{2... | collective-permute-start | bytes 829448 | tf_op jit(solution)/shard_map/ppermute | solution.py:52
  133.4 7.7 %collective-permute-start.39 = (bf16[1080,128]{1,0:T(8,128)(2,1)S(1)}, bf16[1080,128]{1,0:T(8,128)(2,1)S(1)}, u32[]{:S(2)}, u32[]{:S(2)}) collective-permute-start(bf16[1080,128]{1,0:T(8,128)(2,1)S(1)} %add_convert_fusion.9), channel_id=1, source_target_pairs={{0,8},{1,5},{8,16},{9,1},{16,24},{17,9},{24,26},{25,17},{26,18},{2... | collective-permute-start | bytes 829448 | tf_op jit(solution)/shard_map/ppermute | solution.py:52
  135.3 8.8 %collective-permute-start.24 = (bf16[1080,128]{1,0:T(8,128)(2,1)S(1)}, bf16[1080,128]{1,0:T(8,128)(2,1)S(1)}, u32[]{:S(2)}, u32[]{:S(2)}) collective-permute-start(bf16[1080,128]{1,0:T(8,128)(2,1)S(1)} %add_convert_fusion.23), channel_id=1, source_target_pairs={{0,8},{1,5},{8,16},{9,1},{16,24},{17,9},{24,26},{25,17},{26,18},{2... | collective-permute-start | bytes 829448 | tf_op jit(solution)/shard_map/ppermute | solution.py:52
  138.3 8.8 %collective-permute-start.9 = (bf16[1080,128]{1,0:T(8,128)(2,1)S(1)}, bf16[1080,128]{1,0:T(8,128)(2,1)S(1)}, u32[]{:S(2)}, u32[]{:S(2)}) collective-permute-start(bf16[1080,128]{1,0:T(8,128)(2,1)S(1)} %add_convert_fusion.37), channel_id=1, source_target_pairs={{0,8},{1,5},{8,16},{9,1},{16,24},{17,9},{24,26},{25,17},{26,18},{2... | collective-permute-start | bytes 829448 | tf_op jit(solution)/shard_map/ppermute | solution.py:52
  141.2 8.8 %collective-permute-start.40 = (bf16[1080,128]{1,0:T(8,128)(2,1)S(1)}, bf16[1080,128]{1,0:T(8,128)(2,1)S(1)}, u32[]{:S(2)}, u32[]{:S(2)}) collective-permute-start(bf16[1080,128]{1,0:T(8,128)(2,1)S(1)} %add_convert_fusion.8), channel_id=1, source_target_pairs={{0,8},{1,5},{8,16},{9,1},{16,24},{17,9},{24,26},{25,17},{26,18},{2... | collective-permute-start | bytes 829448 | tf_op jit(solution)/shard_map/ppermute | solution.py:52
  144.2 8.8 %collective-permute-start.25 = (bf16[1080,128]{1,0:T(8,128)(2,1)S(1)}, bf16[1080,128]{1,0:T(8,128)(2,1)S(1)}, u32[]{:S(2)}, u32[]{:S(2)}) collective-permute-start(bf16[1080,128]{1,0:T(8,128)(2,1)S(1)} %add_convert_fusion.22), channel_id=1, source_target_pairs={{0,8},{1,5},{8,16},{9,1},{16,24},{17,9},{24,26},{25,17},{26,18},{2... | collective-permute-start | bytes 829448 | tf_op jit(solution)/shard_map/ppermute | solution.py:52
  147.2 8.8 %collective-permute-start.10 = (bf16[1080,128]{1,0:T(8,128)(2,1)S(1)}, bf16[1080,128]{1,0:T(8,128)(2,1)S(1)}, u32[]{:S(2)}, u32[]{:S(2)}) collective-permute-start(bf16[1080,128]{1,0:T(8,128)(2,1)S(1)} %add_convert_fusion.36), channel_id=1, source_target_pairs={{0,8},{1,5},{8,16},{9,1},{16,24},{17,9},{24,26},{25,17},{26,18},{2... | collective-permute-start | bytes 829448 | tf_op jit(solution)/shard_map/ppermute | solution.py:52
  150.1 8.8 %collective-permute-start.41 = (bf16[1080,128]{1,0:T(8,128)(2,1)S(1)}, bf16[1080,128]{1,0:T(8,128)(2,1)S(1)}, u32[]{:S(2)}, u32[]{:S(2)}) collective-permute-start(bf16[1080,128]{1,0:T(8,128)(2,1)S(1)} %add_convert_fusion.7), channel_id=1, source_target_pairs={{0,8},{1,5},{8,16},{9,1},{16,24},{17,9},{24,26},{25,17},{26,18},{2... | collective-permute-start | bytes 829448 | tf_op jit(solution)/shard_map/ppermute | solution.py:52
  153.1 8.8 %collective-permute-start.26 = (bf16[1080,128]{1,0:T(8,128)(2,1)S(1)}, bf16[1080,128]{1,0:T(8,128)(2,1)S(1)}, u32[]{:S(2)}, u32[]{:S(2)}) collective-permute-start(bf16[1080,128]{1,0:T(8,128)(2,1)S(1)} %add_convert_fusion.21), channel_id=1, source_target_pairs={{0,8},{1,5},{8,16},{9,1},{16,24},{17,9},{24,26},{25,17},{26,18},{2... | collective-permute-start | bytes 829448 | tf_op jit(solution)/shard_map/ppermute | solution.py:52
  156.1 8.8 %collective-permute-start.11 = (bf16[1080,128]{1,0:T(8,128)(2,1)S(1)}, bf16[1080,128]{1,0:T(8,128)(2,1)S(1)}, u32[]{:S(2)}, u32[]{:S(2)}) collective-permute-start(bf16[1080,128]{1,0:T(8,128)(2,1)S(1)} %add_convert_fusion.35), channel_id=1, source_target_pairs={{0,8},{1,5},{8,16},{9,1},{16,24},{17,9},{24,26},{25,17},{26,18},{2... | collective-permute-start | bytes 829448 | tf_op jit(solution)/shard_map/ppermute | solution.py:52
  159.0 8.8 %collective-permute-start.42 = (bf16[1080,128]{1,0:T(8,128)(2,1)S(1)}, bf16[1080,128]{1,0:T(8,128)(2,1)S(1)}, u32[]{:S(2)}, u32[]{:S(2)}) collective-permute-start(bf16[1080,128]{1,0:T(8,128)(2,1)S(1)} %add_convert_fusion.6), channel_id=1, source_target_pairs={{0,8},{1,5},{8,16},{9,1},{16,24},{17,9},{24,26},{25,17},{26,18},{2... | collective-permute-start | bytes 829448 | tf_op jit(solution)/shard_map/ppermute | solution.py:52
  162.0 8.8 %collective-permute-start.27 = (bf16[1080,128]{1,0:T(8,128)(2,1)S(1)}, bf16[1080,128]{1,0:T(8,128)(2,1)S(1)}, u32[]{:S(2)}, u32[]{:S(2)}) collective-permute-start(bf16[1080,128]{1,0:T(8,128)(2,1)S(1)} %add_convert_fusion.20), channel_id=1, source_target_pairs={{0,8},{1,5},{8,16},{9,1},{16,24},{17,9},{24,26},{25,17},{26,18},{2... | collective-permute-start | bytes 829448 | tf_op jit(solution)/shard_map/ppermute | solution.py:52
  164.9 8.8 %collective-permute-start.12 = (bf16[1080,128]{1,0:T(8,128)(2,1)S(1)}, bf16[1080,128]{1,0:T(8,128)(2,1)S(1)}, u32[]{:S(2)}, u32[]{:S(2)}) collective-permute-start(bf16[1080,128]{1,0:T(8,128)(2,1)S(1)} %add_convert_fusion.34), channel_id=1, source_target_pairs={{0,8},{1,5},{8,16},{9,1},{16,24},{17,9},{24,26},{25,17},{26,18},{2... | collective-permute-start | bytes 829448 | tf_op jit(solution)/shard_map/ppermute | solution.py:52
  167.9 8.8 %collective-permute-start.43 = (bf16[1080,128]{1,0:T(8,128)(2,1)S(1)}, bf16[1080,128]{1,0:T(8,128)(2,1)S(1)}, u32[]{:S(2)}, u32[]{:S(2)}) collective-permute-start(bf16[1080,128]{1,0:T(8,128)(2,1)S(1)} %add_convert_fusion.5), channel_id=1, source_target_pairs={{0,8},{1,5},{8,16},{9,1},{16,24},{17,9},{24,26},{25,17},{26,18},{2... | collective-permute-start | bytes 829448 | tf_op jit(solution)/shard_map/ppermute | solution.py:52
  170.9 8.8 %collective-permute-start.28 = (bf16[1080,128]{1,0:T(8,128)(2,1)S(1)}, bf16[1080,128]{1,0:T(8,128)(2,1)S(1)}, u32[]{:S(2)}, u32[]{:S(2)}) collective-permute-start(bf16[1080,128]{1,0:T(8,128)(2,1)S(1)} %add_convert_fusion.19), channel_id=1, source_target_pairs={{0,8},{1,5},{8,16},{9,1},{16,24},{17,9},{24,26},{25,17},{26,18},{2... | collective-permute-start | bytes 829448 | tf_op jit(solution)/shard_map/ppermute | solution.py:52
  173.8 8.8 %collective-permute-start.13 = (bf16[1080,128]{1,0:T(8,128)(2,1)S(1)}, bf16[1080,128]{1,0:T(8,128)(2,1)S(1)}, u32[]{:S(2)}, u32[]{:S(2)}) collective-permute-start(bf16[1080,128]{1,0:T(8,128)(2,1)S(1)} %add_convert_fusion.33), channel_id=1, source_target_pairs={{0,8},{1,5},{8,16},{9,1},{16,24},{17,9},{24,26},{25,17},{26,18},{2... | collective-permute-start | bytes 829448 | tf_op jit(solution)/shard_map/ppermute | solution.py:52
  176.8 8.8 %collective-permute-start.44 = (bf16[1080,128]{1,0:T(8,128)(2,1)S(1)}, bf16[1080,128]{1,0:T(8,128)(2,1)S(1)}, u32[]{:S(2)}, u32[]{:S(2)}) collective-permute-start(bf16[1080,128]{1,0:T(8,128)(2,1)S(1)} %add_convert_fusion.4), channel_id=1, source_target_pairs={{0,8},{1,5},{8,16},{9,1},{16,24},{17,9},{24,26},{25,17},{26,18},{2... | collective-permute-start | bytes 829448 | tf_op jit(solution)/shard_map/ppermute | solution.py:52
  179.8 8.8 %collective-permute-start.29 = (bf16[1080,128]{1,0:T(8,128)(2,1)S(1)}, bf16[1080,128]{1,0:T(8,128)(2,1)S(1)}, u32[]{:S(2)}, u32[]{:S(2)}) collective-permute-start(bf16[1080,128]{1,0:T(8,128)(2,1)S(1)} %add_convert_fusion.18), channel_id=1, source_target_pairs={{0,8},{1,5},{8,16},{9,1},{16,24},{17,9},{24,26},{25,17},{26,18},{2... | collective-permute-start | bytes 829448 | tf_op jit(solution)/shard_map/ppermute | solution.py:52
  182.7 8.8 %collective-permute-start.14 = (bf16[1080,128]{1,0:T(8,128)(2,1)S(1)}, bf16[1080,128]{1,0:T(8,128)(2,1)S(1)}, u32[]{:S(2)}, u32[]{:S(2)}) collective-permute-start(bf16[1080,128]{1,0:T(8,128)(2,1)S(1)} %add_convert_fusion.32), channel_id=1, source_target_pairs={{0,8},{1,5},{8,16},{9,1},{16,24},{17,9},{24,26},{25,17},{26,18},{2... | collective-permute-start | bytes 829448 | tf_op jit(solution)/shard_map/ppermute | solution.py:52
  185.7 8.8 %collective-permute-start.45 = (bf16[1080,128]{1,0:T(8,128)(2,1)S(1)}, bf16[1080,128]{1,0:T(8,128)(2,1)S(1)}, u32[]{:S(2)}, u32[]{:S(2)}) collective-permute-start(bf16[1080,128]{1,0:T(8,128)(2,1)S(1)} %add_convert_fusion.3), channel_id=1, source_target_pairs={{0,8},{1,5},{8,16},{9,1},{16,24},{17,9},{24,26},{25,17},{26,18},{2... | collective-permute-start | bytes 829448 | tf_op jit(solution)/shard_map/ppermute | solution.py:52
  188.6 8.8 %collective-permute-start.30 = (bf16[1080,128]{1,0:T(8,128)(2,1)S(1)}, bf16[1080,128]{1,0:T(8,128)(2,1)S(1)}, u32[]{:S(2)}, u32[]{:S(2)}) collective-permute-start(bf16[1080,128]{1,0:T(8,128)(2,1)S(1)} %add_convert_fusion.17), channel_id=1, source_target_pairs={{0,8},{1,5},{8,16},{9,1},{16,24},{17,9},{24,26},{25,17},{26,18},{2... | collective-permute-start | bytes 829448 | tf_op jit(solution)/shard_map/ppermute | solution.py:52
  191.6 8.8 %collective-permute-start.15 = (bf16[1080,128]{1,0:T(8,128)(2,1)S(1)}, bf16[1080,128]{1,0:T(8,128)(2,1)S(1)}, u32[]{:S(2)}, u32[]{:S(2)}) collective-permute-start(bf16[1080,128]{1,0:T(8,128)(2,1)S(1)} %add_convert_fusion.31), channel_id=1, source_target_pairs={{0,8},{1,5},{8,16},{9,1},{16,24},{17,9},{24,26},{25,17},{26,18},{2... | collective-permute-start | bytes 829448 | tf_op jit(solution)/shard_map/ppermute | solution.py:52
  194.6 8.8 %collective-permute-start.46 = (bf16[1080,128]{1,0:T(8,128)(2,1)S(1)}, bf16[1080,128]{1,0:T(8,128)(2,1)S(1)}, u32[]{:S(2)}, u32[]{:S(2)}) collective-permute-start(bf16[1080,128]{1,0:T(8,128)(2,1)S(1)} %add_convert_fusion.2), channel_id=1, source_target_pairs={{0,8},{1,5},{8,16},{9,1},{16,24},{17,9},{24,26},{25,17},{26,18},{2... | collective-permute-start | bytes 829448 | tf_op jit(solution)/shard_map/ppermute | solution.py:52
  197.6 8.8 %collective-permute-start.31 = (bf16[1080,128]{1,0:T(8,128)(2,1)S(1)}, bf16[1080,128]{1,0:T(8,128)(2,1)S(1)}, u32[]{:S(2)}, u32[]{:S(2)}) collective-permute-start(bf16[1080,128]{1,0:T(8,128)(2,1)S(1)} %add_convert_fusion.16), channel_id=1, source_target_pairs={{0,8},{1,5},{8,16},{9,1},{16,24},{17,9},{24,26},{25,17},{26,18},{2... | collective-permute-start | bytes 829448 | tf_op jit(solution)/shard_map/ppermute | solution.py:52
  200.5 8.8 %collective-permute-start.16 = (bf16[1080,128]{1,0:T(8,128)(2,1)S(1)}, bf16[1080,128]{1,0:T(8,128)(2,1)S(1)}, u32[]{:S(2)}, u32[]{:S(2)}) collective-permute-start(bf16[1080,128]{1,0:T(8,128)(2,1)S(1)} %add_convert_fusion.30), channel_id=1, source_target_pairs={{0,8},{1,5},{8,16},{9,1},{16,24},{17,9},{24,26},{25,17},{26,18},{2... | collective-permute-start | bytes 829448 | tf_op jit(solution)/shard_map/ppermute | solution.py:52
  203.5 8.8 %collective-permute-start.47 = (bf16[1080,128]{1,0:T(8,128)(2,1)S(1)}, bf16[1080,128]{1,0:T(8,128)(2,1)S(1)}, u32[]{:S(2)}, u32[]{:S(2)}) collective-permute-start(bf16[1080,128]{1,0:T(8,128)(2,1)S(1)} %add_convert_fusion.1), channel_id=1, source_target_pairs={{0,8},{1,5},{8,16},{9,1},{16,24},{17,9},{24,26},{25,17},{26,18},{2... | collective-permute-start | bytes 829448 | tf_op jit(solution)/shard_map/ppermute | solution.py:52
  206.4 8.8 %collective-permute-start.32 = (bf16[1080,128]{1,0:T(8,128)(2,1)S(1)}, bf16[1080,128]{1,0:T(8,128)(2,1)S(1)}, u32[]{:S(2)}, u32[]{:S(2)}) collective-permute-start(bf16[1080,128]{1,0:T(8,128)(2,1)S(1)} %add_convert_fusion.15), channel_id=1, source_target_pairs={{0,8},{1,5},{8,16},{9,1},{16,24},{17,9},{24,26},{25,17},{26,18},{2... | collective-permute-start | bytes 829448 | tf_op jit(solution)/shard_map/ppermute | solution.py:52
  209.4 8.8 %collective-permute-start.17 = (bf16[1080,128]{1,0:T(8,128)(2,1)S(1)}, bf16[1080,128]{1,0:T(8,128)(2,1)S(1)}, u32[]{:S(2)}, u32[]{:S(2)}) collective-permute-start(bf16[1080,128]{1,0:T(8,128)(2,1)S(1)} %add_convert_fusion.29), channel_id=1, source_target_pairs={{0,8},{1,5},{8,16},{9,1},{16,24},{17,9},{24,26},{25,17},{26,18},{2... | collective-permute-start | bytes 829448 | tf_op jit(solution)/shard_map/ppermute | solution.py:52
  (5 other events, 109.1 us)

commit v6 on v4

--- a/solution.py
+++ b/solution.py
@@ -49,58 +49,67 @@
     return accs
 
 
-def _ffn_kernel(col_ref, cnt_ref, tok_ref, cot_ref, wg_ref, wu_ref, wd_ref,
-                gg_ref, gu_ref, gd_ref, dx_ref):
+def _ffn_kernel(col_ref, cnt_ref, tok_ref, cot_ref, tokt_ref, cott_ref, wg_ref, wu_ref, wdt_ref,
+                gg_ref, gu_ref, gd_ref, dxt_ref):
     h = pl.program_id(0)
     slots = wg_ref.shape[1]
     count = cnt_ref[h]
 
     @pl.when(h == 0)
     def _():
-        dx_ref[...] = jnp.zeros_like(dx_ref)
+        dxt_ref[...] = jnp.zeros_like(dxt_ref)
 
-    offs, xs, dys, wgs, wus, wds = [], [], [], [], [], []
+    f32 = jnp.float32
+    offs, xs, dys, wgs, wus = [], [], [], [], []
+    gate = up = d_hidden = None
     for p in range(slots):
         off = pl.multiple_of(col_ref[h, p] * BLK, BLK)
         live = p < count
+        x = tok_ref[:, pl.ds(off, BLK)]
+        dy = cot_ref[:, pl.ds(off, BLK)]
+        wg = jnp.where(live, wg_ref[0, p], jnp.zeros_like(wg_ref[0, p]))
+        wu = jnp.where(live, wu_ref[0, p], jnp.zeros_like(wu_ref[0, p]))
+        wdt = jnp.where(live, wdt_ref[0, p], jnp.zeros_like(wdt_ref[0, p]))
+        g = jnp.dot(x, wg, preferred_element_type=f32)
+        u = jnp.dot(x, wu, preferred_element_type=f32)
+        d = jnp.dot(dy, wdt, preferred_element_type=f32)
+        gate = g if gate is None else gate + g
+        up = u if up is None else up + u
+        d_hidden = d if d_hidden is None else d_hidden + d
         offs.append(off)
-        xs.append(tok_ref[:, pl.ds(off, BLK)])
-        dys.append(cot_ref[:, pl.ds(off, BLK)])
-        wgs.append(jnp.where(live, wg_ref[0, p], jnp.zeros_like(wg_ref[0, p])))
-        wus.append(jnp.where(live, wu_ref[0, p], jnp.zeros_like(wu_ref[0, p])))
-        wds.append(jnp.where(live, wd_ref[0, p], jnp.zeros_like(wd_ref[0, p])))
-    f32 = jnp.float32
-    nt = (((1,), (1,)), ((), ()))
-    tn = (((0,), (0,)), ((), ()))
-    gate = sum(jnp.dot(xs[p], wgs[p], preferred_element_type=f32) for p in range(slots))
-    up = sum(jnp.dot(xs[p], wus[p], preferred_element_type=f32) for p in range(slots))
-    d_hidden = sum(
-        lax.dot_general(dys[p], wds[p], nt, preferred_element_type=f32) for p in range(slots)
-    )
+        wgs.append(wg)
+        wus.append(wu)
     sig = 1.0 / (1.0 + jnp.exp(-gate))
     silu = gate * sig
     hidden = (silu * up).astype(jnp.bfloat16)
     d_gate = (d_hidden * up * sig * (1.0 + gate * (1.0 - sig))).astype(jnp.bfloat16)
     d_up = (d_hidden * silu).astype(jnp.bfloat16)
+    hidden_t = hidden.T
+    d_gate_t = d_gate.T
+    d_up_t = d_up.T
     for p in range(slots):
         live = p < count
         zero = jnp.zeros((BLK, BLK), f32)
-        gg = lax.dot_general(xs[p], d_gate, tn, preferred_element_type=f32)
-        gu = lax.dot_general(xs[p], d_up, tn, preferred_element_type=f32)
-        gd = lax.dot_general(hidden, dys[p], tn, preferred_element_type=f32)
+        xt = tokt_ref[pl.ds(offs[p], BLK), :]
+        dy = cot_ref[:, pl.ds(offs[p], BLK)]
+        gg = jnp.dot(xt, d_gate, preferred_element_type=f32)
+        gu = jnp.dot(xt, d_up, preferred_element_type=f32)
+        gd = jnp.dot(hidden_t, dy, preferred_element_type=f32)
         gg_ref[0, p] = jnp.where(live, gg, zero)
         gu_ref[0, p] = jnp.where(live, gu, zero)
         gd_ref[0, p] = jnp.where(live, gd, zero)
-        back = lax.dot_general(d_gate, wgs[p], nt, preferred_element_type=f32)
-        back = back + lax.dot_general(d_up, wus[p], nt, preferred_element_type=f32)
-        dx_ref[:, pl.ds(offs[p], BLK)] += back
+        back_t = jnp.dot(wgs[p], d_gate_t, preferred_element_type=f32)
+        back_t = back_t + jnp.dot(wus[p], d_up_t, preferred_element_type=f32)
+        dxt_ref[pl.ds(offs[p], BLK), :] += back_t
 
 
 def ffn_block_terms(col_index, row_count, full_tok, full_cot, gate_w, up_w, down_w):
     hblk, slots = col_index.shape
     rows, width = full_tok.shape
+    down_t = jnp.swapaxes(down_w, 2, 3)
     wspec = pl.BlockSpec((1, slots, BLK, BLK), lambda h, c, n: (h, 0, 0, 0))
     full = pl.BlockSpec((rows, width), lambda h, c, n: (0, 0))
+    full_t = pl.BlockSpec((width, rows), lambda h, c, n: (0, 0))
     grad = jax.ShapeDtypeStruct((hblk, slots, BLK, BLK), jnp.float32)
     flops = 2 * rows * hblk * slots * BLK * BLK * 9
     return pl.pallas_call(
@@ -108,18 +117,18 @@
         grid_spec=pltpu.PrefetchScalarGridSpec(
             num_scalar_prefetch=2,
             grid=(hblk,),
-            in_specs=[full, full, wspec, wspec, wspec],
-            out_specs=[wspec, wspec, wspec, full],
+            in_specs=[full, full, full_t, full_t, wspec, wspec, wspec],
+            out_specs=[wspec, wspec, wspec, full_t],
         ),
-        out_shape=[grad, grad, grad, jax.ShapeDtypeStruct((rows, width), jnp.float32)],
+        out_shape=[grad, grad, grad, jax.ShapeDtypeStruct((width, rows), jnp.float32)],
         compiler_params=pltpu.CompilerParams(dimension_semantics=("arbitrary",)),
         cost_estimate=pl.CostEstimate(
             flops=flops,
             transcendentals=rows * hblk * BLK,
-            bytes_accessed=3 * hblk * slots * BLK * BLK * 6 + rows * width * 8,
+            bytes_accessed=3 * hblk * slots * BLK * BLK * 6 + rows * width * 12,
         ),
         name="ffn_block_terms",
-    )(col_index, row_count, full_tok, full_cot, gate_w, up_w, down_w)
+    )(col_index, row_count, full_tok, full_cot, full_tok.T, full_cot.T, gate_w, up_w, down_t)
 
 
 def shards(n_dp, n_t, tokens, cotangent, w_gate, w_up, w_down, col_index, row_count, adam_m, adam_v):
@@ -152,13 +161,13 @@
     )[:, None]
     if n_t == 2:
         half = tokens.shape[1]
-        lo, hi = dx_part[:, :half], dx_part[:, half:]
+        lo, hi = dx_part[:half].T, dx_part[half:].T
         mine = jnp.where(first, lo, hi)
         theirs = lax.ppermute(jnp.where(first, hi, lo).astype(jnp.bfloat16), "tensor", swap)
         token_grads = (mine + theirs.astype(jnp.float32)).astype(jnp.bfloat16)
     else:
         token_grads = lax.psum_scatter(
-            dx_part.astype(jnp.bfloat16), "tensor", scatter_dimension=1, tiled=True
+            dx_part.T.astype(jnp.bfloat16), "tensor", scatter_dimension=1, tiled=True
         )
     grad_scale = 1.0 / math.sqrt(n_dp * tok_rows)
     grad_all = reduced * grad_scale

time: 215 us -> 227 us (1.056)
  other arithmetic: 25.4 us -> 49.5 us
  waiting for transfers between devices: 42.7 us -> 18.8 us
  local copies, waits for them, and re-layouts: 8.38 us -> 22.1 us
  starting transfers between devices: 78.1 us -> 75.7 us
    convert_element_type x42, other arithmetic: 13.2 us -> 38.7 us  [ring_reduce_scatter(): moved = lax.ppermute(accs[i].astype(wire_dtype), ('dp', 'tensor'), perm)]
    ppermute x45, waiting for transfers between devices: 42.7 us -> 18.8 us  [ring_reduce_scatter(): moved = lax.ppermute(accs[i].astype(wire_dtype), ('dp', 'tensor'), perm)]
    unnamed x11 -> x17, local copies, waits for them, and re-layouts: 1.4 us -> 12.5 us
    convert_element_type x1, other arithmetic: 3.38 us -> 0.17 us  [shards(): token_grads = (mine + theirs.astype(jnp.float32)).astype(jnp.bfloat16)]
    concatenate x0 -> x2, local copies, waits for them, and re-layouts: none -> 2.88 us  [the longest x1 1.44 us: shards(): jnp.concatenate([jnp.where(first, cotangent, other_cot), jnp.where(first,...]
    transpose x0 -> x2, other arithmetic: none -> 2.45 us  [ffn_block_terms(): return pl.pallas_call(_ffn_kernel, grid_spec=pltpu.PrefetchScalarGridSpec...]
    ppermute x45, starting transfers between devices: 76.9 us -> 74.6 us  [ring_reduce_scatter(): moved = lax.ppermute(accs[i].astype(wire_dtype), ('dp', 'tensor'), perm)]
    concatenate x2 -> x0, other arithmetic: 2.38 us -> none  [the longest x1 1.19 us: shards(): jnp.concatenate([jnp.where(first, tokens, other_tok), jnp.where(first, ot...]
  transfers between devices with their start and end apart: 48 -> 48, of which waited for: 36 -> 35; matrix products, arithmetic and copies ran while one was open for 12% -> 26% of each run, Pallas kernels for 0% -> 0%
where the time goes in v6:
time: 227 us; the launch traced here: 223 us
  starting transfers between devices  75.7 us (33%)
  other arithmetic  49.5 us (22%)
  Pallas kernels  35.4 us (16%)
  local copies, waits for them, and re-layouts  22.1 us (10%)
  between operations  21.9 us (10%)
  waiting for transfers between devices  18.8 us (8%)
    ppermute x45, starting transfers between devices, ring_reduce_scatter(): moved = lax.ppermute(accs[i].astype(wire_dtype), ('dp', 'tensor'), perm)  74.6 us
    convert_element_type x42, other arithmetic, ring_reduce_scatter(): moved = lax.ppermute(accs[i].astype(wire_dtype), ('dp', 'tensor'), perm)  38.7 us
    pallas_call x1, Pallas kernels, ffn_block_terms(): pl.pallas_call(_ffn_kernel, grid_spec=pltpu.PrefetchScalarGridSpec(num_sc...  35.4 us
    ppermute x45, waiting for transfers between devices, ring_reduce_scatter(): moved = lax.ppermute(accs[i].astype(wire_dtype), ('dp', 'tensor'), perm)  18.8 us
    unnamed x17, local copies, waits for them, and re-layouts  12.5 us
  transfers between devices with their start and end apart: 48, of which 35 were waited for; matrix products, arithmetic and copies ran while one was open for 26% of the time, Pallas kernels for 0%

profile of v6, /device:TPU:0, one launch (start us, length us, event | category | flops | bytes accessed | tf_op | source)
XLA Modules:
  0.0 223.3 jit_solution(14598064701265800443)
XLA Ops:
  16.0 2.0 fusion.4
  29.7 7.2 %copy.21 = bf16[1,27,5,128,128]{3,4,2,1,0:T(8,128)(2,1)} copy(bf16[1,27,5,128,128]{4,3,2,1,0:T(8,128)(2,1)} %param.15) | data formatting | bytes 8847360 | tf_op args[4]
  43.4 35.4 %ffn_block_terms.1 = (f32[27,5,128,128]{3,2,1,0:T(8,128)}, f32[27,5,128,128]{3,2,1,0:T(8,128)}, f32[27,5,128,128]{3,2,1,0:T(8,128)}, f32[5120,128]{1,0:T(8,128)}) custom-call(s32[27,5]{1,0:T(8,128)} %copy.22.col_ref, s32[27]{0:T(128)} %cnt_ref.1, bf16[128,5120]{1,0:T(8,128)(2,1)} %copy.23.tok_ref, bf16[128,5120]{1,0:T(8,128)(2,1)} %copy.24.cot_ref, ...), custom_call_target="tpu_custom_call" | custom-call | flops 5096079360 | bytes 47677440 | tf_op jit(solution)/shard_map/ffn_block_terms/pallas_call | solution.py:115
  78.8 1.8 fusion.1
  82.5 2.6 %collective-permute-start.33 = (bf16[1080,128]{1,0:T(8,128)(2,1)S(1)}, bf16[1080,128]{1,0:T(8,128)(2,1)S(1)}, u32[]{:S(2)}, u32[]{:S(2)}) collective-permute-start(bf16[1080,128]{1,0:T(8,128)(2,1)S(1)} %dynamic-slice_convert_fusion), channel_id=1, source_target_pairs={{0,8},{1,5},{8,16},{9,1},{16,24},{17,9},{24,26},{25,17},{26,18},{2... | collective-permute-start | bytes 829448 | tf_op jit(solution)/shard_map/ppermute | solution.py:47
  86.2 1.6 collective-permute-start.18
  88.9 1.6 collective-permute-start.3
  96.9 1.8 collective-permute-start.4
  99.8 1.8 collective-permute-start.35
  102.8 1.8 collective-permute-start.20
  105.8 1.8 collective-permute-start.5
  110.2 1.6 collective-permute-start.36
  112.9 1.6 collective-permute-start.21
  120.8 1.6 collective-permute-start.22
  123.8 1.6 collective-permute-start.7
  126.8 1.6 collective-permute-start.38
  129.7 1.6 collective-permute-start.23
  132.7 1.6 collective-permute-start.8
  135.7 1.6 collective-permute-start.39
  138.6 1.6 collective-permute-start.24
  141.6 1.6 collective-permute-start.9
  144.5 1.6 collective-permute-start.40
  147.5 1.6 collective-permute-start.25
  149.4 1.6 collective-permute-start.10
  153.4 1.6 collective-permute-start.41
  156.4 1.6 collective-permute-start.26
  158.3 1.6 collective-permute-start.11
  162.3 1.6 collective-permute-start.42
  165.3 1.6 collective-permute-start.27
  167.2 1.6 collective-permute-start.12
  171.2 1.6 collective-permute-start.43
  174.2 1.6 collective-permute-start.28
  176.1 1.6 collective-permute-start.13
  180.1 1.6 collective-permute-start.44
  183.1 1.6 collective-permute-start.29
  185.0 1.6 collective-permute-start.14
  189.0 1.6 collective-permute-start.45
  192.0 1.6 collective-permute-start.30
  193.9 1.6 collective-permute-start.15
  197.9 1.6 collective-permute-start.46
  200.9 1.6 collective-permute-start.31
  202.7 1.6 collective-permute-start.16
  206.8 1.6 collective-permute-start.47
  209.7 1.6 collective-permute-start.32
  211.6 1.6 collective-permute-start.17
  215.6 1.9 collective-permute-done.32
  218.6 1.9 collective-permute-done.17
  220.5 2.8 %add_divide_fusion = (f32[3,1,1080,128]{3,2,1,0:T(8,128)}, f32[3,1,1080,128]{3,2,1,0:T(8,128)}, f32[3,1,1080,128]{3,2,1,0:T(8,128)}) fusion(f32[1,1,1080,128]{3,2,1,0:T(8,128)S(1)} %add_bitcast_fusion, f32[1,1,1080,128]{3,2,1,0:T(8,128)S(1)} %add_bitcast_fusion.1, f32[1,1,1080,128]{3,2,1,0:T(8,128)S(1)} %add_bitcast_fusion.2, ...), kind=kLoop, calls=%fused_computation.1 | loop fusion | flops 4976640 | bytes 9953280 | tf_op jit(solution)/shard_map/div | solution.py:176
  (125 shorter events, 79.7 us)
Async XLA Ops:
  2.0 34.8 %collective-permute-start.1 = (bf16[128,2560]{0,1:T(8,128)(2,1)S(1)}, bf16[128,2560]{0,1:T(8,128)(2,1)S(1)}, u32[]{:S(2)}, u32[]{:S(2)}) collective-permute-start(bf16[128,2560]{0,1:T(8,128)(2,1)S(1)} %copy.19), channel_id=1, source_target_pairs={{0,1},{1,0},{2,3},{3,2},{4,5},{5,4},{6,7},{7,6},{8,9},{9,8},{10,11... | collective-permute-start | bytes 1966088 | tf_op jit(solution)/shard_map/ppermute | solution.py:138
  4.0 32.9 %collective-permute-start = (bf16[128,2560]{0,1:T(8,128)(2,1)S(1)}, bf16[128,2560]{0,1:T(8,128)(2,1)}, u32[]{:S(2)}, u32[]{:S(2)}) collective-permute-start(bf16[128,2560]{0,1:T(8,128)(2,1)S(1)} %copy.16), channel_id=1, source_target_pairs={{0,1},{1,0},{2,3},{3,2},{4,5},{5,4},{6,7},{7,6},{8,9},{9,8},{10,11... | collective-permute-start | bytes 1966088 | tf_op jit(solution)/shard_map/ppermute | solution.py:138
  80.7 27.0 %collective-permute-start.2 = (bf16[128,2560]{0,1:T(8,128)(2,1)S(1)}, bf16[128,2560]{0,1:T(8,128)(2,1)S(1)}, u32[]{:S(2)}, u32[]{:S(2)}) collective-permute-start(bf16[128,2560]{0,1:T(8,128)(2,1)S(1)} %fusion.1), channel_id=1, source_target_pairs={{0,1},{1,0},{2,3},{3,2},{4,5},{5,4},{6,7},{7,6},{8,9},{9,8},{10,11... | collective-permute-start | bytes 1966088 | tf_op jit(solution)/shard_map/ppermute | solution.py:166
  82.5 8.0 %collective-permute-start.33 = (bf16[1080,128]{1,0:T(8,128)(2,1)S(1)}, bf16[1080,128]{1,0:T(8,128)(2,1)S(1)}, u32[]{:S(2)}, u32[]{:S(2)}) collective-permute-start(bf16[1080,128]{1,0:T(8,128)(2,1)S(1)} %dynamic-slice_convert_fusion), channel_id=1, source_target_pairs={{0,8},{1,5},{8,16},{9,1},{16,24},{17,9},{24,26},{25,17},{26,18},{2... | collective-permute-start | bytes 829448 | tf_op jit(solution)/shard_map/ppermute | solution.py:47
  86.2 7.0 %collective-permute-start.18 = (bf16[1080,128]{1,0:T(8,128)(2,1)S(1)}, bf16[1080,128]{1,0:T(8,128)(2,1)S(1)}, u32[]{:S(2)}, u32[]{:S(2)}) collective-permute-start(bf16[1080,128]{1,0:T(8,128)(2,1)S(1)} %dynamic-slice_convert_fusion.1), channel_id=1, source_target_pairs={{0,8},{1,5},{8,16},{9,1},{16,24},{17,9},{24,26},{25,17},{26,18},{2... | collective-permute-start | bytes 829448 | tf_op jit(solution)/shard_map/ppermute | solution.py:47
  88.9 6.9 %collective-permute-start.3 = (bf16[1080,128]{1,0:T(8,128)(2,1)S(1)}, bf16[1080,128]{1,0:T(8,128)(2,1)S(1)}, u32[]{:S(2)}, u32[]{:S(2)}) collective-permute-start(bf16[1080,128]{1,0:T(8,128)(2,1)S(1)} %dynamic-slice_convert_fusion.2), channel_id=1, source_target_pairs={{0,8},{1,5},{8,16},{9,1},{16,24},{17,9},{24,26},{25,17},{26,18},{2... | collective-permute-start | bytes 829448 | tf_op jit(solution)/shard_map/ppermute | solution.py:47
  91.7 7.1 %collective-permute-start.34 = (bf16[1080,128]{1,0:T(8,128)(2,1)S(1)}, bf16[1080,128]{1,0:T(8,128)(2,1)S(1)}, u32[]{:S(2)}, u32[]{:S(2)}) collective-permute-start(bf16[1080,128]{1,0:T(8,128)(2,1)S(1)} %add_convert_fusion.13), channel_id=1, source_target_pairs={{0,8},{1,5},{8,16},{9,1},{16,24},{17,9},{24,26},{25,17},{26,18},{2... | collective-permute-start | bytes 829448 | tf_op jit(solution)/shard_map/ppermute | solution.py:47
  94.3 7.4 %collective-permute-start.19 = (bf16[1080,128]{1,0:T(8,128)(2,1)S(1)}, bf16[1080,128]{1,0:T(8,128)(2,1)S(1)}, u32[]{:S(2)}, u32[]{:S(2)}) collective-permute-start(bf16[1080,128]{1,0:T(8,128)(2,1)S(1)} %add_convert_fusion.27), channel_id=1, source_target_pairs={{0,8},{1,5},{8,16},{9,1},{16,24},{17,9},{24,26},{25,17},{26,18},{2... | collective-permute-start | bytes 829448 | tf_op jit(solution)/shard_map/ppermute | solution.py:47
  96.9 7.8 %collective-permute-start.4 = (bf16[1080,128]{1,0:T(8,128)(2,1)S(1)}, bf16[1080,128]{1,0:T(8,128)(2,1)S(1)}, u32[]{:S(2)}, u32[]{:S(2)}) collective-permute-start(bf16[1080,128]{1,0:T(8,128)(2,1)S(1)} %add_convert_fusion.41), channel_id=1, source_target_pairs={{0,8},{1,5},{8,16},{9,1},{16,24},{17,9},{24,26},{25,17},{26,18},{2... | collective-permute-start | bytes 829448 | tf_op jit(solution)/shard_map/ppermute | solution.py:47
  99.8 9.1 %collective-permute-start.35 = (bf16[1080,128]{1,0:T(8,128)(2,1)S(1)}, bf16[1080,128]{1,0:T(8,128)(2,1)S(1)}, u32[]{:S(2)}, u32[]{:S(2)}) collective-permute-start(bf16[1080,128]{1,0:T(8,128)(2,1)S(1)} %add_convert_fusion.12), channel_id=1, source_target_pairs={{0,8},{1,5},{8,16},{9,1},{16,24},{17,9},{24,26},{25,17},{26,18},{2... | collective-permute-start | bytes 829448 | tf_op jit(solution)/shard_map/ppermute | solution.py:47
  102.8 9.0 %collective-permute-start.20 = (bf16[1080,128]{1,0:T(8,128)(2,1)S(1)}, bf16[1080,128]{1,0:T(8,128)(2,1)S(1)}, u32[]{:S(2)}, u32[]{:S(2)}) collective-permute-start(bf16[1080,128]{1,0:T(8,128)(2,1)S(1)} %add_convert_fusion.26), channel_id=1, source_target_pairs={{0,8},{1,5},{8,16},{9,1},{16,24},{17,9},{24,26},{25,17},{26,18},{2... | collective-permute-start | bytes 829448 | tf_op jit(solution)/shard_map/ppermute | solution.py:47
  105.8 8.8 %collective-permute-start.5 = (bf16[1080,128]{1,0:T(8,128)(2,1)S(1)}, bf16[1080,128]{1,0:T(8,128)(2,1)S(1)}, u32[]{:S(2)}, u32[]{:S(2)}) collective-permute-start(bf16[1080,128]{1,0:T(8,128)(2,1)S(1)} %add_convert_fusion.40), channel_id=1, source_target_pairs={{0,8},{1,5},{8,16},{9,1},{16,24},{17,9},{24,26},{25,17},{26,18},{2... | collective-permute-start | bytes 829448 | tf_op jit(solution)/shard_map/ppermute | solution.py:47
  110.2 7.0 %collective-permute-start.36 = (bf16[1080,128]{1,0:T(8,128)(2,1)S(1)}, bf16[1080,128]{1,0:T(8,128)(2,1)S(1)}, u32[]{:S(2)}, u32[]{:S(2)}) collective-permute-start(bf16[1080,128]{1,0:T(8,128)(2,1)S(1)} %add_convert_fusion.11), channel_id=1, source_target_pairs={{0,8},{1,5},{8,16},{9,1},{16,24},{17,9},{24,26},{25,17},{26,18},{2... | collective-permute-start | bytes 829448 | tf_op jit(solution)/shard_map/ppermute | solution.py:47
  112.9 6.8 %collective-permute-start.21 = (bf16[1080,128]{1,0:T(8,128)(2,1)S(1)}, bf16[1080,128]{1,0:T(8,128)(2,1)S(1)}, u32[]{:S(2)}, u32[]{:S(2)}) collective-permute-start(bf16[1080,128]{1,0:T(8,128)(2,1)S(1)} %add_convert_fusion.25), channel_id=1, source_target_pairs={{0,8},{1,5},{8,16},{9,1},{16,24},{17,9},{24,26},{25,17},{26,18},{2... | collective-permute-start | bytes 829448 | tf_op jit(solution)/shard_map/ppermute | solution.py:47
  115.7 7.0 %collective-permute-start.6 = (bf16[1080,128]{1,0:T(8,128)(2,1)S(1)}, bf16[1080,128]{1,0:T(8,128)(2,1)S(1)}, u32[]{:S(2)}, u32[]{:S(2)}) collective-permute-start(bf16[1080,128]{1,0:T(8,128)(2,1)S(1)} %add_convert_fusion.39), channel_id=1, source_target_pairs={{0,8},{1,5},{8,16},{9,1},{16,24},{17,9},{24,26},{25,17},{26,18},{2... | collective-permute-start | bytes 829448 | tf_op jit(solution)/shard_map/ppermute | solution.py:47
  118.3 7.3 %collective-permute-start.37 = (bf16[1080,128]{1,0:T(8,128)(2,1)S(1)}, bf16[1080,128]{1,0:T(8,128)(2,1)S(1)}, u32[]{:S(2)}, u32[]{:S(2)}) collective-permute-start(bf16[1080,128]{1,0:T(8,128)(2,1)S(1)} %add_convert_fusion.10), channel_id=1, source_target_pairs={{0,8},{1,5},{8,16},{9,1},{16,24},{17,9},{24,26},{25,17},{26,18},{2... | collective-permute-start | bytes 829448 | tf_op jit(solution)/shard_map/ppermute | solution.py:47
  120.8 7.8 %collective-permute-start.22 = (bf16[1080,128]{1,0:T(8,128)(2,1)S(1)}, bf16[1080,128]{1,0:T(8,128)(2,1)S(1)}, u32[]{:S(2)}, u32[]{:S(2)}) collective-permute-start(bf16[1080,128]{1,0:T(8,128)(2,1)S(1)} %add_convert_fusion.24), channel_id=1, source_target_pairs={{0,8},{1,5},{8,16},{9,1},{16,24},{17,9},{24,26},{25,17},{26,18},{2... | collective-permute-start | bytes 829448 | tf_op jit(solution)/shard_map/ppermute | solution.py:47
  123.8 7.8 %collective-permute-start.7 = (bf16[1080,128]{1,0:T(8,128)(2,1)S(1)}, bf16[1080,128]{1,0:T(8,128)(2,1)S(1)}, u32[]{:S(2)}, u32[]{:S(2)}) collective-permute-start(bf16[1080,128]{1,0:T(8,128)(2,1)S(1)} %add_convert_fusion.38), channel_id=1, source_target_pairs={{0,8},{1,5},{8,16},{9,1},{16,24},{17,9},{24,26},{25,17},{26,18},{2... | collective-permute-start | bytes 829448 | tf_op jit(solution)/shard_map/ppermute | solution.py:47
  126.8 7.8 %collective-permute-start.38 = (bf16[1080,128]{1,0:T(8,128)(2,1)S(1)}, bf16[1080,128]{1,0:T(8,128)(2,1)S(1)}, u32[]{:S(2)}, u32[]{:S(2)}) collective-permute-start(bf16[1080,128]{1,0:T(8,128)(2,1)S(1)} %add_convert_fusion.9), channel_id=1, source_target_pairs={{0,8},{1,5},{8,16},{9,1},{16,24},{17,9},{24,26},{25,17},{26,18},{2... | collective-permute-start | bytes 829448 | tf_op jit(solution)/shard_map/ppermute | solution.py:47
  129.7 7.8 %collective-permute-start.23 = (bf16[1080,128]{1,0:T(8,128)(2,1)S(1)}, bf16[1080,128]{1,0:T(8,128)(2,1)S(1)}, u32[]{:S(2)}, u32[]{:S(2)}) collective-permute-start(bf16[1080,128]{1,0:T(8,128)(2,1)S(1)} %add_convert_fusion.23), channel_id=1, source_target_pairs={{0,8},{1,5},{8,16},{9,1},{16,24},{17,9},{24,26},{25,17},{26,18},{2... | collective-permute-start | bytes 829448 | tf_op jit(solution)/shard_map/ppermute | solution.py:47
  132.7 7.8 %collective-permute-start.8 = (bf16[1080,128]{1,0:T(8,128)(2,1)S(1)}, bf16[1080,128]{1,0:T(8,128)(2,1)S(1)}, u32[]{:S(2)}, u32[]{:S(2)}) collective-permute-start(bf16[1080,128]{1,0:T(8,128)(2,1)S(1)} %add_convert_fusion.37), channel_id=1, source_target_pairs={{0,8},{1,5},{8,16},{9,1},{16,24},{17,9},{24,26},{25,17},{26,18},{2... | collective-permute-start | bytes 829448 | tf_op jit(solution)/shard_map/ppermute | solution.py:47
  135.7 7.8 %collective-permute-start.39 = (bf16[1080,128]{1,0:T(8,128)(2,1)S(1)}, bf16[1080,128]{1,0:T(8,128)(2,1)S(1)}, u32[]{:S(2)}, u32[]{:S(2)}) collective-permute-start(bf16[1080,128]{1,0:T(8,128)(2,1)S(1)} %add_convert_fusion.8), channel_id=1, source_target_pairs={{0,8},{1,5},{8,16},{9,1},{16,24},{17,9},{24,26},{25,17},{26,18},{2... | collective-permute-start | bytes 829448 | tf_op jit(solution)/shard_map/ppermute | solution.py:47
  138.6 7.8 %collective-permute-start.24 = (bf16[1080,128]{1,0:T(8,128)(2,1)S(1)}, bf16[1080,128]{1,0:T(8,128)(2,1)S(1)}, u32[]{:S(2)}, u32[]{:S(2)}) collective-permute-start(bf16[1080,128]{1,0:T(8,128)(2,1)S(1)} %add_convert_fusion.22), channel_id=1, source_target_pairs={{0,8},{1,5},{8,16},{9,1},{16,24},{17,9},{24,26},{25,17},{26,18},{2... | collective-permute-start | bytes 829448 | tf_op jit(solution)/shard_map/ppermute | solution.py:47
  141.6 7.8 %collective-permute-start.9 = (bf16[1080,128]{1,0:T(8,128)(2,1)S(1)}, bf16[1080,128]{1,0:T(8,128)(2,1)S(1)}, u32[]{:S(2)}, u32[]{:S(2)}) collective-permute-start(bf16[1080,128]{1,0:T(8,128)(2,1)S(1)} %add_convert_fusion.36), channel_id=1, source_target_pairs={{0,8},{1,5},{8,16},{9,1},{16,24},{17,9},{24,26},{25,17},{26,18},{2... | collective-permute-start | bytes 829448 | tf_op jit(solution)/shard_map/ppermute | solution.py:47
  144.5 7.8 %collective-permute-start.40 = (bf16[1080,128]{1,0:T(8,128)(2,1)S(1)}, bf16[1080,128]{1,0:T(8,128)(2,1)S(1)}, u32[]{:S(2)}, u32[]{:S(2)}) collective-permute-start(bf16[1080,128]{1,0:T(8,128)(2,1)S(1)} %add_convert_fusion.7), channel_id=1, source_target_pairs={{0,8},{1,5},{8,16},{9,1},{16,24},{17,9},{24,26},{25,17},{26,18},{2... | collective-permute-start | bytes 829448 | tf_op jit(solution)/shard_map/ppermute | solution.py:47
  147.5 7.8 %collective-permute-start.25 = (bf16[1080,128]{1,0:T(8,128)(2,1)S(1)}, bf16[1080,128]{1,0:T(8,128)(2,1)S(1)}, u32[]{:S(2)}, u32[]{:S(2)}) collective-permute-start(bf16[1080,128]{1,0:T(8,128)(2,1)S(1)} %add_convert_fusion.21), channel_id=1, source_target_pairs={{0,8},{1,5},{8,16},{9,1},{16,24},{17,9},{24,26},{25,17},{26,18},{2... | collective-permute-start | bytes 829448 | tf_op jit(solution)/shard_map/ppermute | solution.py:47
  149.4 8.8 %collective-permute-start.10 = (bf16[1080,128]{1,0:T(8,128)(2,1)S(1)}, bf16[1080,128]{1,0:T(8,128)(2,1)S(1)}, u32[]{:S(2)}, u32[]{:S(2)}) collective-permute-start(bf16[1080,128]{1,0:T(8,128)(2,1)S(1)} %add_convert_fusion.35), channel_id=1, source_target_pairs={{0,8},{1,5},{8,16},{9,1},{16,24},{17,9},{24,26},{25,17},{26,18},{2... | collective-permute-start | bytes 829448 | tf_op jit(solution)/shard_map/ppermute | solution.py:47
  153.4 7.8 %collective-permute-start.41 = (bf16[1080,128]{1,0:T(8,128)(2,1)S(1)}, bf16[1080,128]{1,0:T(8,128)(2,1)S(1)}, u32[]{:S(2)}, u32[]{:S(2)}) collective-permute-start(bf16[1080,128]{1,0:T(8,128)(2,1)S(1)} %add_convert_fusion.6), channel_id=1, source_target_pairs={{0,8},{1,5},{8,16},{9,1},{16,24},{17,9},{24,26},{25,17},{26,18},{2... | collective-permute-start | bytes 829448 | tf_op jit(solution)/shard_map/ppermute | solution.py:47
  156.4 7.8 %collective-permute-start.26 = (bf16[1080,128]{1,0:T(8,128)(2,1)S(1)}, bf16[1080,128]{1,0:T(8,128)(2,1)S(1)}, u32[]{:S(2)}, u32[]{:S(2)}) collective-permute-start(bf16[1080,128]{1,0:T(8,128)(2,1)S(1)} %add_convert_fusion.20), channel_id=1, source_target_pairs={{0,8},{1,5},{8,16},{9,1},{16,24},{17,9},{24,26},{25,17},{26,18},{2... | collective-permute-start | bytes 829448 | tf_op jit(solution)/shard_map/ppermute | solution.py:47
  158.3 8.8 %collective-permute-start.11 = (bf16[1080,128]{1,0:T(8,128)(2,1)S(1)}, bf16[1080,128]{1,0:T(8,128)(2,1)S(1)}, u32[]{:S(2)}, u32[]{:S(2)}) collective-permute-start(bf16[1080,128]{1,0:T(8,128)(2,1)S(1)} %add_convert_fusion.34), channel_id=1, source_target_pairs={{0,8},{1,5},{8,16},{9,1},{16,24},{17,9},{24,26},{25,17},{26,18},{2... | collective-permute-start | bytes 829448 | tf_op jit(solution)/shard_map/ppermute | solution.py:47
  162.3 7.8 %collective-permute-start.42 = (bf16[1080,128]{1,0:T(8,128)(2,1)S(1)}, bf16[1080,128]{1,0:T(8,128)(2,1)S(1)}, u32[]{:S(2)}, u32[]{:S(2)}) collective-permute-start(bf16[1080,128]{1,0:T(8,128)(2,1)S(1)} %add_convert_fusion.5), channel_id=1, source_target_pairs={{0,8},{1,5},{8,16},{9,1},{16,24},{17,9},{24,26},{25,17},{26,18},{2... | collective-permute-start | bytes 829448 | tf_op jit(solution)/shard_map/ppermute | solution.py:47
  165.3 7.8 %collective-permute-start.27 = (bf16[1080,128]{1,0:T(8,128)(2,1)S(1)}, bf16[1080,128]{1,0:T(8,128)(2,1)S(1)}, u32[]{:S(2)}, u32[]{:S(2)}) collective-permute-start(bf16[1080,128]{1,0:T(8,128)(2,1)S(1)} %add_convert_fusion.19), channel_id=1, source_target_pairs={{0,8},{1,5},{8,16},{9,1},{16,24},{17,9},{24,26},{25,17},{26,18},{2... | collective-permute-start | bytes 829448 | tf_op jit(solution)/shard_map/ppermute | solution.py:47
  167.2 8.8 %collective-permute-start.12 = (bf16[1080,128]{1,0:T(8,128)(2,1)S(1)}, bf16[1080,128]{1,0:T(8,128)(2,1)S(1)}, u32[]{:S(2)}, u32[]{:S(2)}) collective-permute-start(bf16[1080,128]{1,0:T(8,128)(2,1)S(1)} %add_convert_fusion.33), channel_id=1, source_target_pairs={{0,8},{1,5},{8,16},{9,1},{16,24},{17,9},{24,26},{25,17},{26,18},{2... | collective-permute-start | bytes 829448 | tf_op jit(solution)/shard_map/ppermute | solution.py:47
  171.2 7.8 %collective-permute-start.43 = (bf16[1080,128]{1,0:T(8,128)(2,1)S(1)}, bf16[1080,128]{1,0:T(8,128)(2,1)S(1)}, u32[]{:S(2)}, u32[]{:S(2)}) collective-permute-start(bf16[1080,128]{1,0:T(8,128)(2,1)S(1)} %add_convert_fusion.4), channel_id=1, source_target_pairs={{0,8},{1,5},{8,16},{9,1},{16,24},{17,9},{24,26},{25,17},{26,18},{2... | collective-permute-start | bytes 829448 | tf_op jit(solution)/shard_map/ppermute | solution.py:47
  174.2 7.8 %collective-permute-start.28 = (bf16[1080,128]{1,0:T(8,128)(2,1)S(1)}, bf16[1080,128]{1,0:T(8,128)(2,1)S(1)}, u32[]{:S(2)}, u32[]{:S(2)}) collective-permute-start(bf16[1080,128]{1,0:T(8,128)(2,1)S(1)} %add_convert_fusion.18), channel_id=1, source_target_pairs={{0,8},{1,5},{8,16},{9,1},{16,24},{17,9},{24,26},{25,17},{26,18},{2... | collective-permute-start | bytes 829448 | tf_op jit(solution)/shard_map/ppermute | solution.py:47
  176.1 8.8 %collective-permute-start.13 = (bf16[1080,128]{1,0:T(8,128)(2,1)S(1)}, bf16[1080,128]{1,0:T(8,128)(2,1)S(1)}, u32[]{:S(2)}, u32[]{:S(2)}) collective-permute-start(bf16[1080,128]{1,0:T(8,128)(2,1)S(1)} %add_convert_fusion.32), channel_id=1, source_target_pairs={{0,8},{1,5},{8,16},{9,1},{16,24},{17,9},{24,26},{25,17},{26,18},{2... | collective-permute-start | bytes 829448 | tf_op jit(solution)/shard_map/ppermute | solution.py:47
  180.1 7.8 %collective-permute-start.44 = (bf16[1080,128]{1,0:T(8,128)(2,1)S(1)}, bf16[1080,128]{1,0:T(8,128)(2,1)S(1)}, u32[]{:S(2)}, u32[]{:S(2)}) collective-permute-start(bf16[1080,128]{1,0:T(8,128)(2,1)S(1)} %add_convert_fusion.3), channel_id=1, source_target_pairs={{0,8},{1,5},{8,16},{9,1},{16,24},{17,9},{24,26},{25,17},{26,18},{2... | collective-permute-start | bytes 829448 | tf_op jit(solution)/shard_map/ppermute | solution.py:47
  183.1 7.8 %collective-permute-start.29 = (bf16[1080,128]{1,0:T(8,128)(2,1)S(1)}, bf16[1080,128]{1,0:T(8,128)(2,1)S(1)}, u32[]{:S(2)}, u32[]{:S(2)}) collective-permute-start(bf16[1080,128]{1,0:T(8,128)(2,1)S(1)} %add_convert_fusion.17), channel_id=1, source_target_pairs={{0,8},{1,5},{8,16},{9,1},{16,24},{17,9},{24,26},{25,17},{26,18},{2... | collective-permute-start | bytes 829448 | tf_op jit(solution)/shard_map/ppermute | solution.py:47
  185.0 8.8 %collective-permute-start.14 = (bf16[1080,128]{1,0:T(8,128)(2,1)S(1)}, bf16[1080,128]{1,0:T(8,128)(2,1)S(1)}, u32[]{:S(2)}, u32[]{:S(2)}) collective-permute-start(bf16[1080,128]{1,0:T(8,128)(2,1)S(1)} %add_convert_fusion.31), channel_id=1, source_target_pairs={{0,8},{1,5},{8,16},{9,1},{16,24},{17,9},{24,26},{25,17},{26,18},{2... | collective-permute-start | bytes 829448 | tf_op jit(solution)/shard_map/ppermute | solution.py:47
  189.0 7.8 %collective-permute-start.45 = (bf16[1080,128]{1,0:T(8,128)(2,1)S(1)}, bf16[1080,128]{1,0:T(8,128)(2,1)S(1)}, u32[]{:S(2)}, u32[]{:S(2)}) collective-permute-start(bf16[1080,128]{1,0:T(8,128)(2,1)S(1)} %add_convert_fusion.2), channel_id=1, source_target_pairs={{0,8},{1,5},{8,16},{9,1},{16,24},{17,9},{24,26},{25,17},{26,18},{2... | collective-permute-start | bytes 829448 | tf_op jit(solution)/shard_map/ppermute | solution.py:47
  192.0 7.8 %collective-permute-start.30 = (bf16[1080,128]{1,0:T(8,128)(2,1)S(1)}, bf16[1080,128]{1,0:T(8,128)(2,1)S(1)}, u32[]{:S(2)}, u32[]{:S(2)}) collective-permute-start(bf16[1080,128]{1,0:T(8,128)(2,1)S(1)} %add_convert_fusion.16), channel_id=1, source_target_pairs={{0,8},{1,5},{8,16},{9,1},{16,24},{17,9},{24,26},{25,17},{26,18},{2... | collective-permute-start | bytes 829448 | tf_op jit(solution)/shard_map/ppermute | solution.py:47
  193.9 8.8 %collective-permute-start.15 = (bf16[1080,128]{1,0:T(8,128)(2,1)S(1)}, bf16[1080,128]{1,0:T(8,128)(2,1)S(1)}, u32[]{:S(2)}, u32[]{:S(2)}) collective-permute-start(bf16[1080,128]{1,0:T(8,128)(2,1)S(1)} %add_convert_fusion.30), channel_id=1, source_target_pairs={{0,8},{1,5},{8,16},{9,1},{16,24},{17,9},{24,26},{25,17},{26,18},{2... | collective-permute-start | bytes 829448 | tf_op jit(solution)/shard_map/ppermute | solution.py:47
  197.9 7.8 %collective-permute-start.46 = (bf16[1080,128]{1,0:T(8,128)(2,1)S(1)}, bf16[1080,128]{1,0:T(8,128)(2,1)S(1)}, u32[]{:S(2)}, u32[]{:S(2)}) collective-permute-start(bf16[1080,128]{1,0:T(8,128)(2,1)S(1)} %add_convert_fusion.1), channel_id=1, source_target_pairs={{0,8},{1,5},{8,16},{9,1},{16,24},{17,9},{24,26},{25,17},{26,18},{2... | collective-permute-start | bytes 829448 | tf_op jit(solution)/shard_map/ppermute | solution.py:47
  200.9 7.7 %collective-permute-start.31 = (bf16[1080,128]{1,0:T(8,128)(2,1)S(1)}, bf16[1080,128]{1,0:T(8,128)(2,1)S(1)}, u32[]{:S(2)}, u32[]{:S(2)}) collective-permute-start(bf16[1080,128]{1,0:T(8,128)(2,1)S(1)} %add_convert_fusion.15), channel_id=1, source_target_pairs={{0,8},{1,5},{8,16},{9,1},{16,24},{17,9},{24,26},{25,17},{26,18},{2... | collective-permute-start | bytes 829448 | tf_op jit(solution)/shard_map/ppermute | solution.py:47
  202.7 8.8 %collective-permute-start.16 = (bf16[1080,128]{1,0:T(8,128)(2,1)S(1)}, bf16[1080,128]{1,0:T(8,128)(2,1)S(1)}, u32[]{:S(2)}, u32[]{:S(2)}) collective-permute-start(bf16[1080,128]{1,0:T(8,128)(2,1)S(1)} %add_convert_fusion.29), channel_id=1, source_target_pairs={{0,8},{1,5},{8,16},{9,1},{16,24},{17,9},{24,26},{25,17},{26,18},{2... | collective-permute-start | bytes 829448 | tf_op jit(solution)/shard_map/ppermute | solution.py:47
  206.8 7.8 %collective-permute-start.47 = (bf16[1080,128]{1,0:T(8,128)(2,1)S(1)}, bf16[1080,128]{1,0:T(8,128)(2,1)S(1)}, u32[]{:S(2)}, u32[]{:S(2)}) collective-permute-start(bf16[1080,128]{1,0:T(8,128)(2,1)S(1)} %add_convert_fusion), channel_id=1, source_target_pairs={{0,8},{1,5},{8,16},{9,1},{16,24},{17,9},{24,26},{25,17},{26,18},{2... | collective-permute-start | bytes 829448 | tf_op jit(solution)/shard_map/ppermute | solution.py:47
  209.7 7.8 %collective-permute-start.32 = (bf16[1080,128]{1,0:T(8,128)(2,1)S(1)}, bf16[1080,128]{1,0:T(8,128)(2,1)S(1)}, u32[]{:S(2)}, u32[]{:S(2)}) collective-permute-start(bf16[1080,128]{1,0:T(8,128)(2,1)S(1)} %add_convert_fusion.14), channel_id=1, source_target_pairs={{0,8},{1,5},{8,16},{9,1},{16,24},{17,9},{24,26},{25,17},{26,18},{2... | collective-permute-start | bytes 829448 | tf_op jit(solution)/shard_map/ppermute | solution.py:47
  211.6 8.8 %collective-permute-start.17 = (bf16[1080,128]{1,0:T(8,128)(2,1)S(1)}, bf16[1080,128]{1,0:T(8,128)(2,1)S(1)}, u32[]{:S(2)}, u32[]{:S(2)}) collective-permute-start(bf16[1080,128]{1,0:T(8,128)(2,1)S(1)} %add_convert_fusion.28), channel_id=1, source_target_pairs={{0,8},{1,5},{8,16},{9,1},{16,24},{17,9},{24,26},{25,17},{26,18},{2... | collective-permute-start | bytes 829448 | tf_op jit(solution)/shard_map/ppermute | solution.py:47
  (6 other events, 174.1 us)

commit v7 on v6

--- a/solution.py
+++ b/solution.py
@@ -49,10 +49,10 @@
     return accs
 
 
-def _ffn_kernel(col_ref, cnt_ref, tok_ref, cot_ref, tokt_ref, cott_ref, wg_ref, wu_ref, wdt_ref,
+def _ffn_kernel(col_ref, cnt_ref, tok_ref, cot_ref, wgu_ref, wdt_ref,
                 gg_ref, gu_ref, gd_ref, dxt_ref):
     h = pl.program_id(0)
-    slots = wg_ref.shape[1]
+    slots = gg_ref.shape[1]
     count = cnt_ref[h]
 
     @pl.when(h == 0)
@@ -60,56 +60,45 @@
         dxt_ref[...] = jnp.zeros_like(dxt_ref)
 
     f32 = jnp.float32
-    offs, xs, dys, wgs, wus = [], [], [], [], []
-    gate = up = d_hidden = None
-    for p in range(slots):
-        off = pl.multiple_of(col_ref[h, p] * BLK, BLK)
-        live = p < count
-        x = tok_ref[:, pl.ds(off, BLK)]
-        dy = cot_ref[:, pl.ds(off, BLK)]
-        wg = jnp.where(live, wg_ref[0, p], jnp.zeros_like(wg_ref[0, p]))
-        wu = jnp.where(live, wu_ref[0, p], jnp.zeros_like(wu_ref[0, p]))
-        wdt = jnp.where(live, wdt_ref[0, p], jnp.zeros_like(wdt_ref[0, p]))
-        g = jnp.dot(x, wg, preferred_element_type=f32)
-        u = jnp.dot(x, wu, preferred_element_type=f32)
-        d = jnp.dot(dy, wdt, preferred_element_type=f32)
-        gate = g if gate is None else gate + g
-        up = u if up is None else up + u
-        d_hidden = d if d_hidden is None else d_hidden + d
-        offs.append(off)
-        wgs.append(wg)
-        wus.append(wu)
+    offs = [pl.multiple_of(col_ref[h, p] * BLK, BLK) for p in range(slots)]
+    x = jnp.concatenate([tok_ref[:, pl.ds(o, BLK)] for o in offs], axis=1)
+    dy = jnp.concatenate([cot_ref[:, pl.ds(o, BLK)] for o in offs], axis=1)
+    wgu = wgu_ref[0]
+    wdt = wdt_ref[0]
+    live_gu = lax.broadcasted_iota(jnp.int32, wgu.shape, 0) < count * BLK
+    live_d = lax.broadcasted_iota(jnp.int32, wdt.shape, 0) < count * BLK
+    wgu = jnp.where(live_gu, wgu, jnp.zeros_like(wgu))
+    wdt = jnp.where(live_d, wdt, jnp.zeros_like(wdt))
+    gate_up = jnp.dot(x, wgu, preferred_element_type=f32)
+    gate, up = gate_up[:, :BLK], gate_up[:, BLK:]
+    d_hidden = jnp.dot(dy, wdt, preferred_element_type=f32)
     sig = 1.0 / (1.0 + jnp.exp(-gate))
     silu = gate * sig
     hidden = (silu * up).astype(jnp.bfloat16)
     d_gate = (d_hidden * up * sig * (1.0 + gate * (1.0 - sig))).astype(jnp.bfloat16)
     d_up = (d_hidden * silu).astype(jnp.bfloat16)
-    hidden_t = hidden.T
-    d_gate_t = d_gate.T
-    d_up_t = d_up.T
+    d_gu = jnp.concatenate([d_gate, d_up], axis=1)
+    grad_gu = jnp.dot(x.T, d_gu, preferred_element_type=f32)
+    grad_d = jnp.dot(hidden.T, dy, preferred_element_type=f32)
+    back_t = jnp.dot(wgu, d_gu.T, preferred_element_type=f32)
     for p in range(slots):
         live = p < count
         zero = jnp.zeros((BLK, BLK), f32)
-        xt = tokt_ref[pl.ds(offs[p], BLK), :]
-        dy = cot_ref[:, pl.ds(offs[p], BLK)]
-        gg = jnp.dot(xt, d_gate, preferred_element_type=f32)
-        gu = jnp.dot(xt, d_up, preferred_element_type=f32)
-        gd = jnp.dot(hidden_t, dy, preferred_element_type=f32)
-        gg_ref[0, p] = jnp.where(live, gg, zero)
-        gu_ref[0, p] = jnp.where(live, gu, zero)
-        gd_ref[0, p] = jnp.where(live, gd, zero)
-        back_t = jnp.dot(wgs[p], d_gate_t, preferred_element_type=f32)
-        back_t = back_t + jnp.dot(wus[p], d_up_t, preferred_element_type=f32)
-        dxt_ref[pl.ds(offs[p], BLK), :] += back_t
+        rows = slice(p * BLK, (p + 1) * BLK)
+        gg_ref[0, p] = jnp.where(live, grad_gu[rows, :BLK], zero)
+        gu_ref[0, p] = jnp.where(live, grad_gu[rows, BLK:], zero)
+        gd_ref[0, p] = jnp.where(live, grad_d[:, rows], zero)
+        dxt_ref[pl.ds(offs[p], BLK), :] += back_t[rows]
 
 
 def ffn_block_terms(col_index, row_count, full_tok, full_cot, gate_w, up_w, down_w):
     hblk, slots = col_index.shape
     rows, width = full_tok.shape
-    down_t = jnp.swapaxes(down_w, 2, 3)
-    wspec = pl.BlockSpec((1, slots, BLK, BLK), lambda h, c, n: (h, 0, 0, 0))
+    wgu = jnp.concatenate([gate_w, up_w], axis=3).reshape(hblk, slots * BLK, 2 * BLK)
+    wdt = jnp.swapaxes(down_w, 2, 3).reshape(hblk, slots * BLK, BLK)
     full = pl.BlockSpec((rows, width), lambda h, c, n: (0, 0))
     full_t = pl.BlockSpec((width, rows), lambda h, c, n: (0, 0))
+    gspec = pl.BlockSpec((1, slots, BLK, BLK), lambda h, c, n: (h, 0, 0, 0))
     grad = jax.ShapeDtypeStruct((hblk, slots, BLK, BLK), jnp.float32)
     flops = 2 * rows * hblk * slots * BLK * BLK * 9
     return pl.pallas_call(
@@ -117,18 +106,23 @@
         grid_spec=pltpu.PrefetchScalarGridSpec(
             num_scalar_prefetch=2,
             grid=(hblk,),
-            in_specs=[full, full, full_t, full_t, wspec, wspec, wspec],
-            out_specs=[wspec, wspec, wspec, full_t],
+            in_specs=[
+                full,
+                full,
+                pl.BlockSpec((1, slots * BLK, 2 * BLK), lambda h, c, n: (h, 0, 0)),
+                pl.BlockSpec((1, slots * BLK, BLK), lambda h, c, n: (h, 0, 0)),
+            ],
+            out_specs=[gspec, gspec, gspec, full_t],
         ),
         out_shape=[grad, grad, grad, jax.ShapeDtypeStruct((width, rows), jnp.float32)],
         compiler_params=pltpu.CompilerParams(dimension_semantics=("arbitrary",)),
         cost_estimate=pl.CostEstimate(
             flops=flops,
             transcendentals=rows * hblk * BLK,
-            bytes_accessed=3 * hblk * slots * BLK * BLK * 6 + rows * width * 12,
+            bytes_accessed=3 * hblk * slots * BLK * BLK * 6 + rows * width * 8,
         ),
         name="ffn_block_terms",
-    )(col_index, row_count, full_tok, full_cot, full_tok.T, full_cot.T, gate_w, up_w, down_t)
+    )(col_index, row_count, full_tok, full_cot, wgu, wdt)
 
 
 def shards(n_dp, n_t, tokens, cotangent, w_gate, w_up, w_down, col_index, row_count, adam_m, adam_v):

time: 227 us -> 224 us (0.987)
  other arithmetic: 49.5 us -> 56.8 us
  local copies, waits for them, and re-layouts: 22.1 us -> 16.2 us
  Pallas kernels: 35.4 us -> 31.3 us
    concatenate x0 -> x3, other arithmetic: none -> 10.7 us  [the longest x1 8.29 us: ffn_block_terms(): jnp.concatenate([gate_w, up_w], axis=3).reshape(hblk, slots * BLK, 2 * BLK)]
    unnamed x17 -> x18, local copies, waits for them, and re-layouts: 12.5 us -> 2.5 us
    transpose x0 -> x1, local copies, waits for them, and re-layouts: none -> 7.19 us  [ffn_block_terms(): wdt = jnp.swapaxes(down_w, 2, 3).reshape(hblk, slots * BLK, BLK)]
    pallas_call x1, Pallas kernels: 35.4 us -> 31.3 us  [ffn_block_terms(): pl.pallas_call(_ffn_kernel, grid_spec=pltpu.PrefetchScalarGridSpec(num_sc...]
    concatenate x2 -> x0, local copies, waits for them, and re-layouts: 2.88 us -> none  [the longest x1 1.44 us: shards(): jnp.concatenate([jnp.where(first, cotangent, other_cot), jnp.where(first,...]
    transpose x2 -> x0, other arithmetic: 2.45 us -> none  [ffn_block_terms(): return pl.pallas_call(_ffn_kernel, grid_spec=pltpu.PrefetchScalarGridSpec...]
  transfers between devices with their start and end apart: 48 -> 48, of which waited for: 35 -> 35; matrix products, arithmetic and copies ran while one was open for 26% -> 30% of each run, Pallas kernels for 0% -> 0%
where the time goes in v7:
time: 224 us; the launch traced here: 221 us
  starting transfers between devices  75.5 us (34%)
  other arithmetic  56.8 us (25%)
  Pallas kernels  31.3 us (14%)
  between operations  21.7 us (10%)
  waiting for transfers between devices  19.1 us (9%)
  local copies, waits for them, and re-layouts  16.2 us (7%)
    ppermute x45, starting transfers between devices, ring_reduce_scatter(): moved = lax.ppermute(accs[i].astype(wire_dtype), ('dp', 'tensor'), perm)  74.4 us
    convert_element_type x42, other arithmetic, ring_reduce_scatter(): moved = lax.ppermute(accs[i].astype(wire_dtype), ('dp', 'tensor'), perm)  38.7 us
    pallas_call x1, Pallas kernels, ffn_block_terms(): pl.pallas_call(_ffn_kernel, grid_spec=pltpu.PrefetchScalarGridSpec(num_sc...  31.3 us
    ppermute x45, waiting for transfers between devices, ring_reduce_scatter(): moved = lax.ppermute(accs[i].astype(wire_dtype), ('dp', 'tensor'), perm)  19.1 us
    concatenate x1, other arithmetic, ffn_block_terms(): jnp.concatenate([gate_w, up_w], axis=3).reshape(hblk, slots * BLK, 2 * BLK)  8.29 us
    transpose x1, local copies, waits for them, and re-layouts, ffn_block_terms(): wdt = jnp.swapaxes(down_w, 2, 3).reshape(hblk, slots * BLK, BLK)  7.19 us
  transfers between devices with their start and end apart: 48, of which 35 were waited for; matrix products, arithmetic and copies ran while one was open for 30% of the time, Pallas kernels for 0%

profile of v7, /device:TPU:0, one launch (start us, length us, event | category | flops | bytes accessed | tf_op | source)
XLA Modules:
  0.0 220.6 jit_solution(11092380774661479272)
XLA Ops:
  13.2 2.0 fusion.2
  26.7 7.2 %copy.15 = bf16[27,5,128,128]{3,2,1,0:T(8,128)(2,1)} copy(bf16[27,5,128,128]{2,3,1,0:T(8,128)(2,1)} %bitcast.88) | data formatting | bytes 8847360 | tf_op jit(solution)/shard_map/transpose | solution.py:98
  33.9 8.3 %pad_maximum_fusion.wgu_ref = bf16[27,640,256]{2,1,0:T(8,128)(2,1)} fusion(bf16[27,640,128]{2,1,0:T(8,128)(2,1)} %bitcast.89, bf16[27,640,128]{2,1,0:T(8,128)(2,1)} %bitcast.90), kind=kLoop, calls=%fused_computation | loop fusion | flops 17694720 | bytes 17694720 | tf_op jit(solution)/shard_map/concatenate | solution.py:97
  44.8 31.3 %ffn_block_terms.1 = (f32[27,5,128,128]{3,2,1,0:T(8,128)}, f32[27,5,128,128]{3,2,1,0:T(8,128)}, f32[27,5,128,128]{3,2,1,0:T(8,128)}, f32[5120,128]{1,0:T(8,128)}) custom-call(s32[27,5]{1,0:T(8,128)} %copy.16.col_ref, s32[27]{0:T(128)} %cnt_ref.1, bf16[128,5120]{1,0:T(8,128)(2,1)} %pad_maximum_fusion.2.tok_ref, bf16[128,5120]{1,0:T(8,128)(2,1)} %pad_maximum_fusion.3.cot_ref, ...), custom_call_target="tpu_custom_call" | custom-call | flops 5096079360 | bytes 45056000 | tf_op jit(solution)/shard_map/ffn_block_terms/pallas_call | solution.py:104
  76.1 2.0 fusion.1
  79.6 2.7 %collective-permute-start.33 = (bf16[1080,128]{1,0:T(8,128)(2,1)S(1)}, bf16[1080,128]{1,0:T(8,128)(2,1)S(1)}, u32[]{:S(2)}, u32[]{:S(2)}) collective-permute-start(bf16[1080,128]{1,0:T(8,128)(2,1)S(1)} %dynamic-slice_convert_fusion), channel_id=1, source_target_pairs={{0,8},{1,5},{8,16},{9,1},{16,24},{17,9},{24,26},{25,17},{26,18},{2... | collective-permute-start | bytes 829448 | tf_op jit(solution)/shard_map/ppermute | solution.py:47
  83.4 1.6 collective-permute-start.18
  86.1 1.6 collective-permute-start.3
  94.1 1.8 collective-permute-start.4
  97.1 1.8 collective-permute-start.35
  100.1 1.8 collective-permute-start.20
  103.1 1.8 collective-permute-start.5
  107.4 1.6 collective-permute-start.36
  110.2 1.6 collective-permute-start.21
  118.1 1.6 collective-permute-start.22
  121.1 1.6 collective-permute-start.7
  124.0 1.6 collective-permute-start.38
  127.0 1.6 collective-permute-start.23
  130.0 1.6 collective-permute-start.8
  132.9 1.6 collective-permute-start.39
  135.9 1.6 collective-permute-start.24
  138.8 1.6 collective-permute-start.9
  141.8 1.6 collective-permute-start.40
  144.8 1.6 collective-permute-start.25
  146.7 1.6 collective-permute-start.10
  150.7 1.6 collective-permute-start.41
  153.7 1.6 collective-permute-start.26
  159.6 1.6 collective-permute-start.42
  162.5 1.6 collective-permute-start.27
  164.5 1.6 collective-permute-start.12
  168.5 1.6 collective-permute-start.43
  171.4 1.6 collective-permute-start.28
  173.4 1.6 collective-permute-start.13
  177.4 1.6 collective-permute-start.44
  180.3 1.6 collective-permute-start.29
  182.2 1.6 collective-permute-start.14
  186.2 1.6 collective-permute-start.45
  189.2 1.6 collective-permute-start.30
  191.1 1.6 collective-permute-start.15
  195.1 1.6 collective-permute-start.46
  198.1 1.6 collective-permute-start.31
  200.0 1.6 collective-permute-start.16
  204.0 1.6 collective-permute-start.47
  207.0 1.6 collective-permute-start.32
  208.9 1.6 collective-permute-start.17
  212.9 1.9 collective-permute-done.32
  215.9 1.9 collective-permute-done.17
  217.8 2.8 %add_divide_fusion = (f32[3,1,1080,128]{3,2,1,0:T(8,128)}, f32[3,1,1080,128]{3,2,1,0:T(8,128)}, f32[3,1,1080,128]{3,2,1,0:T(8,128)}) fusion(f32[1,1,1080,128]{3,2,1,0:T(8,128)S(1)} %add_bitcast_fusion, f32[1,1,1080,128]{3,2,1,0:T(8,128)S(1)} %add_bitcast_fusion.1, f32[1,1,1080,128]{3,2,1,0:T(8,128)S(1)} %add_bitcast_fusion.2, ...), kind=kLoop, calls=%fused_computation.2 | loop fusion | flops 4976640 | bytes 9953280 | tf_op jit(solution)/shard_map/div | solution.py:170
  (126 shorter events, 74.5 us)
Async XLA Ops:
  0.6 41.6 %collective-permute-start.1 = (bf16[128,2560]{1,0:T(8,128)(2,1)}, bf16[128,2560]{1,0:T(8,128)(2,1)S(1)}, u32[]{:S(2)}, u32[]{:S(2)}) collective-permute-start(bf16[128,2560]{1,0:T(8,128)(2,1)} %param.12), channel_id=1, source_target_pairs={{0,1},{1,0},{2,3},{3,2},{4,5},{5,4},{6,7},{7,6},{8,9},{9,8},{10,11... | collective-permute-start | bytes 1966088 | tf_op jit(solution)/shard_map/ppermute | solution.py:132
  1.1 41.0 %collective-permute-start = (bf16[128,2560]{1,0:T(8,128)(2,1)}, bf16[128,2560]{1,0:T(8,128)(2,1)S(1)}, u32[]{:S(2)}, u32[]{:S(2)}) collective-permute-start(bf16[128,2560]{1,0:T(8,128)(2,1)} %param.11), channel_id=1, source_target_pairs={{0,1},{1,0},{2,3},{3,2},{4,5},{5,4},{6,7},{7,6},{8,9},{9,8},{10,11... | collective-permute-start | bytes 1966088 | tf_op jit(solution)/shard_map/ppermute | solution.py:132
  78.0 26.9 %collective-permute-start.2 = (bf16[128,2560]{0,1:T(8,128)(2,1)S(1)}, bf16[128,2560]{0,1:T(8,128)(2,1)S(1)}, u32[]{:S(2)}, u32[]{:S(2)}) collective-permute-start(bf16[128,2560]{0,1:T(8,128)(2,1)S(1)} %fusion.1), channel_id=1, source_target_pairs={{0,1},{1,0},{2,3},{3,2},{4,5},{5,4},{6,7},{7,6},{8,9},{9,8},{10,11... | collective-permute-start | bytes 1966088 | tf_op jit(solution)/shard_map/ppermute | solution.py:160
  79.6 8.1 %collective-permute-start.33 = (bf16[1080,128]{1,0:T(8,128)(2,1)S(1)}, bf16[1080,128]{1,0:T(8,128)(2,1)S(1)}, u32[]{:S(2)}, u32[]{:S(2)}) collective-permute-start(bf16[1080,128]{1,0:T(8,128)(2,1)S(1)} %dynamic-slice_convert_fusion), channel_id=1, source_target_pairs={{0,8},{1,5},{8,16},{9,1},{16,24},{17,9},{24,26},{25,17},{26,18},{2... | collective-permute-start | bytes 829448 | tf_op jit(solution)/shard_map/ppermute | solution.py:47
  83.4 7.0 %collective-permute-start.18 = (bf16[1080,128]{1,0:T(8,128)(2,1)S(1)}, bf16[1080,128]{1,0:T(8,128)(2,1)S(1)}, u32[]{:S(2)}, u32[]{:S(2)}) collective-permute-start(bf16[1080,128]{1,0:T(8,128)(2,1)S(1)} %dynamic-slice_convert_fusion.1), channel_id=1, source_target_pairs={{0,8},{1,5},{8,16},{9,1},{16,24},{17,9},{24,26},{25,17},{26,18},{2... | collective-permute-start | bytes 829448 | tf_op jit(solution)/shard_map/ppermute | solution.py:47
  86.1 6.9 %collective-permute-start.3 = (bf16[1080,128]{1,0:T(8,128)(2,1)S(1)}, bf16[1080,128]{1,0:T(8,128)(2,1)S(1)}, u32[]{:S(2)}, u32[]{:S(2)}) collective-permute-start(bf16[1080,128]{1,0:T(8,128)(2,1)S(1)} %dynamic-slice_convert_fusion.2), channel_id=1, source_target_pairs={{0,8},{1,5},{8,16},{9,1},{16,24},{17,9},{24,26},{25,17},{26,18},{2... | collective-permute-start | bytes 829448 | tf_op jit(solution)/shard_map/ppermute | solution.py:47
  88.9 7.1 %collective-permute-start.34 = (bf16[1080,128]{1,0:T(8,128)(2,1)S(1)}, bf16[1080,128]{1,0:T(8,128)(2,1)S(1)}, u32[]{:S(2)}, u32[]{:S(2)}) collective-permute-start(bf16[1080,128]{1,0:T(8,128)(2,1)S(1)} %add_convert_fusion.13), channel_id=1, source_target_pairs={{0,8},{1,5},{8,16},{9,1},{16,24},{17,9},{24,26},{25,17},{26,18},{2... | collective-permute-start | bytes 829448 | tf_op jit(solution)/shard_map/ppermute | solution.py:47
  91.6 7.4 %collective-permute-start.19 = (bf16[1080,128]{1,0:T(8,128)(2,1)S(1)}, bf16[1080,128]{1,0:T(8,128)(2,1)S(1)}, u32[]{:S(2)}, u32[]{:S(2)}) collective-permute-start(bf16[1080,128]{1,0:T(8,128)(2,1)S(1)} %add_convert_fusion.27), channel_id=1, source_target_pairs={{0,8},{1,5},{8,16},{9,1},{16,24},{17,9},{24,26},{25,17},{26,18},{2... | collective-permute-start | bytes 829448 | tf_op jit(solution)/shard_map/ppermute | solution.py:47
  94.1 7.8 %collective-permute-start.4 = (bf16[1080,128]{1,0:T(8,128)(2,1)S(1)}, bf16[1080,128]{1,0:T(8,128)(2,1)S(1)}, u32[]{:S(2)}, u32[]{:S(2)}) collective-permute-start(bf16[1080,128]{1,0:T(8,128)(2,1)S(1)} %add_convert_fusion.41), channel_id=1, source_target_pairs={{0,8},{1,5},{8,16},{9,1},{16,24},{17,9},{24,26},{25,17},{26,18},{2... | collective-permute-start | bytes 829448 | tf_op jit(solution)/shard_map/ppermute | solution.py:47
  97.1 9.1 %collective-permute-start.35 = (bf16[1080,128]{1,0:T(8,128)(2,1)S(1)}, bf16[1080,128]{1,0:T(8,128)(2,1)S(1)}, u32[]{:S(2)}, u32[]{:S(2)}) collective-permute-start(bf16[1080,128]{1,0:T(8,128)(2,1)S(1)} %add_convert_fusion.12), channel_id=1, source_target_pairs={{0,8},{1,5},{8,16},{9,1},{16,24},{17,9},{24,26},{25,17},{26,18},{2... | collective-permute-start | bytes 829448 | tf_op jit(solution)/shard_map/ppermute | solution.py:47
  100.1 9.0 %collective-permute-start.20 = (bf16[1080,128]{1,0:T(8,128)(2,1)S(1)}, bf16[1080,128]{1,0:T(8,128)(2,1)S(1)}, u32[]{:S(2)}, u32[]{:S(2)}) collective-permute-start(bf16[1080,128]{1,0:T(8,128)(2,1)S(1)} %add_convert_fusion.26), channel_id=1, source_target_pairs={{0,8},{1,5},{8,16},{9,1},{16,24},{17,9},{24,26},{25,17},{26,18},{2... | collective-permute-start | bytes 829448 | tf_op jit(solution)/shard_map/ppermute | solution.py:47
  103.1 8.7 %collective-permute-start.5 = (bf16[1080,128]{1,0:T(8,128)(2,1)S(1)}, bf16[1080,128]{1,0:T(8,128)(2,1)S(1)}, u32[]{:S(2)}, u32[]{:S(2)}) collective-permute-start(bf16[1080,128]{1,0:T(8,128)(2,1)S(1)} %add_convert_fusion.40), channel_id=1, source_target_pairs={{0,8},{1,5},{8,16},{9,1},{16,24},{17,9},{24,26},{25,17},{26,18},{2... | collective-permute-start | bytes 829448 | tf_op jit(solution)/shard_map/ppermute | solution.py:47
  107.4 7.0 %collective-permute-start.36 = (bf16[1080,128]{1,0:T(8,128)(2,1)S(1)}, bf16[1080,128]{1,0:T(8,128)(2,1)S(1)}, u32[]{:S(2)}, u32[]{:S(2)}) collective-permute-start(bf16[1080,128]{1,0:T(8,128)(2,1)S(1)} %add_convert_fusion.11), channel_id=1, source_target_pairs={{0,8},{1,5},{8,16},{9,1},{16,24},{17,9},{24,26},{25,17},{26,18},{2... | collective-permute-start | bytes 829448 | tf_op jit(solution)/shard_map/ppermute | solution.py:47
  110.2 6.8 %collective-permute-start.21 = (bf16[1080,128]{1,0:T(8,128)(2,1)S(1)}, bf16[1080,128]{1,0:T(8,128)(2,1)S(1)}, u32[]{:S(2)}, u32[]{:S(2)}) collective-permute-start(bf16[1080,128]{1,0:T(8,128)(2,1)S(1)} %add_convert_fusion.25), channel_id=1, source_target_pairs={{0,8},{1,5},{8,16},{9,1},{16,24},{17,9},{24,26},{25,17},{26,18},{2... | collective-permute-start | bytes 829448 | tf_op jit(solution)/shard_map/ppermute | solution.py:47
  112.9 7.0 %collective-permute-start.6 = (bf16[1080,128]{1,0:T(8,128)(2,1)S(1)}, bf16[1080,128]{1,0:T(8,128)(2,1)S(1)}, u32[]{:S(2)}, u32[]{:S(2)}) collective-permute-start(bf16[1080,128]{1,0:T(8,128)(2,1)S(1)} %add_convert_fusion.39), channel_id=1, source_target_pairs={{0,8},{1,5},{8,16},{9,1},{16,24},{17,9},{24,26},{25,17},{26,18},{2... | collective-permute-start | bytes 829448 | tf_op jit(solution)/shard_map/ppermute | solution.py:47
  115.6 7.3 %collective-permute-start.37 = (bf16[1080,128]{1,0:T(8,128)(2,1)S(1)}, bf16[1080,128]{1,0:T(8,128)(2,1)S(1)}, u32[]{:S(2)}, u32[]{:S(2)}) collective-permute-start(bf16[1080,128]{1,0:T(8,128)(2,1)S(1)} %add_convert_fusion.10), channel_id=1, source_target_pairs={{0,8},{1,5},{8,16},{9,1},{16,24},{17,9},{24,26},{25,17},{26,18},{2... | collective-permute-start | bytes 829448 | tf_op jit(solution)/shard_map/ppermute | solution.py:47
  118.1 7.8 %collective-permute-start.22 = (bf16[1080,128]{1,0:T(8,128)(2,1)S(1)}, bf16[1080,128]{1,0:T(8,128)(2,1)S(1)}, u32[]{:S(2)}, u32[]{:S(2)}) collective-permute-start(bf16[1080,128]{1,0:T(8,128)(2,1)S(1)} %add_convert_fusion.24), channel_id=1, source_target_pairs={{0,8},{1,5},{8,16},{9,1},{16,24},{17,9},{24,26},{25,17},{26,18},{2... | collective-permute-start | bytes 829448 | tf_op jit(solution)/shard_map/ppermute | solution.py:47
  121.1 7.8 %collective-permute-start.7 = (bf16[1080,128]{1,0:T(8,128)(2,1)S(1)}, bf16[1080,128]{1,0:T(8,128)(2,1)S(1)}, u32[]{:S(2)}, u32[]{:S(2)}) collective-permute-start(bf16[1080,128]{1,0:T(8,128)(2,1)S(1)} %add_convert_fusion.38), channel_id=1, source_target_pairs={{0,8},{1,5},{8,16},{9,1},{16,24},{17,9},{24,26},{25,17},{26,18},{2... | collective-permute-start | bytes 829448 | tf_op jit(solution)/shard_map/ppermute | solution.py:47
  124.0 7.8 %collective-permute-start.38 = (bf16[1080,128]{1,0:T(8,128)(2,1)S(1)}, bf16[1080,128]{1,0:T(8,128)(2,1)S(1)}, u32[]{:S(2)}, u32[]{:S(2)}) collective-permute-start(bf16[1080,128]{1,0:T(8,128)(2,1)S(1)} %add_convert_fusion.9), channel_id=1, source_target_pairs={{0,8},{1,5},{8,16},{9,1},{16,24},{17,9},{24,26},{25,17},{26,18},{2... | collective-permute-start | bytes 829448 | tf_op jit(solution)/shard_map/ppermute | solution.py:47
  127.0 7.8 %collective-permute-start.23 = (bf16[1080,128]{1,0:T(8,128)(2,1)S(1)}, bf16[1080,128]{1,0:T(8,128)(2,1)S(1)}, u32[]{:S(2)}, u32[]{:S(2)}) collective-permute-start(bf16[1080,128]{1,0:T(8,128)(2,1)S(1)} %add_convert_fusion.23), channel_id=1, source_target_pairs={{0,8},{1,5},{8,16},{9,1},{16,24},{17,9},{24,26},{25,17},{26,18},{2... | collective-permute-start | bytes 829448 | tf_op jit(solution)/shard_map/ppermute | solution.py:47
  130.0 7.8 %collective-permute-start.8 = (bf16[1080,128]{1,0:T(8,128)(2,1)S(1)}, bf16[1080,128]{1,0:T(8,128)(2,1)S(1)}, u32[]{:S(2)}, u32[]{:S(2)}) collective-permute-start(bf16[1080,128]{1,0:T(8,128)(2,1)S(1)} %add_convert_fusion.37), channel_id=1, source_target_pairs={{0,8},{1,5},{8,16},{9,1},{16,24},{17,9},{24,26},{25,17},{26,18},{2... | collective-permute-start | bytes 829448 | tf_op jit(solution)/shard_map/ppermute | solution.py:47
  132.9 7.8 %collective-permute-start.39 = (bf16[1080,128]{1,0:T(8,128)(2,1)S(1)}, bf16[1080,128]{1,0:T(8,128)(2,1)S(1)}, u32[]{:S(2)}, u32[]{:S(2)}) collective-permute-start(bf16[1080,128]{1,0:T(8,128)(2,1)S(1)} %add_convert_fusion.8), channel_id=1, source_target_pairs={{0,8},{1,5},{8,16},{9,1},{16,24},{17,9},{24,26},{25,17},{26,18},{2... | collective-permute-start | bytes 829448 | tf_op jit(solution)/shard_map/ppermute | solution.py:47
  135.9 7.8 %collective-permute-start.24 = (bf16[1080,128]{1,0:T(8,128)(2,1)S(1)}, bf16[1080,128]{1,0:T(8,128)(2,1)S(1)}, u32[]{:S(2)}, u32[]{:S(2)}) collective-permute-start(bf16[1080,128]{1,0:T(8,128)(2,1)S(1)} %add_convert_fusion.22), channel_id=1, source_target_pairs={{0,8},{1,5},{8,16},{9,1},{16,24},{17,9},{24,26},{25,17},{26,18},{2... | collective-permute-start | bytes 829448 | tf_op jit(solution)/shard_map/ppermute | solution.py:47
  138.8 7.8 %collective-permute-start.9 = (bf16[1080,128]{1,0:T(8,128)(2,1)S(1)}, bf16[1080,128]{1,0:T(8,128)(2,1)S(1)}, u32[]{:S(2)}, u32[]{:S(2)}) collective-permute-start(bf16[1080,128]{1,0:T(8,128)(2,1)S(1)} %add_convert_fusion.36), channel_id=1, source_target_pairs={{0,8},{1,5},{8,16},{9,1},{16,24},{17,9},{24,26},{25,17},{26,18},{2... | collective-permute-start | bytes 829448 | tf_op jit(solution)/shard_map/ppermute | solution.py:47
  141.8 7.8 %collective-permute-start.40 = (bf16[1080,128]{1,0:T(8,128)(2,1)S(1)}, bf16[1080,128]{1,0:T(8,128)(2,1)S(1)}, u32[]{:S(2)}, u32[]{:S(2)}) collective-permute-start(bf16[1080,128]{1,0:T(8,128)(2,1)S(1)} %add_convert_fusion.7), channel_id=1, source_target_pairs={{0,8},{1,5},{8,16},{9,1},{16,24},{17,9},{24,26},{25,17},{26,18},{2... | collective-permute-start | bytes 829448 | tf_op jit(solution)/shard_map/ppermute | solution.py:47
  144.8 7.8 %collective-permute-start.25 = (bf16[1080,128]{1,0:T(8,128)(2,1)S(1)}, bf16[1080,128]{1,0:T(8,128)(2,1)S(1)}, u32[]{:S(2)}, u32[]{:S(2)}) collective-permute-start(bf16[1080,128]{1,0:T(8,128)(2,1)S(1)} %add_convert_fusion.21), channel_id=1, source_target_pairs={{0,8},{1,5},{8,16},{9,1},{16,24},{17,9},{24,26},{25,17},{26,18},{2... | collective-permute-start | bytes 829448 | tf_op jit(solution)/shard_map/ppermute | solution.py:47
  146.7 8.8 %collective-permute-start.10 = (bf16[1080,128]{1,0:T(8,128)(2,1)S(1)}, bf16[1080,128]{1,0:T(8,128)(2,1)S(1)}, u32[]{:S(2)}, u32[]{:S(2)}) collective-permute-start(bf16[1080,128]{1,0:T(8,128)(2,1)S(1)} %add_convert_fusion.35), channel_id=1, source_target_pairs={{0,8},{1,5},{8,16},{9,1},{16,24},{17,9},{24,26},{25,17},{26,18},{2... | collective-permute-start | bytes 829448 | tf_op jit(solution)/shard_map/ppermute | solution.py:47
  150.7 7.8 %collective-permute-start.41 = (bf16[1080,128]{1,0:T(8,128)(2,1)S(1)}, bf16[1080,128]{1,0:T(8,128)(2,1)S(1)}, u32[]{:S(2)}, u32[]{:S(2)}) collective-permute-start(bf16[1080,128]{1,0:T(8,128)(2,1)S(1)} %add_convert_fusion.6), channel_id=1, source_target_pairs={{0,8},{1,5},{8,16},{9,1},{16,24},{17,9},{24,26},{25,17},{26,18},{2... | collective-permute-start | bytes 829448 | tf_op jit(solution)/shard_map/ppermute | solution.py:47
  153.7 7.8 %collective-permute-start.26 = (bf16[1080,128]{1,0:T(8,128)(2,1)S(1)}, bf16[1080,128]{1,0:T(8,128)(2,1)S(1)}, u32[]{:S(2)}, u32[]{:S(2)}) collective-permute-start(bf16[1080,128]{1,0:T(8,128)(2,1)S(1)} %add_convert_fusion.20), channel_id=1, source_target_pairs={{0,8},{1,5},{8,16},{9,1},{16,24},{17,9},{24,26},{25,17},{26,18},{2... | collective-permute-start | bytes 829448 | tf_op jit(solution)/shard_map/ppermute | solution.py:47
  155.6 8.8 %collective-permute-start.11 = (bf16[1080,128]{1,0:T(8,128)(2,1)S(1)}, bf16[1080,128]{1,0:T(8,128)(2,1)S(1)}, u32[]{:S(2)}, u32[]{:S(2)}) collective-permute-start(bf16[1080,128]{1,0:T(8,128)(2,1)S(1)} %add_convert_fusion.34), channel_id=1, source_target_pairs={{0,8},{1,5},{8,16},{9,1},{16,24},{17,9},{24,26},{25,17},{26,18},{2... | collective-permute-start | bytes 829448 | tf_op jit(solution)/shard_map/ppermute | solution.py:47
  159.6 7.8 %collective-permute-start.42 = (bf16[1080,128]{1,0:T(8,128)(2,1)S(1)}, bf16[1080,128]{1,0:T(8,128)(2,1)S(1)}, u32[]{:S(2)}, u32[]{:S(2)}) collective-permute-start(bf16[1080,128]{1,0:T(8,128)(2,1)S(1)} %add_convert_fusion.5), channel_id=1, source_target_pairs={{0,8},{1,5},{8,16},{9,1},{16,24},{17,9},{24,26},{25,17},{26,18},{2... | collective-permute-start | bytes 829448 | tf_op jit(solution)/shard_map/ppermute | solution.py:47
  162.5 7.8 %collective-permute-start.27 = (bf16[1080,128]{1,0:T(8,128)(2,1)S(1)}, bf16[1080,128]{1,0:T(8,128)(2,1)S(1)}, u32[]{:S(2)}, u32[]{:S(2)}) collective-permute-start(bf16[1080,128]{1,0:T(8,128)(2,1)S(1)} %add_convert_fusion.19), channel_id=1, source_target_pairs={{0,8},{1,5},{8,16},{9,1},{16,24},{17,9},{24,26},{25,17},{26,18},{2... | collective-permute-start | bytes 829448 | tf_op jit(solution)/shard_map/ppermute | solution.py:47
  164.5 8.8 %collective-permute-start.12 = (bf16[1080,128]{1,0:T(8,128)(2,1)S(1)}, bf16[1080,128]{1,0:T(8,128)(2,1)S(1)}, u32[]{:S(2)}, u32[]{:S(2)}) collective-permute-start(bf16[1080,128]{1,0:T(8,128)(2,1)S(1)} %add_convert_fusion.33), channel_id=1, source_target_pairs={{0,8},{1,5},{8,16},{9,1},{16,24},{17,9},{24,26},{25,17},{26,18},{2... | collective-permute-start | bytes 829448 | tf_op jit(solution)/shard_map/ppermute | solution.py:47
  168.5 7.8 %collective-permute-start.43 = (bf16[1080,128]{1,0:T(8,128)(2,1)S(1)}, bf16[1080,128]{1,0:T(8,128)(2,1)S(1)}, u32[]{:S(2)}, u32[]{:S(2)}) collective-permute-start(bf16[1080,128]{1,0:T(8,128)(2,1)S(1)} %add_convert_fusion.4), channel_id=1, source_target_pairs={{0,8},{1,5},{8,16},{9,1},{16,24},{17,9},{24,26},{25,17},{26,18},{2... | collective-permute-start | bytes 829448 | tf_op jit(solution)/shard_map/ppermute | solution.py:47
  171.4 7.8 %collective-permute-start.28 = (bf16[1080,128]{1,0:T(8,128)(2,1)S(1)}, bf16[1080,128]{1,0:T(8,128)(2,1)S(1)}, u32[]{:S(2)}, u32[]{:S(2)}) collective-permute-start(bf16[1080,128]{1,0:T(8,128)(2,1)S(1)} %add_convert_fusion.18), channel_id=1, source_target_pairs={{0,8},{1,5},{8,16},{9,1},{16,24},{17,9},{24,26},{25,17},{26,18},{2... | collective-permute-start | bytes 829448 | tf_op jit(solution)/shard_map/ppermute | solution.py:47
  173.4 8.8 %collective-permute-start.13 = (bf16[1080,128]{1,0:T(8,128)(2,1)S(1)}, bf16[1080,128]{1,0:T(8,128)(2,1)S(1)}, u32[]{:S(2)}, u32[]{:S(2)}) collective-permute-start(bf16[1080,128]{1,0:T(8,128)(2,1)S(1)} %add_convert_fusion.32), channel_id=1, source_target_pairs={{0,8},{1,5},{8,16},{9,1},{16,24},{17,9},{24,26},{25,17},{26,18},{2... | collective-permute-start | bytes 829448 | tf_op jit(solution)/shard_map/ppermute | solution.py:47
  177.4 7.8 %collective-permute-start.44 = (bf16[1080,128]{1,0:T(8,128)(2,1)S(1)}, bf16[1080,128]{1,0:T(8,128)(2,1)S(1)}, u32[]{:S(2)}, u32[]{:S(2)}) collective-permute-start(bf16[1080,128]{1,0:T(8,128)(2,1)S(1)} %add_convert_fusion.3), channel_id=1, source_target_pairs={{0,8},{1,5},{8,16},{9,1},{16,24},{17,9},{24,26},{25,17},{26,18},{2... | collective-permute-start | bytes 829448 | tf_op jit(solution)/shard_map/ppermute | solution.py:47
  180.3 7.8 %collective-permute-start.29 = (bf16[1080,128]{1,0:T(8,128)(2,1)S(1)}, bf16[1080,128]{1,0:T(8,128)(2,1)S(1)}, u32[]{:S(2)}, u32[]{:S(2)}) collective-permute-start(bf16[1080,128]{1,0:T(8,128)(2,1)S(1)} %add_convert_fusion.17), channel_id=1, source_target_pairs={{0,8},{1,5},{8,16},{9,1},{16,24},{17,9},{24,26},{25,17},{26,18},{2... | collective-permute-start | bytes 829448 | tf_op jit(solution)/shard_map/ppermute | solution.py:47
  182.2 8.8 %collective-permute-start.14 = (bf16[1080,128]{1,0:T(8,128)(2,1)S(1)}, bf16[1080,128]{1,0:T(8,128)(2,1)S(1)}, u32[]{:S(2)}, u32[]{:S(2)}) collective-permute-start(bf16[1080,128]{1,0:T(8,128)(2,1)S(1)} %add_convert_fusion.31), channel_id=1, source_target_pairs={{0,8},{1,5},{8,16},{9,1},{16,24},{17,9},{24,26},{25,17},{26,18},{2... | collective-permute-start | bytes 829448 | tf_op jit(solution)/shard_map/ppermute | solution.py:47
  186.2 7.8 %collective-permute-start.45 = (bf16[1080,128]{1,0:T(8,128)(2,1)S(1)}, bf16[1080,128]{1,0:T(8,128)(2,1)S(1)}, u32[]{:S(2)}, u32[]{:S(2)}) collective-permute-start(bf16[1080,128]{1,0:T(8,128)(2,1)S(1)} %add_convert_fusion.2), channel_id=1, source_target_pairs={{0,8},{1,5},{8,16},{9,1},{16,24},{17,9},{24,26},{25,17},{26,18},{2... | collective-permute-start | bytes 829448 | tf_op jit(solution)/shard_map/ppermute | solution.py:47
  189.2 7.8 %collective-permute-start.30 = (bf16[1080,128]{1,0:T(8,128)(2,1)S(1)}, bf16[1080,128]{1,0:T(8,128)(2,1)S(1)}, u32[]{:S(2)}, u32[]{:S(2)}) collective-permute-start(bf16[1080,128]{1,0:T(8,128)(2,1)S(1)} %add_convert_fusion.16), channel_id=1, source_target_pairs={{0,8},{1,5},{8,16},{9,1},{16,24},{17,9},{24,26},{25,17},{26,18},{2... | collective-permute-start | bytes 829448 | tf_op jit(solution)/shard_map/ppermute | solution.py:47
  191.1 8.8 %collective-permute-start.15 = (bf16[1080,128]{1,0:T(8,128)(2,1)S(1)}, bf16[1080,128]{1,0:T(8,128)(2,1)S(1)}, u32[]{:S(2)}, u32[]{:S(2)}) collective-permute-start(bf16[1080,128]{1,0:T(8,128)(2,1)S(1)} %add_convert_fusion.30), channel_id=1, source_target_pairs={{0,8},{1,5},{8,16},{9,1},{16,24},{17,9},{24,26},{25,17},{26,18},{2... | collective-permute-start | bytes 829448 | tf_op jit(solution)/shard_map/ppermute | solution.py:47
  195.1 7.8 %collective-permute-start.46 = (bf16[1080,128]{1,0:T(8,128)(2,1)S(1)}, bf16[1080,128]{1,0:T(8,128)(2,1)S(1)}, u32[]{:S(2)}, u32[]{:S(2)}) collective-permute-start(bf16[1080,128]{1,0:T(8,128)(2,1)S(1)} %add_convert_fusion.1), channel_id=1, source_target_pairs={{0,8},{1,5},{8,16},{9,1},{16,24},{17,9},{24,26},{25,17},{26,18},{2... | collective-permute-start | bytes 829448 | tf_op jit(solution)/shard_map/ppermute | solution.py:47
  198.1 7.8 %collective-permute-start.31 = (bf16[1080,128]{1,0:T(8,128)(2,1)S(1)}, bf16[1080,128]{1,0:T(8,128)(2,1)S(1)}, u32[]{:S(2)}, u32[]{:S(2)}) collective-permute-start(bf16[1080,128]{1,0:T(8,128)(2,1)S(1)} %add_convert_fusion.15), channel_id=1, source_target_pairs={{0,8},{1,5},{8,16},{9,1},{16,24},{17,9},{24,26},{25,17},{26,18},{2... | collective-permute-start | bytes 829448 | tf_op jit(solution)/shard_map/ppermute | solution.py:47
  200.0 8.8 %collective-permute-start.16 = (bf16[1080,128]{1,0:T(8,128)(2,1)S(1)}, bf16[1080,128]{1,0:T(8,128)(2,1)S(1)}, u32[]{:S(2)}, u32[]{:S(2)}) collective-permute-start(bf16[1080,128]{1,0:T(8,128)(2,1)S(1)} %add_convert_fusion.29), channel_id=1, source_target_pairs={{0,8},{1,5},{8,16},{9,1},{16,24},{17,9},{24,26},{25,17},{26,18},{2... | collective-permute-start | bytes 829448 | tf_op jit(solution)/shard_map/ppermute | solution.py:47
  204.0 7.8 %collective-permute-start.47 = (bf16[1080,128]{1,0:T(8,128)(2,1)S(1)}, bf16[1080,128]{1,0:T(8,128)(2,1)S(1)}, u32[]{:S(2)}, u32[]{:S(2)}) collective-permute-start(bf16[1080,128]{1,0:T(8,128)(2,1)S(1)} %add_convert_fusion), channel_id=1, source_target_pairs={{0,8},{1,5},{8,16},{9,1},{16,24},{17,9},{24,26},{25,17},{26,18},{2... | collective-permute-start | bytes 829448 | tf_op jit(solution)/shard_map/ppermute | solution.py:47
  207.0 7.8 %collective-permute-start.32 = (bf16[1080,128]{1,0:T(8,128)(2,1)S(1)}, bf16[1080,128]{1,0:T(8,128)(2,1)S(1)}, u32[]{:S(2)}, u32[]{:S(2)}) collective-permute-start(bf16[1080,128]{1,0:T(8,128)(2,1)S(1)} %add_convert_fusion.14), channel_id=1, source_target_pairs={{0,8},{1,5},{8,16},{9,1},{16,24},{17,9},{24,26},{25,17},{26,18},{2... | collective-permute-start | bytes 829448 | tf_op jit(solution)/shard_map/ppermute | solution.py:47
  208.9 8.8 %collective-permute-start.17 = (bf16[1080,128]{1,0:T(8,128)(2,1)S(1)}, bf16[1080,128]{1,0:T(8,128)(2,1)S(1)}, u32[]{:S(2)}, u32[]{:S(2)}) collective-permute-start(bf16[1080,128]{1,0:T(8,128)(2,1)S(1)} %add_convert_fusion.28), channel_id=1, source_target_pairs={{0,8},{1,5},{8,16},{9,1},{16,24},{17,9},{24,26},{25,17},{26,18},{2... | collective-permute-start | bytes 829448 | tf_op jit(solution)/shard_map/ppermute | solution.py:47
  (8 other events, 242.1 us)

commit v8 on v7

--- a/solution.py
+++ b/solution.py
@@ -49,7 +49,7 @@
     return accs
 
 
-def _ffn_kernel(col_ref, cnt_ref, tok_ref, cot_ref, wgu_ref, wdt_ref,
+def _ffn_kernel(col_ref, cnt_ref, tok_ref, cot_ref, wg_ref, wu_ref, wd_ref,
                 gg_ref, gu_ref, gd_ref, dxt_ref):
     h = pl.program_id(0)
     slots = gg_ref.shape[1]
@@ -63,15 +63,18 @@
     offs = [pl.multiple_of(col_ref[h, p] * BLK, BLK) for p in range(slots)]
     x = jnp.concatenate([tok_ref[:, pl.ds(o, BLK)] for o in offs], axis=1)
     dy = jnp.concatenate([cot_ref[:, pl.ds(o, BLK)] for o in offs], axis=1)
-    wgu = wgu_ref[0]
-    wdt = wdt_ref[0]
-    live_gu = lax.broadcasted_iota(jnp.int32, wgu.shape, 0) < count * BLK
-    live_d = lax.broadcasted_iota(jnp.int32, wdt.shape, 0) < count * BLK
-    wgu = jnp.where(live_gu, wgu, jnp.zeros_like(wgu))
-    wdt = jnp.where(live_d, wdt, jnp.zeros_like(wdt))
-    gate_up = jnp.dot(x, wgu, preferred_element_type=f32)
-    gate, up = gate_up[:, :BLK], gate_up[:, BLK:]
-    d_hidden = jnp.dot(dy, wdt, preferred_element_type=f32)
+    stacked = (slots * BLK, BLK)
+    live_rows = lax.broadcasted_iota(jnp.int32, stacked, 0) < count * BLK
+    wg = wg_ref[0].reshape(stacked)
+    wu = wu_ref[0].reshape(stacked)
+    wg = jnp.where(live_rows, wg, jnp.zeros_like(wg))
+    wu = jnp.where(live_rows, wu, jnp.zeros_like(wu))
+    wd = jnp.concatenate([wd_ref[0, p] for p in range(slots)], axis=1)
+    live_cols = lax.broadcasted_iota(jnp.int32, wd.shape, 1) < count * BLK
+    wd = jnp.where(live_cols, wd, jnp.zeros_like(wd))
+    gate = jnp.dot(x, wg, preferred_element_type=f32)
+    up = jnp.dot(x, wu, preferred_element_type=f32)
+    d_hidden = lax.dot_general(dy, wd, (((1,), (1,)), ((), ())), preferred_element_type=f32)
     sig = 1.0 / (1.0 + jnp.exp(-gate))
     silu = gate * sig
     hidden = (silu * up).astype(jnp.bfloat16)
@@ -80,7 +83,8 @@
     d_gu = jnp.concatenate([d_gate, d_up], axis=1)
     grad_gu = jnp.dot(x.T, d_gu, preferred_element_type=f32)
     grad_d = jnp.dot(hidden.T, dy, preferred_element_type=f32)
-    back_t = jnp.dot(wgu, d_gu.T, preferred_element_type=f32)
+    back_t = jnp.dot(wg, d_gate.T, preferred_element_type=f32)
+    back_t = back_t + jnp.dot(wu, d_up.T, preferred_element_type=f32)
     for p in range(slots):
         live = p < count
         zero = jnp.zeros((BLK, BLK), f32)
@@ -94,8 +98,7 @@
 def ffn_block_terms(col_index, row_count, full_tok, full_cot, gate_w, up_w, down_w):
     hblk, slots = col_index.shape
     rows, width = full_tok.shape
-    wgu = jnp.concatenate([gate_w, up_w], axis=3).reshape(hblk, slots * BLK, 2 * BLK)
-    wdt = jnp.swapaxes(down_w, 2, 3).reshape(hblk, slots * BLK, BLK)
+    wspec = pl.BlockSpec((1, slots, BLK, BLK), lambda h, c, n: (h, 0, 0, 0))
     full = pl.BlockSpec((rows, width), lambda h, c, n: (0, 0))
     full_t = pl.BlockSpec((width, rows), lambda h, c, n: (0, 0))
     gspec = pl.BlockSpec((1, slots, BLK, BLK), lambda h, c, n: (h, 0, 0, 0))
@@ -106,12 +109,7 @@
         grid_spec=pltpu.PrefetchScalarGridSpec(
             num_scalar_prefetch=2,
             grid=(hblk,),
-            in_specs=[
-                full,
-                full,
-                pl.BlockSpec((1, slots * BLK, 2 * BLK), lambda h, c, n: (h, 0, 0)),
-                pl.BlockSpec((1, slots * BLK, BLK), lambda h, c, n: (h, 0, 0)),
-            ],
+            in_specs=[full, full, wspec, wspec, wspec],
             out_specs=[gspec, gspec, gspec, full_t],
         ),
         out_shape=[grad, grad, grad, jax.ShapeDtypeStruct((width, rows), jnp.float32)],
@@ -122,7 +120,7 @@
             bytes_accessed=3 * hblk * slots * BLK * BLK * 6 + rows * width * 8,
         ),
         name="ffn_block_terms",
-    )(col_index, row_count, full_tok, full_cot, wgu, wdt)
+    )(col_index, row_count, full_tok, full_cot, gate_w, up_w, down_w)
 
 
 def shards(n_dp, n_t, tokens, cotangent, w_gate, w_up, w_down, col_index, row_count, adam_m, adam_v):

time: 224 us -> 211 us (0.942)
  other arithmetic: 56.8 us -> 49.6 us
  local copies, waits for them, and re-layouts: 16.2 us -> 9.22 us
    concatenate x1 -> x0, other arithmetic: 8.29 us -> none  [ffn_block_terms(): jnp.concatenate([gate_w, up_w], axis=3).reshape(hblk, slots * BLK, 2 * BLK)]
    transpose x1 -> x0, local copies, waits for them, and re-layouts: 7.19 us -> none  [ffn_block_terms(): wdt = jnp.swapaxes(down_w, 2, 3).reshape(hblk, slots * BLK, BLK)]
  transfers between devices with their start and end apart: 48 -> 48, of which waited for: 35 -> 35; matrix products, arithmetic and copies ran while one was open for 30% -> 24% of each run, Pallas kernels for 0% -> 0%
where the time goes in v8:
time: 211 us; the launch traced here: 208 us
  starting transfers between devices  75.1 us (36%)
  other arithmetic  49.6 us (24%)
  Pallas kernels  33.1 us (16%)
  between operations  21.7 us (10%)
  waiting for transfers between devices  19.4 us (9%)
  local copies, waits for them, and re-layouts  9.22 us (4%)
    ppermute x45, starting transfers between devices, ring_reduce_scatter(): moved = lax.ppermute(accs[i].astype(wire_dtype), ('dp', 'tensor'), perm)  74 us
    convert_element_type x42, other arithmetic, ring_reduce_scatter(): moved = lax.ppermute(accs[i].astype(wire_dtype), ('dp', 'tensor'), perm)  38.7 us
    pallas_call x1, Pallas kernels, ffn_block_terms(): pl.pallas_call(_ffn_kernel, grid_spec=pltpu.PrefetchScalarGridSpec(num_sc...  33.1 us
    ppermute x45, waiting for transfers between devices, ring_reduce_scatter(): moved = lax.ppermute(accs[i].astype(wire_dtype), ('dp', 'tensor'), perm)  19.4 us
  transfers between devices with their start and end apart: 48, of which 35 were waited for; matrix products, arithmetic and copies ran while one was open for 24% of the time, Pallas kernels for 0%

profile of v8, /device:TPU:0, one launch (start us, length us, event | category | flops | bytes accessed | tf_op | source)
XLA Modules:
  0.0 208.2 jit_solution(14707158004442348059)
XLA Ops:
  13.2 2.0 fusion.2
  30.5 33.1 %ffn_block_terms.1 = (f32[27,5,128,128]{3,2,1,0:T(8,128)}, f32[27,5,128,128]{3,2,1,0:T(8,128)}, f32[27,5,128,128]{3,2,1,0:T(8,128)}, f32[5120,128]{1,0:T(8,128)}) custom-call(s32[27,5]{1,0:T(8,128)} %copy.15.col_ref, s32[27]{0:T(128)} %cnt_ref.1, bf16[128,5120]{1,0:T(8,128)(2,1)} %pad_maximum_fusion.1.tok_ref, bf16[128,5120]{1,0:T(8,128)(2,1)} %pad_maximum_fusion.2.cot_ref, ...), custom_call_target="tpu_custom_call" | custom-call | flops 5096079360 | bytes 45056000 | tf_op jit(solution)/shard_map/ffn_block_terms/pallas_call | solution.py:107
  63.7 1.8 fusion.1
  67.3 2.6 %collective-permute-start.33 = (bf16[1080,128]{1,0:T(8,128)(2,1)S(1)}, bf16[1080,128]{1,0:T(8,128)(2,1)S(1)}, u32[]{:S(2)}, u32[]{:S(2)}) collective-permute-start(bf16[1080,128]{1,0:T(8,128)(2,1)S(1)} %dynamic-slice_convert_fusion), channel_id=1, source_target_pairs={{0,8},{1,5},{8,16},{9,1},{16,24},{17,9},{24,26},{25,17},{26,18},{2... | collective-permute-start | bytes 829448 | tf_op jit(solution)/shard_map/ppermute | solution.py:47
  71.0 1.6 collective-permute-start.18
  73.7 1.6 collective-permute-start.3
  81.7 1.8 collective-permute-start.4
  84.7 1.8 collective-permute-start.35
  87.6 1.8 collective-permute-start.20
  90.7 1.8 collective-permute-start.5
  95.0 1.6 collective-permute-start.36
  97.8 1.6 collective-permute-start.21
  100.5 1.6 collective-permute-start.6
  105.7 1.6 collective-permute-start.22
  108.7 1.6 collective-permute-start.7
  111.6 1.6 collective-permute-start.38
  114.6 1.6 collective-permute-start.23
  117.6 1.6 collective-permute-start.8
  120.5 1.6 collective-permute-start.39
  123.5 1.6 collective-permute-start.24
  126.4 1.6 collective-permute-start.9
  129.4 1.6 collective-permute-start.40
  132.4 1.6 collective-permute-start.25
  134.3 1.6 collective-permute-start.10
  138.3 1.6 collective-permute-start.41
  141.3 1.6 collective-permute-start.26
  143.2 1.6 collective-permute-start.11
  147.2 1.6 collective-permute-start.42
  150.1 1.6 collective-permute-start.27
  152.1 1.6 collective-permute-start.12
  156.1 1.6 collective-permute-start.43
  159.0 1.6 collective-permute-start.28
  160.9 1.6 collective-permute-start.13
  165.0 1.6 collective-permute-start.44
  167.9 1.6 collective-permute-start.29
  169.8 1.6 collective-permute-start.14
  173.8 1.6 collective-permute-start.45
  176.8 1.6 collective-permute-start.30
  178.7 1.6 collective-permute-start.15
  182.7 1.6 collective-permute-start.46
  185.7 1.6 collective-permute-start.31
  187.6 1.6 collective-permute-start.16
  191.6 1.6 collective-permute-start.47
  194.6 1.6 collective-permute-start.32
  196.5 1.6 collective-permute-start.17
  200.5 1.9 collective-permute-done.32
  203.5 1.9 collective-permute-done.17
  205.4 2.8 %add_divide_fusion = (f32[3,1,1080,128]{3,2,1,0:T(8,128)}, f32[3,1,1080,128]{3,2,1,0:T(8,128)}, f32[3,1,1080,128]{3,2,1,0:T(8,128)}) fusion(f32[1,1,1080,128]{3,2,1,0:T(8,128)S(1)} %add_bitcast_fusion, f32[1,1,1080,128]{3,2,1,0:T(8,128)S(1)} %add_bitcast_fusion.1, f32[1,1,1080,128]{3,2,1,0:T(8,128)S(1)} %add_bitcast_fusion.2, ...), kind=kLoop, calls=%fused_computation.1 | loop fusion | flops 4976640 | bytes 9953280 | tf_op jit(solution)/shard_map/div | solution.py:168
  (120 shorter events, 73.2 us)
Async XLA Ops:
  0.6 26.1 %collective-permute-start.1 = (bf16[128,2560]{1,0:T(8,128)(2,1)}, bf16[128,2560]{1,0:T(8,128)(2,1)S(1)}, u32[]{:S(2)}, u32[]{:S(2)}) collective-permute-start(bf16[128,2560]{1,0:T(8,128)(2,1)} %param.12), channel_id=1, source_target_pairs={{0,1},{1,0},{2,3},{3,2},{4,5},{5,4},{6,7},{7,6},{8,9},{9,8},{10,11... | collective-permute-start | bytes 1966088 | tf_op jit(solution)/shard_map/ppermute | solution.py:130
  1.1 25.6 %collective-permute-start = (bf16[128,2560]{1,0:T(8,128)(2,1)}, bf16[128,2560]{1,0:T(8,128)(2,1)S(1)}, u32[]{:S(2)}, u32[]{:S(2)}) collective-permute-start(bf16[128,2560]{1,0:T(8,128)(2,1)} %param.11), channel_id=1, source_target_pairs={{0,1},{1,0},{2,3},{3,2},{4,5},{5,4},{6,7},{7,6},{8,9},{9,8},{10,11... | collective-permute-start | bytes 1966088 | tf_op jit(solution)/shard_map/ppermute | solution.py:130
  65.5 27.0 %collective-permute-start.2 = (bf16[128,2560]{0,1:T(8,128)(2,1)S(1)}, bf16[128,2560]{0,1:T(8,128)(2,1)S(1)}, u32[]{:S(2)}, u32[]{:S(2)}) collective-permute-start(bf16[128,2560]{0,1:T(8,128)(2,1)S(1)} %fusion.1), channel_id=1, source_target_pairs={{0,1},{1,0},{2,3},{3,2},{4,5},{5,4},{6,7},{7,6},{8,9},{9,8},{10,11... | collective-permute-start | bytes 1966088 | tf_op jit(solution)/shard_map/ppermute | solution.py:158
  67.3 8.0 %collective-permute-start.33 = (bf16[1080,128]{1,0:T(8,128)(2,1)S(1)}, bf16[1080,128]{1,0:T(8,128)(2,1)S(1)}, u32[]{:S(2)}, u32[]{:S(2)}) collective-permute-start(bf16[1080,128]{1,0:T(8,128)(2,1)S(1)} %dynamic-slice_convert_fusion), channel_id=1, source_target_pairs={{0,8},{1,5},{8,16},{9,1},{16,24},{17,9},{24,26},{25,17},{26,18},{2... | collective-permute-start | bytes 829448 | tf_op jit(solution)/shard_map/ppermute | solution.py:47
  71.0 7.0 %collective-permute-start.18 = (bf16[1080,128]{1,0:T(8,128)(2,1)S(1)}, bf16[1080,128]{1,0:T(8,128)(2,1)S(1)}, u32[]{:S(2)}, u32[]{:S(2)}) collective-permute-start(bf16[1080,128]{1,0:T(8,128)(2,1)S(1)} %dynamic-slice_convert_fusion.1), channel_id=1, source_target_pairs={{0,8},{1,5},{8,16},{9,1},{16,24},{17,9},{24,26},{25,17},{26,18},{2... | collective-permute-start | bytes 829448 | tf_op jit(solution)/shard_map/ppermute | solution.py:47
  73.7 6.9 %collective-permute-start.3 = (bf16[1080,128]{1,0:T(8,128)(2,1)S(1)}, bf16[1080,128]{1,0:T(8,128)(2,1)S(1)}, u32[]{:S(2)}, u32[]{:S(2)}) collective-permute-start(bf16[1080,128]{1,0:T(8,128)(2,1)S(1)} %dynamic-slice_convert_fusion.2), channel_id=1, source_target_pairs={{0,8},{1,5},{8,16},{9,1},{16,24},{17,9},{24,26},{25,17},{26,18},{2... | collective-permute-start | bytes 829448 | tf_op jit(solution)/shard_map/ppermute | solution.py:47
  76.5 7.1 %collective-permute-start.34 = (bf16[1080,128]{1,0:T(8,128)(2,1)S(1)}, bf16[1080,128]{1,0:T(8,128)(2,1)S(1)}, u32[]{:S(2)}, u32[]{:S(2)}) collective-permute-start(bf16[1080,128]{1,0:T(8,128)(2,1)S(1)} %add_convert_fusion.13), channel_id=1, source_target_pairs={{0,8},{1,5},{8,16},{9,1},{16,24},{17,9},{24,26},{25,17},{26,18},{2... | collective-permute-start | bytes 829448 | tf_op jit(solution)/shard_map/ppermute | solution.py:47
  79.2 7.4 %collective-permute-start.19 = (bf16[1080,128]{1,0:T(8,128)(2,1)S(1)}, bf16[1080,128]{1,0:T(8,128)(2,1)S(1)}, u32[]{:S(2)}, u32[]{:S(2)}) collective-permute-start(bf16[1080,128]{1,0:T(8,128)(2,1)S(1)} %add_convert_fusion.27), channel_id=1, source_target_pairs={{0,8},{1,5},{8,16},{9,1},{16,24},{17,9},{24,26},{25,17},{26,18},{2... | collective-permute-start | bytes 829448 | tf_op jit(solution)/shard_map/ppermute | solution.py:47
  81.7 7.8 %collective-permute-start.4 = (bf16[1080,128]{1,0:T(8,128)(2,1)S(1)}, bf16[1080,128]{1,0:T(8,128)(2,1)S(1)}, u32[]{:S(2)}, u32[]{:S(2)}) collective-permute-start(bf16[1080,128]{1,0:T(8,128)(2,1)S(1)} %add_convert_fusion.41), channel_id=1, source_target_pairs={{0,8},{1,5},{8,16},{9,1},{16,24},{17,9},{24,26},{25,17},{26,18},{2... | collective-permute-start | bytes 829448 | tf_op jit(solution)/shard_map/ppermute | solution.py:47
  84.7 9.1 %collective-permute-start.35 = (bf16[1080,128]{1,0:T(8,128)(2,1)S(1)}, bf16[1080,128]{1,0:T(8,128)(2,1)S(1)}, u32[]{:S(2)}, u32[]{:S(2)}) collective-permute-start(bf16[1080,128]{1,0:T(8,128)(2,1)S(1)} %add_convert_fusion.12), channel_id=1, source_target_pairs={{0,8},{1,5},{8,16},{9,1},{16,24},{17,9},{24,26},{25,17},{26,18},{2... | collective-permute-start | bytes 829448 | tf_op jit(solution)/shard_map/ppermute | solution.py:47
  87.6 9.0 %collective-permute-start.20 = (bf16[1080,128]{1,0:T(8,128)(2,1)S(1)}, bf16[1080,128]{1,0:T(8,128)(2,1)S(1)}, u32[]{:S(2)}, u32[]{:S(2)}) collective-permute-start(bf16[1080,128]{1,0:T(8,128)(2,1)S(1)} %add_convert_fusion.26), channel_id=1, source_target_pairs={{0,8},{1,5},{8,16},{9,1},{16,24},{17,9},{24,26},{25,17},{26,18},{2... | collective-permute-start | bytes 829448 | tf_op jit(solution)/shard_map/ppermute | solution.py:47
  90.7 8.7 %collective-permute-start.5 = (bf16[1080,128]{1,0:T(8,128)(2,1)S(1)}, bf16[1080,128]{1,0:T(8,128)(2,1)S(1)}, u32[]{:S(2)}, u32[]{:S(2)}) collective-permute-start(bf16[1080,128]{1,0:T(8,128)(2,1)S(1)} %add_convert_fusion.40), channel_id=1, source_target_pairs={{0,8},{1,5},{8,16},{9,1},{16,24},{17,9},{24,26},{25,17},{26,18},{2... | collective-permute-start | bytes 829448 | tf_op jit(solution)/shard_map/ppermute | solution.py:47
  95.0 7.0 %collective-permute-start.36 = (bf16[1080,128]{1,0:T(8,128)(2,1)S(1)}, bf16[1080,128]{1,0:T(8,128)(2,1)S(1)}, u32[]{:S(2)}, u32[]{:S(2)}) collective-permute-start(bf16[1080,128]{1,0:T(8,128)(2,1)S(1)} %add_convert_fusion.11), channel_id=1, source_target_pairs={{0,8},{1,5},{8,16},{9,1},{16,24},{17,9},{24,26},{25,17},{26,18},{2... | collective-permute-start | bytes 829448 | tf_op jit(solution)/shard_map/ppermute | solution.py:47
  97.8 6.8 %collective-permute-start.21 = (bf16[1080,128]{1,0:T(8,128)(2,1)S(1)}, bf16[1080,128]{1,0:T(8,128)(2,1)S(1)}, u32[]{:S(2)}, u32[]{:S(2)}) collective-permute-start(bf16[1080,128]{1,0:T(8,128)(2,1)S(1)} %add_convert_fusion.25), channel_id=1, source_target_pairs={{0,8},{1,5},{8,16},{9,1},{16,24},{17,9},{24,26},{25,17},{26,18},{2... | collective-permute-start | bytes 829448 | tf_op jit(solution)/shard_map/ppermute | solution.py:47
  100.5 7.0 %collective-permute-start.6 = (bf16[1080,128]{1,0:T(8,128)(2,1)S(1)}, bf16[1080,128]{1,0:T(8,128)(2,1)S(1)}, u32[]{:S(2)}, u32[]{:S(2)}) collective-permute-start(bf16[1080,128]{1,0:T(8,128)(2,1)S(1)} %add_convert_fusion.39), channel_id=1, source_target_pairs={{0,8},{1,5},{8,16},{9,1},{16,24},{17,9},{24,26},{25,17},{26,18},{2... | collective-permute-start | bytes 829448 | tf_op jit(solution)/shard_map/ppermute | solution.py:47
  103.2 7.3 %collective-permute-start.37 = (bf16[1080,128]{1,0:T(8,128)(2,1)S(1)}, bf16[1080,128]{1,0:T(8,128)(2,1)S(1)}, u32[]{:S(2)}, u32[]{:S(2)}) collective-permute-start(bf16[1080,128]{1,0:T(8,128)(2,1)S(1)} %add_convert_fusion.10), channel_id=1, source_target_pairs={{0,8},{1,5},{8,16},{9,1},{16,24},{17,9},{24,26},{25,17},{26,18},{2... | collective-permute-start | bytes 829448 | tf_op jit(solution)/shard_map/ppermute | solution.py:47
  105.7 7.8 %collective-permute-start.22 = (bf16[1080,128]{1,0:T(8,128)(2,1)S(1)}, bf16[1080,128]{1,0:T(8,128)(2,1)S(1)}, u32[]{:S(2)}, u32[]{:S(2)}) collective-permute-start(bf16[1080,128]{1,0:T(8,128)(2,1)S(1)} %add_convert_fusion.24), channel_id=1, source_target_pairs={{0,8},{1,5},{8,16},{9,1},{16,24},{17,9},{24,26},{25,17},{26,18},{2... | collective-permute-start | bytes 829448 | tf_op jit(solution)/shard_map/ppermute | solution.py:47
  108.7 7.8 %collective-permute-start.7 = (bf16[1080,128]{1,0:T(8,128)(2,1)S(1)}, bf16[1080,128]{1,0:T(8,128)(2,1)S(1)}, u32[]{:S(2)}, u32[]{:S(2)}) collective-permute-start(bf16[1080,128]{1,0:T(8,128)(2,1)S(1)} %add_convert_fusion.38), channel_id=1, source_target_pairs={{0,8},{1,5},{8,16},{9,1},{16,24},{17,9},{24,26},{25,17},{26,18},{2... | collective-permute-start | bytes 829448 | tf_op jit(solution)/shard_map/ppermute | solution.py:47
  111.6 7.8 %collective-permute-start.38 = (bf16[1080,128]{1,0:T(8,128)(2,1)S(1)}, bf16[1080,128]{1,0:T(8,128)(2,1)S(1)}, u32[]{:S(2)}, u32[]{:S(2)}) collective-permute-start(bf16[1080,128]{1,0:T(8,128)(2,1)S(1)} %add_convert_fusion.9), channel_id=1, source_target_pairs={{0,8},{1,5},{8,16},{9,1},{16,24},{17,9},{24,26},{25,17},{26,18},{2... | collective-permute-start | bytes 829448 | tf_op jit(solution)/shard_map/ppermute | solution.py:47
  114.6 7.8 %collective-permute-start.23 = (bf16[1080,128]{1,0:T(8,128)(2,1)S(1)}, bf16[1080,128]{1,0:T(8,128)(2,1)S(1)}, u32[]{:S(2)}, u32[]{:S(2)}) collective-permute-start(bf16[1080,128]{1,0:T(8,128)(2,1)S(1)} %add_convert_fusion.23), channel_id=1, source_target_pairs={{0,8},{1,5},{8,16},{9,1},{16,24},{17,9},{24,26},{25,17},{26,18},{2... | collective-permute-start | bytes 829448 | tf_op jit(solution)/shard_map/ppermute | solution.py:47
  117.6 7.8 %collective-permute-start.8 = (bf16[1080,128]{1,0:T(8,128)(2,1)S(1)}, bf16[1080,128]{1,0:T(8,128)(2,1)S(1)}, u32[]{:S(2)}, u32[]{:S(2)}) collective-permute-start(bf16[1080,128]{1,0:T(8,128)(2,1)S(1)} %add_convert_fusion.37), channel_id=1, source_target_pairs={{0,8},{1,5},{8,16},{9,1},{16,24},{17,9},{24,26},{25,17},{26,18},{2... | collective-permute-start | bytes 829448 | tf_op jit(solution)/shard_map/ppermute | solution.py:47
  120.5 7.8 %collective-permute-start.39 = (bf16[1080,128]{1,0:T(8,128)(2,1)S(1)}, bf16[1080,128]{1,0:T(8,128)(2,1)S(1)}, u32[]{:S(2)}, u32[]{:S(2)}) collective-permute-start(bf16[1080,128]{1,0:T(8,128)(2,1)S(1)} %add_convert_fusion.8), channel_id=1, source_target_pairs={{0,8},{1,5},{8,16},{9,1},{16,24},{17,9},{24,26},{25,17},{26,18},{2... | collective-permute-start | bytes 829448 | tf_op jit(solution)/shard_map/ppermute | solution.py:47
  123.5 7.8 %collective-permute-start.24 = (bf16[1080,128]{1,0:T(8,128)(2,1)S(1)}, bf16[1080,128]{1,0:T(8,128)(2,1)S(1)}, u32[]{:S(2)}, u32[]{:S(2)}) collective-permute-start(bf16[1080,128]{1,0:T(8,128)(2,1)S(1)} %add_convert_fusion.22), channel_id=1, source_target_pairs={{0,8},{1,5},{8,16},{9,1},{16,24},{17,9},{24,26},{25,17},{26,18},{2... | collective-permute-start | bytes 829448 | tf_op jit(solution)/shard_map/ppermute | solution.py:47
  126.4 7.8 %collective-permute-start.9 = (bf16[1080,128]{1,0:T(8,128)(2,1)S(1)}, bf16[1080,128]{1,0:T(8,128)(2,1)S(1)}, u32[]{:S(2)}, u32[]{:S(2)}) collective-permute-start(bf16[1080,128]{1,0:T(8,128)(2,1)S(1)} %add_convert_fusion.36), channel_id=1, source_target_pairs={{0,8},{1,5},{8,16},{9,1},{16,24},{17,9},{24,26},{25,17},{26,18},{2... | collective-permute-start | bytes 829448 | tf_op jit(solution)/shard_map/ppermute | solution.py:47
  129.4 7.8 %collective-permute-start.40 = (bf16[1080,128]{1,0:T(8,128)(2,1)S(1)}, bf16[1080,128]{1,0:T(8,128)(2,1)S(1)}, u32[]{:S(2)}, u32[]{:S(2)}) collective-permute-start(bf16[1080,128]{1,0:T(8,128)(2,1)S(1)} %add_convert_fusion.7), channel_id=1, source_target_pairs={{0,8},{1,5},{8,16},{9,1},{16,24},{17,9},{24,26},{25,17},{26,18},{2... | collective-permute-start | bytes 829448 | tf_op jit(solution)/shard_map/ppermute | solution.py:47
  132.4 7.8 %collective-permute-start.25 = (bf16[1080,128]{1,0:T(8,128)(2,1)S(1)}, bf16[1080,128]{1,0:T(8,128)(2,1)S(1)}, u32[]{:S(2)}, u32[]{:S(2)}) collective-permute-start(bf16[1080,128]{1,0:T(8,128)(2,1)S(1)} %add_convert_fusion.21), channel_id=1, source_target_pairs={{0,8},{1,5},{8,16},{9,1},{16,24},{17,9},{24,26},{25,17},{26,18},{2... | collective-permute-start | bytes 829448 | tf_op jit(solution)/shard_map/ppermute | solution.py:47
  134.3 8.8 %collective-permute-start.10 = (bf16[1080,128]{1,0:T(8,128)(2,1)S(1)}, bf16[1080,128]{1,0:T(8,128)(2,1)S(1)}, u32[]{:S(2)}, u32[]{:S(2)}) collective-permute-start(bf16[1080,128]{1,0:T(8,128)(2,1)S(1)} %add_convert_fusion.35), channel_id=1, source_target_pairs={{0,8},{1,5},{8,16},{9,1},{16,24},{17,9},{24,26},{25,17},{26,18},{2... | collective-permute-start | bytes 829448 | tf_op jit(solution)/shard_map/ppermute | solution.py:47
  138.3 7.8 %collective-permute-start.41 = (bf16[1080,128]{1,0:T(8,128)(2,1)S(1)}, bf16[1080,128]{1,0:T(8,128)(2,1)S(1)}, u32[]{:S(2)}, u32[]{:S(2)}) collective-permute-start(bf16[1080,128]{1,0:T(8,128)(2,1)S(1)} %add_convert_fusion.6), channel_id=1, source_target_pairs={{0,8},{1,5},{8,16},{9,1},{16,24},{17,9},{24,26},{25,17},{26,18},{2... | collective-permute-start | bytes 829448 | tf_op jit(solution)/shard_map/ppermute | solution.py:47
  141.3 7.8 %collective-permute-start.26 = (bf16[1080,128]{1,0:T(8,128)(2,1)S(1)}, bf16[1080,128]{1,0:T(8,128)(2,1)S(1)}, u32[]{:S(2)}, u32[]{:S(2)}) collective-permute-start(bf16[1080,128]{1,0:T(8,128)(2,1)S(1)} %add_convert_fusion.20), channel_id=1, source_target_pairs={{0,8},{1,5},{8,16},{9,1},{16,24},{17,9},{24,26},{25,17},{26,18},{2... | collective-permute-start | bytes 829448 | tf_op jit(solution)/shard_map/ppermute | solution.py:47
  143.2 8.8 %collective-permute-start.11 = (bf16[1080,128]{1,0:T(8,128)(2,1)S(1)}, bf16[1080,128]{1,0:T(8,128)(2,1)S(1)}, u32[]{:S(2)}, u32[]{:S(2)}) collective-permute-start(bf16[1080,128]{1,0:T(8,128)(2,1)S(1)} %add_convert_fusion.34), channel_id=1, source_target_pairs={{0,8},{1,5},{8,16},{9,1},{16,24},{17,9},{24,26},{25,17},{26,18},{2... | collective-permute-start | bytes 829448 | tf_op jit(solution)/shard_map/ppermute | solution.py:47
  147.2 7.8 %collective-permute-start.42 = (bf16[1080,128]{1,0:T(8,128)(2,1)S(1)}, bf16[1080,128]{1,0:T(8,128)(2,1)S(1)}, u32[]{:S(2)}, u32[]{:S(2)}) collective-permute-start(bf16[1080,128]{1,0:T(8,128)(2,1)S(1)} %add_convert_fusion.5), channel_id=1, source_target_pairs={{0,8},{1,5},{8,16},{9,1},{16,24},{17,9},{24,26},{25,17},{26,18},{2... | collective-permute-start | bytes 829448 | tf_op jit(solution)/shard_map/ppermute | solution.py:47
  150.1 7.8 %collective-permute-start.27 = (bf16[1080,128]{1,0:T(8,128)(2,1)S(1)}, bf16[1080,128]{1,0:T(8,128)(2,1)S(1)}, u32[]{:S(2)}, u32[]{:S(2)}) collective-permute-start(bf16[1080,128]{1,0:T(8,128)(2,1)S(1)} %add_convert_fusion.19), channel_id=1, source_target_pairs={{0,8},{1,5},{8,16},{9,1},{16,24},{17,9},{24,26},{25,17},{26,18},{2... | collective-permute-start | bytes 829448 | tf_op jit(solution)/shard_map/ppermute | solution.py:47
  152.1 8.8 %collective-permute-start.12 = (bf16[1080,128]{1,0:T(8,128)(2,1)S(1)}, bf16[1080,128]{1,0:T(8,128)(2,1)S(1)}, u32[]{:S(2)}, u32[]{:S(2)}) collective-permute-start(bf16[1080,128]{1,0:T(8,128)(2,1)S(1)} %add_convert_fusion.33), channel_id=1, source_target_pairs={{0,8},{1,5},{8,16},{9,1},{16,24},{17,9},{24,26},{25,17},{26,18},{2... | collective-permute-start | bytes 829448 | tf_op jit(solution)/shard_map/ppermute | solution.py:47
  156.1 7.8 %collective-permute-start.43 = (bf16[1080,128]{1,0:T(8,128)(2,1)S(1)}, bf16[1080,128]{1,0:T(8,128)(2,1)S(1)}, u32[]{:S(2)}, u32[]{:S(2)}) collective-permute-start(bf16[1080,128]{1,0:T(8,128)(2,1)S(1)} %add_convert_fusion.4), channel_id=1, source_target_pairs={{0,8},{1,5},{8,16},{9,1},{16,24},{17,9},{24,26},{25,17},{26,18},{2... | collective-permute-start | bytes 829448 | tf_op jit(solution)/shard_map/ppermute | solution.py:47
  159.0 7.8 %collective-permute-start.28 = (bf16[1080,128]{1,0:T(8,128)(2,1)S(1)}, bf16[1080,128]{1,0:T(8,128)(2,1)S(1)}, u32[]{:S(2)}, u32[]{:S(2)}) collective-permute-start(bf16[1080,128]{1,0:T(8,128)(2,1)S(1)} %add_convert_fusion.18), channel_id=1, source_target_pairs={{0,8},{1,5},{8,16},{9,1},{16,24},{17,9},{24,26},{25,17},{26,18},{2... | collective-permute-start | bytes 829448 | tf_op jit(solution)/shard_map/ppermute | solution.py:47
  160.9 8.8 %collective-permute-start.13 = (bf16[1080,128]{1,0:T(8,128)(2,1)S(1)}, bf16[1080,128]{1,0:T(8,128)(2,1)S(1)}, u32[]{:S(2)}, u32[]{:S(2)}) collective-permute-start(bf16[1080,128]{1,0:T(8,128)(2,1)S(1)} %add_convert_fusion.32), channel_id=1, source_target_pairs={{0,8},{1,5},{8,16},{9,1},{16,24},{17,9},{24,26},{25,17},{26,18},{2... | collective-permute-start | bytes 829448 | tf_op jit(solution)/shard_map/ppermute | solution.py:47
  165.0 7.8 %collective-permute-start.44 = (bf16[1080,128]{1,0:T(8,128)(2,1)S(1)}, bf16[1080,128]{1,0:T(8,128)(2,1)S(1)}, u32[]{:S(2)}, u32[]{:S(2)}) collective-permute-start(bf16[1080,128]{1,0:T(8,128)(2,1)S(1)} %add_convert_fusion.3), channel_id=1, source_target_pairs={{0,8},{1,5},{8,16},{9,1},{16,24},{17,9},{24,26},{25,17},{26,18},{2... | collective-permute-start | bytes 829448 | tf_op jit(solution)/shard_map/ppermute | solution.py:47
  167.9 7.8 %collective-permute-start.29 = (bf16[1080,128]{1,0:T(8,128)(2,1)S(1)}, bf16[1080,128]{1,0:T(8,128)(2,1)S(1)}, u32[]{:S(2)}, u32[]{:S(2)}) collective-permute-start(bf16[1080,128]{1,0:T(8,128)(2,1)S(1)} %add_convert_fusion.17), channel_id=1, source_target_pairs={{0,8},{1,5},{8,16},{9,1},{16,24},{17,9},{24,26},{25,17},{26,18},{2... | collective-permute-start | bytes 829448 | tf_op jit(solution)/shard_map/ppermute | solution.py:47
  169.8 8.8 %collective-permute-start.14 = (bf16[1080,128]{1,0:T(8,128)(2,1)S(1)}, bf16[1080,128]{1,0:T(8,128)(2,1)S(1)}, u32[]{:S(2)}, u32[]{:S(2)}) collective-permute-start(bf16[1080,128]{1,0:T(8,128)(2,1)S(1)} %add_convert_fusion.31), channel_id=1, source_target_pairs={{0,8},{1,5},{8,16},{9,1},{16,24},{17,9},{24,26},{25,17},{26,18},{2... | collective-permute-start | bytes 829448 | tf_op jit(solution)/shard_map/ppermute | solution.py:47
  173.8 7.8 %collective-permute-start.45 = (bf16[1080,128]{1,0:T(8,128)(2,1)S(1)}, bf16[1080,128]{1,0:T(8,128)(2,1)S(1)}, u32[]{:S(2)}, u32[]{:S(2)}) collective-permute-start(bf16[1080,128]{1,0:T(8,128)(2,1)S(1)} %add_convert_fusion.2), channel_id=1, source_target_pairs={{0,8},{1,5},{8,16},{9,1},{16,24},{17,9},{24,26},{25,17},{26,18},{2... | collective-permute-start | bytes 829448 | tf_op jit(solution)/shard_map/ppermute | solution.py:47
  176.8 7.8 %collective-permute-start.30 = (bf16[1080,128]{1,0:T(8,128)(2,1)S(1)}, bf16[1080,128]{1,0:T(8,128)(2,1)S(1)}, u32[]{:S(2)}, u32[]{:S(2)}) collective-permute-start(bf16[1080,128]{1,0:T(8,128)(2,1)S(1)} %add_convert_fusion.16), channel_id=1, source_target_pairs={{0,8},{1,5},{8,16},{9,1},{16,24},{17,9},{24,26},{25,17},{26,18},{2... | collective-permute-start | bytes 829448 | tf_op jit(solution)/shard_map/ppermute | solution.py:47
  178.7 8.8 %collective-permute-start.15 = (bf16[1080,128]{1,0:T(8,128)(2,1)S(1)}, bf16[1080,128]{1,0:T(8,128)(2,1)S(1)}, u32[]{:S(2)}, u32[]{:S(2)}) collective-permute-start(bf16[1080,128]{1,0:T(8,128)(2,1)S(1)} %add_convert_fusion.30), channel_id=1, source_target_pairs={{0,8},{1,5},{8,16},{9,1},{16,24},{17,9},{24,26},{25,17},{26,18},{2... | collective-permute-start | bytes 829448 | tf_op jit(solution)/shard_map/ppermute | solution.py:47
  182.7 7.8 %collective-permute-start.46 = (bf16[1080,128]{1,0:T(8,128)(2,1)S(1)}, bf16[1080,128]{1,0:T(8,128)(2,1)S(1)}, u32[]{:S(2)}, u32[]{:S(2)}) collective-permute-start(bf16[1080,128]{1,0:T(8,128)(2,1)S(1)} %add_convert_fusion.1), channel_id=1, source_target_pairs={{0,8},{1,5},{8,16},{9,1},{16,24},{17,9},{24,26},{25,17},{26,18},{2... | collective-permute-start | bytes 829448 | tf_op jit(solution)/shard_map/ppermute | solution.py:47
  185.7 7.7 %collective-permute-start.31 = (bf16[1080,128]{1,0:T(8,128)(2,1)S(1)}, bf16[1080,128]{1,0:T(8,128)(2,1)S(1)}, u32[]{:S(2)}, u32[]{:S(2)}) collective-permute-start(bf16[1080,128]{1,0:T(8,128)(2,1)S(1)} %add_convert_fusion.15), channel_id=1, source_target_pairs={{0,8},{1,5},{8,16},{9,1},{16,24},{17,9},{24,26},{25,17},{26,18},{2... | collective-permute-start | bytes 829448 | tf_op jit(solution)/shard_map/ppermute | solution.py:47
  187.6 8.8 %collective-permute-start.16 = (bf16[1080,128]{1,0:T(8,128)(2,1)S(1)}, bf16[1080,128]{1,0:T(8,128)(2,1)S(1)}, u32[]{:S(2)}, u32[]{:S(2)}) collective-permute-start(bf16[1080,128]{1,0:T(8,128)(2,1)S(1)} %add_convert_fusion.29), channel_id=1, source_target_pairs={{0,8},{1,5},{8,16},{9,1},{16,24},{17,9},{24,26},{25,17},{26,18},{2... | collective-permute-start | bytes 829448 | tf_op jit(solution)/shard_map/ppermute | solution.py:47
  191.6 7.8 %collective-permute-start.47 = (bf16[1080,128]{1,0:T(8,128)(2,1)S(1)}, bf16[1080,128]{1,0:T(8,128)(2,1)S(1)}, u32[]{:S(2)}, u32[]{:S(2)}) collective-permute-start(bf16[1080,128]{1,0:T(8,128)(2,1)S(1)} %add_convert_fusion), channel_id=1, source_target_pairs={{0,8},{1,5},{8,16},{9,1},{16,24},{17,9},{24,26},{25,17},{26,18},{2... | collective-permute-start | bytes 829448 | tf_op jit(solution)/shard_map/ppermute | solution.py:47
  194.6 7.8 %collective-permute-start.32 = (bf16[1080,128]{1,0:T(8,128)(2,1)S(1)}, bf16[1080,128]{1,0:T(8,128)(2,1)S(1)}, u32[]{:S(2)}, u32[]{:S(2)}) collective-permute-start(bf16[1080,128]{1,0:T(8,128)(2,1)S(1)} %add_convert_fusion.14), channel_id=1, source_target_pairs={{0,8},{1,5},{8,16},{9,1},{16,24},{17,9},{24,26},{25,17},{26,18},{2... | collective-permute-start | bytes 829448 | tf_op jit(solution)/shard_map/ppermute | solution.py:47
  196.5 8.8 %collective-permute-start.17 = (bf16[1080,128]{1,0:T(8,128)(2,1)S(1)}, bf16[1080,128]{1,0:T(8,128)(2,1)S(1)}, u32[]{:S(2)}, u32[]{:S(2)}) collective-permute-start(bf16[1080,128]{1,0:T(8,128)(2,1)S(1)} %add_convert_fusion.28), channel_id=1, source_target_pairs={{0,8},{1,5},{8,16},{9,1},{16,24},{17,9},{24,26},{25,17},{26,18},{2... | collective-permute-start | bytes 829448 | tf_op jit(solution)/shard_map/ppermute | solution.py:47
  (6 other events, 174.1 us)

commit v9 on v8

--- a/solution.py
+++ b/solution.py
@@ -49,27 +49,20 @@
     return accs
 
 
-def _ffn_kernel(col_ref, cnt_ref, tok_ref, cot_ref, wg_ref, wu_ref, wd_ref,
-                gg_ref, gu_ref, gd_ref, dxt_ref):
-    h = pl.program_id(0)
+def _ffn_block(hh, h, count, col_ref, tok_ref, cot_ref, wg_ref, wu_ref, wd_ref,
+               gg_ref, gu_ref, gd_ref, dxt_ref):
     slots = gg_ref.shape[1]
-    count = cnt_ref[h]
-
-    @pl.when(h == 0)
-    def _():
-        dxt_ref[...] = jnp.zeros_like(dxt_ref)
-
     f32 = jnp.float32
     offs = [pl.multiple_of(col_ref[h, p] * BLK, BLK) for p in range(slots)]
     x = jnp.concatenate([tok_ref[:, pl.ds(o, BLK)] for o in offs], axis=1)
     dy = jnp.concatenate([cot_ref[:, pl.ds(o, BLK)] for o in offs], axis=1)
     stacked = (slots * BLK, BLK)
     live_rows = lax.broadcasted_iota(jnp.int32, stacked, 0) < count * BLK
-    wg = wg_ref[0].reshape(stacked)
-    wu = wu_ref[0].reshape(stacked)
+    wg = wg_ref[hh].reshape(stacked)
+    wu = wu_ref[hh].reshape(stacked)
     wg = jnp.where(live_rows, wg, jnp.zeros_like(wg))
     wu = jnp.where(live_rows, wu, jnp.zeros_like(wu))
-    wd = jnp.concatenate([wd_ref[0, p] for p in range(slots)], axis=1)
+    wd = jnp.concatenate([wd_ref[hh, p] for p in range(slots)], axis=1)
     live_cols = lax.broadcasted_iota(jnp.int32, wd.shape, 1) < count * BLK
     wd = jnp.where(live_cols, wd, jnp.zeros_like(wd))
     gate = jnp.dot(x, wg, preferred_element_type=f32)
@@ -89,26 +82,42 @@
         live = p < count
         zero = jnp.zeros((BLK, BLK), f32)
         rows = slice(p * BLK, (p + 1) * BLK)
-        gg_ref[0, p] = jnp.where(live, grad_gu[rows, :BLK], zero)
-        gu_ref[0, p] = jnp.where(live, grad_gu[rows, BLK:], zero)
-        gd_ref[0, p] = jnp.where(live, grad_d[:, rows], zero)
+        gg_ref[hh, p] = jnp.where(live, grad_gu[rows, :BLK], zero)
+        gu_ref[hh, p] = jnp.where(live, grad_gu[rows, BLK:], zero)
+        gd_ref[hh, p] = jnp.where(live, grad_d[:, rows], zero)
         dxt_ref[pl.ds(offs[p], BLK), :] += back_t[rows]
+
+
+def _ffn_kernel(col_ref, cnt_ref, tok_ref, cot_ref, wg_ref, wu_ref, wd_ref,
+                gg_ref, gu_ref, gd_ref, dxt_ref):
+    step = pl.program_id(0)
+    per_step = gg_ref.shape[0]
+
+    @pl.when(step == 0)
+    def _():
+        dxt_ref[...] = jnp.zeros_like(dxt_ref)
+
+    for hh in range(per_step):
+        h = step * per_step + hh
+        _ffn_block(hh, h, cnt_ref[h], col_ref, tok_ref, cot_ref, wg_ref, wu_ref, wd_ref,
+                   gg_ref, gu_ref, gd_ref, dxt_ref)
 
 
 def ffn_block_terms(col_index, row_count, full_tok, full_cot, gate_w, up_w, down_w):
     hblk, slots = col_index.shape
     rows, width = full_tok.shape
-    wspec = pl.BlockSpec((1, slots, BLK, BLK), lambda h, c, n: (h, 0, 0, 0))
+    per_step = 3 if hblk % 3 == 0 else 1
+    wspec = pl.BlockSpec((per_step, slots, BLK, BLK), lambda h, c, n: (h, 0, 0, 0))
     full = pl.BlockSpec((rows, width), lambda h, c, n: (0, 0))
     full_t = pl.BlockSpec((width, rows), lambda h, c, n: (0, 0))
-    gspec = pl.BlockSpec((1, slots, BLK, BLK), lambda h, c, n: (h, 0, 0, 0))
+    gspec = wspec
     grad = jax.ShapeDtypeStruct((hblk, slots, BLK, BLK), jnp.float32)
     flops = 2 * rows * hblk * slots * BLK * BLK * 9
     return pl.pallas_call(
         _ffn_kernel,
         grid_spec=pltpu.PrefetchScalarGridSpec(
             num_scalar_prefetch=2,
-            grid=(hblk,),
+            grid=(hblk // per_step,),
             in_specs=[full, full, wspec, wspec, wspec],
             out_specs=[gspec, gspec, gspec, full_t],
         ),

time: 211 us -> 202 us (0.957)
  Pallas kernels: 33.1 us -> 24.7 us
    pallas_call x1, Pallas kernels: 33.1 us -> 24.7 us  [ffn_block_terms(): pl.pallas_call(_ffn_kernel, grid_spec=pltpu.PrefetchScalarGridSpec(num_sc...]
  transfers between devices with their start and end apart: 48 -> 48, of which waited for: 35 -> 35; matrix products, arithmetic and copies ran while one was open for 24% -> 25% of each run, Pallas kernels for 0% -> 0%
where the time goes in v9:
time: 202 us; the launch traced here: 200 us
  starting transfers between devices  75.4 us (37%)
  other arithmetic  49.6 us (25%)
  Pallas kernels  24.7 us (12%)
  between operations  21.7 us (11%)
  waiting for transfers between devices  19.1 us (9%)
  local copies, waits for them, and re-layouts  9.22 us (5%)
    ppermute x45, starting transfers between devices, ring_reduce_scatter(): moved = lax.ppermute(accs[i].astype(wire_dtype), ('dp', 'tensor'), perm)  74.4 us
    convert_element_type x42, other arithmetic, ring_reduce_scatter(): moved = lax.ppermute(accs[i].astype(wire_dtype), ('dp', 'tensor'), perm)  38.7 us
    pallas_call x1, Pallas kernels, ffn_block_terms(): pl.pallas_call(_ffn_kernel, grid_spec=pltpu.PrefetchScalarGridSpec(num_sc...  24.7 us
    ppermute x45, waiting for transfers between devices, ring_reduce_scatter(): moved = lax.ppermute(accs[i].astype(wire_dtype), ('dp', 'tensor'), perm)  19.1 us
  transfers between devices with their start and end apart: 48, of which 35 were waited for; matrix products, arithmetic and copies ran while one was open for 25% of the time, Pallas kernels for 0%

profile of v9, /device:TPU:0, one launch (start us, length us, event | category | flops | bytes accessed | tf_op | source)
XLA Modules:
  0.0 199.8 jit_solution(12344628928071679427)
XLA Ops:
  13.2 2.0 %fusion.2 = (s32[1]{0:T(128)}, s32[1]{0:T(128)}, s32[1]{0:T(128)}, s32[1]{0:T(128)}, s32[1]{0:T(128)}, /*index=5*/s32[1]{0:T(128)}, s32[1]{0:T(128)}, s32[1]{0:T...) fusion(s32[16]{0:T(128)} %constant.221.clone, ...), kind=kLoop, calls=%fused_computation.62 | loop fusion | bytes 192 | tf_op jit(solution)/shard_map/dynamic_slice | solution.py:37
  30.5 24.7 %ffn_block_terms.1 = (f32[27,5,128,128]{3,2,1,0:T(8,128)}, f32[27,5,128,128]{3,2,1,0:T(8,128)}, f32[27,5,128,128]{3,2,1,0:T(8,128)}, f32[5120,128]{1,0:T(8,128)}) custom-call(s32[27,5]{1,0:T(8,128)} %copy.15.col_ref, s32[27]{0:T(128)} %cnt_ref.1, bf16[128,5120]{1,0:T(8,128)(2,1)} %pad_maximum_fusion.1.tok_ref, bf16[128,5120]{1,0:T(8,128)(2,1)} %pad_maximum_fusion.2.cot_ref, ...), custom_call_target="tpu_custom_call" | custom-call | flops 5096079360 | bytes 45056000 | tf_op jit(solution)/shard_map/ffn_block_terms/pallas_call | solution.py:116
  55.3 1.8 fusion.1
  58.9 2.6 %collective-permute-start.33 = (bf16[1080,128]{1,0:T(8,128)(2,1)S(1)}, bf16[1080,128]{1,0:T(8,128)(2,1)S(1)}, u32[]{:S(2)}, u32[]{:S(2)}) collective-permute-start(bf16[1080,128]{1,0:T(8,128)(2,1)S(1)} %dynamic-slice_convert_fusion), channel_id=1, source_target_pairs={{0,8},{1,5},{8,16},{9,1},{16,24},{17,9},{24,26},{25,17},{26,18},{2... | collective-permute-start | bytes 829448 | tf_op jit(solution)/shard_map/ppermute | solution.py:47
  62.6 1.6 collective-permute-start.18
  65.3 1.6 collective-permute-start.3
  68.1 1.5 collective-permute-start.34
  73.3 1.8 collective-permute-start.4
  76.3 1.8 collective-permute-start.35
  79.2 1.8 collective-permute-start.20
  82.2 1.8 collective-permute-start.5
  86.6 1.6 collective-permute-start.36
  89.4 1.6 collective-permute-start.21
  97.3 1.6 collective-permute-start.22
  100.2 1.6 collective-permute-start.7
  103.2 1.6 collective-permute-start.38
  106.2 1.6 collective-permute-start.23
  109.1 1.6 collective-permute-start.8
  112.1 1.6 collective-permute-start.39
  115.1 1.6 collective-permute-start.24
  118.0 1.6 collective-permute-start.9
  121.0 1.6 collective-permute-start.40
  123.9 1.6 collective-permute-start.25
  125.9 1.6 collective-permute-start.10
  129.9 1.6 collective-permute-start.41
  132.8 1.6 collective-permute-start.26
  134.7 1.6 collective-permute-start.11
  138.8 1.6 collective-permute-start.42
  141.7 1.6 collective-permute-start.27
  143.6 1.6 collective-permute-start.12
  147.6 1.6 collective-permute-start.43
  150.6 1.6 collective-permute-start.28
  152.5 1.6 collective-permute-start.13
  156.5 1.6 collective-permute-start.44
  159.5 1.6 collective-permute-start.29
  161.4 1.6 collective-permute-start.14
  165.4 1.6 collective-permute-start.45
  168.4 1.6 collective-permute-start.30
  170.3 1.6 collective-permute-start.15
  174.3 1.6 collective-permute-start.46
  177.3 1.6 collective-permute-start.31
  179.2 1.6 collective-permute-start.16
  183.2 1.6 collective-permute-start.47
  186.2 1.6 collective-permute-start.32
  188.1 1.6 collective-permute-start.17
  192.1 1.9 collective-permute-done.32
  195.0 1.9 collective-permute-done.17
  197.0 2.8 %add_divide_fusion = (f32[3,1,1080,128]{3,2,1,0:T(8,128)}, f32[3,1,1080,128]{3,2,1,0:T(8,128)}, f32[3,1,1080,128]{3,2,1,0:T(8,128)}) fusion(f32[1,1,1080,128]{3,2,1,0:T(8,128)S(1)} %add_bitcast_fusion, f32[1,1,1080,128]{3,2,1,0:T(8,128)S(1)} %add_bitcast_fusion.1, f32[1,1,1080,128]{3,2,1,0:T(8,128)S(1)} %add_bitcast_fusion.2, ...), kind=kLoop, calls=%fused_computation.1 | loop fusion | flops 4976640 | bytes 9953280 | tf_op jit(solution)/shard_map/div | solution.py:177
  (120 shorter events, 72.8 us)
Async XLA Ops:
  0.6 26.1 %collective-permute-start.1 = (bf16[128,2560]{1,0:T(8,128)(2,1)}, bf16[128,2560]{1,0:T(8,128)(2,1)S(1)}, u32[]{:S(2)}, u32[]{:S(2)}) collective-permute-start(bf16[128,2560]{1,0:T(8,128)(2,1)} %param.12), channel_id=1, source_target_pairs={{0,1},{1,0},{2,3},{3,2},{4,5},{5,4},{6,7},{7,6},{8,9},{9,8},{10,11... | collective-permute-start | bytes 1966088 | tf_op jit(solution)/shard_map/ppermute | solution.py:139
  1.1 25.6 %collective-permute-start = (bf16[128,2560]{1,0:T(8,128)(2,1)}, bf16[128,2560]{1,0:T(8,128)(2,1)S(1)}, u32[]{:S(2)}, u32[]{:S(2)}) collective-permute-start(bf16[128,2560]{1,0:T(8,128)(2,1)} %param.11), channel_id=1, source_target_pairs={{0,1},{1,0},{2,3},{3,2},{4,5},{5,4},{6,7},{7,6},{8,9},{9,8},{10,11... | collective-permute-start | bytes 1966088 | tf_op jit(solution)/shard_map/ppermute | solution.py:139
  57.1 27.0 %collective-permute-start.2 = (bf16[128,2560]{0,1:T(8,128)(2,1)S(1)}, bf16[128,2560]{0,1:T(8,128)(2,1)S(1)}, u32[]{:S(2)}, u32[]{:S(2)}) collective-permute-start(bf16[128,2560]{0,1:T(8,128)(2,1)S(1)} %fusion.1), channel_id=1, source_target_pairs={{0,1},{1,0},{2,3},{3,2},{4,5},{5,4},{6,7},{7,6},{8,9},{9,8},{10,11... | collective-permute-start | bytes 1966088 | tf_op jit(solution)/shard_map/ppermute | solution.py:167
  58.9 8.1 %collective-permute-start.33 = (bf16[1080,128]{1,0:T(8,128)(2,1)S(1)}, bf16[1080,128]{1,0:T(8,128)(2,1)S(1)}, u32[]{:S(2)}, u32[]{:S(2)}) collective-permute-start(bf16[1080,128]{1,0:T(8,128)(2,1)S(1)} %dynamic-slice_convert_fusion), channel_id=1, source_target_pairs={{0,8},{1,5},{8,16},{9,1},{16,24},{17,9},{24,26},{25,17},{26,18},{2... | collective-permute-start | bytes 829448 | tf_op jit(solution)/shard_map/ppermute | solution.py:47
  62.6 7.0 %collective-permute-start.18 = (bf16[1080,128]{1,0:T(8,128)(2,1)S(1)}, bf16[1080,128]{1,0:T(8,128)(2,1)S(1)}, u32[]{:S(2)}, u32[]{:S(2)}) collective-permute-start(bf16[1080,128]{1,0:T(8,128)(2,1)S(1)} %dynamic-slice_convert_fusion.1), channel_id=1, source_target_pairs={{0,8},{1,5},{8,16},{9,1},{16,24},{17,9},{24,26},{25,17},{26,18},{2... | collective-permute-start | bytes 829448 | tf_op jit(solution)/shard_map/ppermute | solution.py:47
  65.3 6.9 %collective-permute-start.3 = (bf16[1080,128]{1,0:T(8,128)(2,1)S(1)}, bf16[1080,128]{1,0:T(8,128)(2,1)S(1)}, u32[]{:S(2)}, u32[]{:S(2)}) collective-permute-start(bf16[1080,128]{1,0:T(8,128)(2,1)S(1)} %dynamic-slice_convert_fusion.2), channel_id=1, source_target_pairs={{0,8},{1,5},{8,16},{9,1},{16,24},{17,9},{24,26},{25,17},{26,18},{2... | collective-permute-start | bytes 829448 | tf_op jit(solution)/shard_map/ppermute | solution.py:47
  68.1 7.1 %collective-permute-start.34 = (bf16[1080,128]{1,0:T(8,128)(2,1)S(1)}, bf16[1080,128]{1,0:T(8,128)(2,1)S(1)}, u32[]{:S(2)}, u32[]{:S(2)}) collective-permute-start(bf16[1080,128]{1,0:T(8,128)(2,1)S(1)} %add_convert_fusion.13), channel_id=1, source_target_pairs={{0,8},{1,5},{8,16},{9,1},{16,24},{17,9},{24,26},{25,17},{26,18},{2... | collective-permute-start | bytes 829448 | tf_op jit(solution)/shard_map/ppermute | solution.py:47
  70.7 7.4 %collective-permute-start.19 = (bf16[1080,128]{1,0:T(8,128)(2,1)S(1)}, bf16[1080,128]{1,0:T(8,128)(2,1)S(1)}, u32[]{:S(2)}, u32[]{:S(2)}) collective-permute-start(bf16[1080,128]{1,0:T(8,128)(2,1)S(1)} %add_convert_fusion.27), channel_id=1, source_target_pairs={{0,8},{1,5},{8,16},{9,1},{16,24},{17,9},{24,26},{25,17},{26,18},{2... | collective-permute-start | bytes 829448 | tf_op jit(solution)/shard_map/ppermute | solution.py:47
  73.3 7.8 %collective-permute-start.4 = (bf16[1080,128]{1,0:T(8,128)(2,1)S(1)}, bf16[1080,128]{1,0:T(8,128)(2,1)S(1)}, u32[]{:S(2)}, u32[]{:S(2)}) collective-permute-start(bf16[1080,128]{1,0:T(8,128)(2,1)S(1)} %add_convert_fusion.41), channel_id=1, source_target_pairs={{0,8},{1,5},{8,16},{9,1},{16,24},{17,9},{24,26},{25,17},{26,18},{2... | collective-permute-start | bytes 829448 | tf_op jit(solution)/shard_map/ppermute | solution.py:47
  76.3 9.1 %collective-permute-start.35 = (bf16[1080,128]{1,0:T(8,128)(2,1)S(1)}, bf16[1080,128]{1,0:T(8,128)(2,1)S(1)}, u32[]{:S(2)}, u32[]{:S(2)}) collective-permute-start(bf16[1080,128]{1,0:T(8,128)(2,1)S(1)} %add_convert_fusion.12), channel_id=1, source_target_pairs={{0,8},{1,5},{8,16},{9,1},{16,24},{17,9},{24,26},{25,17},{26,18},{2... | collective-permute-start | bytes 829448 | tf_op jit(solution)/shard_map/ppermute | solution.py:47
  79.2 9.0 %collective-permute-start.20 = (bf16[1080,128]{1,0:T(8,128)(2,1)S(1)}, bf16[1080,128]{1,0:T(8,128)(2,1)S(1)}, u32[]{:S(2)}, u32[]{:S(2)}) collective-permute-start(bf16[1080,128]{1,0:T(8,128)(2,1)S(1)} %add_convert_fusion.26), channel_id=1, source_target_pairs={{0,8},{1,5},{8,16},{9,1},{16,24},{17,9},{24,26},{25,17},{26,18},{2... | collective-permute-start | bytes 829448 | tf_op jit(solution)/shard_map/ppermute | solution.py:47
  82.2 8.8 %collective-permute-start.5 = (bf16[1080,128]{1,0:T(8,128)(2,1)S(1)}, bf16[1080,128]{1,0:T(8,128)(2,1)S(1)}, u32[]{:S(2)}, u32[]{:S(2)}) collective-permute-start(bf16[1080,128]{1,0:T(8,128)(2,1)S(1)} %add_convert_fusion.40), channel_id=1, source_target_pairs={{0,8},{1,5},{8,16},{9,1},{16,24},{17,9},{24,26},{25,17},{26,18},{2... | collective-permute-start | bytes 829448 | tf_op jit(solution)/shard_map/ppermute | solution.py:47
  86.6 7.0 %collective-permute-start.36 = (bf16[1080,128]{1,0:T(8,128)(2,1)S(1)}, bf16[1080,128]{1,0:T(8,128)(2,1)S(1)}, u32[]{:S(2)}, u32[]{:S(2)}) collective-permute-start(bf16[1080,128]{1,0:T(8,128)(2,1)S(1)} %add_convert_fusion.11), channel_id=1, source_target_pairs={{0,8},{1,5},{8,16},{9,1},{16,24},{17,9},{24,26},{25,17},{26,18},{2... | collective-permute-start | bytes 829448 | tf_op jit(solution)/shard_map/ppermute | solution.py:47
  89.4 6.8 %collective-permute-start.21 = (bf16[1080,128]{1,0:T(8,128)(2,1)S(1)}, bf16[1080,128]{1,0:T(8,128)(2,1)S(1)}, u32[]{:S(2)}, u32[]{:S(2)}) collective-permute-start(bf16[1080,128]{1,0:T(8,128)(2,1)S(1)} %add_convert_fusion.25), channel_id=1, source_target_pairs={{0,8},{1,5},{8,16},{9,1},{16,24},{17,9},{24,26},{25,17},{26,18},{2... | collective-permute-start | bytes 829448 | tf_op jit(solution)/shard_map/ppermute | solution.py:47
  92.1 7.0 %collective-permute-start.6 = (bf16[1080,128]{1,0:T(8,128)(2,1)S(1)}, bf16[1080,128]{1,0:T(8,128)(2,1)S(1)}, u32[]{:S(2)}, u32[]{:S(2)}) collective-permute-start(bf16[1080,128]{1,0:T(8,128)(2,1)S(1)} %add_convert_fusion.39), channel_id=1, source_target_pairs={{0,8},{1,5},{8,16},{9,1},{16,24},{17,9},{24,26},{25,17},{26,18},{2... | collective-permute-start | bytes 829448 | tf_op jit(solution)/shard_map/ppermute | solution.py:47
  94.8 7.3 %collective-permute-start.37 = (bf16[1080,128]{1,0:T(8,128)(2,1)S(1)}, bf16[1080,128]{1,0:T(8,128)(2,1)S(1)}, u32[]{:S(2)}, u32[]{:S(2)}) collective-permute-start(bf16[1080,128]{1,0:T(8,128)(2,1)S(1)} %add_convert_fusion.10), channel_id=1, source_target_pairs={{0,8},{1,5},{8,16},{9,1},{16,24},{17,9},{24,26},{25,17},{26,18},{2... | collective-permute-start | bytes 829448 | tf_op jit(solution)/shard_map/ppermute | solution.py:47
  97.3 7.8 %collective-permute-start.22 = (bf16[1080,128]{1,0:T(8,128)(2,1)S(1)}, bf16[1080,128]{1,0:T(8,128)(2,1)S(1)}, u32[]{:S(2)}, u32[]{:S(2)}) collective-permute-start(bf16[1080,128]{1,0:T(8,128)(2,1)S(1)} %add_convert_fusion.24), channel_id=1, source_target_pairs={{0,8},{1,5},{8,16},{9,1},{16,24},{17,9},{24,26},{25,17},{26,18},{2... | collective-permute-start | bytes 829448 | tf_op jit(solution)/shard_map/ppermute | solution.py:47
  100.2 7.8 %collective-permute-start.7 = (bf16[1080,128]{1,0:T(8,128)(2,1)S(1)}, bf16[1080,128]{1,0:T(8,128)(2,1)S(1)}, u32[]{:S(2)}, u32[]{:S(2)}) collective-permute-start(bf16[1080,128]{1,0:T(8,128)(2,1)S(1)} %add_convert_fusion.38), channel_id=1, source_target_pairs={{0,8},{1,5},{8,16},{9,1},{16,24},{17,9},{24,26},{25,17},{26,18},{2... | collective-permute-start | bytes 829448 | tf_op jit(solution)/shard_map/ppermute | solution.py:47
  103.2 7.8 %collective-permute-start.38 = (bf16[1080,128]{1,0:T(8,128)(2,1)S(1)}, bf16[1080,128]{1,0:T(8,128)(2,1)S(1)}, u32[]{:S(2)}, u32[]{:S(2)}) collective-permute-start(bf16[1080,128]{1,0:T(8,128)(2,1)S(1)} %add_convert_fusion.9), channel_id=1, source_target_pairs={{0,8},{1,5},{8,16},{9,1},{16,24},{17,9},{24,26},{25,17},{26,18},{2... | collective-permute-start | bytes 829448 | tf_op jit(solution)/shard_map/ppermute | solution.py:47
  106.2 7.8 %collective-permute-start.23 = (bf16[1080,128]{1,0:T(8,128)(2,1)S(1)}, bf16[1080,128]{1,0:T(8,128)(2,1)S(1)}, u32[]{:S(2)}, u32[]{:S(2)}) collective-permute-start(bf16[1080,128]{1,0:T(8,128)(2,1)S(1)} %add_convert_fusion.23), channel_id=1, source_target_pairs={{0,8},{1,5},{8,16},{9,1},{16,24},{17,9},{24,26},{25,17},{26,18},{2... | collective-permute-start | bytes 829448 | tf_op jit(solution)/shard_map/ppermute | solution.py:47
  109.1 7.8 %collective-permute-start.8 = (bf16[1080,128]{1,0:T(8,128)(2,1)S(1)}, bf16[1080,128]{1,0:T(8,128)(2,1)S(1)}, u32[]{:S(2)}, u32[]{:S(2)}) collective-permute-start(bf16[1080,128]{1,0:T(8,128)(2,1)S(1)} %add_convert_fusion.37), channel_id=1, source_target_pairs={{0,8},{1,5},{8,16},{9,1},{16,24},{17,9},{24,26},{25,17},{26,18},{2... | collective-permute-start | bytes 829448 | tf_op jit(solution)/shard_map/ppermute | solution.py:47
  112.1 7.8 %collective-permute-start.39 = (bf16[1080,128]{1,0:T(8,128)(2,1)S(1)}, bf16[1080,128]{1,0:T(8,128)(2,1)S(1)}, u32[]{:S(2)}, u32[]{:S(2)}) collective-permute-start(bf16[1080,128]{1,0:T(8,128)(2,1)S(1)} %add_convert_fusion.8), channel_id=1, source_target_pairs={{0,8},{1,5},{8,16},{9,1},{16,24},{17,9},{24,26},{25,17},{26,18},{2... | collective-permute-start | bytes 829448 | tf_op jit(solution)/shard_map/ppermute | solution.py:47
  115.1 7.8 %collective-permute-start.24 = (bf16[1080,128]{1,0:T(8,128)(2,1)S(1)}, bf16[1080,128]{1,0:T(8,128)(2,1)S(1)}, u32[]{:S(2)}, u32[]{:S(2)}) collective-permute-start(bf16[1080,128]{1,0:T(8,128)(2,1)S(1)} %add_convert_fusion.22), channel_id=1, source_target_pairs={{0,8},{1,5},{8,16},{9,1},{16,24},{17,9},{24,26},{25,17},{26,18},{2... | collective-permute-start | bytes 829448 | tf_op jit(solution)/shard_map/ppermute | solution.py:47
  118.0 7.8 %collective-permute-start.9 = (bf16[1080,128]{1,0:T(8,128)(2,1)S(1)}, bf16[1080,128]{1,0:T(8,128)(2,1)S(1)}, u32[]{:S(2)}, u32[]{:S(2)}) collective-permute-start(bf16[1080,128]{1,0:T(8,128)(2,1)S(1)} %add_convert_fusion.36), channel_id=1, source_target_pairs={{0,8},{1,5},{8,16},{9,1},{16,24},{17,9},{24,26},{25,17},{26,18},{2... | collective-permute-start | bytes 829448 | tf_op jit(solution)/shard_map/ppermute | solution.py:47
  121.0 7.8 %collective-permute-start.40 = (bf16[1080,128]{1,0:T(8,128)(2,1)S(1)}, bf16[1080,128]{1,0:T(8,128)(2,1)S(1)}, u32[]{:S(2)}, u32[]{:S(2)}) collective-permute-start(bf16[1080,128]{1,0:T(8,128)(2,1)S(1)} %add_convert_fusion.7), channel_id=1, source_target_pairs={{0,8},{1,5},{8,16},{9,1},{16,24},{17,9},{24,26},{25,17},{26,18},{2... | collective-permute-start | bytes 829448 | tf_op jit(solution)/shard_map/ppermute | solution.py:47
  123.9 7.8 %collective-permute-start.25 = (bf16[1080,128]{1,0:T(8,128)(2,1)S(1)}, bf16[1080,128]{1,0:T(8,128)(2,1)S(1)}, u32[]{:S(2)}, u32[]{:S(2)}) collective-permute-start(bf16[1080,128]{1,0:T(8,128)(2,1)S(1)} %add_convert_fusion.21), channel_id=1, source_target_pairs={{0,8},{1,5},{8,16},{9,1},{16,24},{17,9},{24,26},{25,17},{26,18},{2... | collective-permute-start | bytes 829448 | tf_op jit(solution)/shard_map/ppermute | solution.py:47
  125.9 8.8 %collective-permute-start.10 = (bf16[1080,128]{1,0:T(8,128)(2,1)S(1)}, bf16[1080,128]{1,0:T(8,128)(2,1)S(1)}, u32[]{:S(2)}, u32[]{:S(2)}) collective-permute-start(bf16[1080,128]{1,0:T(8,128)(2,1)S(1)} %add_convert_fusion.35), channel_id=1, source_target_pairs={{0,8},{1,5},{8,16},{9,1},{16,24},{17,9},{24,26},{25,17},{26,18},{2... | collective-permute-start | bytes 829448 | tf_op jit(solution)/shard_map/ppermute | solution.py:47
  129.9 7.8 %collective-permute-start.41 = (bf16[1080,128]{1,0:T(8,128)(2,1)S(1)}, bf16[1080,128]{1,0:T(8,128)(2,1)S(1)}, u32[]{:S(2)}, u32[]{:S(2)}) collective-permute-start(bf16[1080,128]{1,0:T(8,128)(2,1)S(1)} %add_convert_fusion.6), channel_id=1, source_target_pairs={{0,8},{1,5},{8,16},{9,1},{16,24},{17,9},{24,26},{25,17},{26,18},{2... | collective-permute-start | bytes 829448 | tf_op jit(solution)/shard_map/ppermute | solution.py:47
  132.8 7.8 %collective-permute-start.26 = (bf16[1080,128]{1,0:T(8,128)(2,1)S(1)}, bf16[1080,128]{1,0:T(8,128)(2,1)S(1)}, u32[]{:S(2)}, u32[]{:S(2)}) collective-permute-start(bf16[1080,128]{1,0:T(8,128)(2,1)S(1)} %add_convert_fusion.20), channel_id=1, source_target_pairs={{0,8},{1,5},{8,16},{9,1},{16,24},{17,9},{24,26},{25,17},{26,18},{2... | collective-permute-start | bytes 829448 | tf_op jit(solution)/shard_map/ppermute | solution.py:47
  134.7 8.8 %collective-permute-start.11 = (bf16[1080,128]{1,0:T(8,128)(2,1)S(1)}, bf16[1080,128]{1,0:T(8,128)(2,1)S(1)}, u32[]{:S(2)}, u32[]{:S(2)}) collective-permute-start(bf16[1080,128]{1,0:T(8,128)(2,1)S(1)} %add_convert_fusion.34), channel_id=1, source_target_pairs={{0,8},{1,5},{8,16},{9,1},{16,24},{17,9},{24,26},{25,17},{26,18},{2... | collective-permute-start | bytes 829448 | tf_op jit(solution)/shard_map/ppermute | solution.py:47
  138.8 7.8 %collective-permute-start.42 = (bf16[1080,128]{1,0:T(8,128)(2,1)S(1)}, bf16[1080,128]{1,0:T(8,128)(2,1)S(1)}, u32[]{:S(2)}, u32[]{:S(2)}) collective-permute-start(bf16[1080,128]{1,0:T(8,128)(2,1)S(1)} %add_convert_fusion.5), channel_id=1, source_target_pairs={{0,8},{1,5},{8,16},{9,1},{16,24},{17,9},{24,26},{25,17},{26,18},{2... | collective-permute-start | bytes 829448 | tf_op jit(solution)/shard_map/ppermute | solution.py:47
  141.7 7.8 %collective-permute-start.27 = (bf16[1080,128]{1,0:T(8,128)(2,1)S(1)}, bf16[1080,128]{1,0:T(8,128)(2,1)S(1)}, u32[]{:S(2)}, u32[]{:S(2)}) collective-permute-start(bf16[1080,128]{1,0:T(8,128)(2,1)S(1)} %add_convert_fusion.19), channel_id=1, source_target_pairs={{0,8},{1,5},{8,16},{9,1},{16,24},{17,9},{24,26},{25,17},{26,18},{2... | collective-permute-start | bytes 829448 | tf_op jit(solution)/shard_map/ppermute | solution.py:47
  143.6 8.8 %collective-permute-start.12 = (bf16[1080,128]{1,0:T(8,128)(2,1)S(1)}, bf16[1080,128]{1,0:T(8,128)(2,1)S(1)}, u32[]{:S(2)}, u32[]{:S(2)}) collective-permute-start(bf16[1080,128]{1,0:T(8,128)(2,1)S(1)} %add_convert_fusion.33), channel_id=1, source_target_pairs={{0,8},{1,5},{8,16},{9,1},{16,24},{17,9},{24,26},{25,17},{26,18},{2... | collective-permute-start | bytes 829448 | tf_op jit(solution)/shard_map/ppermute | solution.py:47
  147.6 7.8 %collective-permute-start.43 = (bf16[1080,128]{1,0:T(8,128)(2,1)S(1)}, bf16[1080,128]{1,0:T(8,128)(2,1)S(1)}, u32[]{:S(2)}, u32[]{:S(2)}) collective-permute-start(bf16[1080,128]{1,0:T(8,128)(2,1)S(1)} %add_convert_fusion.4), channel_id=1, source_target_pairs={{0,8},{1,5},{8,16},{9,1},{16,24},{17,9},{24,26},{25,17},{26,18},{2... | collective-permute-start | bytes 829448 | tf_op jit(solution)/shard_map/ppermute | solution.py:47
  150.6 7.8 %collective-permute-start.28 = (bf16[1080,128]{1,0:T(8,128)(2,1)S(1)}, bf16[1080,128]{1,0:T(8,128)(2,1)S(1)}, u32[]{:S(2)}, u32[]{:S(2)}) collective-permute-start(bf16[1080,128]{1,0:T(8,128)(2,1)S(1)} %add_convert_fusion.18), channel_id=1, source_target_pairs={{0,8},{1,5},{8,16},{9,1},{16,24},{17,9},{24,26},{25,17},{26,18},{2... | collective-permute-start | bytes 829448 | tf_op jit(solution)/shard_map/ppermute | solution.py:47
  152.5 8.8 %collective-permute-start.13 = (bf16[1080,128]{1,0:T(8,128)(2,1)S(1)}, bf16[1080,128]{1,0:T(8,128)(2,1)S(1)}, u32[]{:S(2)}, u32[]{:S(2)}) collective-permute-start(bf16[1080,128]{1,0:T(8,128)(2,1)S(1)} %add_convert_fusion.32), channel_id=1, source_target_pairs={{0,8},{1,5},{8,16},{9,1},{16,24},{17,9},{24,26},{25,17},{26,18},{2... | collective-permute-start | bytes 829448 | tf_op jit(solution)/shard_map/ppermute | solution.py:47
  156.5 7.8 %collective-permute-start.44 = (bf16[1080,128]{1,0:T(8,128)(2,1)S(1)}, bf16[1080,128]{1,0:T(8,128)(2,1)S(1)}, u32[]{:S(2)}, u32[]{:S(2)}) collective-permute-start(bf16[1080,128]{1,0:T(8,128)(2,1)S(1)} %add_convert_fusion.3), channel_id=1, source_target_pairs={{0,8},{1,5},{8,16},{9,1},{16,24},{17,9},{24,26},{25,17},{26,18},{2... | collective-permute-start | bytes 829448 | tf_op jit(solution)/shard_map/ppermute | solution.py:47
  159.5 7.8 %collective-permute-start.29 = (bf16[1080,128]{1,0:T(8,128)(2,1)S(1)}, bf16[1080,128]{1,0:T(8,128)(2,1)S(1)}, u32[]{:S(2)}, u32[]{:S(2)}) collective-permute-start(bf16[1080,128]{1,0:T(8,128)(2,1)S(1)} %add_convert_fusion.17), channel_id=1, source_target_pairs={{0,8},{1,5},{8,16},{9,1},{16,24},{17,9},{24,26},{25,17},{26,18},{2... | collective-permute-start | bytes 829448 | tf_op jit(solution)/shard_map/ppermute | solution.py:47
  161.4 8.8 %collective-permute-start.14 = (bf16[1080,128]{1,0:T(8,128)(2,1)S(1)}, bf16[1080,128]{1,0:T(8,128)(2,1)S(1)}, u32[]{:S(2)}, u32[]{:S(2)}) collective-permute-start(bf16[1080,128]{1,0:T(8,128)(2,1)S(1)} %add_convert_fusion.31), channel_id=1, source_target_pairs={{0,8},{1,5},{8,16},{9,1},{16,24},{17,9},{24,26},{25,17},{26,18},{2... | collective-permute-start | bytes 829448 | tf_op jit(solution)/shard_map/ppermute | solution.py:47
  165.4 7.8 %collective-permute-start.45 = (bf16[1080,128]{1,0:T(8,128)(2,1)S(1)}, bf16[1080,128]{1,0:T(8,128)(2,1)S(1)}, u32[]{:S(2)}, u32[]{:S(2)}) collective-permute-start(bf16[1080,128]{1,0:T(8,128)(2,1)S(1)} %add_convert_fusion.2), channel_id=1, source_target_pairs={{0,8},{1,5},{8,16},{9,1},{16,24},{17,9},{24,26},{25,17},{26,18},{2... | collective-permute-start | bytes 829448 | tf_op jit(solution)/shard_map/ppermute | solution.py:47
  168.4 7.8 %collective-permute-start.30 = (bf16[1080,128]{1,0:T(8,128)(2,1)S(1)}, bf16[1080,128]{1,0:T(8,128)(2,1)S(1)}, u32[]{:S(2)}, u32[]{:S(2)}) collective-permute-start(bf16[1080,128]{1,0:T(8,128)(2,1)S(1)} %add_convert_fusion.16), channel_id=1, source_target_pairs={{0,8},{1,5},{8,16},{9,1},{16,24},{17,9},{24,26},{25,17},{26,18},{2... | collective-permute-start | bytes 829448 | tf_op jit(solution)/shard_map/ppermute | solution.py:47
  170.3 8.8 %collective-permute-start.15 = (bf16[1080,128]{1,0:T(8,128)(2,1)S(1)}, bf16[1080,128]{1,0:T(8,128)(2,1)S(1)}, u32[]{:S(2)}, u32[]{:S(2)}) collective-permute-start(bf16[1080,128]{1,0:T(8,128)(2,1)S(1)} %add_convert_fusion.30), channel_id=1, source_target_pairs={{0,8},{1,5},{8,16},{9,1},{16,24},{17,9},{24,26},{25,17},{26,18},{2... | collective-permute-start | bytes 829448 | tf_op jit(solution)/shard_map/ppermute | solution.py:47
  174.3 7.8 %collective-permute-start.46 = (bf16[1080,128]{1,0:T(8,128)(2,1)S(1)}, bf16[1080,128]{1,0:T(8,128)(2,1)S(1)}, u32[]{:S(2)}, u32[]{:S(2)}) collective-permute-start(bf16[1080,128]{1,0:T(8,128)(2,1)S(1)} %add_convert_fusion.1), channel_id=1, source_target_pairs={{0,8},{1,5},{8,16},{9,1},{16,24},{17,9},{24,26},{25,17},{26,18},{2... | collective-permute-start | bytes 829448 | tf_op jit(solution)/shard_map/ppermute | solution.py:47
  177.3 7.7 %collective-permute-start.31 = (bf16[1080,128]{1,0:T(8,128)(2,1)S(1)}, bf16[1080,128]{1,0:T(8,128)(2,1)S(1)}, u32[]{:S(2)}, u32[]{:S(2)}) collective-permute-start(bf16[1080,128]{1,0:T(8,128)(2,1)S(1)} %add_convert_fusion.15), channel_id=1, source_target_pairs={{0,8},{1,5},{8,16},{9,1},{16,24},{17,9},{24,26},{25,17},{26,18},{2... | collective-permute-start | bytes 829448 | tf_op jit(solution)/shard_map/ppermute | solution.py:47
  179.2 8.8 %collective-permute-start.16 = (bf16[1080,128]{1,0:T(8,128)(2,1)S(1)}, bf16[1080,128]{1,0:T(8,128)(2,1)S(1)}, u32[]{:S(2)}, u32[]{:S(2)}) collective-permute-start(bf16[1080,128]{1,0:T(8,128)(2,1)S(1)} %add_convert_fusion.29), channel_id=1, source_target_pairs={{0,8},{1,5},{8,16},{9,1},{16,24},{17,9},{24,26},{25,17},{26,18},{2... | collective-permute-start | bytes 829448 | tf_op jit(solution)/shard_map/ppermute | solution.py:47
  183.2 7.8 %collective-permute-start.47 = (bf16[1080,128]{1,0:T(8,128)(2,1)S(1)}, bf16[1080,128]{1,0:T(8,128)(2,1)S(1)}, u32[]{:S(2)}, u32[]{:S(2)}) collective-permute-start(bf16[1080,128]{1,0:T(8,128)(2,1)S(1)} %add_convert_fusion), channel_id=1, source_target_pairs={{0,8},{1,5},{8,16},{9,1},{16,24},{17,9},{24,26},{25,17},{26,18},{2... | collective-permute-start | bytes 829448 | tf_op jit(solution)/shard_map/ppermute | solution.py:47
  186.2 7.8 %collective-permute-start.32 = (bf16[1080,128]{1,0:T(8,128)(2,1)S(1)}, bf16[1080,128]{1,0:T(8,128)(2,1)S(1)}, u32[]{:S(2)}, u32[]{:S(2)}) collective-permute-start(bf16[1080,128]{1,0:T(8,128)(2,1)S(1)} %add_convert_fusion.14), channel_id=1, source_target_pairs={{0,8},{1,5},{8,16},{9,1},{16,24},{17,9},{24,26},{25,17},{26,18},{2... | collective-permute-start | bytes 829448 | tf_op jit(solution)/shard_map/ppermute | solution.py:47
  188.1 8.8 %collective-permute-start.17 = (bf16[1080,128]{1,0:T(8,128)(2,1)S(1)}, bf16[1080,128]{1,0:T(8,128)(2,1)S(1)}, u32[]{:S(2)}, u32[]{:S(2)}) collective-permute-start(bf16[1080,128]{1,0:T(8,128)(2,1)S(1)} %add_convert_fusion.28), channel_id=1, source_target_pairs={{0,8},{1,5},{8,16},{9,1},{16,24},{17,9},{24,26},{25,17},{26,18},{2... | collective-permute-start | bytes 829448 | tf_op jit(solution)/shard_map/ppermute | solution.py:47
  (6 other events, 174.1 us)

commit v10 on v9

--- a/solution.py
+++ b/solution.py
@@ -106,7 +106,7 @@
 def ffn_block_terms(col_index, row_count, full_tok, full_cot, gate_w, up_w, down_w):
     hblk, slots = col_index.shape
     rows, width = full_tok.shape
-    per_step = 3 if hblk % 3 == 0 else 1
+    per_step = 9 if hblk % 9 == 0 else (3 if hblk % 3 == 0 else 1)
     wspec = pl.BlockSpec((per_step, slots, BLK, BLK), lambda h, c, n: (h, 0, 0, 0))
     full = pl.BlockSpec((rows, width), lambda h, c, n: (0, 0))
     full_t = pl.BlockSpec((width, rows), lambda h, c, n: (0, 0))

time: 202 us -> 202 us (level)
  no operation moved by 1% of the time
where the time goes in v10:
time: 202 us; the launch traced here: 199 us
  starting transfers between devices  75.6 us (37%)
  other arithmetic  49.6 us (25%)
  Pallas kernels  24.3 us (12%)
  between operations  21.7 us (11%)
  waiting for transfers between devices  18.9 us (9%)
  local copies, waits for them, and re-layouts  9.23 us (5%)
    ppermute x45, starting transfers between devices, ring_reduce_scatter(): moved = lax.ppermute(accs[i].astype(wire_dtype), ('dp', 'tensor'), perm)  74.5 us
    convert_element_type x42, other arithmetic, ring_reduce_scatter(): moved = lax.ppermute(accs[i].astype(wire_dtype), ('dp', 'tensor'), perm)  38.7 us
    pallas_call x1, Pallas kernels, ffn_block_terms(): pl.pallas_call(_ffn_kernel, grid_spec=pltpu.PrefetchScalarGridSpec(num_sc...  24.3 us
    ppermute x45, waiting for transfers between devices, ring_reduce_scatter(): moved = lax.ppermute(accs[i].astype(wire_dtype), ('dp', 'tensor'), perm)  18.9 us
  transfers between devices with their start and end apart: 48, of which 35 were waited for; matrix products, arithmetic and copies ran while one was open for 25% of the time, Pallas kernels for 0%

profile of v10, /device:TPU:0, one launch (start us, length us, event | category | flops | bytes accessed | tf_op | source)
XLA Modules:
  0.0 199.4 jit_solution(8576773348448591036)
XLA Ops:
  13.2 2.0 %fusion.2 = (s32[1]{0:T(128)}, s32[1]{0:T(128)}, s32[1]{0:T(128)}, s32[1]{0:T(128)}, s32[1]{0:T(128)}, /*index=5*/s32[1]{0:T(128)}, s32[1]{0:T(128)}, s32[1]{0:T...) fusion(s32[16]{0:T(128)} %constant.221.clone, ...), kind=kLoop, calls=%fused_computation.62 | loop fusion | bytes 192 | tf_op jit(solution)/shard_map/dynamic_slice | solution.py:37
  30.5 24.3 %ffn_block_terms.1 = (f32[27,5,128,128]{3,2,1,0:T(8,128)}, f32[27,5,128,128]{3,2,1,0:T(8,128)}, f32[27,5,128,128]{3,2,1,0:T(8,128)}, f32[5120,128]{1,0:T(8,128)}) custom-call(s32[27,5]{1,0:T(8,128)} %copy.15.col_ref, s32[27]{0:T(128)} %cnt_ref.1, bf16[128,5120]{1,0:T(8,128)(2,1)} %pad_maximum_fusion.1.tok_ref, bf16[128,5120]{1,0:T(8,128)(2,1)} %pad_maximum_fusion.2.cot_ref, ...), custom_call_target="tpu_custom_call" | custom-call | flops 5096079360 | bytes 45056000 | tf_op jit(solution)/shard_map/ffn_block_terms/pallas_call | solution.py:116
  54.9 1.8 fusion.1
  58.6 2.6 %collective-permute-start.33 = (bf16[1080,128]{1,0:T(8,128)(2,1)S(1)}, bf16[1080,128]{1,0:T(8,128)(2,1)S(1)}, u32[]{:S(2)}, u32[]{:S(2)}) collective-permute-start(bf16[1080,128]{1,0:T(8,128)(2,1)S(1)} %dynamic-slice_convert_fusion), channel_id=1, source_target_pairs={{0,8},{1,5},{8,16},{9,1},{16,24},{17,9},{24,26},{25,17},{26,18},{2... | collective-permute-start | bytes 829448 | tf_op jit(solution)/shard_map/ppermute | solution.py:47
  62.3 1.6 collective-permute-start.18
  65.0 1.6 collective-permute-start.3
  67.7 1.5 collective-permute-start.34
  73.0 1.8 collective-permute-start.4
  75.9 1.8 collective-permute-start.35
  78.9 1.8 collective-permute-start.20
  81.9 1.8 collective-permute-start.5
  86.3 1.6 collective-permute-start.36
  89.0 1.6 collective-permute-start.21
  96.9 1.6 collective-permute-start.22
  99.9 1.6 collective-permute-start.7
  102.9 1.6 collective-permute-start.38
  105.8 1.6 collective-permute-start.23
  108.8 1.6 collective-permute-start.8
  111.7 1.6 collective-permute-start.39
  114.7 1.6 collective-permute-start.24
  117.7 1.6 collective-permute-start.9
  120.6 1.6 collective-permute-start.40
  123.6 1.6 collective-permute-start.25
  125.5 1.6 collective-permute-start.10
  129.5 1.6 collective-permute-start.41
  132.5 1.6 collective-permute-start.26
  134.4 1.6 collective-permute-start.11
  138.4 1.6 collective-permute-start.42
  141.4 1.6 collective-permute-start.27
  143.3 1.8 collective-permute-start.12
  147.3 1.6 collective-permute-start.43
  150.3 1.6 collective-permute-start.28
  152.2 1.6 collective-permute-start.13
  156.2 1.6 collective-permute-start.44
  159.2 1.6 collective-permute-start.29
  161.1 1.6 collective-permute-start.14
  165.1 1.6 collective-permute-start.45
  168.0 1.6 collective-permute-start.30
  169.9 1.6 collective-permute-start.15
  174.0 1.6 collective-permute-start.46
  177.0 1.6 collective-permute-start.31
  178.8 1.6 collective-permute-start.16
  182.9 1.6 collective-permute-start.47
  185.8 1.6 collective-permute-start.32
  187.7 1.6 collective-permute-start.17
  191.7 1.9 collective-permute-done.32
  194.7 1.9 collective-permute-done.17
  196.6 2.8 %add_divide_fusion = (f32[3,1,1080,128]{3,2,1,0:T(8,128)}, f32[3,1,1080,128]{3,2,1,0:T(8,128)}, f32[3,1,1080,128]{3,2,1,0:T(8,128)}) fusion(f32[1,1,1080,128]{3,2,1,0:T(8,128)S(1)} %add_bitcast_fusion, f32[1,1,1080,128]{3,2,1,0:T(8,128)S(1)} %add_bitcast_fusion.1, f32[1,1,1080,128]{3,2,1,0:T(8,128)S(1)} %add_bitcast_fusion.2, ...), kind=kLoop, calls=%fused_computation.1 | loop fusion | flops 4976640 | bytes 9953280 | tf_op jit(solution)/shard_map/div | solution.py:177
  (120 shorter events, 72.6 us)
Async XLA Ops:
  0.6 26.1 %collective-permute-start.1 = (bf16[128,2560]{1,0:T(8,128)(2,1)}, bf16[128,2560]{1,0:T(8,128)(2,1)S(1)}, u32[]{:S(2)}, u32[]{:S(2)}) collective-permute-start(bf16[128,2560]{1,0:T(8,128)(2,1)} %param.12), channel_id=1, source_target_pairs={{0,1},{1,0},{2,3},{3,2},{4,5},{5,4},{6,7},{7,6},{8,9},{9,8},{10,11... | collective-permute-start | bytes 1966088 | tf_op jit(solution)/shard_map/ppermute | solution.py:139
  1.1 25.6 %collective-permute-start = (bf16[128,2560]{1,0:T(8,128)(2,1)}, bf16[128,2560]{1,0:T(8,128)(2,1)S(1)}, u32[]{:S(2)}, u32[]{:S(2)}) collective-permute-start(bf16[128,2560]{1,0:T(8,128)(2,1)} %param.11), channel_id=1, source_target_pairs={{0,1},{1,0},{2,3},{3,2},{4,5},{5,4},{6,7},{7,6},{8,9},{9,8},{10,11... | collective-permute-start | bytes 1966088 | tf_op jit(solution)/shard_map/ppermute | solution.py:139
  56.7 27.0 %collective-permute-start.2 = (bf16[128,2560]{0,1:T(8,128)(2,1)S(1)}, bf16[128,2560]{0,1:T(8,128)(2,1)S(1)}, u32[]{:S(2)}, u32[]{:S(2)}) collective-permute-start(bf16[128,2560]{0,1:T(8,128)(2,1)S(1)} %fusion.1), channel_id=1, source_target_pairs={{0,1},{1,0},{2,3},{3,2},{4,5},{5,4},{6,7},{7,6},{8,9},{9,8},{10,11... | collective-permute-start | bytes 1966088 | tf_op jit(solution)/shard_map/ppermute | solution.py:167
  58.6 8.0 %collective-permute-start.33 = (bf16[1080,128]{1,0:T(8,128)(2,1)S(1)}, bf16[1080,128]{1,0:T(8,128)(2,1)S(1)}, u32[]{:S(2)}, u32[]{:S(2)}) collective-permute-start(bf16[1080,128]{1,0:T(8,128)(2,1)S(1)} %dynamic-slice_convert_fusion), channel_id=1, source_target_pairs={{0,8},{1,5},{8,16},{9,1},{16,24},{17,9},{24,26},{25,17},{26,18},{2... | collective-permute-start | bytes 829448 | tf_op jit(solution)/shard_map/ppermute | solution.py:47
  62.3 7.0 %collective-permute-start.18 = (bf16[1080,128]{1,0:T(8,128)(2,1)S(1)}, bf16[1080,128]{1,0:T(8,128)(2,1)S(1)}, u32[]{:S(2)}, u32[]{:S(2)}) collective-permute-start(bf16[1080,128]{1,0:T(8,128)(2,1)S(1)} %dynamic-slice_convert_fusion.1), channel_id=1, source_target_pairs={{0,8},{1,5},{8,16},{9,1},{16,24},{17,9},{24,26},{25,17},{26,18},{2... | collective-permute-start | bytes 829448 | tf_op jit(solution)/shard_map/ppermute | solution.py:47
  65.0 6.9 %collective-permute-start.3 = (bf16[1080,128]{1,0:T(8,128)(2,1)S(1)}, bf16[1080,128]{1,0:T(8,128)(2,1)S(1)}, u32[]{:S(2)}, u32[]{:S(2)}) collective-permute-start(bf16[1080,128]{1,0:T(8,128)(2,1)S(1)} %dynamic-slice_convert_fusion.2), channel_id=1, source_target_pairs={{0,8},{1,5},{8,16},{9,1},{16,24},{17,9},{24,26},{25,17},{26,18},{2... | collective-permute-start | bytes 829448 | tf_op jit(solution)/shard_map/ppermute | solution.py:47
  67.7 7.1 %collective-permute-start.34 = (bf16[1080,128]{1,0:T(8,128)(2,1)S(1)}, bf16[1080,128]{1,0:T(8,128)(2,1)S(1)}, u32[]{:S(2)}, u32[]{:S(2)}) collective-permute-start(bf16[1080,128]{1,0:T(8,128)(2,1)S(1)} %add_convert_fusion.13), channel_id=1, source_target_pairs={{0,8},{1,5},{8,16},{9,1},{16,24},{17,9},{24,26},{25,17},{26,18},{2... | collective-permute-start | bytes 829448 | tf_op jit(solution)/shard_map/ppermute | solution.py:47
  70.4 7.4 %collective-permute-start.19 = (bf16[1080,128]{1,0:T(8,128)(2,1)S(1)}, bf16[1080,128]{1,0:T(8,128)(2,1)S(1)}, u32[]{:S(2)}, u32[]{:S(2)}) collective-permute-start(bf16[1080,128]{1,0:T(8,128)(2,1)S(1)} %add_convert_fusion.27), channel_id=1, source_target_pairs={{0,8},{1,5},{8,16},{9,1},{16,24},{17,9},{24,26},{25,17},{26,18},{2... | collective-permute-start | bytes 829448 | tf_op jit(solution)/shard_map/ppermute | solution.py:47
  73.0 7.8 %collective-permute-start.4 = (bf16[1080,128]{1,0:T(8,128)(2,1)S(1)}, bf16[1080,128]{1,0:T(8,128)(2,1)S(1)}, u32[]{:S(2)}, u32[]{:S(2)}) collective-permute-start(bf16[1080,128]{1,0:T(8,128)(2,1)S(1)} %add_convert_fusion.41), channel_id=1, source_target_pairs={{0,8},{1,5},{8,16},{9,1},{16,24},{17,9},{24,26},{25,17},{26,18},{2... | collective-permute-start | bytes 829448 | tf_op jit(solution)/shard_map/ppermute | solution.py:47
  75.9 9.1 %collective-permute-start.35 = (bf16[1080,128]{1,0:T(8,128)(2,1)S(1)}, bf16[1080,128]{1,0:T(8,128)(2,1)S(1)}, u32[]{:S(2)}, u32[]{:S(2)}) collective-permute-start(bf16[1080,128]{1,0:T(8,128)(2,1)S(1)} %add_convert_fusion.12), channel_id=1, source_target_pairs={{0,8},{1,5},{8,16},{9,1},{16,24},{17,9},{24,26},{25,17},{26,18},{2... | collective-permute-start | bytes 829448 | tf_op jit(solution)/shard_map/ppermute | solution.py:47
  78.9 9.0 %collective-permute-start.20 = (bf16[1080,128]{1,0:T(8,128)(2,1)S(1)}, bf16[1080,128]{1,0:T(8,128)(2,1)S(1)}, u32[]{:S(2)}, u32[]{:S(2)}) collective-permute-start(bf16[1080,128]{1,0:T(8,128)(2,1)S(1)} %add_convert_fusion.26), channel_id=1, source_target_pairs={{0,8},{1,5},{8,16},{9,1},{16,24},{17,9},{24,26},{25,17},{26,18},{2... | collective-permute-start | bytes 829448 | tf_op jit(solution)/shard_map/ppermute | solution.py:47
  81.9 8.8 %collective-permute-start.5 = (bf16[1080,128]{1,0:T(8,128)(2,1)S(1)}, bf16[1080,128]{1,0:T(8,128)(2,1)S(1)}, u32[]{:S(2)}, u32[]{:S(2)}) collective-permute-start(bf16[1080,128]{1,0:T(8,128)(2,1)S(1)} %add_convert_fusion.40), channel_id=1, source_target_pairs={{0,8},{1,5},{8,16},{9,1},{16,24},{17,9},{24,26},{25,17},{26,18},{2... | collective-permute-start | bytes 829448 | tf_op jit(solution)/shard_map/ppermute | solution.py:47
  86.3 7.0 %collective-permute-start.36 = (bf16[1080,128]{1,0:T(8,128)(2,1)S(1)}, bf16[1080,128]{1,0:T(8,128)(2,1)S(1)}, u32[]{:S(2)}, u32[]{:S(2)}) collective-permute-start(bf16[1080,128]{1,0:T(8,128)(2,1)S(1)} %add_convert_fusion.11), channel_id=1, source_target_pairs={{0,8},{1,5},{8,16},{9,1},{16,24},{17,9},{24,26},{25,17},{26,18},{2... | collective-permute-start | bytes 829448 | tf_op jit(solution)/shard_map/ppermute | solution.py:47
  89.0 6.8 %collective-permute-start.21 = (bf16[1080,128]{1,0:T(8,128)(2,1)S(1)}, bf16[1080,128]{1,0:T(8,128)(2,1)S(1)}, u32[]{:S(2)}, u32[]{:S(2)}) collective-permute-start(bf16[1080,128]{1,0:T(8,128)(2,1)S(1)} %add_convert_fusion.25), channel_id=1, source_target_pairs={{0,8},{1,5},{8,16},{9,1},{16,24},{17,9},{24,26},{25,17},{26,18},{2... | collective-permute-start | bytes 829448 | tf_op jit(solution)/shard_map/ppermute | solution.py:47
  91.8 7.0 %collective-permute-start.6 = (bf16[1080,128]{1,0:T(8,128)(2,1)S(1)}, bf16[1080,128]{1,0:T(8,128)(2,1)S(1)}, u32[]{:S(2)}, u32[]{:S(2)}) collective-permute-start(bf16[1080,128]{1,0:T(8,128)(2,1)S(1)} %add_convert_fusion.39), channel_id=1, source_target_pairs={{0,8},{1,5},{8,16},{9,1},{16,24},{17,9},{24,26},{25,17},{26,18},{2... | collective-permute-start | bytes 829448 | tf_op jit(solution)/shard_map/ppermute | solution.py:47
  94.4 7.3 %collective-permute-start.37 = (bf16[1080,128]{1,0:T(8,128)(2,1)S(1)}, bf16[1080,128]{1,0:T(8,128)(2,1)S(1)}, u32[]{:S(2)}, u32[]{:S(2)}) collective-permute-start(bf16[1080,128]{1,0:T(8,128)(2,1)S(1)} %add_convert_fusion.10), channel_id=1, source_target_pairs={{0,8},{1,5},{8,16},{9,1},{16,24},{17,9},{24,26},{25,17},{26,18},{2... | collective-permute-start | bytes 829448 | tf_op jit(solution)/shard_map/ppermute | solution.py:47
  96.9 7.8 %collective-permute-start.22 = (bf16[1080,128]{1,0:T(8,128)(2,1)S(1)}, bf16[1080,128]{1,0:T(8,128)(2,1)S(1)}, u32[]{:S(2)}, u32[]{:S(2)}) collective-permute-start(bf16[1080,128]{1,0:T(8,128)(2,1)S(1)} %add_convert_fusion.24), channel_id=1, source_target_pairs={{0,8},{1,5},{8,16},{9,1},{16,24},{17,9},{24,26},{25,17},{26,18},{2... | collective-permute-start | bytes 829448 | tf_op jit(solution)/shard_map/ppermute | solution.py:47
  99.9 7.8 %collective-permute-start.7 = (bf16[1080,128]{1,0:T(8,128)(2,1)S(1)}, bf16[1080,128]{1,0:T(8,128)(2,1)S(1)}, u32[]{:S(2)}, u32[]{:S(2)}) collective-permute-start(bf16[1080,128]{1,0:T(8,128)(2,1)S(1)} %add_convert_fusion.38), channel_id=1, source_target_pairs={{0,8},{1,5},{8,16},{9,1},{16,24},{17,9},{24,26},{25,17},{26,18},{2... | collective-permute-start | bytes 829448 | tf_op jit(solution)/shard_map/ppermute | solution.py:47
  102.9 7.8 %collective-permute-start.38 = (bf16[1080,128]{1,0:T(8,128)(2,1)S(1)}, bf16[1080,128]{1,0:T(8,128)(2,1)S(1)}, u32[]{:S(2)}, u32[]{:S(2)}) collective-permute-start(bf16[1080,128]{1,0:T(8,128)(2,1)S(1)} %add_convert_fusion.9), channel_id=1, source_target_pairs={{0,8},{1,5},{8,16},{9,1},{16,24},{17,9},{24,26},{25,17},{26,18},{2... | collective-permute-start | bytes 829448 | tf_op jit(solution)/shard_map/ppermute | solution.py:47
  105.8 7.8 %collective-permute-start.23 = (bf16[1080,128]{1,0:T(8,128)(2,1)S(1)}, bf16[1080,128]{1,0:T(8,128)(2,1)S(1)}, u32[]{:S(2)}, u32[]{:S(2)}) collective-permute-start(bf16[1080,128]{1,0:T(8,128)(2,1)S(1)} %add_convert_fusion.23), channel_id=1, source_target_pairs={{0,8},{1,5},{8,16},{9,1},{16,24},{17,9},{24,26},{25,17},{26,18},{2... | collective-permute-start | bytes 829448 | tf_op jit(solution)/shard_map/ppermute | solution.py:47
  108.8 7.8 %collective-permute-start.8 = (bf16[1080,128]{1,0:T(8,128)(2,1)S(1)}, bf16[1080,128]{1,0:T(8,128)(2,1)S(1)}, u32[]{:S(2)}, u32[]{:S(2)}) collective-permute-start(bf16[1080,128]{1,0:T(8,128)(2,1)S(1)} %add_convert_fusion.37), channel_id=1, source_target_pairs={{0,8},{1,5},{8,16},{9,1},{16,24},{17,9},{24,26},{25,17},{26,18},{2... | collective-permute-start | bytes 829448 | tf_op jit(solution)/shard_map/ppermute | solution.py:47
  111.7 7.8 %collective-permute-start.39 = (bf16[1080,128]{1,0:T(8,128)(2,1)S(1)}, bf16[1080,128]{1,0:T(8,128)(2,1)S(1)}, u32[]{:S(2)}, u32[]{:S(2)}) collective-permute-start(bf16[1080,128]{1,0:T(8,128)(2,1)S(1)} %add_convert_fusion.8), channel_id=1, source_target_pairs={{0,8},{1,5},{8,16},{9,1},{16,24},{17,9},{24,26},{25,17},{26,18},{2... | collective-permute-start | bytes 829448 | tf_op jit(solution)/shard_map/ppermute | solution.py:47
  114.7 7.8 %collective-permute-start.24 = (bf16[1080,128]{1,0:T(8,128)(2,1)S(1)}, bf16[1080,128]{1,0:T(8,128)(2,1)S(1)}, u32[]{:S(2)}, u32[]{:S(2)}) collective-permute-start(bf16[1080,128]{1,0:T(8,128)(2,1)S(1)} %add_convert_fusion.22), channel_id=1, source_target_pairs={{0,8},{1,5},{8,16},{9,1},{16,24},{17,9},{24,26},{25,17},{26,18},{2... | collective-permute-start | bytes 829448 | tf_op jit(solution)/shard_map/ppermute | solution.py:47
  117.7 7.8 %collective-permute-start.9 = (bf16[1080,128]{1,0:T(8,128)(2,1)S(1)}, bf16[1080,128]{1,0:T(8,128)(2,1)S(1)}, u32[]{:S(2)}, u32[]{:S(2)}) collective-permute-start(bf16[1080,128]{1,0:T(8,128)(2,1)S(1)} %add_convert_fusion.36), channel_id=1, source_target_pairs={{0,8},{1,5},{8,16},{9,1},{16,24},{17,9},{24,26},{25,17},{26,18},{2... | collective-permute-start | bytes 829448 | tf_op jit(solution)/shard_map/ppermute | solution.py:47
  120.6 7.8 %collective-permute-start.40 = (bf16[1080,128]{1,0:T(8,128)(2,1)S(1)}, bf16[1080,128]{1,0:T(8,128)(2,1)S(1)}, u32[]{:S(2)}, u32[]{:S(2)}) collective-permute-start(bf16[1080,128]{1,0:T(8,128)(2,1)S(1)} %add_convert_fusion.7), channel_id=1, source_target_pairs={{0,8},{1,5},{8,16},{9,1},{16,24},{17,9},{24,26},{25,17},{26,18},{2... | collective-permute-start | bytes 829448 | tf_op jit(solution)/shard_map/ppermute | solution.py:47
  123.6 7.8 %collective-permute-start.25 = (bf16[1080,128]{1,0:T(8,128)(2,1)S(1)}, bf16[1080,128]{1,0:T(8,128)(2,1)S(1)}, u32[]{:S(2)}, u32[]{:S(2)}) collective-permute-start(bf16[1080,128]{1,0:T(8,128)(2,1)S(1)} %add_convert_fusion.21), channel_id=1, source_target_pairs={{0,8},{1,5},{8,16},{9,1},{16,24},{17,9},{24,26},{25,17},{26,18},{2... | collective-permute-start | bytes 829448 | tf_op jit(solution)/shard_map/ppermute | solution.py:47
  125.5 8.8 %collective-permute-start.10 = (bf16[1080,128]{1,0:T(8,128)(2,1)S(1)}, bf16[1080,128]{1,0:T(8,128)(2,1)S(1)}, u32[]{:S(2)}, u32[]{:S(2)}) collective-permute-start(bf16[1080,128]{1,0:T(8,128)(2,1)S(1)} %add_convert_fusion.35), channel_id=1, source_target_pairs={{0,8},{1,5},{8,16},{9,1},{16,24},{17,9},{24,26},{25,17},{26,18},{2... | collective-permute-start | bytes 829448 | tf_op jit(solution)/shard_map/ppermute | solution.py:47
  129.5 7.8 %collective-permute-start.41 = (bf16[1080,128]{1,0:T(8,128)(2,1)S(1)}, bf16[1080,128]{1,0:T(8,128)(2,1)S(1)}, u32[]{:S(2)}, u32[]{:S(2)}) collective-permute-start(bf16[1080,128]{1,0:T(8,128)(2,1)S(1)} %add_convert_fusion.6), channel_id=1, source_target_pairs={{0,8},{1,5},{8,16},{9,1},{16,24},{17,9},{24,26},{25,17},{26,18},{2... | collective-permute-start | bytes 829448 | tf_op jit(solution)/shard_map/ppermute | solution.py:47
  132.5 7.8 %collective-permute-start.26 = (bf16[1080,128]{1,0:T(8,128)(2,1)S(1)}, bf16[1080,128]{1,0:T(8,128)(2,1)S(1)}, u32[]{:S(2)}, u32[]{:S(2)}) collective-permute-start(bf16[1080,128]{1,0:T(8,128)(2,1)S(1)} %add_convert_fusion.20), channel_id=1, source_target_pairs={{0,8},{1,5},{8,16},{9,1},{16,24},{17,9},{24,26},{25,17},{26,18},{2... | collective-permute-start | bytes 829448 | tf_op jit(solution)/shard_map/ppermute | solution.py:47
  134.4 8.8 %collective-permute-start.11 = (bf16[1080,128]{1,0:T(8,128)(2,1)S(1)}, bf16[1080,128]{1,0:T(8,128)(2,1)S(1)}, u32[]{:S(2)}, u32[]{:S(2)}) collective-permute-start(bf16[1080,128]{1,0:T(8,128)(2,1)S(1)} %add_convert_fusion.34), channel_id=1, source_target_pairs={{0,8},{1,5},{8,16},{9,1},{16,24},{17,9},{24,26},{25,17},{26,18},{2... | collective-permute-start | bytes 829448 | tf_op jit(solution)/shard_map/ppermute | solution.py:47
  138.4 7.8 %collective-permute-start.42 = (bf16[1080,128]{1,0:T(8,128)(2,1)S(1)}, bf16[1080,128]{1,0:T(8,128)(2,1)S(1)}, u32[]{:S(2)}, u32[]{:S(2)}) collective-permute-start(bf16[1080,128]{1,0:T(8,128)(2,1)S(1)} %add_convert_fusion.5), channel_id=1, source_target_pairs={{0,8},{1,5},{8,16},{9,1},{16,24},{17,9},{24,26},{25,17},{26,18},{2... | collective-permute-start | bytes 829448 | tf_op jit(solution)/shard_map/ppermute | solution.py:47
  141.4 7.8 %collective-permute-start.27 = (bf16[1080,128]{1,0:T(8,128)(2,1)S(1)}, bf16[1080,128]{1,0:T(8,128)(2,1)S(1)}, u32[]{:S(2)}, u32[]{:S(2)}) collective-permute-start(bf16[1080,128]{1,0:T(8,128)(2,1)S(1)} %add_convert_fusion.19), channel_id=1, source_target_pairs={{0,8},{1,5},{8,16},{9,1},{16,24},{17,9},{24,26},{25,17},{26,18},{2... | collective-permute-start | bytes 829448 | tf_op jit(solution)/shard_map/ppermute | solution.py:47
  143.3 8.8 %collective-permute-start.12 = (bf16[1080,128]{1,0:T(8,128)(2,1)S(1)}, bf16[1080,128]{1,0:T(8,128)(2,1)S(1)}, u32[]{:S(2)}, u32[]{:S(2)}) collective-permute-start(bf16[1080,128]{1,0:T(8,128)(2,1)S(1)} %add_convert_fusion.33), channel_id=1, source_target_pairs={{0,8},{1,5},{8,16},{9,1},{16,24},{17,9},{24,26},{25,17},{26,18},{2... | collective-permute-start | bytes 829448 | tf_op jit(solution)/shard_map/ppermute | solution.py:47
  147.3 7.8 %collective-permute-start.43 = (bf16[1080,128]{1,0:T(8,128)(2,1)S(1)}, bf16[1080,128]{1,0:T(8,128)(2,1)S(1)}, u32[]{:S(2)}, u32[]{:S(2)}) collective-permute-start(bf16[1080,128]{1,0:T(8,128)(2,1)S(1)} %add_convert_fusion.4), channel_id=1, source_target_pairs={{0,8},{1,5},{8,16},{9,1},{16,24},{17,9},{24,26},{25,17},{26,18},{2... | collective-permute-start | bytes 829448 | tf_op jit(solution)/shard_map/ppermute | solution.py:47
  150.3 7.8 %collective-permute-start.28 = (bf16[1080,128]{1,0:T(8,128)(2,1)S(1)}, bf16[1080,128]{1,0:T(8,128)(2,1)S(1)}, u32[]{:S(2)}, u32[]{:S(2)}) collective-permute-start(bf16[1080,128]{1,0:T(8,128)(2,1)S(1)} %add_convert_fusion.18), channel_id=1, source_target_pairs={{0,8},{1,5},{8,16},{9,1},{16,24},{17,9},{24,26},{25,17},{26,18},{2... | collective-permute-start | bytes 829448 | tf_op jit(solution)/shard_map/ppermute | solution.py:47
  152.2 8.8 %collective-permute-start.13 = (bf16[1080,128]{1,0:T(8,128)(2,1)S(1)}, bf16[1080,128]{1,0:T(8,128)(2,1)S(1)}, u32[]{:S(2)}, u32[]{:S(2)}) collective-permute-start(bf16[1080,128]{1,0:T(8,128)(2,1)S(1)} %add_convert_fusion.32), channel_id=1, source_target_pairs={{0,8},{1,5},{8,16},{9,1},{16,24},{17,9},{24,26},{25,17},{26,18},{2... | collective-permute-start | bytes 829448 | tf_op jit(solution)/shard_map/ppermute | solution.py:47
  156.2 7.8 %collective-permute-start.44 = (bf16[1080,128]{1,0:T(8,128)(2,1)S(1)}, bf16[1080,128]{1,0:T(8,128)(2,1)S(1)}, u32[]{:S(2)}, u32[]{:S(2)}) collective-permute-start(bf16[1080,128]{1,0:T(8,128)(2,1)S(1)} %add_convert_fusion.3), channel_id=1, source_target_pairs={{0,8},{1,5},{8,16},{9,1},{16,24},{17,9},{24,26},{25,17},{26,18},{2... | collective-permute-start | bytes 829448 | tf_op jit(solution)/shard_map/ppermute | solution.py:47
  159.2 7.8 %collective-permute-start.29 = (bf16[1080,128]{1,0:T(8,128)(2,1)S(1)}, bf16[1080,128]{1,0:T(8,128)(2,1)S(1)}, u32[]{:S(2)}, u32[]{:S(2)}) collective-permute-start(bf16[1080,128]{1,0:T(8,128)(2,1)S(1)} %add_convert_fusion.17), channel_id=1, source_target_pairs={{0,8},{1,5},{8,16},{9,1},{16,24},{17,9},{24,26},{25,17},{26,18},{2... | collective-permute-start | bytes 829448 | tf_op jit(solution)/shard_map/ppermute | solution.py:47
  161.1 8.8 %collective-permute-start.14 = (bf16[1080,128]{1,0:T(8,128)(2,1)S(1)}, bf16[1080,128]{1,0:T(8,128)(2,1)S(1)}, u32[]{:S(2)}, u32[]{:S(2)}) collective-permute-start(bf16[1080,128]{1,0:T(8,128)(2,1)S(1)} %add_convert_fusion.31), channel_id=1, source_target_pairs={{0,8},{1,5},{8,16},{9,1},{16,24},{17,9},{24,26},{25,17},{26,18},{2... | collective-permute-start | bytes 829448 | tf_op jit(solution)/shard_map/ppermute | solution.py:47
  165.1 7.8 %collective-permute-start.45 = (bf16[1080,128]{1,0:T(8,128)(2,1)S(1)}, bf16[1080,128]{1,0:T(8,128)(2,1)S(1)}, u32[]{:S(2)}, u32[]{:S(2)}) collective-permute-start(bf16[1080,128]{1,0:T(8,128)(2,1)S(1)} %add_convert_fusion.2), channel_id=1, source_target_pairs={{0,8},{1,5},{8,16},{9,1},{16,24},{17,9},{24,26},{25,17},{26,18},{2... | collective-permute-start | bytes 829448 | tf_op jit(solution)/shard_map/ppermute | solution.py:47
  168.0 7.8 %collective-permute-start.30 = (bf16[1080,128]{1,0:T(8,128)(2,1)S(1)}, bf16[1080,128]{1,0:T(8,128)(2,1)S(1)}, u32[]{:S(2)}, u32[]{:S(2)}) collective-permute-start(bf16[1080,128]{1,0:T(8,128)(2,1)S(1)} %add_convert_fusion.16), channel_id=1, source_target_pairs={{0,8},{1,5},{8,16},{9,1},{16,24},{17,9},{24,26},{25,17},{26,18},{2... | collective-permute-start | bytes 829448 | tf_op jit(solution)/shard_map/ppermute | solution.py:47
  169.9 8.8 %collective-permute-start.15 = (bf16[1080,128]{1,0:T(8,128)(2,1)S(1)}, bf16[1080,128]{1,0:T(8,128)(2,1)S(1)}, u32[]{:S(2)}, u32[]{:S(2)}) collective-permute-start(bf16[1080,128]{1,0:T(8,128)(2,1)S(1)} %add_convert_fusion.30), channel_id=1, source_target_pairs={{0,8},{1,5},{8,16},{9,1},{16,24},{17,9},{24,26},{25,17},{26,18},{2... | collective-permute-start | bytes 829448 | tf_op jit(solution)/shard_map/ppermute | solution.py:47
  174.0 7.8 %collective-permute-start.46 = (bf16[1080,128]{1,0:T(8,128)(2,1)S(1)}, bf16[1080,128]{1,0:T(8,128)(2,1)S(1)}, u32[]{:S(2)}, u32[]{:S(2)}) collective-permute-start(bf16[1080,128]{1,0:T(8,128)(2,1)S(1)} %add_convert_fusion.1), channel_id=1, source_target_pairs={{0,8},{1,5},{8,16},{9,1},{16,24},{17,9},{24,26},{25,17},{26,18},{2... | collective-permute-start | bytes 829448 | tf_op jit(solution)/shard_map/ppermute | solution.py:47
  177.0 7.7 %collective-permute-start.31 = (bf16[1080,128]{1,0:T(8,128)(2,1)S(1)}, bf16[1080,128]{1,0:T(8,128)(2,1)S(1)}, u32[]{:S(2)}, u32[]{:S(2)}) collective-permute-start(bf16[1080,128]{1,0:T(8,128)(2,1)S(1)} %add_convert_fusion.15), channel_id=1, source_target_pairs={{0,8},{1,5},{8,16},{9,1},{16,24},{17,9},{24,26},{25,17},{26,18},{2... | collective-permute-start | bytes 829448 | tf_op jit(solution)/shard_map/ppermute | solution.py:47
  178.8 8.8 %collective-permute-start.16 = (bf16[1080,128]{1,0:T(8,128)(2,1)S(1)}, bf16[1080,128]{1,0:T(8,128)(2,1)S(1)}, u32[]{:S(2)}, u32[]{:S(2)}) collective-permute-start(bf16[1080,128]{1,0:T(8,128)(2,1)S(1)} %add_convert_fusion.29), channel_id=1, source_target_pairs={{0,8},{1,5},{8,16},{9,1},{16,24},{17,9},{24,26},{25,17},{26,18},{2... | collective-permute-start | bytes 829448 | tf_op jit(solution)/shard_map/ppermute | solution.py:47
  182.9 7.8 %collective-permute-start.47 = (bf16[1080,128]{1,0:T(8,128)(2,1)S(1)}, bf16[1080,128]{1,0:T(8,128)(2,1)S(1)}, u32[]{:S(2)}, u32[]{:S(2)}) collective-permute-start(bf16[1080,128]{1,0:T(8,128)(2,1)S(1)} %add_convert_fusion), channel_id=1, source_target_pairs={{0,8},{1,5},{8,16},{9,1},{16,24},{17,9},{24,26},{25,17},{26,18},{2... | collective-permute-start | bytes 829448 | tf_op jit(solution)/shard_map/ppermute | solution.py:47
  185.8 7.8 %collective-permute-start.32 = (bf16[1080,128]{1,0:T(8,128)(2,1)S(1)}, bf16[1080,128]{1,0:T(8,128)(2,1)S(1)}, u32[]{:S(2)}, u32[]{:S(2)}) collective-permute-start(bf16[1080,128]{1,0:T(8,128)(2,1)S(1)} %add_convert_fusion.14), channel_id=1, source_target_pairs={{0,8},{1,5},{8,16},{9,1},{16,24},{17,9},{24,26},{25,17},{26,18},{2... | collective-permute-start | bytes 829448 | tf_op jit(solution)/shard_map/ppermute | solution.py:47
  187.7 8.8 %collective-permute-start.17 = (bf16[1080,128]{1,0:T(8,128)(2,1)S(1)}, bf16[1080,128]{1,0:T(8,128)(2,1)S(1)}, u32[]{:S(2)}, u32[]{:S(2)}) collective-permute-start(bf16[1080,128]{1,0:T(8,128)(2,1)S(1)} %add_convert_fusion.28), channel_id=1, source_target_pairs={{0,8},{1,5},{8,16},{9,1},{16,24},{17,9},{24,26},{25,17},{26,18},{2... | collective-permute-start | bytes 829448 | tf_op jit(solution)/shard_map/ppermute | solution.py:47
  (6 other events, 174.1 us)

commit v11 on v10

--- a/solution.py
+++ b/solution.py
@@ -49,49 +49,50 @@
     return accs
 
 
-def _ffn_block(hh, h, count, col_ref, tok_ref, cot_ref, wg_ref, wu_ref, wd_ref,
-               gg_ref, gu_ref, gd_ref, dxt_ref):
-    slots = gg_ref.shape[1]
+def _slot_offsets(col_ref, h, slots):
+    return [pl.multiple_of(col_ref[h, p] * BLK, BLK) for p in range(slots)]
+
+
+def _stacked(w_ref, hh, count, slots):
+    w = w_ref[hh].reshape(slots * BLK, BLK)
+    live = lax.broadcasted_iota(jnp.int32, w.shape, 0) < count * BLK
+    return jnp.where(live, w, jnp.zeros_like(w))
+
+
+def _forward_kernel(col_ref, cnt_ref, tok_ref, cot_ref, wg_ref, wu_ref, wd_ref, gd_ref, dgu_ref):
+    step = pl.program_id(0)
+    per_step, slots = gd_ref.shape[0], gd_ref.shape[1]
     f32 = jnp.float32
-    offs = [pl.multiple_of(col_ref[h, p] * BLK, BLK) for p in range(slots)]
-    x = jnp.concatenate([tok_ref[:, pl.ds(o, BLK)] for o in offs], axis=1)
-    dy = jnp.concatenate([cot_ref[:, pl.ds(o, BLK)] for o in offs], axis=1)
-    stacked = (slots * BLK, BLK)
-    live_rows = lax.broadcasted_iota(jnp.int32, stacked, 0) < count * BLK
-    wg = wg_ref[hh].reshape(stacked)
-    wu = wu_ref[hh].reshape(stacked)
-    wg = jnp.where(live_rows, wg, jnp.zeros_like(wg))
-    wu = jnp.where(live_rows, wu, jnp.zeros_like(wu))
-    wd = jnp.concatenate([wd_ref[hh, p] for p in range(slots)], axis=1)
-    live_cols = lax.broadcasted_iota(jnp.int32, wd.shape, 1) < count * BLK
-    wd = jnp.where(live_cols, wd, jnp.zeros_like(wd))
-    gate = jnp.dot(x, wg, preferred_element_type=f32)
-    up = jnp.dot(x, wu, preferred_element_type=f32)
-    d_hidden = lax.dot_general(dy, wd, (((1,), (1,)), ((), ())), preferred_element_type=f32)
-    sig = 1.0 / (1.0 + jnp.exp(-gate))
-    silu = gate * sig
-    hidden = (silu * up).astype(jnp.bfloat16)
-    d_gate = (d_hidden * up * sig * (1.0 + gate * (1.0 - sig))).astype(jnp.bfloat16)
-    d_up = (d_hidden * silu).astype(jnp.bfloat16)
-    d_gu = jnp.concatenate([d_gate, d_up], axis=1)
-    grad_gu = jnp.dot(x.T, d_gu, preferred_element_type=f32)
-    grad_d = jnp.dot(hidden.T, dy, preferred_element_type=f32)
-    back_t = jnp.dot(wg, d_gate.T, preferred_element_type=f32)
-    back_t = back_t + jnp.dot(wu, d_up.T, preferred_element_type=f32)
-    for p in range(slots):
-        live = p < count
+    for hh in range(per_step):
+        h = step * per_step + hh
+        count = cnt_ref[h]
+        offs = _slot_offsets(col_ref, h, slots)
+        x = jnp.concatenate([tok_ref[:, pl.ds(o, BLK)] for o in offs], axis=1)
+        dy = jnp.concatenate([cot_ref[:, pl.ds(o, BLK)] for o in offs], axis=1)
+        wg = _stacked(wg_ref, hh, count, slots)
+        wu = _stacked(wu_ref, hh, count, slots)
+        wd = jnp.concatenate([wd_ref[hh, p] for p in range(slots)], axis=1)
+        live_cols = lax.broadcasted_iota(jnp.int32, wd.shape, 1) < count * BLK
+        wd = jnp.where(live_cols, wd, jnp.zeros_like(wd))
+        gate = jnp.dot(x, wg, preferred_element_type=f32)
+        up = jnp.dot(x, wu, preferred_element_type=f32)
+        d_hidden = lax.dot_general(dy, wd, (((1,), (1,)), ((), ())), preferred_element_type=f32)
+        sig = 1.0 / (1.0 + jnp.exp(-gate))
+        silu = gate * sig
+        hidden = (silu * up).astype(jnp.bfloat16)
+        d_gate = (d_hidden * up * sig * (1.0 + gate * (1.0 - sig))).astype(jnp.bfloat16)
+        d_up = (d_hidden * silu).astype(jnp.bfloat16)
+        dgu_ref[hh] = jnp.concatenate([d_gate, d_up], axis=1)
+        grad_d = jnp.dot(hidden.T, dy, preferred_element_type=f32)
         zero = jnp.zeros((BLK, BLK), f32)
-        rows = slice(p * BLK, (p + 1) * BLK)
-        gg_ref[hh, p] = jnp.where(live, grad_gu[rows, :BLK], zero)
-        gu_ref[hh, p] = jnp.where(live, grad_gu[rows, BLK:], zero)
-        gd_ref[hh, p] = jnp.where(live, grad_d[:, rows], zero)
-        dxt_ref[pl.ds(offs[p], BLK), :] += back_t[rows]
-
-
-def _ffn_kernel(col_ref, cnt_ref, tok_ref, cot_ref, wg_ref, wu_ref, wd_ref,
-                gg_ref, gu_ref, gd_ref, dxt_ref):
+        for p in range(slots):
+            gd_ref[hh, p] = jnp.where(p < count, grad_d[:, p * BLK:(p + 1) * BLK], zero)
+
+
+def _backward_kernel(col_ref, cnt_ref, tok_ref, dgu_ref, wg_ref, wu_ref, gg_ref, gu_ref, dxt_ref):
     step = pl.program_id(0)
-    per_step = gg_ref.shape[0]
+    per_step, slots = gg_ref.shape[0], gg_ref.shape[1]
+    f32 = jnp.float32
 
     @pl.when(step == 0)
     def _():
@@ -99,8 +100,21 @@
 
     for hh in range(per_step):
         h = step * per_step + hh
-        _ffn_block(hh, h, cnt_ref[h], col_ref, tok_ref, cot_ref, wg_ref, wu_ref, wd_ref,
-                   gg_ref, gu_ref, gd_ref, dxt_ref)
+        count = cnt_ref[h]
+        offs = _slot_offsets(col_ref, h, slots)
+        x = jnp.concatenate([tok_ref[:, pl.ds(o, BLK)] for o in offs], axis=1)
+        wg = _stacked(wg_ref, hh, count, slots)
+        wu = _stacked(wu_ref, hh, count, slots)
+        d_gu = dgu_ref[hh]
+        grad_gu = jnp.dot(x.T, d_gu, preferred_element_type=f32)
+        back_t = jnp.dot(wg, d_gu[:, :BLK].T, preferred_element_type=f32)
+        back_t = back_t + jnp.dot(wu, d_gu[:, BLK:].T, preferred_element_type=f32)
+        zero = jnp.zeros((BLK, BLK), f32)
+        for p in range(slots):
+            rows = slice(p * BLK, (p + 1) * BLK)
+            gg_ref[hh, p] = jnp.where(p < count, grad_gu[rows, :BLK], zero)
+            gu_ref[hh, p] = jnp.where(p < count, grad_gu[rows, BLK:], zero)
+            dxt_ref[pl.ds(offs[p], BLK), :] += back_t[rows]
 
 
 def ffn_block_terms(col_index, row_count, full_tok, full_cot, gate_w, up_w, down_w):
@@ -108,28 +122,48 @@
     rows, width = full_tok.shape
     per_step = 9 if hblk % 9 == 0 else (3 if hblk % 3 == 0 else 1)
     wspec = pl.BlockSpec((per_step, slots, BLK, BLK), lambda h, c, n: (h, 0, 0, 0))
+    dspec = pl.BlockSpec((per_step, rows, 2 * BLK), lambda h, c, n: (h, 0, 0))
     full = pl.BlockSpec((rows, width), lambda h, c, n: (0, 0))
     full_t = pl.BlockSpec((width, rows), lambda h, c, n: (0, 0))
-    gspec = wspec
     grad = jax.ShapeDtypeStruct((hblk, slots, BLK, BLK), jnp.float32)
-    flops = 2 * rows * hblk * slots * BLK * BLK * 9
-    return pl.pallas_call(
-        _ffn_kernel,
+    dgu = jax.ShapeDtypeStruct((hblk, rows, 2 * BLK), jnp.bfloat16)
+    unit = 2 * rows * hblk * slots * BLK * BLK
+    params = pltpu.CompilerParams(dimension_semantics=("arbitrary",))
+    grad_down, d_gu = pl.pallas_call(
+        _forward_kernel,
         grid_spec=pltpu.PrefetchScalarGridSpec(
             num_scalar_prefetch=2,
             grid=(hblk // per_step,),
             in_specs=[full, full, wspec, wspec, wspec],
-            out_specs=[gspec, gspec, gspec, full_t],
-        ),
-        out_shape=[grad, grad, grad, jax.ShapeDtypeStruct((width, rows), jnp.float32)],
-        compiler_params=pltpu.CompilerParams(dimension_semantics=("arbitrary",)),
+            out_specs=[wspec, dspec],
+        ),
+        out_shape=[grad, dgu],
+        compiler_params=params,
         cost_estimate=pl.CostEstimate(
-            flops=flops,
+            flops=4 * unit,
             transcendentals=rows * hblk * BLK,
-            bytes_accessed=3 * hblk * slots * BLK * BLK * 6 + rows * width * 8,
-        ),
-        name="ffn_block_terms",
+            bytes_accessed=hblk * slots * BLK * BLK * 10 + rows * width * 4,
+        ),
+        name="ffn_forward_terms",
     )(col_index, row_count, full_tok, full_cot, gate_w, up_w, down_w)
+    grad_gate, grad_up, dx_t = pl.pallas_call(
+        _backward_kernel,
+        grid_spec=pltpu.PrefetchScalarGridSpec(
+            num_scalar_prefetch=2,
+            grid=(hblk // per_step,),
+            in_specs=[full, dspec, wspec, wspec],
+            out_specs=[wspec, wspec, full_t],
+        ),
+        out_shape=[grad, grad, jax.ShapeDtypeStruct((width, rows), jnp.float32)],
+        compiler_params=params,
+        cost_estimate=pl.CostEstimate(
+            flops=5 * unit,
+            transcendentals=0,
+            bytes_accessed=hblk * slots * BLK * BLK * 12 + rows * width * 6,
+        ),
+        name="ffn_backward_terms",
+    )(col_index, row_count, full_tok, d_gu, gate_w, up_w)
+    return grad_gate, grad_up, grad_down, dx_t
 
 
 def shards(n_dp, n_t, tokens, cotangent, w_gate, w_up, w_down, col_index, row_count, adam_m, adam_v):
@@ -151,15 +185,14 @@
     grad_gate, grad_up, grad_down, dx_part = ffn_block_terms(
         col_index, row_count, full_tok, full_cot, w_gate[0], w_up[0], w_down[0]
     )
-    reduced = jnp.stack(
-        ring_reduce_scatter(
-            [g.reshape(own_rows, BLK) for g in (grad_gate, grad_up, grad_down)],
-            n_dp,
-            n_t,
-            ring_order(n_dp),
-            jnp.bfloat16,
-        )
-    )[:, None]
+    red_down, red_gate, red_up = ring_reduce_scatter(
+        [g.reshape(own_rows, BLK) for g in (grad_down, grad_gate, grad_up)],
+        n_dp,
+        n_t,
+        ring_order(n_dp),
+        jnp.bfloat16,
+    )
+    reduced = jnp.stack([red_gate, red_up, red_down])[:, None]
     if n_t == 2:
         half = tokens.shape[1]
         lo, hi = dx_part[:half].T, dx_part[half:].T

time: 202 us -> 208 us (1.030)
  Pallas kernels: 24.3 us -> 31.6 us
  starting transfers between devices: 75.6 us -> 70.5 us
  waiting for transfers between devices: 18.9 us -> 23.2 us
    pallas_call x1 -> x2, Pallas kernels: 24.3 us -> 31.6 us  [the longest x1 16.1 us: ffn_block_terms(): pl.pallas_call(_forward_kernel, grid_spec=pltpu.PrefetchScalarGridSpec(nu...]
    ppermute x45, starting transfers between devices: 74.5 us -> 69.8 us  [ring_reduce_scatter(): moved = lax.ppermute(accs[i].astype(wire_dtype), ('dp', 'tensor'), perm)]
    ppermute x45, waiting for transfers between devices: 18.9 us -> 23.2 us  [ring_reduce_scatter(): moved = lax.ppermute(accs[i].astype(wire_dtype), ('dp', 'tensor'), perm)]
  transfers between devices with their start and end apart: 48 -> 48, of which waited for: 35 -> 40; matrix products, arithmetic and copies ran while one was open for 25% -> 25% of each run, Pallas kernels for 0% -> 8%
where the time goes in v11:
time: 208 us; the launch traced here: 206 us
  starting transfers between devices  70.5 us (34%)
  other arithmetic  49.6 us (24%)
  Pallas kernels  31.6 us (15%)
  waiting for transfers between devices  23.2 us (11%)
  between operations  21.8 us (10%)
  local copies, waits for them, and re-layouts  9 us (4%)
    ppermute x45, starting transfers between devices, ring_reduce_scatter(): moved = lax.ppermute(accs[i].astype(wire_dtype), ('dp', 'tensor'), perm)  69.8 us
    convert_element_type x42, other arithmetic, ring_reduce_scatter(): moved = lax.ppermute(accs[i].astype(wire_dtype), ('dp', 'tensor'), perm)  38.7 us
    ppermute x45, waiting for transfers between devices, ring_reduce_scatter(): moved = lax.ppermute(accs[i].astype(wire_dtype), ('dp', 'tensor'), perm)  23.2 us
    pallas_call x1, Pallas kernels, ffn_block_terms(): pl.pallas_call(_forward_kernel, grid_spec=pltpu.PrefetchScalarGridSpec(nu...  16.1 us
    pallas_call x1, Pallas kernels, ffn_block_terms(): pl.pallas_call(_backward_kernel, grid_spec=pltpu.PrefetchScalarGridSpec(n...  15.5 us
  transfers between devices with their start and end apart: 48, of which 40 were waited for; matrix products, arithmetic and copies ran while one was open for 25% of the time, Pallas kernels for 8%

profile of v11, /device:TPU:0, one launch (start us, length us, event | category | flops | bytes accessed | tf_op | source)
XLA Modules:
  0.0 205.7 jit_solution(10573246819053620993)
XLA Ops:
  13.2 2.0 fusion.2
  30.6 16.1 %ffn_forward_terms.1 = (f32[27,5,128,128]{3,2,1,0:T(8,128)}, bf16[27,128,256]{2,1,0:T(8,128)(2,1)}) custom-call(s32[27,5]{1,0:T(8,128)} %copy.16.col_ref, s32[27]{0:T(128)} %cnt_ref.3, bf16[128,5120]{1,0:T(8,128)(2,1)} %pad_maximum_fusion.1.tok_ref, bf16[128,5120]{1,0:T(8,128)(2,1)} %pad_maximum_fusion.2.cot_ref, bf16[27,5,128,128]{3,2,1,0:T(8,128)(2,1)} %bitcast.35, ...), custom_call_target="tpu_custom_call" | custom-call | flops 2264924160 | bytes 24739840 | tf_op jit(solution)/shard_map/ffn_forward_terms/pallas_call | solution.py:132
  47.8 3.1 %collective-permute-start.33 = (bf16[1080,128]{1,0:T(8,128)(2,1)S(1)}, bf16[1080,128]{1,0:T(8,128)(2,1)S(1)}, u32[]{:S(2)}, u32[]{:S(2)}) collective-permute-start(bf16[1080,128]{1,0:T(8,128)(2,1)S(1)} %dynamic-slice_convert_fusion), channel_id=1, source_target_pairs={{0,8},{1,5},{8,16},{9,1},{16,24},{17,9},{24,26},{25,17},{26,18},{2... | collective-permute-start | bytes 829448 | tf_op jit(solution)/shard_map/ppermute | solution.py:47
  50.8 15.5 %ffn_backward_terms.1 = (f32[27,5,128,128]{3,2,1,0:T(8,128)}, f32[27,5,128,128]{3,2,1,0:T(8,128)}, f32[5120,128]{1,0:T(8,128)}) custom-call(s32[27,5]{1,0:T(8,128)} %copy.16.col_ref, s32[27]{0:T(128)} %cnt_ref.3, bf16[128,5120]{1,0:T(8,128)(2,1)} %pad_maximum_fusion.1.tok_ref, bf16[27,128,256]{2,1,0:T(8,128)(2,1)} %get-tuple-element.9.dgu_ref, ...), custom_call_target="tpu_custom_call" | custom-call | flops 2831155200 | bytes 30474240 | tf_op jit(solution)/shard_map/ffn_backward_terms/pallas_call | solution.py:149
  68.5 1.6 collective-permute-start.3
  70.2 1.6 collective-permute-start.18
  71.8 1.8 fusion.1
  74.8 1.5 collective-permute-start.34
  79.2 1.6 collective-permute-start.19
  82.5 1.5 collective-permute-start.35
  85.5 1.5 collective-permute-start.5
  88.5 1.5 collective-permute-start.20
  95.1 1.5 collective-permute-start.6
  100.3 1.5 collective-permute-start.37
  103.2 1.5 collective-permute-start.7
  106.2 1.5 collective-permute-start.22
  109.2 1.5 collective-permute-start.38
  112.1 1.5 collective-permute-start.8
  115.1 1.5 collective-permute-start.23
  118.0 1.5 collective-permute-start.39
  121.0 1.5 collective-permute-start.9
  124.0 1.5 collective-permute-start.24
  126.9 1.5 collective-permute-start.40
  129.9 1.5 collective-permute-start.10
  131.8 1.5 collective-permute-start.25
  135.8 1.5 collective-permute-start.41
  138.8 1.5 collective-permute-start.11
  144.7 1.5 collective-permute-start.42
  147.7 1.5 collective-permute-start.12
  149.6 1.7 collective-permute-start.27
  153.6 1.5 collective-permute-start.43
  156.6 1.5 collective-permute-start.13
  158.5 1.5 collective-permute-start.28
  162.5 1.5 collective-permute-start.44
  165.4 1.5 collective-permute-start.14
  167.4 1.5 collective-permute-start.29
  171.4 1.5 collective-permute-start.45
  174.3 1.5 collective-permute-start.15
  176.2 1.6 collective-permute-start.30
  180.3 1.5 collective-permute-start.46
  183.2 1.5 collective-permute-start.16
  185.1 1.5 collective-permute-start.31
  189.1 1.5 collective-permute-start.47
  192.1 1.5 collective-permute-start.17
  194.0 1.5 collective-permute-start.32
  198.0 1.9 collective-permute-done.17
  201.0 1.9 collective-permute-done.32
  202.9 2.8 %add_divide_fusion = (f32[3,1,1080,128]{3,2,1,0:T(8,128)}, f32[3,1,1080,128]{3,2,1,0:T(8,128)}, f32[3,1,1080,128]{3,2,1,0:T(8,128)}) fusion(f32[1,1,1080,128]{3,2,1,0:T(8,128)S(1)} %add_bitcast_fusion, f32[1,1,1080,128]{3,2,1,0:T(8,128)S(1)} %add_bitcast_fusion.1, f32[1,1,1080,128]{3,2,1,0:T(8,128)S(1)} %add_bitcast_fusion.2, ...), kind=kLoop, calls=%fused_computation.1 | loop fusion | flops 4976640 | bytes 9953280 | tf_op jit(solution)/shard_map/div | solution.py:210
  (121 shorter events, 76.7 us)
Async XLA Ops:
  0.6 26.1 %collective-permute-start = (bf16[128,2560]{1,0:T(8,128)(2,1)}, bf16[128,2560]{1,0:T(8,128)(2,1)S(1)}, u32[]{:S(2)}, u32[]{:S(2)}) collective-permute-start(bf16[128,2560]{1,0:T(8,128)(2,1)} %param.11), channel_id=1, source_target_pairs={{0,1},{1,0},{2,3},{3,2},{4,5},{5,4},{6,7},{7,6},{8,9},{9,8},{10,11... | collective-permute-start | bytes 1966088 | tf_op jit(solution)/shard_map/ppermute | solution.py:173
  1.1 25.6 %collective-permute-start.1 = (bf16[128,2560]{1,0:T(8,128)(2,1)}, bf16[128,2560]{1,0:T(8,128)(2,1)S(1)}, u32[]{:S(2)}, u32[]{:S(2)}) collective-permute-start(bf16[128,2560]{1,0:T(8,128)(2,1)} %param.12), channel_id=1, source_target_pairs={{0,1},{1,0},{2,3},{3,2},{4,5},{5,4},{6,7},{7,6},{8,9},{9,8},{10,11... | collective-permute-start | bytes 1966088 | tf_op jit(solution)/shard_map/ppermute | solution.py:173
  47.8 25.9 %collective-permute-start.33 = (bf16[1080,128]{1,0:T(8,128)(2,1)S(1)}, bf16[1080,128]{1,0:T(8,128)(2,1)S(1)}, u32[]{:S(2)}, u32[]{:S(2)}) collective-permute-start(bf16[1080,128]{1,0:T(8,128)(2,1)S(1)} %dynamic-slice_convert_fusion), channel_id=1, source_target_pairs={{0,8},{1,5},{8,16},{9,1},{16,24},{17,9},{24,26},{25,17},{26,18},{2... | collective-permute-start | bytes 829448 | tf_op jit(solution)/shard_map/ppermute | solution.py:47
  68.5 7.8 %collective-permute-start.3 = (bf16[1080,128]{1,0:T(8,128)(2,1)S(1)}, bf16[1080,128]{1,0:T(8,128)(2,1)S(1)}, u32[]{:S(2)}, u32[]{:S(2)}) collective-permute-start(bf16[1080,128]{1,0:T(8,128)(2,1)S(1)} %dynamic-slice_convert_fusion.2), channel_id=1, source_target_pairs={{0,8},{1,5},{8,16},{9,1},{16,24},{17,9},{24,26},{25,17},{26,18},{2... | collective-permute-start | bytes 829448 | tf_op jit(solution)/shard_map/ppermute | solution.py:47
  70.2 7.9 %collective-permute-start.18 = (bf16[1080,128]{1,0:T(8,128)(2,1)S(1)}, bf16[1080,128]{1,0:T(8,128)(2,1)S(1)}, u32[]{:S(2)}, u32[]{:S(2)}) collective-permute-start(bf16[1080,128]{1,0:T(8,128)(2,1)S(1)} %dynamic-slice_convert_fusion.1), channel_id=1, source_target_pairs={{0,8},{1,5},{8,16},{9,1},{16,24},{17,9},{24,26},{25,17},{26,18},{2... | collective-permute-start | bytes 829448 | tf_op jit(solution)/shard_map/ppermute | solution.py:47
  73.6 16.4 %collective-permute-start.2 = (bf16[128,2560]{0,1:T(8,128)(2,1)S(1)}, bf16[128,2560]{0,1:T(8,128)(2,1)S(1)}, u32[]{:S(2)}, u32[]{:S(2)}) collective-permute-start(bf16[128,2560]{0,1:T(8,128)(2,1)S(1)} %fusion.1), channel_id=1, source_target_pairs={{0,1},{1,0},{2,3},{3,2},{4,5},{5,4},{6,7},{7,6},{8,9},{9,8},{10,11... | collective-permute-start | bytes 1966088 | tf_op jit(solution)/shard_map/ppermute | solution.py:200
  74.8 6.6 %collective-permute-start.34 = (bf16[1080,128]{1,0:T(8,128)(2,1)S(1)}, bf16[1080,128]{1,0:T(8,128)(2,1)S(1)}, u32[]{:S(2)}, u32[]{:S(2)}) collective-permute-start(bf16[1080,128]{1,0:T(8,128)(2,1)S(1)} %add_convert_fusion.13), channel_id=1, source_target_pairs={{0,8},{1,5},{8,16},{9,1},{16,24},{17,9},{24,26},{25,17},{26,18},{2... | collective-permute-start | bytes 829448 | tf_op jit(solution)/shard_map/ppermute | solution.py:47
  77.5 6.9 %collective-permute-start.4 = (bf16[1080,128]{1,0:T(8,128)(2,1)S(1)}, bf16[1080,128]{1,0:T(8,128)(2,1)S(1)}, u32[]{:S(2)}, u32[]{:S(2)}) collective-permute-start(bf16[1080,128]{1,0:T(8,128)(2,1)S(1)} %add_convert_fusion.41), channel_id=1, source_target_pairs={{0,8},{1,5},{8,16},{9,1},{16,24},{17,9},{24,26},{25,17},{26,18},{2... | collective-permute-start | bytes 829448 | tf_op jit(solution)/shard_map/ppermute | solution.py:47
  79.2 8.1 %collective-permute-start.19 = (bf16[1080,128]{1,0:T(8,128)(2,1)S(1)}, bf16[1080,128]{1,0:T(8,128)(2,1)S(1)}, u32[]{:S(2)}, u32[]{:S(2)}) collective-permute-start(bf16[1080,128]{1,0:T(8,128)(2,1)S(1)} %add_convert_fusion.27), channel_id=1, source_target_pairs={{0,8},{1,5},{8,16},{9,1},{16,24},{17,9},{24,26},{25,17},{26,18},{2... | collective-permute-start | bytes 829448 | tf_op jit(solution)/shard_map/ppermute | solution.py:47
  82.5 8.8 %collective-permute-start.35 = (bf16[1080,128]{1,0:T(8,128)(2,1)S(1)}, bf16[1080,128]{1,0:T(8,128)(2,1)S(1)}, u32[]{:S(2)}, u32[]{:S(2)}) collective-permute-start(bf16[1080,128]{1,0:T(8,128)(2,1)S(1)} %add_convert_fusion.12), channel_id=1, source_target_pairs={{0,8},{1,5},{8,16},{9,1},{16,24},{17,9},{24,26},{25,17},{26,18},{2... | collective-permute-start | bytes 829448 | tf_op jit(solution)/shard_map/ppermute | solution.py:47
  85.5 8.5 %collective-permute-start.5 = (bf16[1080,128]{1,0:T(8,128)(2,1)S(1)}, bf16[1080,128]{1,0:T(8,128)(2,1)S(1)}, u32[]{:S(2)}, u32[]{:S(2)}) collective-permute-start(bf16[1080,128]{1,0:T(8,128)(2,1)S(1)} %add_convert_fusion.40), channel_id=1, source_target_pairs={{0,8},{1,5},{8,16},{9,1},{16,24},{17,9},{24,26},{25,17},{26,18},{2... | collective-permute-start | bytes 829448 | tf_op jit(solution)/shard_map/ppermute | solution.py:47
  88.5 8.1 %collective-permute-start.20 = (bf16[1080,128]{1,0:T(8,128)(2,1)S(1)}, bf16[1080,128]{1,0:T(8,128)(2,1)S(1)}, u32[]{:S(2)}, u32[]{:S(2)}) collective-permute-start(bf16[1080,128]{1,0:T(8,128)(2,1)S(1)} %add_convert_fusion.26), channel_id=1, source_target_pairs={{0,8},{1,5},{8,16},{9,1},{16,24},{17,9},{24,26},{25,17},{26,18},{2... | collective-permute-start | bytes 829448 | tf_op jit(solution)/shard_map/ppermute | solution.py:47
  92.6 6.6 %collective-permute-start.36 = (bf16[1080,128]{1,0:T(8,128)(2,1)S(1)}, bf16[1080,128]{1,0:T(8,128)(2,1)S(1)}, u32[]{:S(2)}, u32[]{:S(2)}) collective-permute-start(bf16[1080,128]{1,0:T(8,128)(2,1)S(1)} %add_convert_fusion.11), channel_id=1, source_target_pairs={{0,8},{1,5},{8,16},{9,1},{16,24},{17,9},{24,26},{25,17},{26,18},{2... | collective-permute-start | bytes 829448 | tf_op jit(solution)/shard_map/ppermute | solution.py:47
  95.1 7.0 %collective-permute-start.6 = (bf16[1080,128]{1,0:T(8,128)(2,1)S(1)}, bf16[1080,128]{1,0:T(8,128)(2,1)S(1)}, u32[]{:S(2)}, u32[]{:S(2)}) collective-permute-start(bf16[1080,128]{1,0:T(8,128)(2,1)S(1)} %add_convert_fusion.39), channel_id=1, source_target_pairs={{0,8},{1,5},{8,16},{9,1},{16,24},{17,9},{24,26},{25,17},{26,18},{2... | collective-permute-start | bytes 829448 | tf_op jit(solution)/shard_map/ppermute | solution.py:47
  97.7 7.3 %collective-permute-start.21 = (bf16[1080,128]{1,0:T(8,128)(2,1)S(1)}, bf16[1080,128]{1,0:T(8,128)(2,1)S(1)}, u32[]{:S(2)}, u32[]{:S(2)}) collective-permute-start(bf16[1080,128]{1,0:T(8,128)(2,1)S(1)} %add_convert_fusion.25), channel_id=1, source_target_pairs={{0,8},{1,5},{8,16},{9,1},{16,24},{17,9},{24,26},{25,17},{26,18},{2... | collective-permute-start | bytes 829448 | tf_op jit(solution)/shard_map/ppermute | solution.py:47
  100.3 7.8 %collective-permute-start.37 = (bf16[1080,128]{1,0:T(8,128)(2,1)S(1)}, bf16[1080,128]{1,0:T(8,128)(2,1)S(1)}, u32[]{:S(2)}, u32[]{:S(2)}) collective-permute-start(bf16[1080,128]{1,0:T(8,128)(2,1)S(1)} %add_convert_fusion.10), channel_id=1, source_target_pairs={{0,8},{1,5},{8,16},{9,1},{16,24},{17,9},{24,26},{25,17},{26,18},{2... | collective-permute-start | bytes 829448 | tf_op jit(solution)/shard_map/ppermute | solution.py:47
  103.2 7.8 %collective-permute-start.7 = (bf16[1080,128]{1,0:T(8,128)(2,1)S(1)}, bf16[1080,128]{1,0:T(8,128)(2,1)S(1)}, u32[]{:S(2)}, u32[]{:S(2)}) collective-permute-start(bf16[1080,128]{1,0:T(8,128)(2,1)S(1)} %add_convert_fusion.38), channel_id=1, source_target_pairs={{0,8},{1,5},{8,16},{9,1},{16,24},{17,9},{24,26},{25,17},{26,18},{2... | collective-permute-start | bytes 829448 | tf_op jit(solution)/shard_map/ppermute | solution.py:47
  106.2 7.8 %collective-permute-start.22 = (bf16[1080,128]{1,0:T(8,128)(2,1)S(1)}, bf16[1080,128]{1,0:T(8,128)(2,1)S(1)}, u32[]{:S(2)}, u32[]{:S(2)}) collective-permute-start(bf16[1080,128]{1,0:T(8,128)(2,1)S(1)} %add_convert_fusion.24), channel_id=1, source_target_pairs={{0,8},{1,5},{8,16},{9,1},{16,24},{17,9},{24,26},{25,17},{26,18},{2... | collective-permute-start | bytes 829448 | tf_op jit(solution)/shard_map/ppermute | solution.py:47
  109.2 7.8 %collective-permute-start.38 = (bf16[1080,128]{1,0:T(8,128)(2,1)S(1)}, bf16[1080,128]{1,0:T(8,128)(2,1)S(1)}, u32[]{:S(2)}, u32[]{:S(2)}) collective-permute-start(bf16[1080,128]{1,0:T(8,128)(2,1)S(1)} %add_convert_fusion.9), channel_id=1, source_target_pairs={{0,8},{1,5},{8,16},{9,1},{16,24},{17,9},{24,26},{25,17},{26,18},{2... | collective-permute-start | bytes 829448 | tf_op jit(solution)/shard_map/ppermute | solution.py:47
  112.1 7.8 %collective-permute-start.8 = (bf16[1080,128]{1,0:T(8,128)(2,1)S(1)}, bf16[1080,128]{1,0:T(8,128)(2,1)S(1)}, u32[]{:S(2)}, u32[]{:S(2)}) collective-permute-start(bf16[1080,128]{1,0:T(8,128)(2,1)S(1)} %add_convert_fusion.37), channel_id=1, source_target_pairs={{0,8},{1,5},{8,16},{9,1},{16,24},{17,9},{24,26},{25,17},{26,18},{2... | collective-permute-start | bytes 829448 | tf_op jit(solution)/shard_map/ppermute | solution.py:47
  115.1 7.8 %collective-permute-start.23 = (bf16[1080,128]{1,0:T(8,128)(2,1)S(1)}, bf16[1080,128]{1,0:T(8,128)(2,1)S(1)}, u32[]{:S(2)}, u32[]{:S(2)}) collective-permute-start(bf16[1080,128]{1,0:T(8,128)(2,1)S(1)} %add_convert_fusion.23), channel_id=1, source_target_pairs={{0,8},{1,5},{8,16},{9,1},{16,24},{17,9},{24,26},{25,17},{26,18},{2... | collective-permute-start | bytes 829448 | tf_op jit(solution)/shard_map/ppermute | solution.py:47
  118.0 7.8 %collective-permute-start.39 = (bf16[1080,128]{1,0:T(8,128)(2,1)S(1)}, bf16[1080,128]{1,0:T(8,128)(2,1)S(1)}, u32[]{:S(2)}, u32[]{:S(2)}) collective-permute-start(bf16[1080,128]{1,0:T(8,128)(2,1)S(1)} %add_convert_fusion.8), channel_id=1, source_target_pairs={{0,8},{1,5},{8,16},{9,1},{16,24},{17,9},{24,26},{25,17},{26,18},{2... | collective-permute-start | bytes 829448 | tf_op jit(solution)/shard_map/ppermute | solution.py:47
  121.0 7.8 %collective-permute-start.9 = (bf16[1080,128]{1,0:T(8,128)(2,1)S(1)}, bf16[1080,128]{1,0:T(8,128)(2,1)S(1)}, u32[]{:S(2)}, u32[]{:S(2)}) collective-permute-start(bf16[1080,128]{1,0:T(8,128)(2,1)S(1)} %add_convert_fusion.36), channel_id=1, source_target_pairs={{0,8},{1,5},{8,16},{9,1},{16,24},{17,9},{24,26},{25,17},{26,18},{2... | collective-permute-start | bytes 829448 | tf_op jit(solution)/shard_map/ppermute | solution.py:47
  124.0 7.8 %collective-permute-start.24 = (bf16[1080,128]{1,0:T(8,128)(2,1)S(1)}, bf16[1080,128]{1,0:T(8,128)(2,1)S(1)}, u32[]{:S(2)}, u32[]{:S(2)}) collective-permute-start(bf16[1080,128]{1,0:T(8,128)(2,1)S(1)} %add_convert_fusion.22), channel_id=1, source_target_pairs={{0,8},{1,5},{8,16},{9,1},{16,24},{17,9},{24,26},{25,17},{26,18},{2... | collective-permute-start | bytes 829448 | tf_op jit(solution)/shard_map/ppermute | solution.py:47
  126.9 7.8 %collective-permute-start.40 = (bf16[1080,128]{1,0:T(8,128)(2,1)S(1)}, bf16[1080,128]{1,0:T(8,128)(2,1)S(1)}, u32[]{:S(2)}, u32[]{:S(2)}) collective-permute-start(bf16[1080,128]{1,0:T(8,128)(2,1)S(1)} %add_convert_fusion.7), channel_id=1, source_target_pairs={{0,8},{1,5},{8,16},{9,1},{16,24},{17,9},{24,26},{25,17},{26,18},{2... | collective-permute-start | bytes 829448 | tf_op jit(solution)/shard_map/ppermute | solution.py:47
  129.9 7.8 %collective-permute-start.10 = (bf16[1080,128]{1,0:T(8,128)(2,1)S(1)}, bf16[1080,128]{1,0:T(8,128)(2,1)S(1)}, u32[]{:S(2)}, u32[]{:S(2)}) collective-permute-start(bf16[1080,128]{1,0:T(8,128)(2,1)S(1)} %add_convert_fusion.35), channel_id=1, source_target_pairs={{0,8},{1,5},{8,16},{9,1},{16,24},{17,9},{24,26},{25,17},{26,18},{2... | collective-permute-start | bytes 829448 | tf_op jit(solution)/shard_map/ppermute | solution.py:47
  131.8 8.8 %collective-permute-start.25 = (bf16[1080,128]{1,0:T(8,128)(2,1)S(1)}, bf16[1080,128]{1,0:T(8,128)(2,1)S(1)}, u32[]{:S(2)}, u32[]{:S(2)}) collective-permute-start(bf16[1080,128]{1,0:T(8,128)(2,1)S(1)} %add_convert_fusion.21), channel_id=1, source_target_pairs={{0,8},{1,5},{8,16},{9,1},{16,24},{17,9},{24,26},{25,17},{26,18},{2... | collective-permute-start | bytes 829448 | tf_op jit(solution)/shard_map/ppermute | solution.py:47
  135.8 7.8 %collective-permute-start.41 = (bf16[1080,128]{1,0:T(8,128)(2,1)S(1)}, bf16[1080,128]{1,0:T(8,128)(2,1)S(1)}, u32[]{:S(2)}, u32[]{:S(2)}) collective-permute-start(bf16[1080,128]{1,0:T(8,128)(2,1)S(1)} %add_convert_fusion.6), channel_id=1, source_target_pairs={{0,8},{1,5},{8,16},{9,1},{16,24},{17,9},{24,26},{25,17},{26,18},{2... | collective-permute-start | bytes 829448 | tf_op jit(solution)/shard_map/ppermute | solution.py:47
  138.8 7.8 %collective-permute-start.11 = (bf16[1080,128]{1,0:T(8,128)(2,1)S(1)}, bf16[1080,128]{1,0:T(8,128)(2,1)S(1)}, u32[]{:S(2)}, u32[]{:S(2)}) collective-permute-start(bf16[1080,128]{1,0:T(8,128)(2,1)S(1)} %add_convert_fusion.34), channel_id=1, source_target_pairs={{0,8},{1,5},{8,16},{9,1},{16,24},{17,9},{24,26},{25,17},{26,18},{2... | collective-permute-start | bytes 829448 | tf_op jit(solution)/shard_map/ppermute | solution.py:47
  140.7 8.8 %collective-permute-start.26 = (bf16[1080,128]{1,0:T(8,128)(2,1)S(1)}, bf16[1080,128]{1,0:T(8,128)(2,1)S(1)}, u32[]{:S(2)}, u32[]{:S(2)}) collective-permute-start(bf16[1080,128]{1,0:T(8,128)(2,1)S(1)} %add_convert_fusion.20), channel_id=1, source_target_pairs={{0,8},{1,5},{8,16},{9,1},{16,24},{17,9},{24,26},{25,17},{26,18},{2... | collective-permute-start | bytes 829448 | tf_op jit(solution)/shard_map/ppermute | solution.py:47
  144.7 7.8 %collective-permute-start.42 = (bf16[1080,128]{1,0:T(8,128)(2,1)S(1)}, bf16[1080,128]{1,0:T(8,128)(2,1)S(1)}, u32[]{:S(2)}, u32[]{:S(2)}) collective-permute-start(bf16[1080,128]{1,0:T(8,128)(2,1)S(1)} %add_convert_fusion.5), channel_id=1, source_target_pairs={{0,8},{1,5},{8,16},{9,1},{16,24},{17,9},{24,26},{25,17},{26,18},{2... | collective-permute-start | bytes 829448 | tf_op jit(solution)/shard_map/ppermute | solution.py:47
  147.7 7.8 %collective-permute-start.12 = (bf16[1080,128]{1,0:T(8,128)(2,1)S(1)}, bf16[1080,128]{1,0:T(8,128)(2,1)S(1)}, u32[]{:S(2)}, u32[]{:S(2)}) collective-permute-start(bf16[1080,128]{1,0:T(8,128)(2,1)S(1)} %add_convert_fusion.33), channel_id=1, source_target_pairs={{0,8},{1,5},{8,16},{9,1},{16,24},{17,9},{24,26},{25,17},{26,18},{2... | collective-permute-start | bytes 829448 | tf_op jit(solution)/shard_map/ppermute | solution.py:47
  149.6 8.8 %collective-permute-start.27 = (bf16[1080,128]{1,0:T(8,128)(2,1)S(1)}, bf16[1080,128]{1,0:T(8,128)(2,1)S(1)}, u32[]{:S(2)}, u32[]{:S(2)}) collective-permute-start(bf16[1080,128]{1,0:T(8,128)(2,1)S(1)} %add_convert_fusion.19), channel_id=1, source_target_pairs={{0,8},{1,5},{8,16},{9,1},{16,24},{17,9},{24,26},{25,17},{26,18},{2... | collective-permute-start | bytes 829448 | tf_op jit(solution)/shard_map/ppermute | solution.py:47
  153.6 7.8 %collective-permute-start.43 = (bf16[1080,128]{1,0:T(8,128)(2,1)S(1)}, bf16[1080,128]{1,0:T(8,128)(2,1)S(1)}, u32[]{:S(2)}, u32[]{:S(2)}) collective-permute-start(bf16[1080,128]{1,0:T(8,128)(2,1)S(1)} %add_convert_fusion.4), channel_id=1, source_target_pairs={{0,8},{1,5},{8,16},{9,1},{16,24},{17,9},{24,26},{25,17},{26,18},{2... | collective-permute-start | bytes 829448 | tf_op jit(solution)/shard_map/ppermute | solution.py:47
  156.6 7.8 %collective-permute-start.13 = (bf16[1080,128]{1,0:T(8,128)(2,1)S(1)}, bf16[1080,128]{1,0:T(8,128)(2,1)S(1)}, u32[]{:S(2)}, u32[]{:S(2)}) collective-permute-start(bf16[1080,128]{1,0:T(8,128)(2,1)S(1)} %add_convert_fusion.32), channel_id=1, source_target_pairs={{0,8},{1,5},{8,16},{9,1},{16,24},{17,9},{24,26},{25,17},{26,18},{2... | collective-permute-start | bytes 829448 | tf_op jit(solution)/shard_map/ppermute | solution.py:47
  158.5 8.8 %collective-permute-start.28 = (bf16[1080,128]{1,0:T(8,128)(2,1)S(1)}, bf16[1080,128]{1,0:T(8,128)(2,1)S(1)}, u32[]{:S(2)}, u32[]{:S(2)}) collective-permute-start(bf16[1080,128]{1,0:T(8,128)(2,1)S(1)} %add_convert_fusion.18), channel_id=1, source_target_pairs={{0,8},{1,5},{8,16},{9,1},{16,24},{17,9},{24,26},{25,17},{26,18},{2... | collective-permute-start | bytes 829448 | tf_op jit(solution)/shard_map/ppermute | solution.py:47
  162.5 7.8 %collective-permute-start.44 = (bf16[1080,128]{1,0:T(8,128)(2,1)S(1)}, bf16[1080,128]{1,0:T(8,128)(2,1)S(1)}, u32[]{:S(2)}, u32[]{:S(2)}) collective-permute-start(bf16[1080,128]{1,0:T(8,128)(2,1)S(1)} %add_convert_fusion.3), channel_id=1, source_target_pairs={{0,8},{1,5},{8,16},{9,1},{16,24},{17,9},{24,26},{25,17},{26,18},{2... | collective-permute-start | bytes 829448 | tf_op jit(solution)/shard_map/ppermute | solution.py:47
  165.4 7.8 %collective-permute-start.14 = (bf16[1080,128]{1,0:T(8,128)(2,1)S(1)}, bf16[1080,128]{1,0:T(8,128)(2,1)S(1)}, u32[]{:S(2)}, u32[]{:S(2)}) collective-permute-start(bf16[1080,128]{1,0:T(8,128)(2,1)S(1)} %add_convert_fusion.31), channel_id=1, source_target_pairs={{0,8},{1,5},{8,16},{9,1},{16,24},{17,9},{24,26},{25,17},{26,18},{2... | collective-permute-start | bytes 829448 | tf_op jit(solution)/shard_map/ppermute | solution.py:47
  167.4 8.8 %collective-permute-start.29 = (bf16[1080,128]{1,0:T(8,128)(2,1)S(1)}, bf16[1080,128]{1,0:T(8,128)(2,1)S(1)}, u32[]{:S(2)}, u32[]{:S(2)}) collective-permute-start(bf16[1080,128]{1,0:T(8,128)(2,1)S(1)} %add_convert_fusion.17), channel_id=1, source_target_pairs={{0,8},{1,5},{8,16},{9,1},{16,24},{17,9},{24,26},{25,17},{26,18},{2... | collective-permute-start | bytes 829448 | tf_op jit(solution)/shard_map/ppermute | solution.py:47
  171.4 7.8 %collective-permute-start.45 = (bf16[1080,128]{1,0:T(8,128)(2,1)S(1)}, bf16[1080,128]{1,0:T(8,128)(2,1)S(1)}, u32[]{:S(2)}, u32[]{:S(2)}) collective-permute-start(bf16[1080,128]{1,0:T(8,128)(2,1)S(1)} %add_convert_fusion.2), channel_id=1, source_target_pairs={{0,8},{1,5},{8,16},{9,1},{16,24},{17,9},{24,26},{25,17},{26,18},{2... | collective-permute-start | bytes 829448 | tf_op jit(solution)/shard_map/ppermute | solution.py:47
  174.3 7.8 %collective-permute-start.15 = (bf16[1080,128]{1,0:T(8,128)(2,1)S(1)}, bf16[1080,128]{1,0:T(8,128)(2,1)S(1)}, u32[]{:S(2)}, u32[]{:S(2)}) collective-permute-start(bf16[1080,128]{1,0:T(8,128)(2,1)S(1)} %add_convert_fusion.30), channel_id=1, source_target_pairs={{0,8},{1,5},{8,16},{9,1},{16,24},{17,9},{24,26},{25,17},{26,18},{2... | collective-permute-start | bytes 829448 | tf_op jit(solution)/shard_map/ppermute | solution.py:47
  176.2 8.8 %collective-permute-start.30 = (bf16[1080,128]{1,0:T(8,128)(2,1)S(1)}, bf16[1080,128]{1,0:T(8,128)(2,1)S(1)}, u32[]{:S(2)}, u32[]{:S(2)}) collective-permute-start(bf16[1080,128]{1,0:T(8,128)(2,1)S(1)} %add_convert_fusion.16), channel_id=1, source_target_pairs={{0,8},{1,5},{8,16},{9,1},{16,24},{17,9},{24,26},{25,17},{26,18},{2... | collective-permute-start | bytes 829448 | tf_op jit(solution)/shard_map/ppermute | solution.py:47
  180.3 7.8 %collective-permute-start.46 = (bf16[1080,128]{1,0:T(8,128)(2,1)S(1)}, bf16[1080,128]{1,0:T(8,128)(2,1)S(1)}, u32[]{:S(2)}, u32[]{:S(2)}) collective-permute-start(bf16[1080,128]{1,0:T(8,128)(2,1)S(1)} %add_convert_fusion.1), channel_id=1, source_target_pairs={{0,8},{1,5},{8,16},{9,1},{16,24},{17,9},{24,26},{25,17},{26,18},{2... | collective-permute-start | bytes 829448 | tf_op jit(solution)/shard_map/ppermute | solution.py:47
  183.2 7.7 %collective-permute-start.16 = (bf16[1080,128]{1,0:T(8,128)(2,1)S(1)}, bf16[1080,128]{1,0:T(8,128)(2,1)S(1)}, u32[]{:S(2)}, u32[]{:S(2)}) collective-permute-start(bf16[1080,128]{1,0:T(8,128)(2,1)S(1)} %add_convert_fusion.29), channel_id=1, source_target_pairs={{0,8},{1,5},{8,16},{9,1},{16,24},{17,9},{24,26},{25,17},{26,18},{2... | collective-permute-start | bytes 829448 | tf_op jit(solution)/shard_map/ppermute | solution.py:47
  185.1 8.8 %collective-permute-start.31 = (bf16[1080,128]{1,0:T(8,128)(2,1)S(1)}, bf16[1080,128]{1,0:T(8,128)(2,1)S(1)}, u32[]{:S(2)}, u32[]{:S(2)}) collective-permute-start(bf16[1080,128]{1,0:T(8,128)(2,1)S(1)} %add_convert_fusion.15), channel_id=1, source_target_pairs={{0,8},{1,5},{8,16},{9,1},{16,24},{17,9},{24,26},{25,17},{26,18},{2... | collective-permute-start | bytes 829448 | tf_op jit(solution)/shard_map/ppermute | solution.py:47
  189.1 7.8 %collective-permute-start.47 = (bf16[1080,128]{1,0:T(8,128)(2,1)S(1)}, bf16[1080,128]{1,0:T(8,128)(2,1)S(1)}, u32[]{:S(2)}, u32[]{:S(2)}) collective-permute-start(bf16[1080,128]{1,0:T(8,128)(2,1)S(1)} %add_convert_fusion), channel_id=1, source_target_pairs={{0,8},{1,5},{8,16},{9,1},{16,24},{17,9},{24,26},{25,17},{26,18},{2... | collective-permute-start | bytes 829448 | tf_op jit(solution)/shard_map/ppermute | solution.py:47
  192.1 7.8 %collective-permute-start.17 = (bf16[1080,128]{1,0:T(8,128)(2,1)S(1)}, bf16[1080,128]{1,0:T(8,128)(2,1)S(1)}, u32[]{:S(2)}, u32[]{:S(2)}) collective-permute-start(bf16[1080,128]{1,0:T(8,128)(2,1)S(1)} %add_convert_fusion.28), channel_id=1, source_target_pairs={{0,8},{1,5},{8,16},{9,1},{16,24},{17,9},{24,26},{25,17},{26,18},{2... | collective-permute-start | bytes 829448 | tf_op jit(solution)/shard_map/ppermute | solution.py:47
  194.0 8.8 %collective-permute-start.32 = (bf16[1080,128]{1,0:T(8,128)(2,1)S(1)}, bf16[1080,128]{1,0:T(8,128)(2,1)S(1)}, u32[]{:S(2)}, u32[]{:S(2)}) collective-permute-start(bf16[1080,128]{1,0:T(8,128)(2,1)S(1)} %add_convert_fusion.14), channel_id=1, source_target_pairs={{0,8},{1,5},{8,16},{9,1},{16,24},{17,9},{24,26},{25,17},{26,18},{2... | collective-permute-start | bytes 829448 | tf_op jit(solution)/shard_map/ppermute | solution.py:47
  (6 other events, 168.3 us)

commit v12 on v10

--- a/solution.py
+++ b/solution.py
@@ -136,7 +136,7 @@
     swap = [(0, 1), (1, 0)]
     first = lax.axis_index("tensor") == 0
     if n_t == 2:
-        other_tok, other_cot = lax.ppermute((tokens, cotangent), "tensor", swap)
+        other_tok, other_cot = lax.ppermute(jnp.stack([tokens, cotangent]), "tensor", swap)
         full_tok = jnp.concatenate(
             [jnp.where(first, tokens, other_tok), jnp.where(first, other_tok, tokens)], axis=1
         )

time: 202 us -> 200 us (0.990)
  local copies, waits for them, and re-layouts: 9.23 us -> 6.44 us
  transfers between devices with their start and end apart: 48 -> 47, of which waited for: 35 -> 34; matrix products, arithmetic and copies ran while one was open for 25% -> 24% of each run, Pallas kernels for 0% -> 0%
where the time goes in v12:
time: 200 us; the launch traced here: 198 us
  starting transfers between devices  75.9 us (38%)
  other arithmetic  50.5 us (25%)
  Pallas kernels  24.4 us (12%)
  between operations  21.7 us (11%)
  waiting for transfers between devices  18.6 us (9%)
  local copies, waits for them, and re-layouts  6.44 us (3%)
    ppermute x45, starting transfers between devices, ring_reduce_scatter(): moved = lax.ppermute(accs[i].astype(wire_dtype), ('dp', 'tensor'), perm)  75.3 us
    convert_element_type x42, other arithmetic, ring_reduce_scatter(): moved = lax.ppermute(accs[i].astype(wire_dtype), ('dp', 'tensor'), perm)  38.7 us
    pallas_call x1, Pallas kernels, ffn_block_terms(): pl.pallas_call(_ffn_kernel, grid_spec=pltpu.PrefetchScalarGridSpec(num_sc...  24.4 us
    ppermute x45, waiting for transfers between devices, ring_reduce_scatter(): moved = lax.ppermute(accs[i].astype(wire_dtype), ('dp', 'tensor'), perm)  18.6 us
  transfers between devices with their start and end apart: 47, of which 34 were waited for; matrix products, arithmetic and copies ran while one was open for 24% of the time, Pallas kernels for 0%

profile of v12, /device:TPU:0, one launch (start us, length us, event | category | flops | bytes accessed | tf_op | source)
XLA Modules:
  0.0 197.5 jit_solution(3743362871939256388)
XLA Ops:
  27.0 1.8 pad_maximum_fusion.2
  28.8 24.4 %ffn_block_terms.1 = (f32[27,5,128,128]{3,2,1,0:T(8,128)}, f32[27,5,128,128]{3,2,1,0:T(8,128)}, f32[27,5,128,128]{3,2,1,0:T(8,128)}, f32[5120,128]{1,0:T(8,128)}) custom-call(s32[27,5]{1,0:T(8,128)} %copy.15.col_ref, s32[27]{0:T(128)} %cnt_ref.1, bf16[128,5120]{1,0:T(8,128)(2,1)} %get-tuple-element.41.tok_ref, bf16[128,5120]{1,0:T(8,128)(2,1)} %get-tuple-element.42.cot_ref, ...), custom_call_target="tpu_custom_call" | custom-call | flops 5096079360 | bytes 45056000 | tf_op jit(solution)/shard_map/ffn_block_terms/pallas_call | solution.py:116
  53.2 1.8 fusion.1
  56.2 3.1 %collective-permute-start.32 = (bf16[1080,128]{1,0:T(8,128)(2,1)S(1)}, bf16[1080,128]{1,0:T(8,128)(2,1)S(1)}, u32[]{:S(2)}, u32[]{:S(2)}) collective-permute-start(bf16[1080,128]{1,0:T(8,128)(2,1)S(1)} %dynamic-slice_convert_fusion), channel_id=1, source_target_pairs={{0,8},{1,5},{8,16},{9,1},{16,24},{17,9},{24,26},{25,17},{26,18},{2... | collective-permute-start | bytes 829448 | tf_op jit(solution)/shard_map/ppermute | solution.py:47
  60.4 1.6 collective-permute-start.17
  63.1 1.6 collective-permute-start.2
  65.9 1.5 collective-permute-start.33
  71.1 1.8 collective-permute-start.3
  74.0 1.8 collective-permute-start.34
  77.0 1.8 collective-permute-start.19
  80.0 1.8 collective-permute-start.4
  84.4 1.6 collective-permute-start.35
  87.2 1.6 collective-permute-start.20
  95.0 1.6 collective-permute-start.21
  98.0 1.6 collective-permute-start.6
  101.0 1.6 collective-permute-start.37
  103.9 1.6 collective-permute-start.22
  106.9 1.6 collective-permute-start.7
  109.9 1.6 collective-permute-start.38
  112.8 1.6 collective-permute-start.23
  115.8 1.6 collective-permute-start.8
  118.7 1.6 collective-permute-start.39
  121.7 1.6 collective-permute-start.24
  123.7 1.6 collective-permute-start.9
  127.6 1.6 collective-permute-start.40
  130.6 1.6 collective-permute-start.25
  132.5 1.6 collective-permute-start.10
  136.5 1.6 collective-permute-start.41
  139.5 1.8 collective-permute-start.26
  141.4 1.6 collective-permute-start.11
  145.4 1.6 collective-permute-start.42
  148.4 1.6 collective-permute-start.27
  150.3 1.6 collective-permute-start.12
  154.3 1.6 collective-permute-start.43
  157.3 1.6 collective-permute-start.28
  159.2 1.6 collective-permute-start.13
  163.2 1.6 collective-permute-start.44
  166.2 1.6 collective-permute-start.29
  168.1 1.6 collective-permute-start.14
  172.1 1.6 collective-permute-start.45
  175.0 1.6 collective-permute-start.30
  176.9 1.6 collective-permute-start.15
  181.0 1.6 collective-permute-start.46
  184.0 1.6 collective-permute-start.31
  185.8 1.6 collective-permute-start.16
  189.8 1.9 collective-permute-done.31
  192.8 1.9 collective-permute-done.16
  194.7 2.8 %add_divide_fusion = (f32[3,1,1080,128]{3,2,1,0:T(8,128)}, f32[3,1,1080,128]{3,2,1,0:T(8,128)}, f32[3,1,1080,128]{3,2,1,0:T(8,128)}) fusion(f32[1,1,1080,128]{3,2,1,0:T(8,128)S(1)} %add_bitcast_fusion, f32[1,1,1080,128]{3,2,1,0:T(8,128)S(1)} %add_bitcast_fusion.1, f32[1,1,1080,128]{3,2,1,0:T(8,128)S(1)} %add_bitcast_fusion.2, ...), kind=kLoop, calls=%fused_computation.1 | loop fusion | flops 4976640 | bytes 9953280 | tf_op jit(solution)/shard_map/div | solution.py:177
  (128 shorter events, 70.2 us)
Async XLA Ops:
  2.2 23.4 %collective-permute-start = (bf16[2,128,2560]{2,1,0:T(8,128)(2,1)S(1)}, bf16[2,128,2560]{2,1,0:T(8,128)(2,1)}, u32[]{:S(2)}, u32[]{:S(2)}) collective-permute-start(bf16[2,128,2560]{2,1,0:T(8,128)(2,1)S(1)} %pad_maximum_fusion.1), channel_id=1, source_target_pairs={{0,1},{1,0},{2,3},{3,2},{4,5},{5,4},{6,7},{7,6},{8,9},{9,8},{10,11... | collective-permute-start | bytes 3932168 | tf_op jit(solution)/shard_map/ppermute | solution.py:139
  55.0 26.8 %collective-permute-start.1 = (bf16[128,2560]{0,1:T(8,128)(2,1)S(1)}, bf16[128,2560]{0,1:T(8,128)(2,1)S(1)}, u32[]{:S(2)}, u32[]{:S(2)}) collective-permute-start(bf16[128,2560]{0,1:T(8,128)(2,1)S(1)} %fusion.1), channel_id=1, source_target_pairs={{0,1},{1,0},{2,3},{3,2},{4,5},{5,4},{6,7},{7,6},{8,9},{9,8},{10,11... | collective-permute-start | bytes 1966088 | tf_op jit(solution)/shard_map/ppermute | solution.py:167
  56.2 8.5 %collective-permute-start.32 = (bf16[1080,128]{1,0:T(8,128)(2,1)S(1)}, bf16[1080,128]{1,0:T(8,128)(2,1)S(1)}, u32[]{:S(2)}, u32[]{:S(2)}) collective-permute-start(bf16[1080,128]{1,0:T(8,128)(2,1)S(1)} %dynamic-slice_convert_fusion), channel_id=1, source_target_pairs={{0,8},{1,5},{8,16},{9,1},{16,24},{17,9},{24,26},{25,17},{26,18},{2... | collective-permute-start | bytes 829448 | tf_op jit(solution)/shard_map/ppermute | solution.py:47
  60.4 7.0 %collective-permute-start.17 = (bf16[1080,128]{1,0:T(8,128)(2,1)S(1)}, bf16[1080,128]{1,0:T(8,128)(2,1)S(1)}, u32[]{:S(2)}, u32[]{:S(2)}) collective-permute-start(bf16[1080,128]{1,0:T(8,128)(2,1)S(1)} %dynamic-slice_convert_fusion.1), channel_id=1, source_target_pairs={{0,8},{1,5},{8,16},{9,1},{16,24},{17,9},{24,26},{25,17},{26,18},{2... | collective-permute-start | bytes 829448 | tf_op jit(solution)/shard_map/ppermute | solution.py:47
  63.1 6.9 %collective-permute-start.2 = (bf16[1080,128]{1,0:T(8,128)(2,1)S(1)}, bf16[1080,128]{1,0:T(8,128)(2,1)S(1)}, u32[]{:S(2)}, u32[]{:S(2)}) collective-permute-start(bf16[1080,128]{1,0:T(8,128)(2,1)S(1)} %dynamic-slice_convert_fusion.2), channel_id=1, source_target_pairs={{0,8},{1,5},{8,16},{9,1},{16,24},{17,9},{24,26},{25,17},{26,18},{2... | collective-permute-start | bytes 829448 | tf_op jit(solution)/shard_map/ppermute | solution.py:47
  65.9 7.1 %collective-permute-start.33 = (bf16[1080,128]{1,0:T(8,128)(2,1)S(1)}, bf16[1080,128]{1,0:T(8,128)(2,1)S(1)}, u32[]{:S(2)}, u32[]{:S(2)}) collective-permute-start(bf16[1080,128]{1,0:T(8,128)(2,1)S(1)} %add_convert_fusion.13), channel_id=1, source_target_pairs={{0,8},{1,5},{8,16},{9,1},{16,24},{17,9},{24,26},{25,17},{26,18},{2... | collective-permute-start | bytes 829448 | tf_op jit(solution)/shard_map/ppermute | solution.py:47
  68.5 7.4 %collective-permute-start.18 = (bf16[1080,128]{1,0:T(8,128)(2,1)S(1)}, bf16[1080,128]{1,0:T(8,128)(2,1)S(1)}, u32[]{:S(2)}, u32[]{:S(2)}) collective-permute-start(bf16[1080,128]{1,0:T(8,128)(2,1)S(1)} %add_convert_fusion.27), channel_id=1, source_target_pairs={{0,8},{1,5},{8,16},{9,1},{16,24},{17,9},{24,26},{25,17},{26,18},{2... | collective-permute-start | bytes 829448 | tf_op jit(solution)/shard_map/ppermute | solution.py:47
  71.1 7.8 %collective-permute-start.3 = (bf16[1080,128]{1,0:T(8,128)(2,1)S(1)}, bf16[1080,128]{1,0:T(8,128)(2,1)S(1)}, u32[]{:S(2)}, u32[]{:S(2)}) collective-permute-start(bf16[1080,128]{1,0:T(8,128)(2,1)S(1)} %add_convert_fusion.41), channel_id=1, source_target_pairs={{0,8},{1,5},{8,16},{9,1},{16,24},{17,9},{24,26},{25,17},{26,18},{2... | collective-permute-start | bytes 829448 | tf_op jit(solution)/shard_map/ppermute | solution.py:47
  74.0 9.1 %collective-permute-start.34 = (bf16[1080,128]{1,0:T(8,128)(2,1)S(1)}, bf16[1080,128]{1,0:T(8,128)(2,1)S(1)}, u32[]{:S(2)}, u32[]{:S(2)}) collective-permute-start(bf16[1080,128]{1,0:T(8,128)(2,1)S(1)} %add_convert_fusion.12), channel_id=1, source_target_pairs={{0,8},{1,5},{8,16},{9,1},{16,24},{17,9},{24,26},{25,17},{26,18},{2... | collective-permute-start | bytes 829448 | tf_op jit(solution)/shard_map/ppermute | solution.py:47
  77.0 9.0 %collective-permute-start.19 = (bf16[1080,128]{1,0:T(8,128)(2,1)S(1)}, bf16[1080,128]{1,0:T(8,128)(2,1)S(1)}, u32[]{:S(2)}, u32[]{:S(2)}) collective-permute-start(bf16[1080,128]{1,0:T(8,128)(2,1)S(1)} %add_convert_fusion.26), channel_id=1, source_target_pairs={{0,8},{1,5},{8,16},{9,1},{16,24},{17,9},{24,26},{25,17},{26,18},{2... | collective-permute-start | bytes 829448 | tf_op jit(solution)/shard_map/ppermute | solution.py:47
  78.8 44.7 %slice-start = ((s8[8847360]{0:T(1024)(128)(4,1)}), s8[458752]{0:T(1024)(128)(4,1)S(1)}, s32[]{:S(2)}) async-start(s8[8847360]{0:T(1024)(128)(4,1)} %bitcast.56), calls=%async_computation | async-start | bytes 917504
  80.0 8.8 %collective-permute-start.4 = (bf16[1080,128]{1,0:T(8,128)(2,1)S(1)}, bf16[1080,128]{1,0:T(8,128)(2,1)S(1)}, u32[]{:S(2)}, u32[]{:S(2)}) collective-permute-start(bf16[1080,128]{1,0:T(8,128)(2,1)S(1)} %add_convert_fusion.40), channel_id=1, source_target_pairs={{0,8},{1,5},{8,16},{9,1},{16,24},{17,9},{24,26},{25,17},{26,18},{2... | collective-permute-start | bytes 829448 | tf_op jit(solution)/shard_map/ppermute | solution.py:47
  84.4 7.0 %collective-permute-start.35 = (bf16[1080,128]{1,0:T(8,128)(2,1)S(1)}, bf16[1080,128]{1,0:T(8,128)(2,1)S(1)}, u32[]{:S(2)}, u32[]{:S(2)}) collective-permute-start(bf16[1080,128]{1,0:T(8,128)(2,1)S(1)} %add_convert_fusion.11), channel_id=1, source_target_pairs={{0,8},{1,5},{8,16},{9,1},{16,24},{17,9},{24,26},{25,17},{26,18},{2... | collective-permute-start | bytes 829448 | tf_op jit(solution)/shard_map/ppermute | solution.py:47
  87.2 6.8 %collective-permute-start.20 = (bf16[1080,128]{1,0:T(8,128)(2,1)S(1)}, bf16[1080,128]{1,0:T(8,128)(2,1)S(1)}, u32[]{:S(2)}, u32[]{:S(2)}) collective-permute-start(bf16[1080,128]{1,0:T(8,128)(2,1)S(1)} %add_convert_fusion.25), channel_id=1, source_target_pairs={{0,8},{1,5},{8,16},{9,1},{16,24},{17,9},{24,26},{25,17},{26,18},{2... | collective-permute-start | bytes 829448 | tf_op jit(solution)/shard_map/ppermute | solution.py:47
  89.9 7.0 %collective-permute-start.5 = (bf16[1080,128]{1,0:T(8,128)(2,1)S(1)}, bf16[1080,128]{1,0:T(8,128)(2,1)S(1)}, u32[]{:S(2)}, u32[]{:S(2)}) collective-permute-start(bf16[1080,128]{1,0:T(8,128)(2,1)S(1)} %add_convert_fusion.39), channel_id=1, source_target_pairs={{0,8},{1,5},{8,16},{9,1},{16,24},{17,9},{24,26},{25,17},{26,18},{2... | collective-permute-start | bytes 829448 | tf_op jit(solution)/shard_map/ppermute | solution.py:47
  92.5 7.3 %collective-permute-start.36 = (bf16[1080,128]{1,0:T(8,128)(2,1)S(1)}, bf16[1080,128]{1,0:T(8,128)(2,1)S(1)}, u32[]{:S(2)}, u32[]{:S(2)}) collective-permute-start(bf16[1080,128]{1,0:T(8,128)(2,1)S(1)} %add_convert_fusion.10), channel_id=1, source_target_pairs={{0,8},{1,5},{8,16},{9,1},{16,24},{17,9},{24,26},{25,17},{26,18},{2... | collective-permute-start | bytes 829448 | tf_op jit(solution)/shard_map/ppermute | solution.py:47
  95.0 7.8 %collective-permute-start.21 = (bf16[1080,128]{1,0:T(8,128)(2,1)S(1)}, bf16[1080,128]{1,0:T(8,128)(2,1)S(1)}, u32[]{:S(2)}, u32[]{:S(2)}) collective-permute-start(bf16[1080,128]{1,0:T(8,128)(2,1)S(1)} %add_convert_fusion.24), channel_id=1, source_target_pairs={{0,8},{1,5},{8,16},{9,1},{16,24},{17,9},{24,26},{25,17},{26,18},{2... | collective-permute-start | bytes 829448 | tf_op jit(solution)/shard_map/ppermute | solution.py:47
  98.0 7.8 %collective-permute-start.6 = (bf16[1080,128]{1,0:T(8,128)(2,1)S(1)}, bf16[1080,128]{1,0:T(8,128)(2,1)S(1)}, u32[]{:S(2)}, u32[]{:S(2)}) collective-permute-start(bf16[1080,128]{1,0:T(8,128)(2,1)S(1)} %add_convert_fusion.38), channel_id=1, source_target_pairs={{0,8},{1,5},{8,16},{9,1},{16,24},{17,9},{24,26},{25,17},{26,18},{2... | collective-permute-start | bytes 829448 | tf_op jit(solution)/shard_map/ppermute | solution.py:47
  101.0 7.8 %collective-permute-start.37 = (bf16[1080,128]{1,0:T(8,128)(2,1)S(1)}, bf16[1080,128]{1,0:T(8,128)(2,1)S(1)}, u32[]{:S(2)}, u32[]{:S(2)}) collective-permute-start(bf16[1080,128]{1,0:T(8,128)(2,1)S(1)} %add_convert_fusion.9), channel_id=1, source_target_pairs={{0,8},{1,5},{8,16},{9,1},{16,24},{17,9},{24,26},{25,17},{26,18},{2... | collective-permute-start | bytes 829448 | tf_op jit(solution)/shard_map/ppermute | solution.py:47
  103.9 7.8 %collective-permute-start.22 = (bf16[1080,128]{1,0:T(8,128)(2,1)S(1)}, bf16[1080,128]{1,0:T(8,128)(2,1)S(1)}, u32[]{:S(2)}, u32[]{:S(2)}) collective-permute-start(bf16[1080,128]{1,0:T(8,128)(2,1)S(1)} %add_convert_fusion.23), channel_id=1, source_target_pairs={{0,8},{1,5},{8,16},{9,1},{16,24},{17,9},{24,26},{25,17},{26,18},{2... | collective-permute-start | bytes 829448 | tf_op jit(solution)/shard_map/ppermute | solution.py:47
  106.9 7.8 %collective-permute-start.7 = (bf16[1080,128]{1,0:T(8,128)(2,1)S(1)}, bf16[1080,128]{1,0:T(8,128)(2,1)S(1)}, u32[]{:S(2)}, u32[]{:S(2)}) collective-permute-start(bf16[1080,128]{1,0:T(8,128)(2,1)S(1)} %add_convert_fusion.37), channel_id=1, source_target_pairs={{0,8},{1,5},{8,16},{9,1},{16,24},{17,9},{24,26},{25,17},{26,18},{2... | collective-permute-start | bytes 829448 | tf_op jit(solution)/shard_map/ppermute | solution.py:47
  109.9 7.8 %collective-permute-start.38 = (bf16[1080,128]{1,0:T(8,128)(2,1)S(1)}, bf16[1080,128]{1,0:T(8,128)(2,1)S(1)}, u32[]{:S(2)}, u32[]{:S(2)}) collective-permute-start(bf16[1080,128]{1,0:T(8,128)(2,1)S(1)} %add_convert_fusion.8), channel_id=1, source_target_pairs={{0,8},{1,5},{8,16},{9,1},{16,24},{17,9},{24,26},{25,17},{26,18},{2... | collective-permute-start | bytes 829448 | tf_op jit(solution)/shard_map/ppermute | solution.py:47
  112.8 7.8 %collective-permute-start.23 = (bf16[1080,128]{1,0:T(8,128)(2,1)S(1)}, bf16[1080,128]{1,0:T(8,128)(2,1)S(1)}, u32[]{:S(2)}, u32[]{:S(2)}) collective-permute-start(bf16[1080,128]{1,0:T(8,128)(2,1)S(1)} %add_convert_fusion.22), channel_id=1, source_target_pairs={{0,8},{1,5},{8,16},{9,1},{16,24},{17,9},{24,26},{25,17},{26,18},{2... | collective-permute-start | bytes 829448 | tf_op jit(solution)/shard_map/ppermute | solution.py:47
  115.8 7.8 %collective-permute-start.8 = (bf16[1080,128]{1,0:T(8,128)(2,1)S(1)}, bf16[1080,128]{1,0:T(8,128)(2,1)S(1)}, u32[]{:S(2)}, u32[]{:S(2)}) collective-permute-start(bf16[1080,128]{1,0:T(8,128)(2,1)S(1)} %add_convert_fusion.36), channel_id=1, source_target_pairs={{0,8},{1,5},{8,16},{9,1},{16,24},{17,9},{24,26},{25,17},{26,18},{2... | collective-permute-start | bytes 829448 | tf_op jit(solution)/shard_map/ppermute | solution.py:47
  118.7 7.8 %collective-permute-start.39 = (bf16[1080,128]{1,0:T(8,128)(2,1)S(1)}, bf16[1080,128]{1,0:T(8,128)(2,1)S(1)}, u32[]{:S(2)}, u32[]{:S(2)}) collective-permute-start(bf16[1080,128]{1,0:T(8,128)(2,1)S(1)} %add_convert_fusion.7), channel_id=1, source_target_pairs={{0,8},{1,5},{8,16},{9,1},{16,24},{17,9},{24,26},{25,17},{26,18},{2... | collective-permute-start | bytes 829448 | tf_op jit(solution)/shard_map/ppermute | solution.py:47
  121.7 7.8 %collective-permute-start.24 = (bf16[1080,128]{1,0:T(8,128)(2,1)S(1)}, bf16[1080,128]{1,0:T(8,128)(2,1)S(1)}, u32[]{:S(2)}, u32[]{:S(2)}) collective-permute-start(bf16[1080,128]{1,0:T(8,128)(2,1)S(1)} %add_convert_fusion.21), channel_id=1, source_target_pairs={{0,8},{1,5},{8,16},{9,1},{16,24},{17,9},{24,26},{25,17},{26,18},{2... | collective-permute-start | bytes 829448 | tf_op jit(solution)/shard_map/ppermute | solution.py:47
  123.7 8.8 %collective-permute-start.9 = (bf16[1080,128]{1,0:T(8,128)(2,1)S(1)}, bf16[1080,128]{1,0:T(8,128)(2,1)S(1)}, u32[]{:S(2)}, u32[]{:S(2)}) collective-permute-start(bf16[1080,128]{1,0:T(8,128)(2,1)S(1)} %add_convert_fusion.35), channel_id=1, source_target_pairs={{0,8},{1,5},{8,16},{9,1},{16,24},{17,9},{24,26},{25,17},{26,18},{2... | collective-permute-start | bytes 829448 | tf_op jit(solution)/shard_map/ppermute | solution.py:47
  127.6 7.8 %collective-permute-start.40 = (bf16[1080,128]{1,0:T(8,128)(2,1)S(1)}, bf16[1080,128]{1,0:T(8,128)(2,1)S(1)}, u32[]{:S(2)}, u32[]{:S(2)}) collective-permute-start(bf16[1080,128]{1,0:T(8,128)(2,1)S(1)} %add_convert_fusion.6), channel_id=1, source_target_pairs={{0,8},{1,5},{8,16},{9,1},{16,24},{17,9},{24,26},{25,17},{26,18},{2... | collective-permute-start | bytes 829448 | tf_op jit(solution)/shard_map/ppermute | solution.py:47
  130.6 7.8 %collective-permute-start.25 = (bf16[1080,128]{1,0:T(8,128)(2,1)S(1)}, bf16[1080,128]{1,0:T(8,128)(2,1)S(1)}, u32[]{:S(2)}, u32[]{:S(2)}) collective-permute-start(bf16[1080,128]{1,0:T(8,128)(2,1)S(1)} %add_convert_fusion.20), channel_id=1, source_target_pairs={{0,8},{1,5},{8,16},{9,1},{16,24},{17,9},{24,26},{25,17},{26,18},{2... | collective-permute-start | bytes 829448 | tf_op jit(solution)/shard_map/ppermute | solution.py:47
  132.5 8.8 %collective-permute-start.10 = (bf16[1080,128]{1,0:T(8,128)(2,1)S(1)}, bf16[1080,128]{1,0:T(8,128)(2,1)S(1)}, u32[]{:S(2)}, u32[]{:S(2)}) collective-permute-start(bf16[1080,128]{1,0:T(8,128)(2,1)S(1)} %add_convert_fusion.34), channel_id=1, source_target_pairs={{0,8},{1,5},{8,16},{9,1},{16,24},{17,9},{24,26},{25,17},{26,18},{2... | collective-permute-start | bytes 829448 | tf_op jit(solution)/shard_map/ppermute | solution.py:47
  136.5 7.8 %collective-permute-start.41 = (bf16[1080,128]{1,0:T(8,128)(2,1)S(1)}, bf16[1080,128]{1,0:T(8,128)(2,1)S(1)}, u32[]{:S(2)}, u32[]{:S(2)}) collective-permute-start(bf16[1080,128]{1,0:T(8,128)(2,1)S(1)} %add_convert_fusion.5), channel_id=1, source_target_pairs={{0,8},{1,5},{8,16},{9,1},{16,24},{17,9},{24,26},{25,17},{26,18},{2... | collective-permute-start | bytes 829448 | tf_op jit(solution)/shard_map/ppermute | solution.py:47
  139.5 7.8 %collective-permute-start.26 = (bf16[1080,128]{1,0:T(8,128)(2,1)S(1)}, bf16[1080,128]{1,0:T(8,128)(2,1)S(1)}, u32[]{:S(2)}, u32[]{:S(2)}) collective-permute-start(bf16[1080,128]{1,0:T(8,128)(2,1)S(1)} %add_convert_fusion.19), channel_id=1, source_target_pairs={{0,8},{1,5},{8,16},{9,1},{16,24},{17,9},{24,26},{25,17},{26,18},{2... | collective-permute-start | bytes 829448 | tf_op jit(solution)/shard_map/ppermute | solution.py:47
  141.4 8.8 %collective-permute-start.11 = (bf16[1080,128]{1,0:T(8,128)(2,1)S(1)}, bf16[1080,128]{1,0:T(8,128)(2,1)S(1)}, u32[]{:S(2)}, u32[]{:S(2)}) collective-permute-start(bf16[1080,128]{1,0:T(8,128)(2,1)S(1)} %add_convert_fusion.33), channel_id=1, source_target_pairs={{0,8},{1,5},{8,16},{9,1},{16,24},{17,9},{24,26},{25,17},{26,18},{2... | collective-permute-start | bytes 829448 | tf_op jit(solution)/shard_map/ppermute | solution.py:47
  145.4 7.8 %collective-permute-start.42 = (bf16[1080,128]{1,0:T(8,128)(2,1)S(1)}, bf16[1080,128]{1,0:T(8,128)(2,1)S(1)}, u32[]{:S(2)}, u32[]{:S(2)}) collective-permute-start(bf16[1080,128]{1,0:T(8,128)(2,1)S(1)} %add_convert_fusion.4), channel_id=1, source_target_pairs={{0,8},{1,5},{8,16},{9,1},{16,24},{17,9},{24,26},{25,17},{26,18},{2... | collective-permute-start | bytes 829448 | tf_op jit(solution)/shard_map/ppermute | solution.py:47
  148.4 7.8 %collective-permute-start.27 = (bf16[1080,128]{1,0:T(8,128)(2,1)S(1)}, bf16[1080,128]{1,0:T(8,128)(2,1)S(1)}, u32[]{:S(2)}, u32[]{:S(2)}) collective-permute-start(bf16[1080,128]{1,0:T(8,128)(2,1)S(1)} %add_convert_fusion.18), channel_id=1, source_target_pairs={{0,8},{1,5},{8,16},{9,1},{16,24},{17,9},{24,26},{25,17},{26,18},{2... | collective-permute-start | bytes 829448 | tf_op jit(solution)/shard_map/ppermute | solution.py:47
  150.3 8.8 %collective-permute-start.12 = (bf16[1080,128]{1,0:T(8,128)(2,1)S(1)}, bf16[1080,128]{1,0:T(8,128)(2,1)S(1)}, u32[]{:S(2)}, u32[]{:S(2)}) collective-permute-start(bf16[1080,128]{1,0:T(8,128)(2,1)S(1)} %add_convert_fusion.32), channel_id=1, source_target_pairs={{0,8},{1,5},{8,16},{9,1},{16,24},{17,9},{24,26},{25,17},{26,18},{2... | collective-permute-start | bytes 829448 | tf_op jit(solution)/shard_map/ppermute | solution.py:47
  154.3 7.8 %collective-permute-start.43 = (bf16[1080,128]{1,0:T(8,128)(2,1)S(1)}, bf16[1080,128]{1,0:T(8,128)(2,1)S(1)}, u32[]{:S(2)}, u32[]{:S(2)}) collective-permute-start(bf16[1080,128]{1,0:T(8,128)(2,1)S(1)} %add_convert_fusion.3), channel_id=1, source_target_pairs={{0,8},{1,5},{8,16},{9,1},{16,24},{17,9},{24,26},{25,17},{26,18},{2... | collective-permute-start | bytes 829448 | tf_op jit(solution)/shard_map/ppermute | solution.py:47
  157.3 7.8 %collective-permute-start.28 = (bf16[1080,128]{1,0:T(8,128)(2,1)S(1)}, bf16[1080,128]{1,0:T(8,128)(2,1)S(1)}, u32[]{:S(2)}, u32[]{:S(2)}) collective-permute-start(bf16[1080,128]{1,0:T(8,128)(2,1)S(1)} %add_convert_fusion.17), channel_id=1, source_target_pairs={{0,8},{1,5},{8,16},{9,1},{16,24},{17,9},{24,26},{25,17},{26,18},{2... | collective-permute-start | bytes 829448 | tf_op jit(solution)/shard_map/ppermute | solution.py:47
  159.2 8.8 %collective-permute-start.13 = (bf16[1080,128]{1,0:T(8,128)(2,1)S(1)}, bf16[1080,128]{1,0:T(8,128)(2,1)S(1)}, u32[]{:S(2)}, u32[]{:S(2)}) collective-permute-start(bf16[1080,128]{1,0:T(8,128)(2,1)S(1)} %add_convert_fusion.31), channel_id=1, source_target_pairs={{0,8},{1,5},{8,16},{9,1},{16,24},{17,9},{24,26},{25,17},{26,18},{2... | collective-permute-start | bytes 829448 | tf_op jit(solution)/shard_map/ppermute | solution.py:47
  163.2 7.8 %collective-permute-start.44 = (bf16[1080,128]{1,0:T(8,128)(2,1)S(1)}, bf16[1080,128]{1,0:T(8,128)(2,1)S(1)}, u32[]{:S(2)}, u32[]{:S(2)}) collective-permute-start(bf16[1080,128]{1,0:T(8,128)(2,1)S(1)} %add_convert_fusion.2), channel_id=1, source_target_pairs={{0,8},{1,5},{8,16},{9,1},{16,24},{17,9},{24,26},{25,17},{26,18},{2... | collective-permute-start | bytes 829448 | tf_op jit(solution)/shard_map/ppermute | solution.py:47
  166.2 7.8 %collective-permute-start.29 = (bf16[1080,128]{1,0:T(8,128)(2,1)S(1)}, bf16[1080,128]{1,0:T(8,128)(2,1)S(1)}, u32[]{:S(2)}, u32[]{:S(2)}) collective-permute-start(bf16[1080,128]{1,0:T(8,128)(2,1)S(1)} %add_convert_fusion.16), channel_id=1, source_target_pairs={{0,8},{1,5},{8,16},{9,1},{16,24},{17,9},{24,26},{25,17},{26,18},{2... | collective-permute-start | bytes 829448 | tf_op jit(solution)/shard_map/ppermute | solution.py:47
  168.1 8.8 %collective-permute-start.14 = (bf16[1080,128]{1,0:T(8,128)(2,1)S(1)}, bf16[1080,128]{1,0:T(8,128)(2,1)S(1)}, u32[]{:S(2)}, u32[]{:S(2)}) collective-permute-start(bf16[1080,128]{1,0:T(8,128)(2,1)S(1)} %add_convert_fusion.30), channel_id=1, source_target_pairs={{0,8},{1,5},{8,16},{9,1},{16,24},{17,9},{24,26},{25,17},{26,18},{2... | collective-permute-start | bytes 829448 | tf_op jit(solution)/shard_map/ppermute | solution.py:47
  172.1 7.8 %collective-permute-start.45 = (bf16[1080,128]{1,0:T(8,128)(2,1)S(1)}, bf16[1080,128]{1,0:T(8,128)(2,1)S(1)}, u32[]{:S(2)}, u32[]{:S(2)}) collective-permute-start(bf16[1080,128]{1,0:T(8,128)(2,1)S(1)} %add_convert_fusion.1), channel_id=1, source_target_pairs={{0,8},{1,5},{8,16},{9,1},{16,24},{17,9},{24,26},{25,17},{26,18},{2... | collective-permute-start | bytes 829448 | tf_op jit(solution)/shard_map/ppermute | solution.py:47
  175.0 7.8 %collective-permute-start.30 = (bf16[1080,128]{1,0:T(8,128)(2,1)S(1)}, bf16[1080,128]{1,0:T(8,128)(2,1)S(1)}, u32[]{:S(2)}, u32[]{:S(2)}) collective-permute-start(bf16[1080,128]{1,0:T(8,128)(2,1)S(1)} %add_convert_fusion.15), channel_id=1, source_target_pairs={{0,8},{1,5},{8,16},{9,1},{16,24},{17,9},{24,26},{25,17},{26,18},{2... | collective-permute-start | bytes 829448 | tf_op jit(solution)/shard_map/ppermute | solution.py:47
  176.9 8.8 %collective-permute-start.15 = (bf16[1080,128]{1,0:T(8,128)(2,1)S(1)}, bf16[1080,128]{1,0:T(8,128)(2,1)S(1)}, u32[]{:S(2)}, u32[]{:S(2)}) collective-permute-start(bf16[1080,128]{1,0:T(8,128)(2,1)S(1)} %add_convert_fusion.29), channel_id=1, source_target_pairs={{0,8},{1,5},{8,16},{9,1},{16,24},{17,9},{24,26},{25,17},{26,18},{2... | collective-permute-start | bytes 829448 | tf_op jit(solution)/shard_map/ppermute | solution.py:47
  181.0 7.8 %collective-permute-start.46 = (bf16[1080,128]{1,0:T(8,128)(2,1)S(1)}, bf16[1080,128]{1,0:T(8,128)(2,1)S(1)}, u32[]{:S(2)}, u32[]{:S(2)}) collective-permute-start(bf16[1080,128]{1,0:T(8,128)(2,1)S(1)} %add_convert_fusion), channel_id=1, source_target_pairs={{0,8},{1,5},{8,16},{9,1},{16,24},{17,9},{24,26},{25,17},{26,18},{2... | collective-permute-start | bytes 829448 | tf_op jit(solution)/shard_map/ppermute | solution.py:47
  184.0 7.7 %collective-permute-start.31 = (bf16[1080,128]{1,0:T(8,128)(2,1)S(1)}, bf16[1080,128]{1,0:T(8,128)(2,1)S(1)}, u32[]{:S(2)}, u32[]{:S(2)}) collective-permute-start(bf16[1080,128]{1,0:T(8,128)(2,1)S(1)} %add_convert_fusion.14), channel_id=1, source_target_pairs={{0,8},{1,5},{8,16},{9,1},{16,24},{17,9},{24,26},{25,17},{26,18},{2... | collective-permute-start | bytes 829448 | tf_op jit(solution)/shard_map/ppermute | solution.py:47
  185.8 8.8 %collective-permute-start.16 = (bf16[1080,128]{1,0:T(8,128)(2,1)S(1)}, bf16[1080,128]{1,0:T(8,128)(2,1)S(1)}, u32[]{:S(2)}, u32[]{:S(2)}) collective-permute-start(bf16[1080,128]{1,0:T(8,128)(2,1)S(1)} %add_convert_fusion.28), channel_id=1, source_target_pairs={{0,8},{1,5},{8,16},{9,1},{16,24},{17,9},{24,26},{25,17},{26,18},{2... | collective-permute-start | bytes 829448 | tf_op jit(solution)/shard_map/ppermute | solution.py:47
  (10 other events, 190.1 us)

commit v13 on v12

--- a/solution.py
+++ b/solution.py
@@ -49,13 +49,19 @@
     return accs
 
 
-def _ffn_block(hh, h, count, col_ref, tok_ref, cot_ref, wg_ref, wu_ref, wd_ref,
-               gg_ref, gu_ref, gd_ref, dxt_ref):
+def _pick(own_ref, other_ref, use_other, off):
+    return jnp.where(use_other, other_ref[:, pl.ds(off, BLK)], own_ref[:, pl.ds(off, BLK)])
+
+
+def _ffn_block(hh, h, count, col_ref, loc_ref, src_ref, tok_ref, cot_ref, otok_ref, ocot_ref,
+               wg_ref, wu_ref, wd_ref, gg_ref, gu_ref, gd_ref, dxt_ref):
     slots = gg_ref.shape[1]
     f32 = jnp.float32
     offs = [pl.multiple_of(col_ref[h, p] * BLK, BLK) for p in range(slots)]
-    x = jnp.concatenate([tok_ref[:, pl.ds(o, BLK)] for o in offs], axis=1)
-    dy = jnp.concatenate([cot_ref[:, pl.ds(o, BLK)] for o in offs], axis=1)
+    locs = [pl.multiple_of(loc_ref[h, p] * BLK, BLK) for p in range(slots)]
+    far = [src_ref[h, p] != 0 for p in range(slots)]
+    x = jnp.concatenate([_pick(tok_ref, otok_ref, f, o) for f, o in zip(far, locs)], axis=1)
+    dy = jnp.concatenate([_pick(cot_ref, ocot_ref, f, o) for f, o in zip(far, locs)], axis=1)
     stacked = (slots * BLK, BLK)
     live_rows = lax.broadcasted_iota(jnp.int32, stacked, 0) < count * BLK
     wg = wg_ref[hh].reshape(stacked)
@@ -88,8 +94,8 @@
         dxt_ref[pl.ds(offs[p], BLK), :] += back_t[rows]
 
 
-def _ffn_kernel(col_ref, cnt_ref, tok_ref, cot_ref, wg_ref, wu_ref, wd_ref,
-                gg_ref, gu_ref, gd_ref, dxt_ref):
+def _ffn_kernel(col_ref, loc_ref, src_ref, cnt_ref, tok_ref, cot_ref, otok_ref, ocot_ref,
+                wg_ref, wu_ref, wd_ref, gg_ref, gu_ref, gd_ref, dxt_ref):
     step = pl.program_id(0)
     per_step = gg_ref.shape[0]
 
@@ -99,26 +105,28 @@
 
     for hh in range(per_step):
         h = step * per_step + hh
-        _ffn_block(hh, h, cnt_ref[h], col_ref, tok_ref, cot_ref, wg_ref, wu_ref, wd_ref,
-                   gg_ref, gu_ref, gd_ref, dxt_ref)
-
-
-def ffn_block_terms(col_index, row_count, full_tok, full_cot, gate_w, up_w, down_w):
+        _ffn_block(hh, h, cnt_ref[h], col_ref, loc_ref, src_ref, tok_ref, cot_ref, otok_ref,
+                   ocot_ref, wg_ref, wu_ref, wd_ref, gg_ref, gu_ref, gd_ref, dxt_ref)
+
+
+def ffn_block_terms(col_index, col_local, col_far, row_count, tok, cot, other_tok, other_cot,
+                    gate_w, up_w, down_w):
     hblk, slots = col_index.shape
-    rows, width = full_tok.shape
+    rows, part = tok.shape
+    width = part * (2 if other_tok is not tok else 1)
     per_step = 9 if hblk % 9 == 0 else (3 if hblk % 3 == 0 else 1)
-    wspec = pl.BlockSpec((per_step, slots, BLK, BLK), lambda h, c, n: (h, 0, 0, 0))
-    full = pl.BlockSpec((rows, width), lambda h, c, n: (0, 0))
-    full_t = pl.BlockSpec((width, rows), lambda h, c, n: (0, 0))
+    wspec = pl.BlockSpec((per_step, slots, BLK, BLK), lambda h, c, l, s, n: (h, 0, 0, 0))
+    full = pl.BlockSpec((rows, part), lambda h, c, l, s, n: (0, 0))
+    full_t = pl.BlockSpec((width, rows), lambda h, c, l, s, n: (0, 0))
     gspec = wspec
     grad = jax.ShapeDtypeStruct((hblk, slots, BLK, BLK), jnp.float32)
     flops = 2 * rows * hblk * slots * BLK * BLK * 9
     return pl.pallas_call(
         _ffn_kernel,
         grid_spec=pltpu.PrefetchScalarGridSpec(
-            num_scalar_prefetch=2,
+            num_scalar_prefetch=4,
             grid=(hblk // per_step,),
-            in_specs=[full, full, wspec, wspec, wspec],
+            in_specs=[full, full, full, full, wspec, wspec, wspec],
             out_specs=[gspec, gspec, gspec, full_t],
         ),
         out_shape=[grad, grad, grad, jax.ShapeDtypeStruct((width, rows), jnp.float32)],
@@ -129,7 +137,7 @@
             bytes_accessed=3 * hblk * slots * BLK * BLK * 6 + rows * width * 8,
         ),
         name="ffn_block_terms",
-    )(col_index, row_count, full_tok, full_cot, gate_w, up_w, down_w)
+    )(col_index, col_local, col_far, row_count, tok, cot, other_tok, other_cot, gate_w, up_w, down_w)
 
 
 def shards(n_dp, n_t, tokens, cotangent, w_gate, w_up, w_down, col_index, row_count, adam_m, adam_v):
@@ -137,19 +145,19 @@
     first = lax.axis_index("tensor") == 0
     if n_t == 2:
         other_tok, other_cot = lax.ppermute(jnp.stack([tokens, cotangent]), "tensor", swap)
-        full_tok = jnp.concatenate(
-            [jnp.where(first, tokens, other_tok), jnp.where(first, other_tok, tokens)], axis=1
-        )
-        full_cot = jnp.concatenate(
-            [jnp.where(first, cotangent, other_cot), jnp.where(first, other_cot, cotangent)], axis=1
-        )
+        half_blocks = tokens.shape[1] // BLK
+        col_local = col_index % half_blocks
+        col_far = (col_index // half_blocks != lax.axis_index("tensor")).astype(jnp.int32)
+        halves = (tokens, cotangent, other_tok, other_cot)
     else:
         full_tok = lax.all_gather(tokens, "tensor", axis=1, tiled=True)
         full_cot = lax.all_gather(cotangent, "tensor", axis=1, tiled=True)
-    tok_rows = full_tok.shape[0]
+        col_local, col_far = col_index, jnp.zeros_like(col_index)
+        halves = (full_tok, full_cot, full_tok, full_cot)
+    tok_rows = tokens.shape[0]
     own_rows = w_gate.shape[1] * w_gate.shape[2] * BLK
     grad_gate, grad_up, grad_down, dx_part = ffn_block_terms(
-        col_index, row_count, full_tok, full_cot, w_gate[0], w_up[0], w_down[0]
+        col_index, col_local, col_far, row_count, *halves, w_gate[0], w_up[0], w_down[0]
     )
     reduced = jnp.stack(
         ring_reduce_scatter(

time: 200 us -> 202 us (1.010)
  local copies, waits for them, and re-layouts: 6.44 us -> 9.53 us
  transfers between devices with their start and end apart: 47 -> 47, of which waited for: 34 -> 35; matrix products, arithmetic and copies ran while one was open for 24% -> 25% of each run, Pallas kernels for 0% -> 0%
where the time goes in v13:
time: 202 us; the launch traced here: 199 us
  starting transfers between devices  75.4 us (37%)
  other arithmetic  48.6 us (24%)
  Pallas kernels  25 us (12%)
  between operations  21.7 us (11%)
  waiting for transfers between devices  19.2 us (10%)
  local copies, waits for them, and re-layouts  9.53 us (5%)
    ppermute x45, starting transfers between devices, ring_reduce_scatter(): moved = lax.ppermute(accs[i].astype(wire_dtype), ('dp', 'tensor'), perm)  74.7 us
    convert_element_type x42, other arithmetic, ring_reduce_scatter(): moved = lax.ppermute(accs[i].astype(wire_dtype), ('dp', 'tensor'), perm)  38.7 us
    pallas_call x1, Pallas kernels, ffn_block_terms(): pl.pallas_call(_ffn_kernel, grid_spec=pltpu.PrefetchScalarGridSpec(num_sc...  25 us
    ppermute x45, waiting for transfers between devices, ring_reduce_scatter(): moved = lax.ppermute(accs[i].astype(wire_dtype), ('dp', 'tensor'), perm)  19.2 us
  transfers between devices with their start and end apart: 47, of which 35 were waited for; matrix products, arithmetic and copies ran while one was open for 25% of the time, Pallas kernels for 0%

profile of v13, /device:TPU:0, one launch (start us, length us, event | category | flops | bytes accessed | tf_op | source)
XLA Modules:
  0.0 199.3 jit_solution(2846925496065980845)
XLA Ops:
  14.5 2.0 %fusion.5 = (s32[1]{0:T(128)}, s32[1]{0:T(128)}, s32[1]{0:T(128)}, s32[1]{0:T(128)}, s32[1]{0:T(128)}, /*index=5*/s32[1]{0:T(128)}, s32[1]{0:T(128)}, s32[1]{0:T...) fusion(s32[16]{0:T(128)} %constant.239.clone, ...), kind=kLoop, calls=%fused_computation.66 | loop fusion | bytes 192 | tf_op jit(solution)/shard_map/dynamic_slice | solution.py:37
  29.8 25.0 %ffn_block_terms.1 = (f32[27,5,128,128]{3,2,1,0:T(8,128)}, f32[27,5,128,128]{3,2,1,0:T(8,128)}, f32[27,5,128,128]{3,2,1,0:T(8,128)}, f32[5120,128]{1,0:T(8,128)}) custom-call(s32[27,5]{1,0:T(8,128)} %copy-done.3, s32[27,5]{1,0:T(8,128)} %add_select_fusion.1.loc_ref, s32[27,5]{1,0:T(8,128)} %fusion.4.src_ref, s32[27]{0:T(128)} %cnt_ref.1, ...), custom_call_target="tpu_custom_call" | custom-call | flops 5096079360 | bytes 45056000 | tf_op jit(solution)/shard_map/ffn_block_terms/pallas_call | solution.py:124
  54.8 2.0 fusion.1
  58.0 3.1 %collective-permute-start.32 = (bf16[1080,128]{1,0:T(8,128)(2,1)S(1)}, bf16[1080,128]{1,0:T(8,128)(2,1)S(1)}, u32[]{:S(2)}, u32[]{:S(2)}) collective-permute-start(bf16[1080,128]{1,0:T(8,128)(2,1)S(1)} %dynamic-slice_convert_fusion), channel_id=1, source_target_pairs={{0,8},{1,5},{8,16},{9,1},{16,24},{17,9},{24,26},{25,17},{26,18},{2... | collective-permute-start | bytes 829448 | tf_op jit(solution)/shard_map/ppermute | solution.py:47
  62.1 1.6 collective-permute-start.17
  64.8 1.6 collective-permute-start.2
  67.6 1.6 collective-permute-start.33
  72.8 1.8 collective-permute-start.3
  75.8 1.8 collective-permute-start.34
  78.8 1.8 collective-permute-start.19
  81.8 1.8 collective-permute-start.4
  86.2 1.6 collective-permute-start.35
  88.9 1.6 collective-permute-start.20
  96.8 1.6 collective-permute-start.21
  99.8 1.6 collective-permute-start.6
  102.7 1.6 collective-permute-start.37
  105.7 1.6 collective-permute-start.22
  108.7 1.6 collective-permute-start.7
  111.6 1.6 collective-permute-start.38
  114.6 1.6 collective-permute-start.23
  117.6 1.6 collective-permute-start.8
  120.5 1.6 collective-permute-start.39
  123.5 1.6 collective-permute-start.24
  125.4 1.6 collective-permute-start.9
  129.4 1.6 collective-permute-start.40
  132.4 1.6 collective-permute-start.25
  134.3 1.6 collective-permute-start.10
  138.3 1.6 collective-permute-start.41
  141.3 1.6 collective-permute-start.26
  143.2 1.8 collective-permute-start.11
  147.2 1.6 collective-permute-start.42
  150.2 1.6 collective-permute-start.27
  152.1 1.6 collective-permute-start.12
  156.1 1.6 collective-permute-start.43
  159.0 1.6 collective-permute-start.28
  160.9 1.6 collective-permute-start.13
  165.0 1.6 collective-permute-start.44
  167.9 1.6 collective-permute-start.29
  169.8 1.6 collective-permute-start.14
  173.8 1.6 collective-permute-start.45
  176.8 1.6 collective-permute-start.30
  178.7 1.6 collective-permute-start.15
  182.7 1.6 collective-permute-start.46
  185.7 1.6 collective-permute-start.31
  187.6 1.6 collective-permute-start.16
  191.6 1.9 collective-permute-done.31
  194.6 1.9 collective-permute-done.16
  196.5 2.8 %add_divide_fusion = (f32[3,1,1080,128]{3,2,1,0:T(8,128)}, f32[3,1,1080,128]{3,2,1,0:T(8,128)}, f32[3,1,1080,128]{3,2,1,0:T(8,128)}) fusion(f32[1,1,1080,128]{3,2,1,0:T(8,128)S(1)} %add_bitcast_fusion, f32[1,1,1080,128]{3,2,1,0:T(8,128)S(1)} %add_bitcast_fusion.1, f32[1,1,1080,128]{3,2,1,0:T(8,128)S(1)} %add_bitcast_fusion.2, ...), kind=kLoop, calls=%fused_computation.1 | loop fusion | flops 4976640 | bytes 9953280 | tf_op jit(solution)/shard_map/div | solution.py:185
  (121 shorter events, 71.6 us)
Async XLA Ops:
  2.0 26.6 %collective-permute-start = (bf16[2,128,2560]{2,1,0:T(8,128)(2,1)S(1)}, bf16[2,128,2560]{2,1,0:T(8,128)(2,1)S(1)}, u32[]{:S(2)}, u32[]{:S(2)}) collective-permute-start(bf16[2,128,2560]{2,1,0:T(8,128)(2,1)S(1)} %pad_maximum_fusion.1), channel_id=1, source_target_pairs={{0,1},{1,0},{2,3},{3,2},{4,5},{5,4},{6,7},{7,6},{8,9},{9,8},{10,11... | collective-permute-start | bytes 3932168 | tf_op jit(solution)/shard_map/ppermute | solution.py:147
  56.8 26.9 %collective-permute-start.1 = (bf16[128,2560]{0,1:T(8,128)(2,1)S(1)}, bf16[128,2560]{0,1:T(8,128)(2,1)S(1)}, u32[]{:S(2)}, u32[]{:S(2)}) collective-permute-start(bf16[128,2560]{0,1:T(8,128)(2,1)S(1)} %fusion.1), channel_id=1, source_target_pairs={{0,1},{1,0},{2,3},{3,2},{4,5},{5,4},{6,7},{7,6},{8,9},{9,8},{10,11... | collective-permute-start | bytes 1966088 | tf_op jit(solution)/shard_map/ppermute | solution.py:175
  58.0 8.5 %collective-permute-start.32 = (bf16[1080,128]{1,0:T(8,128)(2,1)S(1)}, bf16[1080,128]{1,0:T(8,128)(2,1)S(1)}, u32[]{:S(2)}, u32[]{:S(2)}) collective-permute-start(bf16[1080,128]{1,0:T(8,128)(2,1)S(1)} %dynamic-slice_convert_fusion), channel_id=1, source_target_pairs={{0,8},{1,5},{8,16},{9,1},{16,24},{17,9},{24,26},{25,17},{26,18},{2... | collective-permute-start | bytes 829448 | tf_op jit(solution)/shard_map/ppermute | solution.py:47
  62.1 7.0 %collective-permute-start.17 = (bf16[1080,128]{1,0:T(8,128)(2,1)S(1)}, bf16[1080,128]{1,0:T(8,128)(2,1)S(1)}, u32[]{:S(2)}, u32[]{:S(2)}) collective-permute-start(bf16[1080,128]{1,0:T(8,128)(2,1)S(1)} %dynamic-slice_convert_fusion.1), channel_id=1, source_target_pairs={{0,8},{1,5},{8,16},{9,1},{16,24},{17,9},{24,26},{25,17},{26,18},{2... | collective-permute-start | bytes 829448 | tf_op jit(solution)/shard_map/ppermute | solution.py:47
  64.8 6.9 %collective-permute-start.2 = (bf16[1080,128]{1,0:T(8,128)(2,1)S(1)}, bf16[1080,128]{1,0:T(8,128)(2,1)S(1)}, u32[]{:S(2)}, u32[]{:S(2)}) collective-permute-start(bf16[1080,128]{1,0:T(8,128)(2,1)S(1)} %dynamic-slice_convert_fusion.2), channel_id=1, source_target_pairs={{0,8},{1,5},{8,16},{9,1},{16,24},{17,9},{24,26},{25,17},{26,18},{2... | collective-permute-start | bytes 829448 | tf_op jit(solution)/shard_map/ppermute | solution.py:47
  67.6 7.1 %collective-permute-start.33 = (bf16[1080,128]{1,0:T(8,128)(2,1)S(1)}, bf16[1080,128]{1,0:T(8,128)(2,1)S(1)}, u32[]{:S(2)}, u32[]{:S(2)}) collective-permute-start(bf16[1080,128]{1,0:T(8,128)(2,1)S(1)} %add_convert_fusion.13), channel_id=1, source_target_pairs={{0,8},{1,5},{8,16},{9,1},{16,24},{17,9},{24,26},{25,17},{26,18},{2... | collective-permute-start | bytes 829448 | tf_op jit(solution)/shard_map/ppermute | solution.py:47
  70.3 7.4 %collective-permute-start.18 = (bf16[1080,128]{1,0:T(8,128)(2,1)S(1)}, bf16[1080,128]{1,0:T(8,128)(2,1)S(1)}, u32[]{:S(2)}, u32[]{:S(2)}) collective-permute-start(bf16[1080,128]{1,0:T(8,128)(2,1)S(1)} %add_convert_fusion.27), channel_id=1, source_target_pairs={{0,8},{1,5},{8,16},{9,1},{16,24},{17,9},{24,26},{25,17},{26,18},{2... | collective-permute-start | bytes 829448 | tf_op jit(solution)/shard_map/ppermute | solution.py:47
  72.8 7.8 %collective-permute-start.3 = (bf16[1080,128]{1,0:T(8,128)(2,1)S(1)}, bf16[1080,128]{1,0:T(8,128)(2,1)S(1)}, u32[]{:S(2)}, u32[]{:S(2)}) collective-permute-start(bf16[1080,128]{1,0:T(8,128)(2,1)S(1)} %add_convert_fusion.41), channel_id=1, source_target_pairs={{0,8},{1,5},{8,16},{9,1},{16,24},{17,9},{24,26},{25,17},{26,18},{2... | collective-permute-start | bytes 829448 | tf_op jit(solution)/shard_map/ppermute | solution.py:47
  75.8 9.1 %collective-permute-start.34 = (bf16[1080,128]{1,0:T(8,128)(2,1)S(1)}, bf16[1080,128]{1,0:T(8,128)(2,1)S(1)}, u32[]{:S(2)}, u32[]{:S(2)}) collective-permute-start(bf16[1080,128]{1,0:T(8,128)(2,1)S(1)} %add_convert_fusion.12), channel_id=1, source_target_pairs={{0,8},{1,5},{8,16},{9,1},{16,24},{17,9},{24,26},{25,17},{26,18},{2... | collective-permute-start | bytes 829448 | tf_op jit(solution)/shard_map/ppermute | solution.py:47
  78.8 9.0 %collective-permute-start.19 = (bf16[1080,128]{1,0:T(8,128)(2,1)S(1)}, bf16[1080,128]{1,0:T(8,128)(2,1)S(1)}, u32[]{:S(2)}, u32[]{:S(2)}) collective-permute-start(bf16[1080,128]{1,0:T(8,128)(2,1)S(1)} %add_convert_fusion.26), channel_id=1, source_target_pairs={{0,8},{1,5},{8,16},{9,1},{16,24},{17,9},{24,26},{25,17},{26,18},{2... | collective-permute-start | bytes 829448 | tf_op jit(solution)/shard_map/ppermute | solution.py:47
  80.6 44.7 %slice-start = ((s8[8847360]{0:T(1024)(128)(4,1)}), s8[458752]{0:T(1024)(128)(4,1)S(1)}, s32[]{:S(2)}) async-start(s8[8847360]{0:T(1024)(128)(4,1)} %bitcast.48), calls=%async_computation | async-start | bytes 917504
  81.8 8.7 %collective-permute-start.4 = (bf16[1080,128]{1,0:T(8,128)(2,1)S(1)}, bf16[1080,128]{1,0:T(8,128)(2,1)S(1)}, u32[]{:S(2)}, u32[]{:S(2)}) collective-permute-start(bf16[1080,128]{1,0:T(8,128)(2,1)S(1)} %add_convert_fusion.40), channel_id=1, source_target_pairs={{0,8},{1,5},{8,16},{9,1},{16,24},{17,9},{24,26},{25,17},{26,18},{2... | collective-permute-start | bytes 829448 | tf_op jit(solution)/shard_map/ppermute | solution.py:47
  86.2 7.0 %collective-permute-start.35 = (bf16[1080,128]{1,0:T(8,128)(2,1)S(1)}, bf16[1080,128]{1,0:T(8,128)(2,1)S(1)}, u32[]{:S(2)}, u32[]{:S(2)}) collective-permute-start(bf16[1080,128]{1,0:T(8,128)(2,1)S(1)} %add_convert_fusion.11), channel_id=1, source_target_pairs={{0,8},{1,5},{8,16},{9,1},{16,24},{17,9},{24,26},{25,17},{26,18},{2... | collective-permute-start | bytes 829448 | tf_op jit(solution)/shard_map/ppermute | solution.py:47
  88.9 6.8 %collective-permute-start.20 = (bf16[1080,128]{1,0:T(8,128)(2,1)S(1)}, bf16[1080,128]{1,0:T(8,128)(2,1)S(1)}, u32[]{:S(2)}, u32[]{:S(2)}) collective-permute-start(bf16[1080,128]{1,0:T(8,128)(2,1)S(1)} %add_convert_fusion.25), channel_id=1, source_target_pairs={{0,8},{1,5},{8,16},{9,1},{16,24},{17,9},{24,26},{25,17},{26,18},{2... | collective-permute-start | bytes 829448 | tf_op jit(solution)/shard_map/ppermute | solution.py:47
  91.6 7.0 %collective-permute-start.5 = (bf16[1080,128]{1,0:T(8,128)(2,1)S(1)}, bf16[1080,128]{1,0:T(8,128)(2,1)S(1)}, u32[]{:S(2)}, u32[]{:S(2)}) collective-permute-start(bf16[1080,128]{1,0:T(8,128)(2,1)S(1)} %add_convert_fusion.39), channel_id=1, source_target_pairs={{0,8},{1,5},{8,16},{9,1},{16,24},{17,9},{24,26},{25,17},{26,18},{2... | collective-permute-start | bytes 829448 | tf_op jit(solution)/shard_map/ppermute | solution.py:47
  94.3 7.3 %collective-permute-start.36 = (bf16[1080,128]{1,0:T(8,128)(2,1)S(1)}, bf16[1080,128]{1,0:T(8,128)(2,1)S(1)}, u32[]{:S(2)}, u32[]{:S(2)}) collective-permute-start(bf16[1080,128]{1,0:T(8,128)(2,1)S(1)} %add_convert_fusion.10), channel_id=1, source_target_pairs={{0,8},{1,5},{8,16},{9,1},{16,24},{17,9},{24,26},{25,17},{26,18},{2... | collective-permute-start | bytes 829448 | tf_op jit(solution)/shard_map/ppermute | solution.py:47
  96.8 7.8 %collective-permute-start.21 = (bf16[1080,128]{1,0:T(8,128)(2,1)S(1)}, bf16[1080,128]{1,0:T(8,128)(2,1)S(1)}, u32[]{:S(2)}, u32[]{:S(2)}) collective-permute-start(bf16[1080,128]{1,0:T(8,128)(2,1)S(1)} %add_convert_fusion.24), channel_id=1, source_target_pairs={{0,8},{1,5},{8,16},{9,1},{16,24},{17,9},{24,26},{25,17},{26,18},{2... | collective-permute-start | bytes 829448 | tf_op jit(solution)/shard_map/ppermute | solution.py:47
  99.8 7.8 %collective-permute-start.6 = (bf16[1080,128]{1,0:T(8,128)(2,1)S(1)}, bf16[1080,128]{1,0:T(8,128)(2,1)S(1)}, u32[]{:S(2)}, u32[]{:S(2)}) collective-permute-start(bf16[1080,128]{1,0:T(8,128)(2,1)S(1)} %add_convert_fusion.38), channel_id=1, source_target_pairs={{0,8},{1,5},{8,16},{9,1},{16,24},{17,9},{24,26},{25,17},{26,18},{2... | collective-permute-start | bytes 829448 | tf_op jit(solution)/shard_map/ppermute | solution.py:47
  102.7 7.8 %collective-permute-start.37 = (bf16[1080,128]{1,0:T(8,128)(2,1)S(1)}, bf16[1080,128]{1,0:T(8,128)(2,1)S(1)}, u32[]{:S(2)}, u32[]{:S(2)}) collective-permute-start(bf16[1080,128]{1,0:T(8,128)(2,1)S(1)} %add_convert_fusion.9), channel_id=1, source_target_pairs={{0,8},{1,5},{8,16},{9,1},{16,24},{17,9},{24,26},{25,17},{26,18},{2... | collective-permute-start | bytes 829448 | tf_op jit(solution)/shard_map/ppermute | solution.py:47
  105.7 7.8 %collective-permute-start.22 = (bf16[1080,128]{1,0:T(8,128)(2,1)S(1)}, bf16[1080,128]{1,0:T(8,128)(2,1)S(1)}, u32[]{:S(2)}, u32[]{:S(2)}) collective-permute-start(bf16[1080,128]{1,0:T(8,128)(2,1)S(1)} %add_convert_fusion.23), channel_id=1, source_target_pairs={{0,8},{1,5},{8,16},{9,1},{16,24},{17,9},{24,26},{25,17},{26,18},{2... | collective-permute-start | bytes 829448 | tf_op jit(solution)/shard_map/ppermute | solution.py:47
  108.7 7.8 %collective-permute-start.7 = (bf16[1080,128]{1,0:T(8,128)(2,1)S(1)}, bf16[1080,128]{1,0:T(8,128)(2,1)S(1)}, u32[]{:S(2)}, u32[]{:S(2)}) collective-permute-start(bf16[1080,128]{1,0:T(8,128)(2,1)S(1)} %add_convert_fusion.37), channel_id=1, source_target_pairs={{0,8},{1,5},{8,16},{9,1},{16,24},{17,9},{24,26},{25,17},{26,18},{2... | collective-permute-start | bytes 829448 | tf_op jit(solution)/shard_map/ppermute | solution.py:47
  111.6 7.8 %collective-permute-start.38 = (bf16[1080,128]{1,0:T(8,128)(2,1)S(1)}, bf16[1080,128]{1,0:T(8,128)(2,1)S(1)}, u32[]{:S(2)}, u32[]{:S(2)}) collective-permute-start(bf16[1080,128]{1,0:T(8,128)(2,1)S(1)} %add_convert_fusion.8), channel_id=1, source_target_pairs={{0,8},{1,5},{8,16},{9,1},{16,24},{17,9},{24,26},{25,17},{26,18},{2... | collective-permute-start | bytes 829448 | tf_op jit(solution)/shard_map/ppermute | solution.py:47
  114.6 7.8 %collective-permute-start.23 = (bf16[1080,128]{1,0:T(8,128)(2,1)S(1)}, bf16[1080,128]{1,0:T(8,128)(2,1)S(1)}, u32[]{:S(2)}, u32[]{:S(2)}) collective-permute-start(bf16[1080,128]{1,0:T(8,128)(2,1)S(1)} %add_convert_fusion.22), channel_id=1, source_target_pairs={{0,8},{1,5},{8,16},{9,1},{16,24},{17,9},{24,26},{25,17},{26,18},{2... | collective-permute-start | bytes 829448 | tf_op jit(solution)/shard_map/ppermute | solution.py:47
  117.6 7.8 %collective-permute-start.8 = (bf16[1080,128]{1,0:T(8,128)(2,1)S(1)}, bf16[1080,128]{1,0:T(8,128)(2,1)S(1)}, u32[]{:S(2)}, u32[]{:S(2)}) collective-permute-start(bf16[1080,128]{1,0:T(8,128)(2,1)S(1)} %add_convert_fusion.36), channel_id=1, source_target_pairs={{0,8},{1,5},{8,16},{9,1},{16,24},{17,9},{24,26},{25,17},{26,18},{2... | collective-permute-start | bytes 829448 | tf_op jit(solution)/shard_map/ppermute | solution.py:47
  120.5 7.8 %collective-permute-start.39 = (bf16[1080,128]{1,0:T(8,128)(2,1)S(1)}, bf16[1080,128]{1,0:T(8,128)(2,1)S(1)}, u32[]{:S(2)}, u32[]{:S(2)}) collective-permute-start(bf16[1080,128]{1,0:T(8,128)(2,1)S(1)} %add_convert_fusion.7), channel_id=1, source_target_pairs={{0,8},{1,5},{8,16},{9,1},{16,24},{17,9},{24,26},{25,17},{26,18},{2... | collective-permute-start | bytes 829448 | tf_op jit(solution)/shard_map/ppermute | solution.py:47
  123.5 7.8 %collective-permute-start.24 = (bf16[1080,128]{1,0:T(8,128)(2,1)S(1)}, bf16[1080,128]{1,0:T(8,128)(2,1)S(1)}, u32[]{:S(2)}, u32[]{:S(2)}) collective-permute-start(bf16[1080,128]{1,0:T(8,128)(2,1)S(1)} %add_convert_fusion.21), channel_id=1, source_target_pairs={{0,8},{1,5},{8,16},{9,1},{16,24},{17,9},{24,26},{25,17},{26,18},{2... | collective-permute-start | bytes 829448 | tf_op jit(solution)/shard_map/ppermute | solution.py:47
  125.4 8.8 %collective-permute-start.9 = (bf16[1080,128]{1,0:T(8,128)(2,1)S(1)}, bf16[1080,128]{1,0:T(8,128)(2,1)S(1)}, u32[]{:S(2)}, u32[]{:S(2)}) collective-permute-start(bf16[1080,128]{1,0:T(8,128)(2,1)S(1)} %add_convert_fusion.35), channel_id=1, source_target_pairs={{0,8},{1,5},{8,16},{9,1},{16,24},{17,9},{24,26},{25,17},{26,18},{2... | collective-permute-start | bytes 829448 | tf_op jit(solution)/shard_map/ppermute | solution.py:47
  129.4 7.8 %collective-permute-start.40 = (bf16[1080,128]{1,0:T(8,128)(2,1)S(1)}, bf16[1080,128]{1,0:T(8,128)(2,1)S(1)}, u32[]{:S(2)}, u32[]{:S(2)}) collective-permute-start(bf16[1080,128]{1,0:T(8,128)(2,1)S(1)} %add_convert_fusion.6), channel_id=1, source_target_pairs={{0,8},{1,5},{8,16},{9,1},{16,24},{17,9},{24,26},{25,17},{26,18},{2... | collective-permute-start | bytes 829448 | tf_op jit(solution)/shard_map/ppermute | solution.py:47
  132.4 7.8 %collective-permute-start.25 = (bf16[1080,128]{1,0:T(8,128)(2,1)S(1)}, bf16[1080,128]{1,0:T(8,128)(2,1)S(1)}, u32[]{:S(2)}, u32[]{:S(2)}) collective-permute-start(bf16[1080,128]{1,0:T(8,128)(2,1)S(1)} %add_convert_fusion.20), channel_id=1, source_target_pairs={{0,8},{1,5},{8,16},{9,1},{16,24},{17,9},{24,26},{25,17},{26,18},{2... | collective-permute-start | bytes 829448 | tf_op jit(solution)/shard_map/ppermute | solution.py:47
  134.3 8.8 %collective-permute-start.10 = (bf16[1080,128]{1,0:T(8,128)(2,1)S(1)}, bf16[1080,128]{1,0:T(8,128)(2,1)S(1)}, u32[]{:S(2)}, u32[]{:S(2)}) collective-permute-start(bf16[1080,128]{1,0:T(8,128)(2,1)S(1)} %add_convert_fusion.34), channel_id=1, source_target_pairs={{0,8},{1,5},{8,16},{9,1},{16,24},{17,9},{24,26},{25,17},{26,18},{2... | collective-permute-start | bytes 829448 | tf_op jit(solution)/shard_map/ppermute | solution.py:47
  138.3 7.8 %collective-permute-start.41 = (bf16[1080,128]{1,0:T(8,128)(2,1)S(1)}, bf16[1080,128]{1,0:T(8,128)(2,1)S(1)}, u32[]{:S(2)}, u32[]{:S(2)}) collective-permute-start(bf16[1080,128]{1,0:T(8,128)(2,1)S(1)} %add_convert_fusion.5), channel_id=1, source_target_pairs={{0,8},{1,5},{8,16},{9,1},{16,24},{17,9},{24,26},{25,17},{26,18},{2... | collective-permute-start | bytes 829448 | tf_op jit(solution)/shard_map/ppermute | solution.py:47
  141.3 7.8 %collective-permute-start.26 = (bf16[1080,128]{1,0:T(8,128)(2,1)S(1)}, bf16[1080,128]{1,0:T(8,128)(2,1)S(1)}, u32[]{:S(2)}, u32[]{:S(2)}) collective-permute-start(bf16[1080,128]{1,0:T(8,128)(2,1)S(1)} %add_convert_fusion.19), channel_id=1, source_target_pairs={{0,8},{1,5},{8,16},{9,1},{16,24},{17,9},{24,26},{25,17},{26,18},{2... | collective-permute-start | bytes 829448 | tf_op jit(solution)/shard_map/ppermute | solution.py:47
  143.2 8.8 %collective-permute-start.11 = (bf16[1080,128]{1,0:T(8,128)(2,1)S(1)}, bf16[1080,128]{1,0:T(8,128)(2,1)S(1)}, u32[]{:S(2)}, u32[]{:S(2)}) collective-permute-start(bf16[1080,128]{1,0:T(8,128)(2,1)S(1)} %add_convert_fusion.33), channel_id=1, source_target_pairs={{0,8},{1,5},{8,16},{9,1},{16,24},{17,9},{24,26},{25,17},{26,18},{2... | collective-permute-start | bytes 829448 | tf_op jit(solution)/shard_map/ppermute | solution.py:47
  147.2 7.8 %collective-permute-start.42 = (bf16[1080,128]{1,0:T(8,128)(2,1)S(1)}, bf16[1080,128]{1,0:T(8,128)(2,1)S(1)}, u32[]{:S(2)}, u32[]{:S(2)}) collective-permute-start(bf16[1080,128]{1,0:T(8,128)(2,1)S(1)} %add_convert_fusion.4), channel_id=1, source_target_pairs={{0,8},{1,5},{8,16},{9,1},{16,24},{17,9},{24,26},{25,17},{26,18},{2... | collective-permute-start | bytes 829448 | tf_op jit(solution)/shard_map/ppermute | solution.py:47
  150.2 7.8 %collective-permute-start.27 = (bf16[1080,128]{1,0:T(8,128)(2,1)S(1)}, bf16[1080,128]{1,0:T(8,128)(2,1)S(1)}, u32[]{:S(2)}, u32[]{:S(2)}) collective-permute-start(bf16[1080,128]{1,0:T(8,128)(2,1)S(1)} %add_convert_fusion.18), channel_id=1, source_target_pairs={{0,8},{1,5},{8,16},{9,1},{16,24},{17,9},{24,26},{25,17},{26,18},{2... | collective-permute-start | bytes 829448 | tf_op jit(solution)/shard_map/ppermute | solution.py:47
  152.1 8.8 %collective-permute-start.12 = (bf16[1080,128]{1,0:T(8,128)(2,1)S(1)}, bf16[1080,128]{1,0:T(8,128)(2,1)S(1)}, u32[]{:S(2)}, u32[]{:S(2)}) collective-permute-start(bf16[1080,128]{1,0:T(8,128)(2,1)S(1)} %add_convert_fusion.32), channel_id=1, source_target_pairs={{0,8},{1,5},{8,16},{9,1},{16,24},{17,9},{24,26},{25,17},{26,18},{2... | collective-permute-start | bytes 829448 | tf_op jit(solution)/shard_map/ppermute | solution.py:47
  156.1 7.8 %collective-permute-start.43 = (bf16[1080,128]{1,0:T(8,128)(2,1)S(1)}, bf16[1080,128]{1,0:T(8,128)(2,1)S(1)}, u32[]{:S(2)}, u32[]{:S(2)}) collective-permute-start(bf16[1080,128]{1,0:T(8,128)(2,1)S(1)} %add_convert_fusion.3), channel_id=1, source_target_pairs={{0,8},{1,5},{8,16},{9,1},{16,24},{17,9},{24,26},{25,17},{26,18},{2... | collective-permute-start | bytes 829448 | tf_op jit(solution)/shard_map/ppermute | solution.py:47
  159.0 7.8 %collective-permute-start.28 = (bf16[1080,128]{1,0:T(8,128)(2,1)S(1)}, bf16[1080,128]{1,0:T(8,128)(2,1)S(1)}, u32[]{:S(2)}, u32[]{:S(2)}) collective-permute-start(bf16[1080,128]{1,0:T(8,128)(2,1)S(1)} %add_convert_fusion.17), channel_id=1, source_target_pairs={{0,8},{1,5},{8,16},{9,1},{16,24},{17,9},{24,26},{25,17},{26,18},{2... | collective-permute-start | bytes 829448 | tf_op jit(solution)/shard_map/ppermute | solution.py:47
  160.9 8.8 %collective-permute-start.13 = (bf16[1080,128]{1,0:T(8,128)(2,1)S(1)}, bf16[1080,128]{1,0:T(8,128)(2,1)S(1)}, u32[]{:S(2)}, u32[]{:S(2)}) collective-permute-start(bf16[1080,128]{1,0:T(8,128)(2,1)S(1)} %add_convert_fusion.31), channel_id=1, source_target_pairs={{0,8},{1,5},{8,16},{9,1},{16,24},{17,9},{24,26},{25,17},{26,18},{2... | collective-permute-start | bytes 829448 | tf_op jit(solution)/shard_map/ppermute | solution.py:47
  165.0 7.8 %collective-permute-start.44 = (bf16[1080,128]{1,0:T(8,128)(2,1)S(1)}, bf16[1080,128]{1,0:T(8,128)(2,1)S(1)}, u32[]{:S(2)}, u32[]{:S(2)}) collective-permute-start(bf16[1080,128]{1,0:T(8,128)(2,1)S(1)} %add_convert_fusion.2), channel_id=1, source_target_pairs={{0,8},{1,5},{8,16},{9,1},{16,24},{17,9},{24,26},{25,17},{26,18},{2... | collective-permute-start | bytes 829448 | tf_op jit(solution)/shard_map/ppermute | solution.py:47
  167.9 7.8 %collective-permute-start.29 = (bf16[1080,128]{1,0:T(8,128)(2,1)S(1)}, bf16[1080,128]{1,0:T(8,128)(2,1)S(1)}, u32[]{:S(2)}, u32[]{:S(2)}) collective-permute-start(bf16[1080,128]{1,0:T(8,128)(2,1)S(1)} %add_convert_fusion.16), channel_id=1, source_target_pairs={{0,8},{1,5},{8,16},{9,1},{16,24},{17,9},{24,26},{25,17},{26,18},{2... | collective-permute-start | bytes 829448 | tf_op jit(solution)/shard_map/ppermute | solution.py:47
  169.8 8.8 %collective-permute-start.14 = (bf16[1080,128]{1,0:T(8,128)(2,1)S(1)}, bf16[1080,128]{1,0:T(8,128)(2,1)S(1)}, u32[]{:S(2)}, u32[]{:S(2)}) collective-permute-start(bf16[1080,128]{1,0:T(8,128)(2,1)S(1)} %add_convert_fusion.30), channel_id=1, source_target_pairs={{0,8},{1,5},{8,16},{9,1},{16,24},{17,9},{24,26},{25,17},{26,18},{2... | collective-permute-start | bytes 829448 | tf_op jit(solution)/shard_map/ppermute | solution.py:47
  173.8 7.8 %collective-permute-start.45 = (bf16[1080,128]{1,0:T(8,128)(2,1)S(1)}, bf16[1080,128]{1,0:T(8,128)(2,1)S(1)}, u32[]{:S(2)}, u32[]{:S(2)}) collective-permute-start(bf16[1080,128]{1,0:T(8,128)(2,1)S(1)} %add_convert_fusion.1), channel_id=1, source_target_pairs={{0,8},{1,5},{8,16},{9,1},{16,24},{17,9},{24,26},{25,17},{26,18},{2... | collective-permute-start | bytes 829448 | tf_op jit(solution)/shard_map/ppermute | solution.py:47
  176.8 7.8 %collective-permute-start.30 = (bf16[1080,128]{1,0:T(8,128)(2,1)S(1)}, bf16[1080,128]{1,0:T(8,128)(2,1)S(1)}, u32[]{:S(2)}, u32[]{:S(2)}) collective-permute-start(bf16[1080,128]{1,0:T(8,128)(2,1)S(1)} %add_convert_fusion.15), channel_id=1, source_target_pairs={{0,8},{1,5},{8,16},{9,1},{16,24},{17,9},{24,26},{25,17},{26,18},{2... | collective-permute-start | bytes 829448 | tf_op jit(solution)/shard_map/ppermute | solution.py:47
  178.7 8.8 %collective-permute-start.15 = (bf16[1080,128]{1,0:T(8,128)(2,1)S(1)}, bf16[1080,128]{1,0:T(8,128)(2,1)S(1)}, u32[]{:S(2)}, u32[]{:S(2)}) collective-permute-start(bf16[1080,128]{1,0:T(8,128)(2,1)S(1)} %add_convert_fusion.29), channel_id=1, source_target_pairs={{0,8},{1,5},{8,16},{9,1},{16,24},{17,9},{24,26},{25,17},{26,18},{2... | collective-permute-start | bytes 829448 | tf_op jit(solution)/shard_map/ppermute | solution.py:47
  182.7 7.8 %collective-permute-start.46 = (bf16[1080,128]{1,0:T(8,128)(2,1)S(1)}, bf16[1080,128]{1,0:T(8,128)(2,1)S(1)}, u32[]{:S(2)}, u32[]{:S(2)}) collective-permute-start(bf16[1080,128]{1,0:T(8,128)(2,1)S(1)} %add_convert_fusion), channel_id=1, source_target_pairs={{0,8},{1,5},{8,16},{9,1},{16,24},{17,9},{24,26},{25,17},{26,18},{2... | collective-permute-start | bytes 829448 | tf_op jit(solution)/shard_map/ppermute | solution.py:47
  185.7 7.8 %collective-permute-start.31 = (bf16[1080,128]{1,0:T(8,128)(2,1)S(1)}, bf16[1080,128]{1,0:T(8,128)(2,1)S(1)}, u32[]{:S(2)}, u32[]{:S(2)}) collective-permute-start(bf16[1080,128]{1,0:T(8,128)(2,1)S(1)} %add_convert_fusion.14), channel_id=1, source_target_pairs={{0,8},{1,5},{8,16},{9,1},{16,24},{17,9},{24,26},{25,17},{26,18},{2... | collective-permute-start | bytes 829448 | tf_op jit(solution)/shard_map/ppermute | solution.py:47
  187.6 8.8 %collective-permute-start.16 = (bf16[1080,128]{1,0:T(8,128)(2,1)S(1)}, bf16[1080,128]{1,0:T(8,128)(2,1)S(1)}, u32[]{:S(2)}, u32[]{:S(2)}) collective-permute-start(bf16[1080,128]{1,0:T(8,128)(2,1)S(1)} %add_convert_fusion.28), channel_id=1, source_target_pairs={{0,8},{1,5},{8,16},{9,1},{16,24},{17,9},{24,26},{25,17},{26,18},{2... | collective-permute-start | bytes 829448 | tf_op jit(solution)/shard_map/ppermute | solution.py:47
  (6 other events, 183.1 us)

commit v14 on v12

--- a/solution.py
+++ b/solution.py
@@ -53,7 +53,7 @@
                gg_ref, gu_ref, gd_ref, dxt_ref):
     slots = gg_ref.shape[1]
     f32 = jnp.float32
-    offs = [pl.multiple_of(col_ref[h, p] * BLK, BLK) for p in range(slots)]
+    offs = [pl.multiple_of(col_ref[p, h] * BLK, BLK) for p in range(slots)]
     x = jnp.concatenate([tok_ref[:, pl.ds(o, BLK)] for o in offs], axis=1)
     dy = jnp.concatenate([cot_ref[:, pl.ds(o, BLK)] for o in offs], axis=1)
     stacked = (slots * BLK, BLK)
@@ -129,7 +129,7 @@
             bytes_accessed=3 * hblk * slots * BLK * BLK * 6 + rows * width * 8,
         ),
         name="ffn_block_terms",
-    )(col_index, row_count, full_tok, full_cot, gate_w, up_w, down_w)
+    )(col_index.T, row_count, full_tok, full_cot, gate_w, up_w, down_w)
 
 
 def shards(n_dp, n_t, tokens, cotangent, w_gate, w_up, w_down, col_index, row_count, adam_m, adam_v):

time: 200 us -> 199 us (level)
  transfers between devices with their start and end apart: 47 -> 47, of which waited for: 34 -> 35; matrix products, arithmetic and copies ran while one was open for 24% -> 24% of each run, Pallas kernels for 0% -> 0%
where the time goes in v14:
time: 199 us; the launch traced here: 197 us
  starting transfers between devices  75.6 us (38%)
  other arithmetic  50.5 us (25%)
  Pallas kernels  24.1 us (12%)
  between operations  21.8 us (11%)
  waiting for transfers between devices  18.9 us (9%)
  local copies, waits for them, and re-layouts  5.73 us (3%)
    ppermute x45, starting transfers between devices, ring_reduce_scatter(): moved = lax.ppermute(accs[i].astype(wire_dtype), ('dp', 'tensor'), perm)  75 us
    convert_element_type x42, other arithmetic, ring_reduce_scatter(): moved = lax.ppermute(accs[i].astype(wire_dtype), ('dp', 'tensor'), perm)  38.7 us
    pallas_call x1, Pallas kernels, ffn_block_terms(): pl.pallas_call(_ffn_kernel, grid_spec=pltpu.PrefetchScalarGridSpec(num_sc...  24.1 us
    ppermute x45, waiting for transfers between devices, ring_reduce_scatter(): moved = lax.ppermute(accs[i].astype(wire_dtype), ('dp', 'tensor'), perm)  18.9 us
  transfers between devices with their start and end apart: 47, of which 35 were waited for; matrix products, arithmetic and copies ran while one was open for 24% of the time, Pallas kernels for 0%

profile of v14, /device:TPU:0, one launch (start us, length us, event | category | flops | bytes accessed | tf_op | source)
XLA Modules:
  0.0 196.7 jit_solution(17146541275381009444)
XLA Ops:
  26.4 1.8 pad_maximum_fusion.2
  28.2 24.1 %ffn_block_terms.1 = (f32[27,5,128,128]{3,2,1,0:T(8,128)}, f32[27,5,128,128]{3,2,1,0:T(8,128)}, f32[27,5,128,128]{3,2,1,0:T(8,128)}, f32[5120,128]{1,0:T(8,128)}) custom-call(s32[5,27]{1,0:T(8,128)} %bitcast.105, s32[27]{0:T(128)} %cnt_ref.1, bf16[128,5120]{1,0:T(8,128)(2,1)} %get-tuple-element.41.tok_ref, bf16[128,5120]{1,0:T(8,128)(2,1)} %get-tuple-element.42.cot_ref, ...), custom_call_target="tpu_custom_call" | custom-call | flops 5096079360 | bytes 45056000 | tf_op jit(solution)/shard_map/ffn_block_terms/pallas_call | solution.py:116
  52.3 1.8 fusion.1
  55.4 3.1 %collective-permute-start.32 = (bf16[1080,128]{1,0:T(8,128)(2,1)S(1)}, bf16[1080,128]{1,0:T(8,128)(2,1)S(1)}, u32[]{:S(2)}, u32[]{:S(2)}) collective-permute-start(bf16[1080,128]{1,0:T(8,128)(2,1)S(1)} %dynamic-slice_convert_fusion), channel_id=1, source_target_pairs={{0,8},{1,5},{8,16},{9,1},{16,24},{17,9},{24,26},{25,17},{26,18},{2... | collective-permute-start | bytes 829448 | tf_op jit(solution)/shard_map/ppermute | solution.py:47
  59.5 1.6 collective-permute-start.17
  62.3 1.6 collective-permute-start.2
  65.0 1.5 collective-permute-start.33
  70.3 1.8 collective-permute-start.3
  73.2 1.8 collective-permute-start.34
  76.2 1.8 collective-permute-start.19
  79.2 1.8 collective-permute-start.4
  83.6 1.6 collective-permute-start.35
  86.3 1.6 collective-permute-start.20
  94.2 1.6 collective-permute-start.21
  97.2 1.6 collective-permute-start.6
  100.2 1.6 collective-permute-start.37
  103.1 1.6 collective-permute-start.22
  106.1 1.6 collective-permute-start.7
  109.0 1.6 collective-permute-start.38
  112.0 1.6 collective-permute-start.23
  115.0 1.6 collective-permute-start.8
  117.9 1.6 collective-permute-start.39
  120.9 1.6 collective-permute-start.24
  122.8 1.6 collective-permute-start.9
  126.8 1.6 collective-permute-start.40
  129.8 1.6 collective-permute-start.25
  131.7 1.6 collective-permute-start.10
  135.7 1.6 collective-permute-start.41
  138.7 1.6 collective-permute-start.26
  140.6 1.8 collective-permute-start.11
  144.6 1.6 collective-permute-start.42
  147.6 1.6 collective-permute-start.27
  149.5 1.6 collective-permute-start.12
  153.5 1.6 collective-permute-start.43
  156.4 1.6 collective-permute-start.28
  158.4 1.6 collective-permute-start.13
  162.4 1.6 collective-permute-start.44
  165.3 1.6 collective-permute-start.29
  167.2 1.6 collective-permute-start.14
  171.3 1.6 collective-permute-start.45
  174.2 1.6 collective-permute-start.30
  176.1 1.6 collective-permute-start.15
  180.1 1.6 collective-permute-start.46
  183.1 1.6 collective-permute-start.31
  185.0 1.6 collective-permute-start.16
  189.0 1.9 collective-permute-done.31
  192.0 1.9 collective-permute-done.16
  193.9 2.8 %add_divide_fusion = (f32[3,1,1080,128]{3,2,1,0:T(8,128)}, f32[3,1,1080,128]{3,2,1,0:T(8,128)}, f32[3,1,1080,128]{3,2,1,0:T(8,128)}) fusion(f32[1,1,1080,128]{3,2,1,0:T(8,128)S(1)} %add_bitcast_fusion, f32[1,1,1080,128]{3,2,1,0:T(8,128)S(1)} %add_bitcast_fusion.1, f32[1,1,1080,128]{3,2,1,0:T(8,128)S(1)} %add_bitcast_fusion.2, ...), kind=kLoop, calls=%fused_computation.1 | loop fusion | flops 4976640 | bytes 9953280 | tf_op jit(solution)/shard_map/div | solution.py:177
  (125 shorter events, 69.8 us)
Async XLA Ops:
  2.2 22.7 %collective-permute-start = (bf16[2,128,2560]{2,1,0:T(8,128)(2,1)S(1)}, bf16[2,128,2560]{2,1,0:T(8,128)(2,1)}, u32[]{:S(2)}, u32[]{:S(2)}) collective-permute-start(bf16[2,128,2560]{2,1,0:T(8,128)(2,1)S(1)} %pad_maximum_fusion.1), channel_id=1, source_target_pairs={{0,1},{1,0},{2,3},{3,2},{4,5},{5,4},{6,7},{7,6},{8,9},{9,8},{10,11... | collective-permute-start | bytes 3932168 | tf_op jit(solution)/shard_map/ppermute | solution.py:139
  54.2 26.9 %collective-permute-start.1 = (bf16[128,2560]{0,1:T(8,128)(2,1)S(1)}, bf16[128,2560]{0,1:T(8,128)(2,1)S(1)}, u32[]{:S(2)}, u32[]{:S(2)}) collective-permute-start(bf16[128,2560]{0,1:T(8,128)(2,1)S(1)} %fusion.1), channel_id=1, source_target_pairs={{0,1},{1,0},{2,3},{3,2},{4,5},{5,4},{6,7},{7,6},{8,9},{9,8},{10,11... | collective-permute-start | bytes 1966088 | tf_op jit(solution)/shard_map/ppermute | solution.py:167
  55.4 8.5 %collective-permute-start.32 = (bf16[1080,128]{1,0:T(8,128)(2,1)S(1)}, bf16[1080,128]{1,0:T(8,128)(2,1)S(1)}, u32[]{:S(2)}, u32[]{:S(2)}) collective-permute-start(bf16[1080,128]{1,0:T(8,128)(2,1)S(1)} %dynamic-slice_convert_fusion), channel_id=1, source_target_pairs={{0,8},{1,5},{8,16},{9,1},{16,24},{17,9},{24,26},{25,17},{26,18},{2... | collective-permute-start | bytes 829448 | tf_op jit(solution)/shard_map/ppermute | solution.py:47
  59.5 7.0 %collective-permute-start.17 = (bf16[1080,128]{1,0:T(8,128)(2,1)S(1)}, bf16[1080,128]{1,0:T(8,128)(2,1)S(1)}, u32[]{:S(2)}, u32[]{:S(2)}) collective-permute-start(bf16[1080,128]{1,0:T(8,128)(2,1)S(1)} %dynamic-slice_convert_fusion.1), channel_id=1, source_target_pairs={{0,8},{1,5},{8,16},{9,1},{16,24},{17,9},{24,26},{25,17},{26,18},{2... | collective-permute-start | bytes 829448 | tf_op jit(solution)/shard_map/ppermute | solution.py:47
  62.3 6.9 %collective-permute-start.2 = (bf16[1080,128]{1,0:T(8,128)(2,1)S(1)}, bf16[1080,128]{1,0:T(8,128)(2,1)S(1)}, u32[]{:S(2)}, u32[]{:S(2)}) collective-permute-start(bf16[1080,128]{1,0:T(8,128)(2,1)S(1)} %dynamic-slice_convert_fusion.2), channel_id=1, source_target_pairs={{0,8},{1,5},{8,16},{9,1},{16,24},{17,9},{24,26},{25,17},{26,18},{2... | collective-permute-start | bytes 829448 | tf_op jit(solution)/shard_map/ppermute | solution.py:47
  65.0 7.1 %collective-permute-start.33 = (bf16[1080,128]{1,0:T(8,128)(2,1)S(1)}, bf16[1080,128]{1,0:T(8,128)(2,1)S(1)}, u32[]{:S(2)}, u32[]{:S(2)}) collective-permute-start(bf16[1080,128]{1,0:T(8,128)(2,1)S(1)} %add_convert_fusion.13), channel_id=1, source_target_pairs={{0,8},{1,5},{8,16},{9,1},{16,24},{17,9},{24,26},{25,17},{26,18},{2... | collective-permute-start | bytes 829448 | tf_op jit(solution)/shard_map/ppermute | solution.py:47
  67.7 7.4 %collective-permute-start.18 = (bf16[1080,128]{1,0:T(8,128)(2,1)S(1)}, bf16[1080,128]{1,0:T(8,128)(2,1)S(1)}, u32[]{:S(2)}, u32[]{:S(2)}) collective-permute-start(bf16[1080,128]{1,0:T(8,128)(2,1)S(1)} %add_convert_fusion.27), channel_id=1, source_target_pairs={{0,8},{1,5},{8,16},{9,1},{16,24},{17,9},{24,26},{25,17},{26,18},{2... | collective-permute-start | bytes 829448 | tf_op jit(solution)/shard_map/ppermute | solution.py:47
  70.3 7.8 %collective-permute-start.3 = (bf16[1080,128]{1,0:T(8,128)(2,1)S(1)}, bf16[1080,128]{1,0:T(8,128)(2,1)S(1)}, u32[]{:S(2)}, u32[]{:S(2)}) collective-permute-start(bf16[1080,128]{1,0:T(8,128)(2,1)S(1)} %add_convert_fusion.41), channel_id=1, source_target_pairs={{0,8},{1,5},{8,16},{9,1},{16,24},{17,9},{24,26},{25,17},{26,18},{2... | collective-permute-start | bytes 829448 | tf_op jit(solution)/shard_map/ppermute | solution.py:47
  73.2 9.1 %collective-permute-start.34 = (bf16[1080,128]{1,0:T(8,128)(2,1)S(1)}, bf16[1080,128]{1,0:T(8,128)(2,1)S(1)}, u32[]{:S(2)}, u32[]{:S(2)}) collective-permute-start(bf16[1080,128]{1,0:T(8,128)(2,1)S(1)} %add_convert_fusion.12), channel_id=1, source_target_pairs={{0,8},{1,5},{8,16},{9,1},{16,24},{17,9},{24,26},{25,17},{26,18},{2... | collective-permute-start | bytes 829448 | tf_op jit(solution)/shard_map/ppermute | solution.py:47
  76.2 9.0 %collective-permute-start.19 = (bf16[1080,128]{1,0:T(8,128)(2,1)S(1)}, bf16[1080,128]{1,0:T(8,128)(2,1)S(1)}, u32[]{:S(2)}, u32[]{:S(2)}) collective-permute-start(bf16[1080,128]{1,0:T(8,128)(2,1)S(1)} %add_convert_fusion.26), channel_id=1, source_target_pairs={{0,8},{1,5},{8,16},{9,1},{16,24},{17,9},{24,26},{25,17},{26,18},{2... | collective-permute-start | bytes 829448 | tf_op jit(solution)/shard_map/ppermute | solution.py:47
  78.0 44.7 %slice-start = ((s8[8847360]{0:T(1024)(128)(4,1)}), s8[458752]{0:T(1024)(128)(4,1)S(1)}, s32[]{:S(2)}) async-start(s8[8847360]{0:T(1024)(128)(4,1)} %bitcast.57), calls=%async_computation | async-start | bytes 917504
  79.2 8.8 %collective-permute-start.4 = (bf16[1080,128]{1,0:T(8,128)(2,1)S(1)}, bf16[1080,128]{1,0:T(8,128)(2,1)S(1)}, u32[]{:S(2)}, u32[]{:S(2)}) collective-permute-start(bf16[1080,128]{1,0:T(8,128)(2,1)S(1)} %add_convert_fusion.40), channel_id=1, source_target_pairs={{0,8},{1,5},{8,16},{9,1},{16,24},{17,9},{24,26},{25,17},{26,18},{2... | collective-permute-start | bytes 829448 | tf_op jit(solution)/shard_map/ppermute | solution.py:47
  83.6 7.0 %collective-permute-start.35 = (bf16[1080,128]{1,0:T(8,128)(2,1)S(1)}, bf16[1080,128]{1,0:T(8,128)(2,1)S(1)}, u32[]{:S(2)}, u32[]{:S(2)}) collective-permute-start(bf16[1080,128]{1,0:T(8,128)(2,1)S(1)} %add_convert_fusion.11), channel_id=1, source_target_pairs={{0,8},{1,5},{8,16},{9,1},{16,24},{17,9},{24,26},{25,17},{26,18},{2... | collective-permute-start | bytes 829448 | tf_op jit(solution)/shard_map/ppermute | solution.py:47
  86.3 6.8 %collective-permute-start.20 = (bf16[1080,128]{1,0:T(8,128)(2,1)S(1)}, bf16[1080,128]{1,0:T(8,128)(2,1)S(1)}, u32[]{:S(2)}, u32[]{:S(2)}) collective-permute-start(bf16[1080,128]{1,0:T(8,128)(2,1)S(1)} %add_convert_fusion.25), channel_id=1, source_target_pairs={{0,8},{1,5},{8,16},{9,1},{16,24},{17,9},{24,26},{25,17},{26,18},{2... | collective-permute-start | bytes 829448 | tf_op jit(solution)/shard_map/ppermute | solution.py:47
  89.1 7.0 %collective-permute-start.5 = (bf16[1080,128]{1,0:T(8,128)(2,1)S(1)}, bf16[1080,128]{1,0:T(8,128)(2,1)S(1)}, u32[]{:S(2)}, u32[]{:S(2)}) collective-permute-start(bf16[1080,128]{1,0:T(8,128)(2,1)S(1)} %add_convert_fusion.39), channel_id=1, source_target_pairs={{0,8},{1,5},{8,16},{9,1},{16,24},{17,9},{24,26},{25,17},{26,18},{2... | collective-permute-start | bytes 829448 | tf_op jit(solution)/shard_map/ppermute | solution.py:47
  91.7 7.3 %collective-permute-start.36 = (bf16[1080,128]{1,0:T(8,128)(2,1)S(1)}, bf16[1080,128]{1,0:T(8,128)(2,1)S(1)}, u32[]{:S(2)}, u32[]{:S(2)}) collective-permute-start(bf16[1080,128]{1,0:T(8,128)(2,1)S(1)} %add_convert_fusion.10), channel_id=1, source_target_pairs={{0,8},{1,5},{8,16},{9,1},{16,24},{17,9},{24,26},{25,17},{26,18},{2... | collective-permute-start | bytes 829448 | tf_op jit(solution)/shard_map/ppermute | solution.py:47
  94.2 7.8 %collective-permute-start.21 = (bf16[1080,128]{1,0:T(8,128)(2,1)S(1)}, bf16[1080,128]{1,0:T(8,128)(2,1)S(1)}, u32[]{:S(2)}, u32[]{:S(2)}) collective-permute-start(bf16[1080,128]{1,0:T(8,128)(2,1)S(1)} %add_convert_fusion.24), channel_id=1, source_target_pairs={{0,8},{1,5},{8,16},{9,1},{16,24},{17,9},{24,26},{25,17},{26,18},{2... | collective-permute-start | bytes 829448 | tf_op jit(solution)/shard_map/ppermute | solution.py:47
  97.2 7.8 %collective-permute-start.6 = (bf16[1080,128]{1,0:T(8,128)(2,1)S(1)}, bf16[1080,128]{1,0:T(8,128)(2,1)S(1)}, u32[]{:S(2)}, u32[]{:S(2)}) collective-permute-start(bf16[1080,128]{1,0:T(8,128)(2,1)S(1)} %add_convert_fusion.38), channel_id=1, source_target_pairs={{0,8},{1,5},{8,16},{9,1},{16,24},{17,9},{24,26},{25,17},{26,18},{2... | collective-permute-start | bytes 829448 | tf_op jit(solution)/shard_map/ppermute | solution.py:47
  100.2 7.8 %collective-permute-start.37 = (bf16[1080,128]{1,0:T(8,128)(2,1)S(1)}, bf16[1080,128]{1,0:T(8,128)(2,1)S(1)}, u32[]{:S(2)}, u32[]{:S(2)}) collective-permute-start(bf16[1080,128]{1,0:T(8,128)(2,1)S(1)} %add_convert_fusion.9), channel_id=1, source_target_pairs={{0,8},{1,5},{8,16},{9,1},{16,24},{17,9},{24,26},{25,17},{26,18},{2... | collective-permute-start | bytes 829448 | tf_op jit(solution)/shard_map/ppermute | solution.py:47
  103.1 7.8 %collective-permute-start.22 = (bf16[1080,128]{1,0:T(8,128)(2,1)S(1)}, bf16[1080,128]{1,0:T(8,128)(2,1)S(1)}, u32[]{:S(2)}, u32[]{:S(2)}) collective-permute-start(bf16[1080,128]{1,0:T(8,128)(2,1)S(1)} %add_convert_fusion.23), channel_id=1, source_target_pairs={{0,8},{1,5},{8,16},{9,1},{16,24},{17,9},{24,26},{25,17},{26,18},{2... | collective-permute-start | bytes 829448 | tf_op jit(solution)/shard_map/ppermute | solution.py:47
  106.1 7.8 %collective-permute-start.7 = (bf16[1080,128]{1,0:T(8,128)(2,1)S(1)}, bf16[1080,128]{1,0:T(8,128)(2,1)S(1)}, u32[]{:S(2)}, u32[]{:S(2)}) collective-permute-start(bf16[1080,128]{1,0:T(8,128)(2,1)S(1)} %add_convert_fusion.37), channel_id=1, source_target_pairs={{0,8},{1,5},{8,16},{9,1},{16,24},{17,9},{24,26},{25,17},{26,18},{2... | collective-permute-start | bytes 829448 | tf_op jit(solution)/shard_map/ppermute | solution.py:47
  109.0 7.8 %collective-permute-start.38 = (bf16[1080,128]{1,0:T(8,128)(2,1)S(1)}, bf16[1080,128]{1,0:T(8,128)(2,1)S(1)}, u32[]{:S(2)}, u32[]{:S(2)}) collective-permute-start(bf16[1080,128]{1,0:T(8,128)(2,1)S(1)} %add_convert_fusion.8), channel_id=1, source_target_pairs={{0,8},{1,5},{8,16},{9,1},{16,24},{17,9},{24,26},{25,17},{26,18},{2... | collective-permute-start | bytes 829448 | tf_op jit(solution)/shard_map/ppermute | solution.py:47
  112.0 7.8 %collective-permute-start.23 = (bf16[1080,128]{1,0:T(8,128)(2,1)S(1)}, bf16[1080,128]{1,0:T(8,128)(2,1)S(1)}, u32[]{:S(2)}, u32[]{:S(2)}) collective-permute-start(bf16[1080,128]{1,0:T(8,128)(2,1)S(1)} %add_convert_fusion.22), channel_id=1, source_target_pairs={{0,8},{1,5},{8,16},{9,1},{16,24},{17,9},{24,26},{25,17},{26,18},{2... | collective-permute-start | bytes 829448 | tf_op jit(solution)/shard_map/ppermute | solution.py:47
  115.0 7.8 %collective-permute-start.8 = (bf16[1080,128]{1,0:T(8,128)(2,1)S(1)}, bf16[1080,128]{1,0:T(8,128)(2,1)S(1)}, u32[]{:S(2)}, u32[]{:S(2)}) collective-permute-start(bf16[1080,128]{1,0:T(8,128)(2,1)S(1)} %add_convert_fusion.36), channel_id=1, source_target_pairs={{0,8},{1,5},{8,16},{9,1},{16,24},{17,9},{24,26},{25,17},{26,18},{2... | collective-permute-start | bytes 829448 | tf_op jit(solution)/shard_map/ppermute | solution.py:47
  117.9 7.8 %collective-permute-start.39 = (bf16[1080,128]{1,0:T(8,128)(2,1)S(1)}, bf16[1080,128]{1,0:T(8,128)(2,1)S(1)}, u32[]{:S(2)}, u32[]{:S(2)}) collective-permute-start(bf16[1080,128]{1,0:T(8,128)(2,1)S(1)} %add_convert_fusion.7), channel_id=1, source_target_pairs={{0,8},{1,5},{8,16},{9,1},{16,24},{17,9},{24,26},{25,17},{26,18},{2... | collective-permute-start | bytes 829448 | tf_op jit(solution)/shard_map/ppermute | solution.py:47
  120.9 7.8 %collective-permute-start.24 = (bf16[1080,128]{1,0:T(8,128)(2,1)S(1)}, bf16[1080,128]{1,0:T(8,128)(2,1)S(1)}, u32[]{:S(2)}, u32[]{:S(2)}) collective-permute-start(bf16[1080,128]{1,0:T(8,128)(2,1)S(1)} %add_convert_fusion.21), channel_id=1, source_target_pairs={{0,8},{1,5},{8,16},{9,1},{16,24},{17,9},{24,26},{25,17},{26,18},{2... | collective-permute-start | bytes 829448 | tf_op jit(solution)/shard_map/ppermute | solution.py:47
  122.8 8.8 %collective-permute-start.9 = (bf16[1080,128]{1,0:T(8,128)(2,1)S(1)}, bf16[1080,128]{1,0:T(8,128)(2,1)S(1)}, u32[]{:S(2)}, u32[]{:S(2)}) collective-permute-start(bf16[1080,128]{1,0:T(8,128)(2,1)S(1)} %add_convert_fusion.35), channel_id=1, source_target_pairs={{0,8},{1,5},{8,16},{9,1},{16,24},{17,9},{24,26},{25,17},{26,18},{2... | collective-permute-start | bytes 829448 | tf_op jit(solution)/shard_map/ppermute | solution.py:47
  126.8 7.8 %collective-permute-start.40 = (bf16[1080,128]{1,0:T(8,128)(2,1)S(1)}, bf16[1080,128]{1,0:T(8,128)(2,1)S(1)}, u32[]{:S(2)}, u32[]{:S(2)}) collective-permute-start(bf16[1080,128]{1,0:T(8,128)(2,1)S(1)} %add_convert_fusion.6), channel_id=1, source_target_pairs={{0,8},{1,5},{8,16},{9,1},{16,24},{17,9},{24,26},{25,17},{26,18},{2... | collective-permute-start | bytes 829448 | tf_op jit(solution)/shard_map/ppermute | solution.py:47
  129.8 7.8 %collective-permute-start.25 = (bf16[1080,128]{1,0:T(8,128)(2,1)S(1)}, bf16[1080,128]{1,0:T(8,128)(2,1)S(1)}, u32[]{:S(2)}, u32[]{:S(2)}) collective-permute-start(bf16[1080,128]{1,0:T(8,128)(2,1)S(1)} %add_convert_fusion.20), channel_id=1, source_target_pairs={{0,8},{1,5},{8,16},{9,1},{16,24},{17,9},{24,26},{25,17},{26,18},{2... | collective-permute-start | bytes 829448 | tf_op jit(solution)/shard_map/ppermute | solution.py:47
  131.7 8.8 %collective-permute-start.10 = (bf16[1080,128]{1,0:T(8,128)(2,1)S(1)}, bf16[1080,128]{1,0:T(8,128)(2,1)S(1)}, u32[]{:S(2)}, u32[]{:S(2)}) collective-permute-start(bf16[1080,128]{1,0:T(8,128)(2,1)S(1)} %add_convert_fusion.34), channel_id=1, source_target_pairs={{0,8},{1,5},{8,16},{9,1},{16,24},{17,9},{24,26},{25,17},{26,18},{2... | collective-permute-start | bytes 829448 | tf_op jit(solution)/shard_map/ppermute | solution.py:47
  135.7 7.8 %collective-permute-start.41 = (bf16[1080,128]{1,0:T(8,128)(2,1)S(1)}, bf16[1080,128]{1,0:T(8,128)(2,1)S(1)}, u32[]{:S(2)}, u32[]{:S(2)}) collective-permute-start(bf16[1080,128]{1,0:T(8,128)(2,1)S(1)} %add_convert_fusion.5), channel_id=1, source_target_pairs={{0,8},{1,5},{8,16},{9,1},{16,24},{17,9},{24,26},{25,17},{26,18},{2... | collective-permute-start | bytes 829448 | tf_op jit(solution)/shard_map/ppermute | solution.py:47
  138.7 7.8 %collective-permute-start.26 = (bf16[1080,128]{1,0:T(8,128)(2,1)S(1)}, bf16[1080,128]{1,0:T(8,128)(2,1)S(1)}, u32[]{:S(2)}, u32[]{:S(2)}) collective-permute-start(bf16[1080,128]{1,0:T(8,128)(2,1)S(1)} %add_convert_fusion.19), channel_id=1, source_target_pairs={{0,8},{1,5},{8,16},{9,1},{16,24},{17,9},{24,26},{25,17},{26,18},{2... | collective-permute-start | bytes 829448 | tf_op jit(solution)/shard_map/ppermute | solution.py:47
  140.6 8.8 %collective-permute-start.11 = (bf16[1080,128]{1,0:T(8,128)(2,1)S(1)}, bf16[1080,128]{1,0:T(8,128)(2,1)S(1)}, u32[]{:S(2)}, u32[]{:S(2)}) collective-permute-start(bf16[1080,128]{1,0:T(8,128)(2,1)S(1)} %add_convert_fusion.33), channel_id=1, source_target_pairs={{0,8},{1,5},{8,16},{9,1},{16,24},{17,9},{24,26},{25,17},{26,18},{2... | collective-permute-start | bytes 829448 | tf_op jit(solution)/shard_map/ppermute | solution.py:47
  144.6 7.8 %collective-permute-start.42 = (bf16[1080,128]{1,0:T(8,128)(2,1)S(1)}, bf16[1080,128]{1,0:T(8,128)(2,1)S(1)}, u32[]{:S(2)}, u32[]{:S(2)}) collective-permute-start(bf16[1080,128]{1,0:T(8,128)(2,1)S(1)} %add_convert_fusion.4), channel_id=1, source_target_pairs={{0,8},{1,5},{8,16},{9,1},{16,24},{17,9},{24,26},{25,17},{26,18},{2... | collective-permute-start | bytes 829448 | tf_op jit(solution)/shard_map/ppermute | solution.py:47
  147.6 7.8 %collective-permute-start.27 = (bf16[1080,128]{1,0:T(8,128)(2,1)S(1)}, bf16[1080,128]{1,0:T(8,128)(2,1)S(1)}, u32[]{:S(2)}, u32[]{:S(2)}) collective-permute-start(bf16[1080,128]{1,0:T(8,128)(2,1)S(1)} %add_convert_fusion.18), channel_id=1, source_target_pairs={{0,8},{1,5},{8,16},{9,1},{16,24},{17,9},{24,26},{25,17},{26,18},{2... | collective-permute-start | bytes 829448 | tf_op jit(solution)/shard_map/ppermute | solution.py:47
  149.5 8.8 %collective-permute-start.12 = (bf16[1080,128]{1,0:T(8,128)(2,1)S(1)}, bf16[1080,128]{1,0:T(8,128)(2,1)S(1)}, u32[]{:S(2)}, u32[]{:S(2)}) collective-permute-start(bf16[1080,128]{1,0:T(8,128)(2,1)S(1)} %add_convert_fusion.32), channel_id=1, source_target_pairs={{0,8},{1,5},{8,16},{9,1},{16,24},{17,9},{24,26},{25,17},{26,18},{2... | collective-permute-start | bytes 829448 | tf_op jit(solution)/shard_map/ppermute | solution.py:47
  153.5 7.8 %collective-permute-start.43 = (bf16[1080,128]{1,0:T(8,128)(2,1)S(1)}, bf16[1080,128]{1,0:T(8,128)(2,1)S(1)}, u32[]{:S(2)}, u32[]{:S(2)}) collective-permute-start(bf16[1080,128]{1,0:T(8,128)(2,1)S(1)} %add_convert_fusion.3), channel_id=1, source_target_pairs={{0,8},{1,5},{8,16},{9,1},{16,24},{17,9},{24,26},{25,17},{26,18},{2... | collective-permute-start | bytes 829448 | tf_op jit(solution)/shard_map/ppermute | solution.py:47
  156.4 7.8 %collective-permute-start.28 = (bf16[1080,128]{1,0:T(8,128)(2,1)S(1)}, bf16[1080,128]{1,0:T(8,128)(2,1)S(1)}, u32[]{:S(2)}, u32[]{:S(2)}) collective-permute-start(bf16[1080,128]{1,0:T(8,128)(2,1)S(1)} %add_convert_fusion.17), channel_id=1, source_target_pairs={{0,8},{1,5},{8,16},{9,1},{16,24},{17,9},{24,26},{25,17},{26,18},{2... | collective-permute-start | bytes 829448 | tf_op jit(solution)/shard_map/ppermute | solution.py:47
  158.4 8.8 %collective-permute-start.13 = (bf16[1080,128]{1,0:T(8,128)(2,1)S(1)}, bf16[1080,128]{1,0:T(8,128)(2,1)S(1)}, u32[]{:S(2)}, u32[]{:S(2)}) collective-permute-start(bf16[1080,128]{1,0:T(8,128)(2,1)S(1)} %add_convert_fusion.31), channel_id=1, source_target_pairs={{0,8},{1,5},{8,16},{9,1},{16,24},{17,9},{24,26},{25,17},{26,18},{2... | collective-permute-start | bytes 829448 | tf_op jit(solution)/shard_map/ppermute | solution.py:47
  162.4 7.8 %collective-permute-start.44 = (bf16[1080,128]{1,0:T(8,128)(2,1)S(1)}, bf16[1080,128]{1,0:T(8,128)(2,1)S(1)}, u32[]{:S(2)}, u32[]{:S(2)}) collective-permute-start(bf16[1080,128]{1,0:T(8,128)(2,1)S(1)} %add_convert_fusion.2), channel_id=1, source_target_pairs={{0,8},{1,5},{8,16},{9,1},{16,24},{17,9},{24,26},{25,17},{26,18},{2... | collective-permute-start | bytes 829448 | tf_op jit(solution)/shard_map/ppermute | solution.py:47
  165.3 7.8 %collective-permute-start.29 = (bf16[1080,128]{1,0:T(8,128)(2,1)S(1)}, bf16[1080,128]{1,0:T(8,128)(2,1)S(1)}, u32[]{:S(2)}, u32[]{:S(2)}) collective-permute-start(bf16[1080,128]{1,0:T(8,128)(2,1)S(1)} %add_convert_fusion.16), channel_id=1, source_target_pairs={{0,8},{1,5},{8,16},{9,1},{16,24},{17,9},{24,26},{25,17},{26,18},{2... | collective-permute-start | bytes 829448 | tf_op jit(solution)/shard_map/ppermute | solution.py:47
  167.2 8.8 %collective-permute-start.14 = (bf16[1080,128]{1,0:T(8,128)(2,1)S(1)}, bf16[1080,128]{1,0:T(8,128)(2,1)S(1)}, u32[]{:S(2)}, u32[]{:S(2)}) collective-permute-start(bf16[1080,128]{1,0:T(8,128)(2,1)S(1)} %add_convert_fusion.30), channel_id=1, source_target_pairs={{0,8},{1,5},{8,16},{9,1},{16,24},{17,9},{24,26},{25,17},{26,18},{2... | collective-permute-start | bytes 829448 | tf_op jit(solution)/shard_map/ppermute | solution.py:47
  171.3 7.8 %collective-permute-start.45 = (bf16[1080,128]{1,0:T(8,128)(2,1)S(1)}, bf16[1080,128]{1,0:T(8,128)(2,1)S(1)}, u32[]{:S(2)}, u32[]{:S(2)}) collective-permute-start(bf16[1080,128]{1,0:T(8,128)(2,1)S(1)} %add_convert_fusion.1), channel_id=1, source_target_pairs={{0,8},{1,5},{8,16},{9,1},{16,24},{17,9},{24,26},{25,17},{26,18},{2... | collective-permute-start | bytes 829448 | tf_op jit(solution)/shard_map/ppermute | solution.py:47
  174.2 7.8 %collective-permute-start.30 = (bf16[1080,128]{1,0:T(8,128)(2,1)S(1)}, bf16[1080,128]{1,0:T(8,128)(2,1)S(1)}, u32[]{:S(2)}, u32[]{:S(2)}) collective-permute-start(bf16[1080,128]{1,0:T(8,128)(2,1)S(1)} %add_convert_fusion.15), channel_id=1, source_target_pairs={{0,8},{1,5},{8,16},{9,1},{16,24},{17,9},{24,26},{25,17},{26,18},{2... | collective-permute-start | bytes 829448 | tf_op jit(solution)/shard_map/ppermute | solution.py:47
  176.1 8.8 %collective-permute-start.15 = (bf16[1080,128]{1,0:T(8,128)(2,1)S(1)}, bf16[1080,128]{1,0:T(8,128)(2,1)S(1)}, u32[]{:S(2)}, u32[]{:S(2)}) collective-permute-start(bf16[1080,128]{1,0:T(8,128)(2,1)S(1)} %add_convert_fusion.29), channel_id=1, source_target_pairs={{0,8},{1,5},{8,16},{9,1},{16,24},{17,9},{24,26},{25,17},{26,18},{2... | collective-permute-start | bytes 829448 | tf_op jit(solution)/shard_map/ppermute | solution.py:47
  180.1 7.8 %collective-permute-start.46 = (bf16[1080,128]{1,0:T(8,128)(2,1)S(1)}, bf16[1080,128]{1,0:T(8,128)(2,1)S(1)}, u32[]{:S(2)}, u32[]{:S(2)}) collective-permute-start(bf16[1080,128]{1,0:T(8,128)(2,1)S(1)} %add_convert_fusion), channel_id=1, source_target_pairs={{0,8},{1,5},{8,16},{9,1},{16,24},{17,9},{24,26},{25,17},{26,18},{2... | collective-permute-start | bytes 829448 | tf_op jit(solution)/shard_map/ppermute | solution.py:47
  183.1 7.7 %collective-permute-start.31 = (bf16[1080,128]{1,0:T(8,128)(2,1)S(1)}, bf16[1080,128]{1,0:T(8,128)(2,1)S(1)}, u32[]{:S(2)}, u32[]{:S(2)}) collective-permute-start(bf16[1080,128]{1,0:T(8,128)(2,1)S(1)} %add_convert_fusion.14), channel_id=1, source_target_pairs={{0,8},{1,5},{8,16},{9,1},{16,24},{17,9},{24,26},{25,17},{26,18},{2... | collective-permute-start | bytes 829448 | tf_op jit(solution)/shard_map/ppermute | solution.py:47
  185.0 8.8 %collective-permute-start.16 = (bf16[1080,128]{1,0:T(8,128)(2,1)S(1)}, bf16[1080,128]{1,0:T(8,128)(2,1)S(1)}, u32[]{:S(2)}, u32[]{:S(2)}) collective-permute-start(bf16[1080,128]{1,0:T(8,128)(2,1)S(1)} %add_convert_fusion.28), channel_id=1, source_target_pairs={{0,8},{1,5},{8,16},{9,1},{16,24},{17,9},{24,26},{25,17},{26,18},{2... | collective-permute-start | bytes 829448 | tf_op jit(solution)/shard_map/ppermute | solution.py:47
  (9 other events, 164.6 us)
